TPU v7x, 32 devices: a whole 2x2x4 slice. The times are simulated.
32 devices in a mesh: groups: 2 (over y), cent: 4 (over z), dp: 2 (over x), sub: 2 (over core).
Axes of the slice: x: 2, y: 2, z: 4, core: 2. Of those that a mesh axis runs over, the one named last changes fastest.
Arguments:
- embeddings: bfloat16 [1024, 768], P(('groups', 'cent', 'dp', 'sub')), parts along dimension 0, may hold values from -6 to 6
- weights: int32 [1024], P(('groups', 'cent', 'dp', 'sub')), parts along dimension 0, may hold values from 1 to 4
- centroids: bfloat16 [16384, 768], P(('groups', 'cent')), parts along dimension 0, may hold values from -6 to 6
- inverse_temp: float32 [1], replicated, may hold values from 16 to 256
Outputs:
- centroid_sums: float32 [16384, 768], P(('groups', 'cent', 'dp', 'sub')), parts along dimension 0
- renormed: bfloat16 [16384, 768], P(('groups', 'cent', 'dp', 'sub')), parts along dimension 0
- objective: float32 [1024], P(('groups', 'cent', 'dp', 'sub')), parts along dimension 0
There are 2 independent parts, one for each index of `groups`. A program takes and returns all parts, laid end to end along the dimension named above; an argument that names none is the same for every part. Nothing has to cross between parts.
All inputs are finite; a program needn't handle non-finite values.
Results may differ from a plain program's by a relative error of at most 0.0075.
The roundings to bfloat16 on the way count: a program that leaves them out, or rounds other values in their place, can miss the bound.
Values may be sent and summed in bfloat16 or wider, within the bound.
No kernel may reach another device: no remote copies, remote signals or barrier semaphores. Data moves between devices by JAX's collectives and lax.ppermute only.
A program may use at most 64 MiB of HBM per device.

v0:
```python
import jax
import jax.numpy as jnp
from jax import lax
from jax.sharding import PartitionSpec as P


def normalize(values):
    floats = values.astype(jnp.float32)
    return floats * lax.rsqrt(jnp.sum(floats * floats, axis=-1, keepdims=True) + 1e-06)


def shards(embeddings, weights, centroids, inverse_temp):
    sharpness = inverse_temp[0]
    unit_rows = normalize(embeddings).astype(jnp.bfloat16)
    unit_panel = normalize(centroids).astype(jnp.bfloat16)
    gathered_rows, gathered_weights = (
        lax.all_gather(unit_rows, "cent", axis=0, tiled=True),
        lax.all_gather(weights, "cent", axis=0, tiled=True),
    )
    scores = (
        lax.dot_general(
            gathered_rows, unit_panel, (((1,), (1,)), ((), ())), preferred_element_type=jnp.float32
        )
        * sharpness
    )
    local_peak = jnp.max(scores, axis=1)
    row_peak = lax.pmax(local_peak, "cent")
    row_total = lax.psum(jnp.sum(jnp.exp(scores - row_peak[:, None]), axis=1), "cent")
    log_sum = row_peak + jnp.log(row_total)
    weight_float = gathered_weights.astype(jnp.float32)
    responsibility = (weight_float[:, None] * jnp.exp(scores - log_sum[:, None])).astype(
        jnp.bfloat16
    )
    partial_value = lax.dot_general(
        responsibility, gathered_rows, (((0,), (0,)), ((), ())), preferred_element_type=jnp.float32
    ).astype(jnp.bfloat16)
    ones_row = jnp.ones((1, responsibility.shape[0]), jnp.bfloat16)
    weight_mass = jnp.dot(ones_row, responsibility, preferred_element_type=jnp.float32)[0].astype(
        jnp.bfloat16
    )
    own_count = centroids.shape[0] // lax.axis_size(("dp", "sub"))
    offset = lax.axis_index(("dp", "sub")) * own_count
    panel_sums, panel_mass = (
        lax.psum(partial_value, ("dp", "sub")).astype(jnp.float32),
        lax.psum(weight_mass, ("dp", "sub")).astype(jnp.float32),
    )
    centroid_sums = lax.dynamic_slice_in_dim(panel_sums, offset, own_count, 0)
    own_mass = lax.dynamic_slice_in_dim(panel_mass, offset, own_count, 0)
    own_cents = lax.dynamic_slice_in_dim(unit_panel, offset, own_count, 0).astype(jnp.float32)
    moved = own_cents + centroid_sums / (own_mass + 1.0)[:, None]
    renormed = normalize(moved).astype(jnp.bfloat16)
    row_offset = lax.axis_index("cent") * embeddings.shape[0]
    weighted_log_sum = weight_float * log_sum / sharpness
    objective = lax.dynamic_slice_in_dim(weighted_log_sum, row_offset, embeddings.shape[0], 0)
    return (centroid_sums, renormed, objective)


def solution(mesh):
    in_specs = (
        P(("groups", "cent", "dp", "sub"), None),
        P(("groups", "cent", "dp", "sub")),
        P(("groups", "cent"), None),
        P(),
    )
    out_specs = (
        P(("groups", "cent", "dp", "sub"), None),
        P(("groups", "cent", "dp", "sub"), None),
        P(("groups", "cent", "dp", "sub")),
    )
    return jax.shard_map(shards, mesh=mesh, in_specs=in_specs, out_specs=out_specs, check_vma=False)
```

profile of v0, /device:TPU:0, one launch (start us, length us, event | category | flops | bytes accessed | tf_op | source)
XLA Modules:
  0.0 144.0 jit_solution(1710212666322466163)
XLA Ops:
  7.2 0.0 copy-start.3
  7.2 0.0 all-reduce.3.cloned.1.call-start
  7.9 0.9 fusion.2
  8.8 1.2 dynamic-slice
  10.7 0.9 dynamic-update-slice
  11.6 9.9 %all-reduce = s32[128]{0:T(128)S(1)} all-reduce(s32[128]{0:T(128)S(1)} %dynamic-update-slice), channel_id=1, replica_groups=mesh['groups'=2,'cent'=4,'dp'=2,'sub'=2] {'cent'}, use_global_device_ids=true, to_apply=%add | all-reduce | flops 128 | bytes 1024
  21.5 0.0 copy-start
  21.5 2.7 %fusion = f32[2048]{0:T(1024)S(1)} fusion(bf16[2048,768]{1,0:T(8,128)(2,1)} %param.6), kind=kLoop, calls=%fused_computation.2 | loop fusion | flops 4716544 | bytes 3153920 | tf_op jit(solution)/shard_map/reduce_sum | solution.py:9
  24.2 0.0 copy-done.3
  24.2 0.1 fusion.3
  24.3 13.6 %all_gather.7 = bf16[128,768]{1,0:T(8,128)(2,1)S(1)} all-gather(bf16[32,768]{1,0:T(8,128)(2,1)S(1)} %fusion.3), channel_id=1, replica_groups=mesh['groups'=2,'cent'=4,'dp'=2,'sub'=2] {'cent'}, dimensions={0}, use_global_device_ids=true | all-gather | bytes 245760 | tf_op jit(solution)/shard_map/all_gather | solution.py:17
  37.9 0.0 copy-done
  37.9 0.6 fusion.1
  38.4 2.1 %fusion.7 = (f32[128]{0:T(128)S(1)}, f32[128,2048]{1,0:T(8,128)}) fusion(f32[]{:T(128)} %bitcast.8, bf16[128,768]{1,0:T(8,128)(2,1)S(1)} %all_gather.7, bf16[2048,768]{1,0:T(8,128)(2,1)S(1)} %fusion.1), kind=kOutput, calls=%fused_computation.25 | convolution fusion | flops 403177344 | bytes 4391428 | tf_op jit(solution)/shard_map/dot_general | solution.py:21
  40.6 10.4 %pmax.7 = f32[128]{0:T(128)S(1)} all-reduce(f32[128]{0:T(128)S(1)} %get-tuple-element.7), channel_id=1, replica_groups=mesh['groups'=2,'cent'=4,'dp'=2,'sub'=2] {'cent'}, use_global_device_ids=true, to_apply=%region_3.0 | all-reduce | flops 128 | bytes 1024 | tf_op jit(solution)/shard_map/pmax | solution.py:27
  51.0 1.5 %exponential_reduce_fusion = f32[128]{0:T(128)S(1)} fusion(f32[128,2048]{1,0:T(8,128)} %get-tuple-element.8, f32[128]{0:T(128)S(1)} %pmax.7), kind=kLoop, calls=%fused_computation.10 | loop fusion | flops 524160 | bytes 1049600 | tf_op jit(solution)/shard_map/reduce_sum | solution.py:28
  52.5 8.4 %psum.21 = f32[128]{0:T(128)S(1)} all-reduce(f32[128]{0:T(128)S(1)} %exponential_reduce_fusion), channel_id=1, replica_groups=mesh['groups'=2,'cent'=4,'dp'=2,'sub'=2] {'cent'}, use_global_device_ids=true, to_apply=%region_5.0 | all-reduce | flops 128 | bytes 1024 | tf_op jit(solution)/shard_map/psum | solution.py:28
  60.9 1.5 %multiply_convert_fusion.1 = bf16[128,2048]{1,0:T(8,128)(2,1)S(1)} fusion(f32[128,2048]{1,0:T(8,128)} %get-tuple-element.8, f32[128]{0:T(128)S(1)} %get-tuple-element.4, f32[128]{0:T(128)S(1)} %convert_element_type.36), kind=kLoop, calls=%fused_computation.9 | loop fusion | flops 786432 | bytes 1573888 | tf_op jit(solution)/shard_map/convert_element_type | solution.py:31
  62.4 0.0 copy-start.2
  62.4 0.8 copy-done.2
  63.2 2.7 %convolution_convert_fusion = bf16[2048,768]{1,0:T(8,128)(2,1)} fusion(bf16[128,2048]{1,0:T(8,128)(2,1)S(1)} %multiply_convert_fusion.1, bf16[128,768]{1,0:T(8,128)(2,1)S(1)} %all_gather.7), kind=kOutput, calls=%fused_computation.4 | convolution fusion | flops 404226048 | bytes 3866624 | tf_op jit(solution)/shard_map/dot_general | solution.py:34
  65.9 0.0 all-reduce.3.cloned.1.call-update
  65.9 1.2 fusion.4
  67.2 0.6 dynamic_slice.15
  67.7 5.6 %psum.23 = bf16[2048]{0:T(1024)(128)(2,1)S(1)} all-reduce(bf16[2048]{0:T(1024)(128)(2,1)S(1)} %convert_element_type.45), channel_id=1, replica_groups=mesh['groups'=2,'cent'=4,'dp'=2,'sub'=2] {'dp','sub'}, use_global_device_ids=true, to_apply=%region_7.0 | all-reduce | flops 2048 | bytes 8192 | tf_op jit(solution)/shard_map/psum | solution.py:45
  73.4 0.1 convert_add_fusion
  73.5 60.7 %all-reduce.3.cloned.1.call-done = bf16[2048,768]{1,0:T(8,128)(2,1)} async-done(((bf16[2048,768]{1,0:T(8,128)(2,1)}), bf16[2048,768]{1,0:T(8,128)(2,1)}) %all-reduce.3.cloned.1.call-update) | async-done | bytes 3145744 | tf_op jit(solution)/shard_map/psum | solution.py:44
  134.2 1.6 %multiply_reduce_fusion = (f32[512]{0:T(512)S(1)}, f32[512,768]{1,0:T(8,128)S(1)}) fusion(f32[512]{0:T(512)S(1)} %convert_add_fusion, bf16[2048,768]{1,0:T(8,128)(2,1)S(1)} %fusion.1, s32[]{:T(128)S(6)} %select_n.8, bf16[2048,768]{1,0:T(8,128)(2,1)} %all-reduce.3.cloned.1.call-done), kind=kLoop, calls=%fused_computation.7 | loop fusion | flops 2358784 | bytes 3149828 | tf_op jit(solution)/shard_map/reduce_sum | solution.py:9
  135.8 0.0 copy-start.1
  135.8 1.4 multiply_convert_fusion
  137.2 0.0 copy-done.1
  (7 shorter events, 0.0 us)
Async XLA Ops:
  7.2 17.0 %copy-start.3 = (bf16[32,768]{1,0:T(8,128)(2,1)S(1)}, bf16[32,768]{1,0:T(8,128)(2,1)}, u32[]{:S(2)}) copy-start(bf16[32,768]{1,0:T(8,128)(2,1)} %param.4) | copy-start | bytes 147460
  7.2 127.0 %all-reduce.3.cloned.1.call-start = ((), (), s32[]{:S(2)}) async-start(), calls=%async_computation | async-start | bytes 6291456 | tf_op jit(solution)/shard_map/psum | solution.py:44
  21.5 16.4 %copy-start = (bf16[2048,768]{1,0:T(8,128)(2,1)S(1)}, bf16[2048,768]{1,0:T(8,128)(2,1)}, u32[]{:S(2)}) copy-start(bf16[2048,768]{1,0:T(8,128)(2,1)} %param.6) | copy-start | bytes 9437188
  62.4 0.8 copy-start.2
  135.8 1.4 copy-start.1
Sparse Core Ops, SparseCore 0:
  66.0 68.1 all-reduce.2
where the time goes:
time: 145 us; the launch traced here: 144 us
  waiting for transfers between devices  60.8 us (42%)
  blocking collectives  47.9 us (33%)
  between operations  15.4 us (11%)
  other arithmetic  10.4 us (7%)
  matrix products  6.06 us (4%)
  local copies, waits for them, and re-layouts  3.49 us (2%)
    psum x1, waiting for transfers between devices, shards(): lax.psum(partial_value, ('dp', 'sub')).astype(jnp.float32)  60.7 us
    all_gather x1, blocking collectives, shards(): lax.all_gather(unit_rows, 'cent', axis=0, tiled=True)  13.6 us
    pmax x1, blocking collectives, shards(): row_peak = lax.pmax(local_peak, 'cent')  10.4 us
    unnamed x1, blocking collectives  9.89 us
    psum x1, blocking collectives, shards(): lax.psum(jnp.sum(jnp.exp(scores - row_peak[:, None]), axis=1), 'cent')  8.37 us
    psum x1, blocking collectives, shards(): lax.psum(weight_mass, ('dp', 'sub')).astype(jnp.float32)  5.64 us
    reduce_sum x3, other arithmetic, normalize(): jnp.sum(floats * floats, axis=-1, keepdims=True) + 1e-06  5.22 us
    unnamed x11, local copies, waits for them, and re-layouts  2.9 us
  transfers between devices with their start and end apart: 1, of which 1 were waited for; matrix products, arithmetic and copies ran while one was open for 1% of the time, Pallas kernels for 0%

commit v1 on v0

v1 whole, which is shorter than its diff:
```python
import jax
import jax.numpy as jnp
from jax import lax
from jax.sharding import PartitionSpec as P

PART_AXES = ("cent", "dp", "sub")


def normalize(values):
    floats = values.astype(jnp.float32)
    return floats * lax.rsqrt(jnp.sum(floats * floats, axis=-1, keepdims=True) + 1e-06)


def merged_log_sum(local_peak, local_total):
    stats = jnp.stack([local_peak, local_total])
    if stats.size * 4 * lax.axis_size(PART_AXES) <= (8 << 20):
        gathered = lax.all_gather(stats, PART_AXES, axis=0)
        peaks, totals = gathered[:, 0], gathered[:, 1]
        row_peak = jnp.max(peaks, axis=0)
        row_total = jnp.sum(totals * jnp.exp(peaks - row_peak[None, :]), axis=0)
    else:
        row_peak = lax.pmax(local_peak, PART_AXES)
        row_total = lax.psum(local_total * jnp.exp(local_peak - row_peak), PART_AXES)
    return row_peak + jnp.log(row_total)


def shards(embeddings, weights, centroids, inverse_temp):
    sharpness = inverse_temp[0]
    row_dev, width = embeddings.shape
    n_cent = lax.axis_size("cent")
    n_groups = lax.axis_size(("dp", "sub"))
    own_count = centroids.shape[0] // n_groups

    weight_cols = jnp.broadcast_to(weights.astype(jnp.bfloat16)[:, None], (row_dev, 128))
    packed = jnp.concatenate([embeddings, weight_cols], axis=1)
    gathered = lax.all_gather(packed, PART_AXES, axis=0, tiled=True)
    unit_rows = normalize(gathered[:, :width]).astype(jnp.bfloat16)
    weight_float = gathered[:, width].astype(jnp.float32)

    offset = lax.axis_index(("dp", "sub")) * own_count
    own_cents = normalize(lax.dynamic_slice_in_dim(centroids, offset, own_count, 0)).astype(jnp.bfloat16)

    scores = (
        lax.dot_general(
            unit_rows, own_cents, (((1,), (1,)), ((), ())), preferred_element_type=jnp.float32
        )
        * sharpness
    )
    local_peak = jnp.max(scores, axis=1)
    local_total = jnp.sum(jnp.exp(scores - local_peak[:, None]), axis=1)
    log_sum = merged_log_sum(local_peak, local_total)

    responsibility = (weight_float[:, None] * jnp.exp(scores - log_sum[:, None])).astype(jnp.bfloat16)
    grouped_resp = responsibility.reshape(n_cent, n_groups, row_dev, own_count)
    grouped_rows = unit_rows.reshape(n_cent, n_groups, row_dev, width)
    partial_value = lax.dot_general(
        grouped_resp,
        grouped_rows,
        (((0, 2), (0, 2)), ((1,), (1,))),
        preferred_element_type=jnp.float32,
    ).astype(jnp.bfloat16)
    centroid_sums = jnp.sum(partial_value.astype(jnp.float32), axis=0)
    weight_mass = jnp.sum(grouped_resp.astype(jnp.float32), axis=(0, 2)).astype(jnp.bfloat16)
    own_mass = jnp.sum(weight_mass.astype(jnp.float32), axis=0)

    moved = own_cents.astype(jnp.float32) + centroid_sums / (own_mass + 1.0)[:, None]
    renormed = normalize(moved).astype(jnp.bfloat16)

    row_offset = lax.axis_index(PART_AXES) * row_dev
    weighted_log_sum = weight_float * log_sum / sharpness
    objective = lax.dynamic_slice_in_dim(weighted_log_sum, row_offset, row_dev, 0)
    return (centroid_sums, renormed, objective)


def solution(mesh):
    in_specs = (
        P(("groups", "cent", "dp", "sub"), None),
        P(("groups", "cent", "dp", "sub")),
        P(("groups", "cent"), None),
        P(),
    )
    out_specs = (
        P(("groups", "cent", "dp", "sub"), None),
        P(("groups", "cent", "dp", "sub"), None),
        P(("groups", "cent", "dp", "sub")),
    )
    return jax.shard_map(shards, mesh=mesh, in_specs=in_specs, out_specs=out_specs, check_vma=False)
```

time: 145 us -> 56.2 us (0.39)
  waiting for transfers between devices: 60.8 us -> 0 us
  between operations: 15.4 us -> 1.36 us
  blocking collectives: 47.9 us -> 43.4 us
  matrix products: 6.06 us -> 2.95 us
  other arithmetic: 10.4 us -> 7.41 us
  local copies, waits for them, and re-layouts: 3.49 us -> 0.67 us
    psum x1 -> x0, waiting for transfers between devices: 60.7 us -> none  [shards(): lax.psum(partial_value, ('dp', 'sub')).astype(jnp.float32)]
    all_gather x1 -> x2, blocking collectives: 13.6 us -> 43.4 us  [the longest x1 25.8 us: shards(): gathered = lax.all_gather(packed, PART_AXES, axis=0, tiled=True)]
    psum x2 -> x0, blocking collectives: 14 us -> none  [the longest x1 8.37 us: shards(): lax.psum(jnp.sum(jnp.exp(scores - row_peak[:, None]), axis=1), 'cent')]
    pmax x1 -> x0, blocking collectives: 10.4 us -> none  [shards(): row_peak = lax.pmax(local_peak, 'cent')]
    unnamed x1 -> x0, blocking collectives: 9.89 us -> none
    dot_general x3 -> x2, matrix products: 6.06 us -> 2.95 us  [the longest x1 1.93 us: shards(): lax.dot_general(unit_rows, own_cents, (((1,), (1,)), ((), ())), preferred...]
    unnamed x11 -> x2, local copies, waits for them, and re-layouts: 2.9 us -> 0.01 us
  transfers between devices with their start and end apart: 1 -> 0, of which waited for: 1 -> 0; matrix products, arithmetic and copies ran while one was open for 1% -> 0% of each run, Pallas kernels for 0% -> 0%
where the time goes in v1:
time: 56.2 us; the launch traced here: 55.8 us
  blocking collectives  43.4 us (77%)
  other arithmetic  7.41 us (13%)
  matrix products  2.95 us (5%)
  between operations  1.36 us (2%)
  local copies, waits for them, and re-layouts  0.67 us (1%)
    all_gather x1, blocking collectives, shards(): gathered = lax.all_gather(packed, PART_AXES, axis=0, tiled=True)  25.8 us
    all_gather x1, blocking collectives, merged_log_sum(): gathered = lax.all_gather(stats, PART_AXES, axis=0)  17.6 us
    reduce_sum x3, other arithmetic, normalize(): jnp.sum(floats * floats, axis=-1, keepdims=True) + 1e-06  3.81 us
    dot_general x1, matrix products, shards(): lax.dot_general(unit_rows, own_cents, (((1,), (1,)), ((), ())), preferred...  1.93 us

profile of v1, /device:TPU:0, one launch (start us, length us, event | category | flops | bytes accessed | tf_op | source)
XLA Modules:
  0.0 55.8 jit_solution(16644514448525370519)
XLA Ops:
  1.3 0.7 %convert_element_type.38 = bf16[32]{0:T(256)(128)(2,1)S(1)} convert(s32[32]{0:T(128)} %param.5) | non-fusion elementwise | flops 32 | bytes 192 | tf_op jit(solution)/shard_map/convert_element_type | solution.py:34
  1.9 1.4 %fusion.2 = f32[512]{0:T(512)S(1)} fusion(bf16[2048,768]{1,0:T(8,128)(2,1)} %param.6, s32[]{:T(128)S(6)} %select_n.6), kind=kLoop, calls=%fused_computation.8 | loop fusion | flops 1179136 | bytes 788484 | tf_op jit(solution)/shard_map/reduce_sum | solution.py:11
  3.3 0.1 broadcast_in_dim.2
  3.4 0.8 %pad_maximum_fusion = bf16[32,896]{1,0:T(8,128)(2,1)S(1)} fusion(bf16[32,128]{1,0:T(8,128)(2,1)S(1)} %broadcast_in_dim.2, bf16[32,768]{1,0:T(8,128)(2,1)} %param.4), kind=kLoop, calls=%fused_computation.17 | loop fusion | flops 114688 | bytes 114688 | tf_op jit(solution)/shard_map/concatenate | solution.py:35
  4.2 25.8 %all_gather.9 = bf16[512,896]{1,0:T(8,128)(2,1)S(1)} all-gather(bf16[32,896]{1,0:T(8,128)(2,1)S(1)} %pad_maximum_fusion), channel_id=1, replica_groups=mesh['groups'=2,'cent'=4,'dp'=2,'sub'=2] {'cent','dp','sub'}, dimensions={0}, use_global_device_ids=true | all-gather | bytes 974848 | tf_op jit(solution)/shard_map/all_gather | solution.py:36
  30.0 0.1 convert_reduce_fusion.1
  30.1 0.2 fusion
  30.4 0.2 fusion.1
  30.6 1.9 %fusion.10 = (f32[512]{0:T(512)S(1)}, f32[512,512]{1,0:T(8,128)S(1)}) fusion(f32[]{:T(128)} %bitcast.26, bf16[512,768]{1,0:T(8,128)(2,1)S(1)} %fusion.1, f32[512]{0:T(512)S(1)} %add_rsqrt_fusion.1, bf16[2048,768]{1,0:T(8,128)(2,1)} %param.6, s32[]{:T(128)S(6)} %select_n.6), kind=kOutput, calls=%fused_computation.34 | convolution fusion | flops 404356608 | bytes 2626052 | tf_op jit(solution)/shard_map/dot_general | solution.py:44
  32.5 0.3 exponential_reduce_fusion
  32.8 17.6 %all-gather.1 = f32[16,2,512]{2,1,0:T(2,128)S(1)} all-gather(f32[1,2,512]{2,1,0:T(2,128)S(1)} %maximum_bitcast_fusion), channel_id=2, replica_groups=mesh['groups'=2,'cent'=4,'dp'=2,'sub'=2] {'cent','dp','sub'}, dimensions={0}, use_global_device_ids=true | all-gather | bytes 69632 | tf_op jit(solution)/shard_map/all_gather | solution.py:17
  50.4 0.1 fusion.9
  50.6 0.2 multiply_convert_fusion.1
  50.8 0.6 %dynamic_slice.7 = f32[32]{0:T(128)} dynamic-slice(f32[512]{0:T(512)S(1)} %get-tuple-element.3, s32[]{:T(128)S(6)} %select_n.7), dynamic_slice_sizes={32} | dynamic-slice | bytes 260 | tf_op jit(solution)/shard_map/dynamic_slice | solution.py:71
  51.4 0.1 reduce_sum.80
  51.5 1.0 %convert_reduce_fusion = f32[512,768]{1,0:T(8,128)S(1)} fusion(bf16[4,4,32,512]{3,2,1,0:T(8,128)(2,1)S(1)} %bitcast.29, bf16[4,4,32,768]{3,2,1,0:T(8,128)(2,1)S(1)} %bitcast.30), kind=kOutput, calls=%fused_computation.1 | convolution fusion | flops 406978560 | bytes 2883584 | tf_op jit(solution)/shard_map/dot_general | solution.py:56
  52.5 0.0 copy-start
  52.6 2.2 %multiply_reduce_fusion = (f32[512]{0:T(512)S(1)}, f32[512,768]{1,0:T(8,128)S(1)}) fusion(f32[512,768]{1,0:T(8,128)S(1)} %convert_reduce_fusion, f32[512]{0:T(512)S(1)} %broadcast_add_fusion, f32[512]{0:T(512)S(1)} %add_rsqrt_fusion.1, bf16[2048,768]{1,0:T(8,128)(2,1)} %param.6, s32[]{:T(128)S(6)} %select_n.6), kind=kLoop, calls=%fused_computation.11 | loop fusion | flops 3145216 | bytes 3938308 | tf_op jit(solution)/shard_map/reduce_sum | solution.py:11
  54.8 0.0 copy-done
  54.8 1.0 %multiply_convert_fusion = bf16[512,768]{1,0:T(8,128)(2,1)} fusion(f32[512,768]{1,0:T(8,128)S(1)} %get-tuple-element.6, f32[512]{0:T(512)S(1)} %add_rsqrt_fusion), kind=kLoop, calls=%fused_computation.10 | loop fusion | flops 786432 | bytes 2361344 | tf_op jit(solution)/shard_map/convert_element_type | solution.py:67
  (8 shorter events, 0.1 us)
Async XLA Ops:
  52.5 2.2 %copy-start = (f32[512,768]{1,0:T(8,128)}, f32[512,768]{1,0:T(8,128)S(1)}, u32[]{:S(2)}) copy-start(f32[512,768]{1,0:T(8,128)S(1)} %convert_reduce_fusion) | copy-start | bytes 4718596

commit v2 on v1

v2 whole, which is shorter than its diff:
```python
import jax
import jax.numpy as jnp
from jax import lax
from jax.sharding import PartitionSpec as P

STAGES = ("cent", "dp", "sub")
SHIFT_MAX = 4


def normalize(values):
    floats = values.astype(jnp.float32)
    return floats * lax.rsqrt(jnp.sum(floats * floats, axis=-1, keepdims=True) + 1e-06)


def relative(name):
    return lax.axis_size(name) <= SHIFT_MAX


def gather_stage(value, name):
    size = lax.axis_size(name)
    if relative(name):
        parts = [value] + [
            lax.ppermute(value, name, [(j, (j + q) % size) for j in range(size)]) for q in range(1, size)
        ]
        return jnp.stack(parts)
    return lax.all_gather(value, name, axis=0)


def own_block(name):
    return 0 if relative(name) else lax.axis_index(name)


def shards(embeddings, weights, centroids, inverse_temp):
    sharpness = inverse_temp[0]
    row_dev, width = embeddings.shape
    sizes = {name: lax.axis_size(name) for name in STAGES}
    n_groups = sizes["dp"] * sizes["sub"]
    own_count = centroids.shape[0] // n_groups

    weight_cols = jnp.broadcast_to(weights.astype(jnp.bfloat16)[:, None], (row_dev, 128))
    blocks = jnp.concatenate([embeddings, weight_cols], axis=1)
    for name in STAGES:
        blocks = gather_stage(blocks, name)
    gathered = blocks.reshape(-1, width + 128)
    unit_rows = normalize(gathered[:, :width]).astype(jnp.bfloat16)
    weight_float = gathered[:, width].astype(jnp.float32)

    offset = lax.axis_index(("dp", "sub")) * own_count
    own_cents = normalize(lax.dynamic_slice_in_dim(centroids, offset, own_count, 0)).astype(jnp.bfloat16)

    scores = (
        lax.dot_general(
            unit_rows, own_cents, (((1,), (1,)), ((), ())), preferred_element_type=jnp.float32
        )
        * sharpness
    )
    block_shape = (sizes["sub"], sizes["dp"], sizes["cent"], row_dev)
    local_peak = jnp.max(scores, axis=1)
    local_total = jnp.sum(jnp.exp(scores - local_peak[:, None]), axis=1)

    stats = jnp.stack([local_peak.reshape(block_shape), local_total.reshape(block_shape)])
    block_axis = {"sub": 1, "dp": 2, "cent": 3}
    for name in STAGES:
        stacked = gather_stage(stats, name)
        if relative(name):
            stacked = jnp.stack(
                [jnp.roll(stacked[q], q, axis=block_axis[name]) for q in range(sizes[name])]
            )
        peaks, totals = stacked[:, 0], stacked[:, 1]
        row_peak = jnp.max(peaks, axis=0)
        row_total = jnp.sum(totals * jnp.exp(peaks - row_peak[None]), axis=0)
        stats = jnp.stack([row_peak, row_total])
    log_sum = (stats[0] + jnp.log(stats[1])).reshape(-1)

    responsibility = (weight_float[:, None] * jnp.exp(scores - log_sum[:, None])).astype(jnp.bfloat16)
    grouped_resp = responsibility.reshape(n_groups, -1, own_count)
    grouped_rows = unit_rows.reshape(n_groups, -1, width)
    partial_value = lax.dot_general(
        grouped_resp, grouped_rows, (((1,), (1,)), ((0,), (0,))), preferred_element_type=jnp.float32
    ).astype(jnp.bfloat16)
    centroid_sums = jnp.sum(partial_value.astype(jnp.float32), axis=0)
    weight_mass = jnp.sum(grouped_resp.astype(jnp.float32), axis=1).astype(jnp.bfloat16)
    own_mass = jnp.sum(weight_mass.astype(jnp.float32), axis=0)

    moved = own_cents.astype(jnp.float32) + centroid_sums / (own_mass + 1.0)[:, None]
    renormed = normalize(moved).astype(jnp.bfloat16)

    weighted_log_sum = (weight_float * log_sum / sharpness).reshape(block_shape)
    objective = weighted_log_sum[own_block("sub"), own_block("dp"), own_block("cent")]
    return (centroid_sums, renormed, objective)


def solution(mesh):
    in_specs = (
        P(("groups", "cent", "dp", "sub"), None),
        P(("groups", "cent", "dp", "sub")),
        P(("groups", "cent"), None),
        P(),
    )
    out_specs = (
        P(("groups", "cent", "dp", "sub"), None),
        P(("groups", "cent", "dp", "sub"), None),
        P(("groups", "cent", "dp", "sub")),
    )
    return jax.shard_map(shards, mesh=mesh, in_specs=in_specs, out_specs=out_specs, check_vma=False)
```

time: 56.2 us -> 43.9 us (0.78)
  blocking collectives: 43.4 us -> 0 us
  starting transfers between devices: 0 us -> 15.3 us
  waiting for transfers between devices: 0 us -> 15.1 us
  other arithmetic: 7.41 us -> 8.15 us
    all_gather x2 -> x0, blocking collectives: 43.4 us -> none  [the longest x1 25.8 us: shards(): gathered = lax.all_gather(packed, PART_AXES, axis=0, tiled=True)]
    ppermute x0 -> x10, starting transfers between devices: none -> 15.3 us  [gather_stage(): lax.ppermute(value, name, [(j, (j + q) % size) for j in range(size)])]
    ppermute x0 -> x10, waiting for transfers between devices: none -> 15.1 us  [gather_stage(): lax.ppermute(value, name, [(j, (j + q) % size) for j in range(size)])]
    another operation x0 -> x12, other arithmetic: none -> 1.12 us  [the longest x4 1.02 us: gather_stage(): return jnp.stack(parts)]
    concatenate x1 -> x0, other arithmetic: 0.81 us -> none  [shards(): packed = jnp.concatenate([embeddings, weight_cols], axis=1)]
    dynamic_slice x1 -> x0, local copies, waits for them, and re-layouts: 0.59 us -> none  [shards(): lax.dynamic_slice_in_dim(weighted_log_sum, row_offset, row_dev, 0)]
  transfers between devices with their start and end apart: 0 -> 10, of which waited for: 0 -> 8; matrix products, arithmetic and copies ran while one was open for 0% -> 4% of each run, Pallas kernels for 0% -> 0%
where the time goes in v2:
time: 43.9 us; the launch traced here: 43.5 us
  starting transfers between devices  15.3 us (35%)
  waiting for transfers between devices  15.1 us (34%)
  other arithmetic  8.15 us (19%)
  matrix products  2.96 us (7%)
  between operations  1.49 us (3%)
  local copies, waits for them, and re-layouts  0.58 us (1%)
    ppermute x10, starting transfers between devices, gather_stage(): lax.ppermute(value, name, [(j, (j + q) % size) for j in range(size)])  15.3 us
    ppermute x10, waiting for transfers between devices, gather_stage(): lax.ppermute(value, name, [(j, (j + q) % size) for j in range(size)])  15.1 us
    reduce_sum x3, other arithmetic, normalize(): jnp.sum(floats * floats, axis=-1, keepdims=True) + 1e-06  3.81 us
    dot_general x1, matrix products, shards(): lax.dot_general(unit_rows, own_cents, (((1,), (1,)), ((), ())), preferred...  1.93 us
    convert_element_type x1, other arithmetic, shards(): renormed = normalize(moved).astype(jnp.bfloat16)  1.03 us
    dot_general x1, matrix products, shards(): lax.dot_general(grouped_resp, grouped_rows, (((1,), (1,)), ((0,), (0,))),...  1.02 us
    another operation x4, other arithmetic, gather_stage(): return jnp.stack(parts)  1.02 us
  transfers between devices with their start and end apart: 10, of which 8 were waited for; matrix products, arithmetic and copies ran while one was open for 4% of the time, Pallas kernels for 0%

profile of v2, /device:TPU:0, one launch (start us, length us, event | category | flops | bytes accessed | tf_op | source)
XLA Modules:
  0.0 43.5 jit_solution(16183167891121069908)
XLA Ops:
  0.6 0.7 %convert_element_type.43 = bf16[32]{0:T(256)(128)(2,1)S(1)} convert(s32[32]{0:T(128)} %param.5) | non-fusion elementwise | flops 32 | bytes 192 | tf_op jit(solution)/shard_map/convert_element_type | solution.py:40
  1.3 0.1 broadcast_in_dim.2
  1.4 0.8 %fusion.23 = (bf16[1,32,896]{2,1,0:T(8,128)(2,1)S(1)}, bf16[32,896]{1,0:T(8,128)(2,1)S(1)}) fusion(bf16[32,128]{1,0:T(8,128)(2,1)S(1)} %broadcast_in_dim.2, bf16[32,768]{1,0:T(8,128)(2,1)} %param.4), kind=kLoop, calls=%fused_computation.69 | loop fusion | flops 114688 | bytes 172032 | tf_op jit(solution)/shard_map/stack | solution.py:25
  2.2 4.1 %collective-permute-start.1 = (bf16[32,896]{1,0:T(8,128)(2,1)S(1)}, bf16[32,896]{1,0:T(8,128)(2,1)S(1)}, u32[]{:S(2)}, u32[]{:S(2)}) collective-permute-start(bf16[32,896]{1,0:T(8,128)(2,1)S(1)} %get-tuple-element.12), channel_id=1, source_target_pairs={{0,8},{4,12},{8,0},{12,4},{1,9},{5,13},{9,1},{13,5},{2,10},{6,14},... | collective-permute-start | bytes 172040 | tf_op jit(solution)/shard_map/ppermute | solution.py:23
  6.3 1.6 %collective-permute-start = (bf16[32,896]{1,0:T(8,128)(2,1)S(1)}, bf16[32,896]{1,0:T(8,128)(2,1)S(1)}, u32[]{:S(2)}, u32[]{:S(2)}) collective-permute-start(bf16[32,896]{1,0:T(8,128)(2,1)S(1)} %get-tuple-element.12), channel_id=1, source_target_pairs={{0,4},{4,8},{8,12},{12,0},{1,5},{5,9},{9,13},{13,1},{2,6},{6,10},{... | collective-permute-start | bytes 172040 | tf_op jit(solution)/shard_map/ppermute | solution.py:23
  7.9 2.2 %collective-permute-start.2 = (bf16[32,896]{1,0:T(8,128)(2,1)S(1)}, bf16[32,896]{1,0:T(8,128)(2,1)S(1)}, u32[]{:S(2)}, u32[]{:S(2)}) collective-permute-start(bf16[32,896]{1,0:T(8,128)(2,1)S(1)} %get-tuple-element.12), channel_id=1, source_target_pairs={{0,12},{4,0},{8,4},{12,8},{1,13},{5,1},{9,5},{13,9},{2,14},{6,2},{... | collective-permute-start | bytes 172040 | tf_op jit(solution)/shard_map/ppermute | solution.py:23
  10.1 0.0 collective-permute-done.1
  10.1 2.3 %collective-permute-done = bf16[32,896]{1,0:T(8,128)(2,1)S(1)} collective-permute-done((bf16[32,896]{1,0:T(8,128)(2,1)S(1)}, bf16[32,896]{1,0:T(8,128)(2,1)S(1)}, u32[]{:S(2)}, u32[]{:S(2)}) %collective-permute-start) | collective-permute-done | bytes 57376 | tf_op jit(solution)/shard_map/ppermute | solution.py:23
  12.4 0.3 collective-permute-done.2
  12.7 1.6 %collective-permute-start.3 = (bf16[4,32,896]{2,1,0:T(8,128)(2,1)S(1)}, bf16[4,32,896]{2,1,0:T(8,128)(2,1)S(1)}, u32[]{:S(2)}, u32[]{:S(2)}) collective-permute-start(bf16[4,32,896]{2,1,0:T(8,128)(2,1)S(1)} %get-tuple-element.10), channel_id=1, source_target_pairs={{0,2},{2,0},{1,3},{3,1},{4,6},{6,4},{5,7},{7,5},{8,10},{10,8},{9,1... | collective-permute-start | bytes 688136 | tf_op jit(solution)/shard_map/ppermute | solution.py:23
  14.3 4.5 %collective-permute-done.3 = bf16[4,32,896]{2,1,0:T(8,128)(2,1)S(1)} collective-permute-done((bf16[4,32,896]{2,1,0:T(8,128)(2,1)S(1)}, bf16[4,32,896]{2,1,0:T(8,128)(2,1)S(1)}, u32[]{:S(2)}, u32[]{:S(2)}) %collective-permute-start.3) | collective-permute-done | bytes 229408 | tf_op jit(solution)/shard_map/ppermute | solution.py:23
  18.8 0.1 fusion.24
  18.9 0.1 collective-permute-start.4
  19.6 1.4 %fusion.2 = f32[512]{0:T(512)S(1)} fusion(bf16[2048,768]{1,0:T(8,128)(2,1)} %param.6, s32[]{:T(128)S(6)} %select_n.3), kind=kLoop, calls=%fused_computation.7 | loop fusion | flops 1179136 | bytes 788484 | tf_op jit(solution)/shard_map/reduce_sum | solution.py:12
  21.0 0.0 collective-permute-done.4
  21.0 0.1 pad_maximum_fusion
  21.1 0.2 fusion
  21.3 0.2 fusion.1
  21.5 1.9 %fusion.29 = (f32[512]{0:T(512)S(1)}, f32[512,512]{1,0:T(8,128)S(1)}) fusion(f32[]{:T(128)} %bitcast.93, bf16[512,768]{1,0:T(8,128)(2,1)S(1)} %fusion.1, f32[512]{0:T(512)S(1)} %add_rsqrt_fusion.1, bf16[2048,768]{1,0:T(8,128)(2,1)} %param.6, s32[]{:T(128)S(6)} %select_n.3), kind=kOutput, calls=%fused_computation.75 | convolution fusion | flops 404356608 | bytes 2626052 | tf_op jit(solution)/shard_map/dot_general | solution.py:52
  23.5 0.1 stack_reshape.6
  23.5 0.3 exponential_reduce_fusion
  23.8 0.1 stack_reshape.7
  23.9 3.5 %collective-permute-start.7 = (f32[2,2,2,4,32]{4,3,2,1,0:T(4,128)S(1)}, f32[2,2,2,4,32]{4,3,2,1,0:T(4,128)S(1)}, u32[]{:S(2)}, u32[]{:S(2)}) collective-permute-start(f32[2,2,2,4,32]{4,3,2,1,0:T(4,128)S(1)} %constant_dynamic-update-slice_fusion), channel_id=1, source_target_pairs={{0,12},{4,0},{8,4},{12,8},{1,13},{5,1},{9,5},{13,9},{2,14},{6,2},{... | collective-permute-start | bytes 12296 | tf_op jit(solution)/shard_map/ppermute | solution.py:23
  27.4 0.0 collective-permute-start.6
  27.4 0.6 %collective-permute-start.5 = (f32[2,2,2,4,32]{4,3,2,1,0:T(4,128)S(1)}, f32[2,2,2,4,32]{4,3,2,1,0:T(4,128)S(1)}, u32[]{:S(2)}, u32[]{:S(2)}) collective-permute-start(f32[2,2,2,4,32]{4,3,2,1,0:T(4,128)S(1)} %constant_dynamic-update-slice_fusion), channel_id=1, source_target_pairs={{0,4},{4,8},{8,12},{12,0},{1,5},{5,9},{9,13},{13,1},{2,6},{6,10},{... | collective-permute-start | bytes 12296 | tf_op jit(solution)/shard_map/ppermute | solution.py:23
  28.0 0.8 %collective-permute-done.7 = f32[2,2,2,4,32]{4,3,2,1,0:T(4,128)S(1)} collective-permute-done((f32[2,2,2,4,32]{4,3,2,1,0:T(4,128)S(1)}, f32[2,2,2,4,32]{4,3,2,1,0:T(4,128)S(1)}, u32[]{:S(2)}, u32[]{:S(2)}) %collective-permute-start.7) | collective-permute-done | bytes 4128 | tf_op jit(solution)/shard_map/ppermute | solution.py:23
  28.9 3.2 %collective-permute-done.6 = f32[2,2,2,4,32]{4,3,2,1,0:T(4,128)S(1)} collective-permute-done((f32[2,2,2,4,32]{4,3,2,1,0:T(4,128)S(1)}, f32[2,2,2,4,32]{4,3,2,1,0:T(4,128)S(1)}, u32[]{:S(2)}, u32[]{:S(2)}) %collective-permute-start.6) | collective-permute-done | bytes 4128 | tf_op jit(solution)/shard_map/ppermute | solution.py:23
  32.1 0.9 %collective-permute-done.5 = f32[2,2,2,4,32]{4,3,2,1,0:T(4,128)S(1)} collective-permute-done((f32[2,2,2,4,32]{4,3,2,1,0:T(4,128)S(1)}, f32[2,2,2,4,32]{4,3,2,1,0:T(4,128)S(1)}, u32[]{:S(2)}, u32[]{:S(2)}) %collective-permute-start.5) | collective-permute-done | bytes 4128 | tf_op jit(solution)/shard_map/ppermute | solution.py:23
  33.1 1.6 %collective-permute-start.8 = (f32[2,2,2,4,32]{4,3,2,1,0:T(4,128)S(1)}, f32[2,2,2,4,32]{4,3,2,1,0:T(4,128)S(1)}, u32[]{:S(2)}, u32[]{:S(2)}) collective-permute-start(f32[2,2,2,4,32]{4,3,2,1,0:T(4,128)S(1)} %get-tuple-element.18), channel_id=1, source_target_pairs={{0,2},{2,0},{1,3},{3,1},{4,6},{6,4},{5,7},{7,5},{8,10},{10,8},{9,1... | collective-permute-start | bytes 12296 | tf_op jit(solution)/shard_map/ppermute | solution.py:23
  34.6 0.1 copy.24
  34.8 2.1 %collective-permute-done.8 = f32[2,2,2,4,32]{4,3,2,1,0:T(4,128)S(1)} collective-permute-done((f32[2,2,2,4,32]{4,3,2,1,0:T(4,128)S(1)}, f32[2,2,2,4,32]{4,3,2,1,0:T(4,128)S(1)}, u32[]{:S(2)}, u32[]{:S(2)}) %collective-permute-start.8) | collective-permute-done | bytes 4128 | tf_op jit(solution)/shard_map/ppermute | solution.py:23
  37.0 0.1 collective-permute-start.9
  37.1 0.1 reshape.64
  37.2 1.1 %collective-permute-done.9 = f32[2,2,2,4,32]{4,3,2,1,0:T(4,128)S(1)} collective-permute-done((f32[2,2,2,4,32]{4,3,2,1,0:T(4,128)S(1)}, f32[2,2,2,4,32]{4,3,2,1,0:T(4,128)S(1)}, u32[]{:S(2)}, u32[]{:S(2)}) %collective-permute-start.9) | collective-permute-done | bytes 4128 | tf_op jit(solution)/shard_map/ppermute | solution.py:23
  38.3 0.1 add.60
  38.4 0.3 bitcast_reduce_fusion.2
  38.7 1.0 %convert_reduce_fusion = f32[512,768]{1,0:T(8,128)S(1)} fusion(bf16[4,128,512]{2,1,0:T(8,128)(2,1)S(1)} %bitcast.99, bf16[4,128,768]{2,1,0:T(8,128)(2,1)S(1)} %bitcast.98), kind=kOutput, calls=%fused_computation | convolution fusion | flops 406978560 | bytes 2883584 | tf_op jit(solution)/shard_map/dot_general | solution.py:78
  39.7 0.0 copy-start
  39.7 2.2 %multiply_reduce_fusion = (f32[512]{0:T(512)S(1)}, f32[512,768]{1,0:T(8,128)S(1)}) fusion(f32[512,768]{1,0:T(8,128)S(1)} %convert_reduce_fusion, f32[512]{0:T(512)S(1)} %broadcast_add_fusion, f32[512]{0:T(512)S(1)} %add_rsqrt_fusion.1, bf16[2048,768]{1,0:T(8,128)(2,1)} %param.6, s32[]{:T(128)S(6)} %select_n.3), kind=kLoop, calls=%fused_computation.10 | loop fusion | flops 3145216 | bytes 3938308 | tf_op jit(solution)/shard_map/reduce_sum | solution.py:12
  42.0 0.0 copy-done
  42.0 0.5 %fusion.19 = f32[32]{0:T(128)} fusion(f32[2,2,4,32]{3,2,1,0:T(4,128)S(1)} %bitcast.110, f32[2,2,4,32]{3,2,1,0:T(4,128)S(1)} %reshape.64, f32[]{:T(128)} %bitcast.94), kind=kLoop, calls=%fused_computation.63 | loop fusion | flops 64 | bytes 388 | tf_op jit(solution)/shard_map/squeeze | solution.py:89
  42.5 1.0 %multiply_convert_fusion = bf16[512,768]{1,0:T(8,128)(2,1)} fusion(f32[512,768]{1,0:T(8,128)S(1)} %get-tuple-element.4, f32[512]{0:T(512)S(1)} %add_rsqrt_fusion), kind=kLoop, calls=%fused_computation.9 | loop fusion | flops 786432 | bytes 2361344 | tf_op jit(solution)/shard_map/convert_element_type | solution.py:86
  (32 shorter events, 0.4 us)
Async XLA Ops:
  2.2 7.9 %collective-permute-start.1 = (bf16[32,896]{1,0:T(8,128)(2,1)S(1)}, bf16[32,896]{1,0:T(8,128)(2,1)S(1)}, u32[]{:S(2)}, u32[]{:S(2)}) collective-permute-start(bf16[32,896]{1,0:T(8,128)(2,1)S(1)} %get-tuple-element.12), channel_id=1, source_target_pairs={{0,8},{4,12},{8,0},{12,4},{1,9},{5,13},{9,1},{13,5},{2,10},{6,14},... | collective-permute-start | bytes 172040 | tf_op jit(solution)/shard_map/ppermute | solution.py:23
  6.3 6.1 %collective-permute-start = (bf16[32,896]{1,0:T(8,128)(2,1)S(1)}, bf16[32,896]{1,0:T(8,128)(2,1)S(1)}, u32[]{:S(2)}, u32[]{:S(2)}) collective-permute-start(bf16[32,896]{1,0:T(8,128)(2,1)S(1)} %get-tuple-element.12), channel_id=1, source_target_pairs={{0,4},{4,8},{8,12},{12,0},{1,5},{5,9},{9,13},{13,1},{2,6},{6,10},{... | collective-permute-start | bytes 172040 | tf_op jit(solution)/shard_map/ppermute | solution.py:23
  7.9 4.8 %collective-permute-start.2 = (bf16[32,896]{1,0:T(8,128)(2,1)S(1)}, bf16[32,896]{1,0:T(8,128)(2,1)S(1)}, u32[]{:S(2)}, u32[]{:S(2)}) collective-permute-start(bf16[32,896]{1,0:T(8,128)(2,1)S(1)} %get-tuple-element.12), channel_id=1, source_target_pairs={{0,12},{4,0},{8,4},{12,8},{1,13},{5,1},{9,5},{13,9},{2,14},{6,2},{... | collective-permute-start | bytes 172040 | tf_op jit(solution)/shard_map/ppermute | solution.py:23
  12.7 6.1 %collective-permute-start.3 = (bf16[4,32,896]{2,1,0:T(8,128)(2,1)S(1)}, bf16[4,32,896]{2,1,0:T(8,128)(2,1)S(1)}, u32[]{:S(2)}, u32[]{:S(2)}) collective-permute-start(bf16[4,32,896]{2,1,0:T(8,128)(2,1)S(1)} %get-tuple-element.10), channel_id=1, source_target_pairs={{0,2},{2,0},{1,3},{3,1},{4,6},{6,4},{5,7},{7,5},{8,10},{10,8},{9,1... | collective-permute-start | bytes 688136 | tf_op jit(solution)/shard_map/ppermute | solution.py:23
  18.9 2.1 %collective-permute-start.4 = (bf16[2,4,32,896]{3,2,1,0:T(8,128)(2,1)S(1)}, bf16[2,4,32,896]{3,2,1,0:T(8,128)(2,1)S(1)}, u32[]{:S(2)}, u32[]{:S(2)}) collective-permute-start(bf16[2,4,32,896]{3,2,1,0:T(8,128)(2,1)S(1)} %get-tuple-element.8), channel_id=1, source_target_pairs={{0,1},{1,0},{2,3},{3,2},{4,5},{5,4},{6,7},{7,6},{8,9},{9,8},{10,11... | collective-permute-start | bytes 1376264 | tf_op jit(solution)/shard_map/ppermute | solution.py:23
  23.9 4.9 %collective-permute-start.7 = (f32[2,2,2,4,32]{4,3,2,1,0:T(4,128)S(1)}, f32[2,2,2,4,32]{4,3,2,1,0:T(4,128)S(1)}, u32[]{:S(2)}, u32[]{:S(2)}) collective-permute-start(f32[2,2,2,4,32]{4,3,2,1,0:T(4,128)S(1)} %constant_dynamic-update-slice_fusion), channel_id=1, source_target_pairs={{0,12},{4,0},{8,4},{12,8},{1,13},{5,1},{9,5},{13,9},{2,14},{6,2},{... | collective-permute-start | bytes 12296 | tf_op jit(solution)/shard_map/ppermute | solution.py:23
  27.4 4.6 %collective-permute-start.6 = (f32[2,2,2,4,32]{4,3,2,1,0:T(4,128)S(1)}, f32[2,2,2,4,32]{4,3,2,1,0:T(4,128)S(1)}, u32[]{:S(2)}, u32[]{:S(2)}) collective-permute-start(f32[2,2,2,4,32]{4,3,2,1,0:T(4,128)S(1)} %constant_dynamic-update-slice_fusion), channel_id=1, source_target_pairs={{0,8},{4,12},{8,0},{12,4},{1,9},{5,13},{9,1},{13,5},{2,10},{6,14},... | collective-permute-start | bytes 12296 | tf_op jit(solution)/shard_map/ppermute | solution.py:23
  27.4 5.5 %collective-permute-start.5 = (f32[2,2,2,4,32]{4,3,2,1,0:T(4,128)S(1)}, f32[2,2,2,4,32]{4,3,2,1,0:T(4,128)S(1)}, u32[]{:S(2)}, u32[]{:S(2)}) collective-permute-start(f32[2,2,2,4,32]{4,3,2,1,0:T(4,128)S(1)} %constant_dynamic-update-slice_fusion), channel_id=1, source_target_pairs={{0,4},{4,8},{8,12},{12,0},{1,5},{5,9},{9,13},{13,1},{2,6},{6,10},{... | collective-permute-start | bytes 12296 | tf_op jit(solution)/shard_map/ppermute | solution.py:23
  33.1 3.8 %collective-permute-start.8 = (f32[2,2,2,4,32]{4,3,2,1,0:T(4,128)S(1)}, f32[2,2,2,4,32]{4,3,2,1,0:T(4,128)S(1)}, u32[]{:S(2)}, u32[]{:S(2)}) collective-permute-start(f32[2,2,2,4,32]{4,3,2,1,0:T(4,128)S(1)} %get-tuple-element.18), channel_id=1, source_target_pairs={{0,2},{2,0},{1,3},{3,1},{4,6},{6,4},{5,7},{7,5},{8,10},{10,8},{9,1... | collective-permute-start | bytes 12296 | tf_op jit(solution)/shard_map/ppermute | solution.py:23
  37.0 1.2 %collective-permute-start.9 = (f32[2,2,2,4,32]{4,3,2,1,0:T(4,128)S(1)}, f32[2,2,2,4,32]{4,3,2,1,0:T(4,128)S(1)}, u32[]{:S(2)}, u32[]{:S(2)}) collective-permute-start(f32[2,2,2,4,32]{4,3,2,1,0:T(4,128)S(1)} %get-tuple-element.14), channel_id=1, source_target_pairs={{0,1},{1,0},{2,3},{3,2},{4,5},{5,4},{6,7},{7,6},{8,9},{9,8},{10,11... | collective-permute-start | bytes 12296 | tf_op jit(solution)/shard_map/ppermute | solution.py:23
  39.7 2.2 %copy-start = (f32[512,768]{1,0:T(8,128)}, f32[512,768]{1,0:T(8,128)S(1)}, u32[]{:S(2)}) copy-start(f32[512,768]{1,0:T(8,128)S(1)} %convert_reduce_fusion) | copy-start | bytes 4718596

commit v3 on v2

--- a/solution.py
+++ b/solution.py
@@ -37,16 +37,14 @@
     n_groups = sizes["dp"] * sizes["sub"]
     own_count = centroids.shape[0] // n_groups
 
-    weight_cols = jnp.broadcast_to(weights.astype(jnp.bfloat16)[:, None], (row_dev, 128))
-    blocks = jnp.concatenate([embeddings, weight_cols], axis=1)
+    blocks = embeddings
     for name in STAGES:
         blocks = gather_stage(blocks, name)
-    gathered = blocks.reshape(-1, width + 128)
-    unit_rows = normalize(gathered[:, :width]).astype(jnp.bfloat16)
-    weight_float = gathered[:, width].astype(jnp.float32)
+    unit_rows = normalize(blocks.reshape(-1, width)).astype(jnp.bfloat16)
 
     offset = lax.axis_index(("dp", "sub")) * own_count
     own_cents = normalize(lax.dynamic_slice_in_dim(centroids, offset, own_count, 0)).astype(jnp.bfloat16)
+    own_cents = lax.optimization_barrier(own_cents)
 
     scores = (
         lax.dot_general(
@@ -58,7 +56,11 @@
     local_peak = jnp.max(scores, axis=1)
     local_total = jnp.sum(jnp.exp(scores - local_peak[:, None]), axis=1)
 
-    stats = jnp.stack([local_peak.reshape(block_shape), local_total.reshape(block_shape)])
+    own_index = (own_block("sub"), own_block("dp"), own_block("cent"), 0)
+    known_weights = lax.dynamic_update_slice(
+        jnp.zeros(block_shape, jnp.float32), weights.astype(jnp.float32)[None, None, None], own_index
+    )
+    stats = jnp.stack([local_peak.reshape(block_shape), local_total.reshape(block_shape), known_weights])
     block_axis = {"sub": 1, "dp": 2, "cent": 3}
     for name in STAGES:
         stacked = gather_stage(stats, name)
@@ -69,7 +71,8 @@
         peaks, totals = stacked[:, 0], stacked[:, 1]
         row_peak = jnp.max(peaks, axis=0)
         row_total = jnp.sum(totals * jnp.exp(peaks - row_peak[None]), axis=0)
-        stats = jnp.stack([row_peak, row_total])
+        stats = jnp.stack([row_peak, row_total, jnp.sum(stacked[:, 2], axis=0)])
+    weight_float = stats[2].reshape(-1)
     log_sum = (stats[0] + jnp.log(stats[1])).reshape(-1)
 
     responsibility = (weight_float[:, None] * jnp.exp(scores - log_sum[:, None])).astype(jnp.bfloat16)
@@ -85,8 +88,8 @@
     moved = own_cents.astype(jnp.float32) + centroid_sums / (own_mass + 1.0)[:, None]
     renormed = normalize(moved).astype(jnp.bfloat16)
 
-    weighted_log_sum = (weight_float * log_sum / sharpness).reshape(block_shape)
-    objective = weighted_log_sum[own_block("sub"), own_block("dp"), own_block("cent")]
+    own_log_sum = log_sum.reshape(block_shape)[own_index[:3]]
+    objective = weights.astype(jnp.float32) * own_log_sum / sharpness
     return (centroid_sums, renormed, objective)
 
 

time: 43.9 us -> 38.4 us (0.87)
  waiting for transfers between devices: 15.1 us -> 13 us
  starting transfers between devices: 15.3 us -> 14.1 us
  matrix products: 2.96 us -> 1.77 us
  other arithmetic: 8.15 us -> 7.24 us
    ppermute x10, waiting for transfers between devices: 15.1 us -> 13 us  [gather_stage(): lax.ppermute(value, name, [(j, (j + q) % size) for j in range(size)])]
    reduce_sum x3, other arithmetic: 3.81 us -> 2.02 us  [normalize(): jnp.sum(floats * floats, axis=-1, keepdims=True) + 1e-06]
    dot_general x1, matrix products: 1.93 us -> 0.69 us  [shards(): lax.dot_general(unit_rows, own_cents, (((1,), (1,)), ((), ())), preferred...]
    ppermute x10, starting transfers between devices: 15.3 us -> 14.1 us  [gather_stage(): lax.ppermute(value, name, [(j, (j + q) % size) for j in range(size)])]
    convert_element_type x2 -> x3, other arithmetic: 0.86 us -> 1.59 us  [the longest x1 1.33 us: shards(): normalize(lax.dynamic_slice_in_dim(centroids, offset, own_count, 0))]
    div x0 -> x1, other arithmetic: none -> 0.52 us  [shards(): objective = weights.astype(jnp.float32) * own_log_sum / sharpness]
    squeeze x1 -> x0, other arithmetic: 0.52 us -> none  [shards(): weighted_log_sum[own_block('sub'), own_block('dp'), own_block('cent')]]
    another operation x4 -> x2, other arithmetic: 1.02 us -> 0.9 us  [gather_stage(): return jnp.stack(parts)]
  transfers between devices with their start and end apart: 10 -> 10, of which waited for: 8 -> 8; matrix products, arithmetic and copies ran while one was open for 4% -> 7% of each run, Pallas kernels for 0% -> 0%
where the time goes in v3:
time: 38.4 us; the launch traced here: 38.2 us
  starting transfers between devices  14.1 us (37%)
  waiting for transfers between devices  13 us (34%)
  other arithmetic  7.24 us (19%)
  matrix products  1.77 us (5%)
  between operations  1.51 us (4%)
  local copies, waits for them, and re-layouts  0.56 us (1%)
    ppermute x10, starting transfers between devices, gather_stage(): lax.ppermute(value, name, [(j, (j + q) % size) for j in range(size)])  14.1 us
    ppermute x10, waiting for transfers between devices, gather_stage(): lax.ppermute(value, name, [(j, (j + q) % size) for j in range(size)])  13 us
    reduce_sum x3, other arithmetic, normalize(): jnp.sum(floats * floats, axis=-1, keepdims=True) + 1e-06  2.02 us
    convert_element_type x1, other arithmetic, shards(): normalize(lax.dynamic_slice_in_dim(centroids, offset, own_count, 0))  1.33 us
    convert_element_type x1, other arithmetic, shards(): renormed = normalize(moved).astype(jnp.bfloat16)  1.25 us
    dot_general x1, matrix products, shards(): lax.dot_general(grouped_resp, grouped_rows, (((1,), (1,)), ((0,), (0,))),...  1.08 us
    another operation x2, other arithmetic, gather_stage(): return jnp.stack(parts)  0.9 us
  transfers between devices with their start and end apart: 10, of which 8 were waited for; matrix products, arithmetic and copies ran while one was open for 7% of the time, Pallas kernels for 0%

profile of v3, /device:TPU:0, one launch (start us, length us, event | category | flops | bytes accessed | tf_op | source)
XLA Modules:
  0.0 38.2 jit_solution(17868283335020313415)
XLA Ops:
  0.6 3.1 %collective-permute-start = (bf16[32,768]{1,0:T(8,128)(2,1)}, bf16[32,768]{1,0:T(8,128)(2,1)S(1)}, u32[]{:S(2)}, u32[]{:S(2)}) collective-permute-start(bf16[32,768]{1,0:T(8,128)(2,1)} %param.4), channel_id=1, source_target_pairs={{0,4},{4,8},{8,12},{12,0},{1,5},{5,9},{9,13},{13,1},{2,6},{6,10},{... | collective-permute-start | bytes 147464 | tf_op jit(solution)/shard_map/ppermute | solution.py:23
  3.7 2.1 %collective-permute-start.2 = (bf16[32,768]{1,0:T(8,128)(2,1)}, bf16[32,768]{1,0:T(8,128)(2,1)S(1)}, u32[]{:S(2)}, u32[]{:S(2)}) collective-permute-start(bf16[32,768]{1,0:T(8,128)(2,1)} %param.4), channel_id=1, source_target_pairs={{0,12},{4,0},{8,4},{12,8},{1,13},{5,1},{9,5},{13,9},{2,14},{6,2},{... | collective-permute-start | bytes 147464 | tf_op jit(solution)/shard_map/ppermute | solution.py:23
  5.8 0.9 %collective-permute-start.1 = (bf16[32,768]{1,0:T(8,128)(2,1)}, bf16[32,768]{1,0:T(8,128)(2,1)S(1)}, u32[]{:S(2)}, u32[]{:S(2)}) collective-permute-start(bf16[32,768]{1,0:T(8,128)(2,1)} %param.4), channel_id=1, source_target_pairs={{0,8},{4,12},{8,0},{12,4},{1,9},{5,13},{9,1},{13,5},{2,10},{6,14},... | collective-permute-start | bytes 147464 | tf_op jit(solution)/shard_map/ppermute | solution.py:23
  6.7 1.4 %fusion = f32[512]{0:T(512)S(1)} fusion(bf16[2048,768]{1,0:T(8,128)(2,1)} %param.6, s32[]{:T(128)S(6)} %select_n.3), kind=kLoop, calls=%fused_computation.3 | loop fusion | flops 1179136 | bytes 788484 | tf_op jit(solution)/shard_map/reduce_sum | solution.py:12
  8.1 0.0 collective-permute-done
  8.1 0.4 %collective-permute-done.2 = bf16[32,768]{1,0:T(8,128)(2,1)S(1)} collective-permute-done((bf16[32,768]{1,0:T(8,128)(2,1)}, bf16[32,768]{1,0:T(8,128)(2,1)S(1)}, u32[]{:S(2)}, u32[]{:S(2)}) %collective-permute-start.2) | collective-permute-done | bytes 49184 | tf_op jit(solution)/shard_map/ppermute | solution.py:23
  8.5 2.6 %collective-permute-done.1 = bf16[32,768]{1,0:T(8,128)(2,1)S(1)} collective-permute-done((bf16[32,768]{1,0:T(8,128)(2,1)}, bf16[32,768]{1,0:T(8,128)(2,1)S(1)}, u32[]{:S(2)}, u32[]{:S(2)}) %collective-permute-start.1) | collective-permute-done | bytes 49184 | tf_op jit(solution)/shard_map/ppermute | solution.py:23
  11.1 0.0 copy-start.1
  11.1 0.8 %fusion.27 = (bf16[1,4,32,768]{3,2,1,0:T(8,128)(2,1)S(1)}, bf16[4,32,768]{2,1,0:T(8,128)(2,1)S(1)}) fusion(bf16[1,32,768]{2,1,0:T(8,128)(2,1)S(1)} %bitcast.114, bf16[1,32,768]{2,1,0:T(8,128)(2,1)S(1)} %bitcast.115, bf16[1,32,768]{2,1,0:T(8,128)(2,1)S(1)} %bitcast.113, bf16[1,32,768]{2,1,0:T(8,128)(2,1)} %bitcast.112), kind=kLoop, calls=%fused_computation.79 | loop fusion | flops 294912 | bytes 589824 | tf_op jit(solution)/shard_map/stack | solution.py:25
  12.0 1.6 %collective-permute-start.3 = (bf16[4,32,768]{2,1,0:T(8,128)(2,1)S(1)}, bf16[4,32,768]{2,1,0:T(8,128)(2,1)S(1)}, u32[]{:S(2)}, u32[]{:S(2)}) collective-permute-start(bf16[4,32,768]{2,1,0:T(8,128)(2,1)S(1)} %get-tuple-element.8), channel_id=1, source_target_pairs={{0,2},{2,0},{1,3},{3,1},{4,6},{6,4},{5,7},{7,5},{8,10},{10,8},{9,1... | collective-permute-start | bytes 589832 | tf_op jit(solution)/shard_map/ppermute | solution.py:23
  13.6 4.1 %collective-permute-done.3 = bf16[4,32,768]{2,1,0:T(8,128)(2,1)S(1)} collective-permute-done((bf16[4,32,768]{2,1,0:T(8,128)(2,1)S(1)}, bf16[4,32,768]{2,1,0:T(8,128)(2,1)S(1)}, u32[]{:S(2)}, u32[]{:S(2)}) %collective-permute-start.3) | collective-permute-done | bytes 196640 | tf_op jit(solution)/shard_map/ppermute | solution.py:23
  17.7 0.1 fusion.26
  17.8 0.1 collective-permute-start.4
  17.8 1.3 %fusion.1 = bf16[512,768]{1,0:T(8,128)(2,1)S(1)} fusion(f32[512]{0:T(512)S(1)} %add_rsqrt_fusion.2, bf16[2048,768]{1,0:T(8,128)(2,1)} %param.6, s32[]{:T(128)S(6)} %select_n.3), kind=kLoop, calls=%fused_computation.4 | loop fusion | flops 1179648 | bytes 1574916 | tf_op jit(solution)/shard_map/convert_element_type | solution.py:46
  19.8 0.0 copy-done.1
  19.9 0.0 collective-permute-done.4
  19.9 0.2 multiply_reduce_fusion.1
  20.1 0.1 maximum_convert_fusion
  20.2 0.1 rsqrt.32
  20.3 0.2 fusion.2
  20.5 0.7 %fusion.31 = (f32[512]{0:T(512)S(1)}, f32[512,512]{1,0:T(8,128)S(1)}) fusion(f32[]{:T(128)} %bitcast.102, bf16[512,768]{1,0:T(8,128)(2,1)S(1)} %fusion.2, bf16[512,768]{1,0:T(8,128)(2,1)S(1)} %fusion.1), kind=kOutput, calls=%fused_computation.83 | convolution fusion | flops 403176960 | bytes 2623492 | tf_op jit(solution)/shard_map/dot_general | solution.py:50
  21.2 0.1 stack_reshape.6
  21.3 0.3 exponential_reduce_fusion
  21.6 0.1 stack_reshape.7
  21.7 0.9 %collective-permute-start.6 = (f32[3,2,2,4,32]{4,3,2,1,0:T(4,128)S(1)}, f32[3,2,2,4,32]{4,3,2,1,0:T(4,128)S(1)}, u32[]{:S(2)}, u32[]{:S(2)}) collective-permute-start(f32[3,2,2,4,32]{4,3,2,1,0:T(4,128)S(1)} %get-tuple-element.18), channel_id=1, source_target_pairs={{0,8},{4,12},{8,0},{12,4},{1,9},{5,13},{9,1},{13,5},{2,10},{6,14},... | collective-permute-start | bytes 18440 | tf_op jit(solution)/shard_map/ppermute | solution.py:23
  22.6 2.4 %collective-permute-start.5 = (f32[3,2,2,4,32]{4,3,2,1,0:T(4,128)S(1)}, f32[3,2,2,4,32]{4,3,2,1,0:T(4,128)S(1)}, u32[]{:S(2)}, u32[]{:S(2)}) collective-permute-start(f32[3,2,2,4,32]{4,3,2,1,0:T(4,128)S(1)} %get-tuple-element.18), channel_id=1, source_target_pairs={{0,4},{4,8},{8,12},{12,0},{1,5},{5,9},{9,13},{13,1},{2,6},{6,10},{... | collective-permute-start | bytes 18440 | tf_op jit(solution)/shard_map/ppermute | solution.py:23
  25.0 1.4 %collective-permute-start.7 = (f32[3,2,2,4,32]{4,3,2,1,0:T(4,128)S(1)}, f32[3,2,2,4,32]{4,3,2,1,0:T(4,128)S(1)}, u32[]{:S(2)}, u32[]{:S(2)}) collective-permute-start(f32[3,2,2,4,32]{4,3,2,1,0:T(4,128)S(1)} %get-tuple-element.18), channel_id=1, source_target_pairs={{0,12},{4,0},{8,4},{12,8},{1,13},{5,1},{9,5},{13,9},{2,14},{6,2},{... | collective-permute-start | bytes 18440 | tf_op jit(solution)/shard_map/ppermute | solution.py:23
  26.4 0.4 %collective-permute-done.6 = f32[3,2,2,4,32]{4,3,2,1,0:T(4,128)S(1)} collective-permute-done((f32[3,2,2,4,32]{4,3,2,1,0:T(4,128)S(1)}, f32[3,2,2,4,32]{4,3,2,1,0:T(4,128)S(1)}, u32[]{:S(2)}, u32[]{:S(2)}) %collective-permute-start.6) | collective-permute-done | bytes 6176 | tf_op jit(solution)/shard_map/ppermute | solution.py:23
  26.8 1.4 %collective-permute-done.5 = f32[3,2,2,4,32]{4,3,2,1,0:T(4,128)S(1)} collective-permute-done((f32[3,2,2,4,32]{4,3,2,1,0:T(4,128)S(1)}, f32[3,2,2,4,32]{4,3,2,1,0:T(4,128)S(1)}, u32[]{:S(2)}, u32[]{:S(2)}) %collective-permute-start.5) | collective-permute-done | bytes 6176 | tf_op jit(solution)/shard_map/ppermute | solution.py:23
  28.2 0.6 %collective-permute-done.7 = f32[3,2,2,4,32]{4,3,2,1,0:T(4,128)S(1)} collective-permute-done((f32[3,2,2,4,32]{4,3,2,1,0:T(4,128)S(1)}, f32[3,2,2,4,32]{4,3,2,1,0:T(4,128)S(1)}, u32[]{:S(2)}, u32[]{:S(2)}) %collective-permute-start.7) | collective-permute-done | bytes 6176 | tf_op jit(solution)/shard_map/ppermute | solution.py:23
  29.0 1.6 %collective-permute-start.8 = (f32[3,2,2,4,32]{4,3,2,1,0:T(4,128)S(1)}, f32[3,2,2,4,32]{4,3,2,1,0:T(4,128)S(1)}, u32[]{:S(2)}, u32[]{:S(2)}) collective-permute-start(f32[3,2,2,4,32]{4,3,2,1,0:T(4,128)S(1)} %get-tuple-element.14), channel_id=1, source_target_pairs={{0,2},{2,0},{1,3},{3,1},{4,6},{6,4},{5,7},{7,5},{8,10},{10,8},{9,1... | collective-permute-start | bytes 18440 | tf_op jit(solution)/shard_map/ppermute | solution.py:23
  30.6 2.3 %collective-permute-done.8 = f32[3,2,2,4,32]{4,3,2,1,0:T(4,128)S(1)} collective-permute-done((f32[3,2,2,4,32]{4,3,2,1,0:T(4,128)S(1)}, f32[3,2,2,4,32]{4,3,2,1,0:T(4,128)S(1)}, u32[]{:S(2)}, u32[]{:S(2)}) %collective-permute-start.8) | collective-permute-done | bytes 6176 | tf_op jit(solution)/shard_map/ppermute | solution.py:23
  33.0 0.1 collective-permute-start.9
  33.1 0.1 rsqrt.34
  33.2 1.1 %collective-permute-done.9 = f32[3,2,2,4,32]{4,3,2,1,0:T(4,128)S(1)} collective-permute-done((f32[3,2,2,4,32]{4,3,2,1,0:T(4,128)S(1)}, f32[3,2,2,4,32]{4,3,2,1,0:T(4,128)S(1)}, u32[]{:S(2)}, u32[]{:S(2)}) %collective-permute-start.9) | collective-permute-done | bytes 6176 | tf_op jit(solution)/shard_map/ppermute | solution.py:23
  34.4 0.1 mul.85
  34.4 0.1 add.63
  34.5 0.5 %fusion.22 = f32[32]{0:T(128)} fusion(f32[2,2,4,32]{3,2,1,0:T(4,128)S(1)} %bitcast.118, s32[32]{0:T(128)S(1)} %copy-done.1, f32[]{:T(128)} %bitcast.103), kind=kLoop, calls=%fused_computation.72 | loop fusion | flops 96 | bytes 388 | tf_op jit(solution)/shard_map/div | solution.py:92
  35.1 0.3 bitcast_reduce_fusion.3
  35.4 1.1 %convert_reduce_fusion = f32[512,768]{1,0:T(8,128)S(1)} fusion(bf16[4,128,512]{2,1,0:T(8,128)(2,1)S(1)} %bitcast.105, f32[4,128,768]{2,1,0:T(8,128)S(1)} %bitcast.104, f32[4,128]{1,0:T(4,128)S(1)} %rsqrt.34), kind=kOutput, calls=%fused_computation | convolution fusion | flops 407764992 | bytes 3672064 | tf_op jit(solution)/shard_map/dot_general | solution.py:81
  36.5 0.0 copy-start
  36.5 0.4 %multiply_reduce_fusion = f32[512]{0:T(512)S(1)} fusion(f32[512,768]{1,0:T(8,128)S(1)} %convert_reduce_fusion, f32[512]{0:T(512)S(1)} %broadcast_add_fusion, bf16[512,768]{1,0:T(8,128)(2,1)S(1)} %fusion.1), kind=kLoop, calls=%fused_computation.8 | loop fusion | flops 1965568 | bytes 2363392 | tf_op jit(solution)/shard_map/reduce_sum | solution.py:12
  36.9 1.2 %multiply_convert_fusion = bf16[512,768]{1,0:T(8,128)(2,1)} fusion(f32[512]{0:T(512)S(1)} %add_rsqrt_fusion.1, f32[512,768]{1,0:T(8,128)S(1)} %convert_reduce_fusion, f32[512]{0:T(512)S(1)} %broadcast_add_fusion, bf16[512,768]{1,0:T(8,128)(2,1)S(1)} %fusion.1), kind=kLoop, calls=%fused_computation.7 | loop fusion | flops 1966080 | bytes 3149824 | tf_op jit(solution)/shard_map/convert_element_type | solution.py:89
  38.2 0.0 copy-done
  (32 shorter events, 0.4 us)
Async XLA Ops:
  0.6 7.5 %collective-permute-start = (bf16[32,768]{1,0:T(8,128)(2,1)}, bf16[32,768]{1,0:T(8,128)(2,1)S(1)}, u32[]{:S(2)}, u32[]{:S(2)}) collective-permute-start(bf16[32,768]{1,0:T(8,128)(2,1)} %param.4), channel_id=1, source_target_pairs={{0,4},{4,8},{8,12},{12,0},{1,5},{5,9},{9,13},{13,1},{2,6},{6,10},{... | collective-permute-start | bytes 147464 | tf_op jit(solution)/shard_map/ppermute | solution.py:23
  3.7 4.8 %collective-permute-start.2 = (bf16[32,768]{1,0:T(8,128)(2,1)}, bf16[32,768]{1,0:T(8,128)(2,1)S(1)}, u32[]{:S(2)}, u32[]{:S(2)}) collective-permute-start(bf16[32,768]{1,0:T(8,128)(2,1)} %param.4), channel_id=1, source_target_pairs={{0,12},{4,0},{8,4},{12,8},{1,13},{5,1},{9,5},{13,9},{2,14},{6,2},{... | collective-permute-start | bytes 147464 | tf_op jit(solution)/shard_map/ppermute | solution.py:23
  5.8 5.3 %collective-permute-start.1 = (bf16[32,768]{1,0:T(8,128)(2,1)}, bf16[32,768]{1,0:T(8,128)(2,1)S(1)}, u32[]{:S(2)}, u32[]{:S(2)}) collective-permute-start(bf16[32,768]{1,0:T(8,128)(2,1)} %param.4), channel_id=1, source_target_pairs={{0,8},{4,12},{8,0},{12,4},{1,9},{5,13},{9,1},{13,5},{2,10},{6,14},... | collective-permute-start | bytes 147464 | tf_op jit(solution)/shard_map/ppermute | solution.py:23
  11.1 8.7 %copy-start.1 = (s32[32]{0:T(128)S(1)}, s32[32]{0:T(128)}, u32[]{:S(2)}) copy-start(s32[32]{0:T(128)} %param.5) | copy-start | bytes 388
  12.0 5.7 %collective-permute-start.3 = (bf16[4,32,768]{2,1,0:T(8,128)(2,1)S(1)}, bf16[4,32,768]{2,1,0:T(8,128)(2,1)S(1)}, u32[]{:S(2)}, u32[]{:S(2)}) collective-permute-start(bf16[4,32,768]{2,1,0:T(8,128)(2,1)S(1)} %get-tuple-element.8), channel_id=1, source_target_pairs={{0,2},{2,0},{1,3},{3,1},{4,6},{6,4},{5,7},{7,5},{8,10},{10,8},{9,1... | collective-permute-start | bytes 589832 | tf_op jit(solution)/shard_map/ppermute | solution.py:23
  17.8 2.1 %collective-permute-start.4 = (bf16[2,4,32,768]{3,2,1,0:T(8,128)(2,1)S(1)}, bf16[2,4,32,768]{3,2,1,0:T(8,128)(2,1)S(1)}, u32[]{:S(2)}, u32[]{:S(2)}) collective-permute-start(bf16[2,4,32,768]{3,2,1,0:T(8,128)(2,1)S(1)} %get-tuple-element.6), channel_id=1, source_target_pairs={{0,1},{1,0},{2,3},{3,2},{4,5},{5,4},{6,7},{7,6},{8,9},{9,8},{10,11... | collective-permute-start | bytes 1179656 | tf_op jit(solution)/shard_map/ppermute | solution.py:23
  21.7 5.1 %collective-permute-start.6 = (f32[3,2,2,4,32]{4,3,2,1,0:T(4,128)S(1)}, f32[3,2,2,4,32]{4,3,2,1,0:T(4,128)S(1)}, u32[]{:S(2)}, u32[]{:S(2)}) collective-permute-start(f32[3,2,2,4,32]{4,3,2,1,0:T(4,128)S(1)} %get-tuple-element.18), channel_id=1, source_target_pairs={{0,8},{4,12},{8,0},{12,4},{1,9},{5,13},{9,1},{13,5},{2,10},{6,14},... | collective-permute-start | bytes 18440 | tf_op jit(solution)/shard_map/ppermute | solution.py:23
  22.6 5.6 %collective-permute-start.5 = (f32[3,2,2,4,32]{4,3,2,1,0:T(4,128)S(1)}, f32[3,2,2,4,32]{4,3,2,1,0:T(4,128)S(1)}, u32[]{:S(2)}, u32[]{:S(2)}) collective-permute-start(f32[3,2,2,4,32]{4,3,2,1,0:T(4,128)S(1)} %get-tuple-element.18), channel_id=1, source_target_pairs={{0,4},{4,8},{8,12},{12,0},{1,5},{5,9},{9,13},{13,1},{2,6},{6,10},{... | collective-permute-start | bytes 18440 | tf_op jit(solution)/shard_map/ppermute | solution.py:23
  25.0 3.8 %collective-permute-start.7 = (f32[3,2,2,4,32]{4,3,2,1,0:T(4,128)S(1)}, f32[3,2,2,4,32]{4,3,2,1,0:T(4,128)S(1)}, u32[]{:S(2)}, u32[]{:S(2)}) collective-permute-start(f32[3,2,2,4,32]{4,3,2,1,0:T(4,128)S(1)} %get-tuple-element.18), channel_id=1, source_target_pairs={{0,12},{4,0},{8,4},{12,8},{1,13},{5,1},{9,5},{13,9},{2,14},{6,2},{... | collective-permute-start | bytes 18440 | tf_op jit(solution)/shard_map/ppermute | solution.py:23
  29.0 3.9 %collective-permute-start.8 = (f32[3,2,2,4,32]{4,3,2,1,0:T(4,128)S(1)}, f32[3,2,2,4,32]{4,3,2,1,0:T(4,128)S(1)}, u32[]{:S(2)}, u32[]{:S(2)}) collective-permute-start(f32[3,2,2,4,32]{4,3,2,1,0:T(4,128)S(1)} %get-tuple-element.14), channel_id=1, source_target_pairs={{0,2},{2,0},{1,3},{3,1},{4,6},{6,4},{5,7},{7,5},{8,10},{10,8},{9,1... | collective-permute-start | bytes 18440 | tf_op jit(solution)/shard_map/ppermute | solution.py:23
  33.0 1.3 %collective-permute-start.9 = (f32[3,2,2,4,32]{4,3,2,1,0:T(4,128)S(1)}, f32[3,2,2,4,32]{4,3,2,1,0:T(4,128)S(1)}, u32[]{:S(2)}, u32[]{:S(2)}) collective-permute-start(f32[3,2,2,4,32]{4,3,2,1,0:T(4,128)S(1)} %get-tuple-element.10), channel_id=1, source_target_pairs={{0,1},{1,0},{2,3},{3,2},{4,5},{5,4},{6,7},{7,6},{8,9},{9,8},{10,11... | collective-permute-start | bytes 18440 | tf_op jit(solution)/shard_map/ppermute | solution.py:23
  36.5 1.7 %copy-start = (f32[512,768]{1,0:T(8,128)}, f32[512,768]{1,0:T(8,128)S(1)}, u32[]{:S(2)}) copy-start(f32[512,768]{1,0:T(8,128)S(1)} %convert_reduce_fusion) | copy-start | bytes 4718596

commit v4 on v3

--- a/solution.py
+++ b/solution.py
@@ -3,7 +3,7 @@
 from jax import lax
 from jax.sharding import PartitionSpec as P
 
-STAGES = ("cent", "dp", "sub")
+STAGES = ("cent", ("dp", "sub"))
 SHIFT_MAX = 4
 
 
@@ -34,7 +34,7 @@
     sharpness = inverse_temp[0]
     row_dev, width = embeddings.shape
     sizes = {name: lax.axis_size(name) for name in STAGES}
-    n_groups = sizes["dp"] * sizes["sub"]
+    n_groups = sizes[STAGES[1]]
     own_count = centroids.shape[0] // n_groups
 
     blocks = embeddings
@@ -52,16 +52,16 @@
         )
         * sharpness
     )
-    block_shape = (sizes["sub"], sizes["dp"], sizes["cent"], row_dev)
+    block_shape = (n_groups, sizes["cent"], row_dev)
     local_peak = jnp.max(scores, axis=1)
     local_total = jnp.sum(jnp.exp(scores - local_peak[:, None]), axis=1)
 
-    own_index = (own_block("sub"), own_block("dp"), own_block("cent"), 0)
+    own_index = (own_block(STAGES[1]), own_block("cent"), 0)
     known_weights = lax.dynamic_update_slice(
-        jnp.zeros(block_shape, jnp.float32), weights.astype(jnp.float32)[None, None, None], own_index
+        jnp.zeros(block_shape, jnp.float32), weights.astype(jnp.float32)[None, None], own_index
     )
     stats = jnp.stack([local_peak.reshape(block_shape), local_total.reshape(block_shape), known_weights])
-    block_axis = {"sub": 1, "dp": 2, "cent": 3}
+    block_axis = {STAGES[1]: 1, "cent": 2}
     for name in STAGES:
         stacked = gather_stage(stats, name)
         if relative(name):
@@ -88,7 +88,7 @@
     moved = own_cents.astype(jnp.float32) + centroid_sums / (own_mass + 1.0)[:, None]
     renormed = normalize(moved).astype(jnp.bfloat16)
 
-    own_log_sum = log_sum.reshape(block_shape)[own_index[:3]]
+    own_log_sum = log_sum.reshape(block_shape)[own_index[:2]]
     objective = weights.astype(jnp.float32) * own_log_sum / sharpness
     return (centroid_sums, renormed, objective)
 

time: 38.4 us -> 39.7 us (1.034)
  the two profiles are of different devices: /device:TPU:0 before, /device:TPU:1 now
where the time goes in v4:
time: 39.7 us; the launch traced here: 39.5 us
  starting transfers between devices  14.7 us (37%)
  waiting for transfers between devices  14.5 us (37%)
  other arithmetic  6.39 us (16%)
  matrix products  1.76 us (4%)
  between operations  1.53 us (4%)
  local copies, waits for them, and re-layouts  0.57 us (1%)
    ppermute x12, starting transfers between devices, gather_stage(): lax.ppermute(value, name, [(j, (j + q) % size) for j in range(size)])  14.7 us
    ppermute x12, waiting for transfers between devices, gather_stage(): lax.ppermute(value, name, [(j, (j + q) % size) for j in range(size)])  14.5 us
    reduce_sum x3, other arithmetic, normalize(): jnp.sum(floats * floats, axis=-1, keepdims=True) + 1e-06  2.02 us
    convert_element_type x1, other arithmetic, shards(): normalize(lax.dynamic_slice_in_dim(centroids, offset, own_count, 0))  1.33 us
    convert_element_type x1, other arithmetic, shards(): renormed = normalize(moved).astype(jnp.bfloat16)  1.25 us
    dot_general x1, matrix products, shards(): lax.dot_general(grouped_resp, grouped_rows, (((1,), (1,)), ((0,), (0,))),...  1.07 us
  transfers between devices with their start and end apart: 12, of which 9 were waited for; matrix products, arithmetic and copies ran while one was open for 7% of the time, Pallas kernels for 0%

profile of v4, /device:TPU:1, one launch (start us, length us, event | category | flops | bytes accessed | tf_op | source)
XLA Modules:
  0.0 39.5 jit_solution(3541131210185927951)
XLA Ops:
  0.6 0.0 copy-start.1
  0.6 0.0 copy-start.2
  0.6 2.2 %collective-permute-start = (bf16[32,768]{1,0:T(8,128)(2,1)}, bf16[32,768]{1,0:T(8,128)(2,1)S(1)}, u32[]{:S(2)}, u32[]{:S(2)}) collective-permute-start(bf16[32,768]{1,0:T(8,128)(2,1)} %param.4), channel_id=1, source_target_pairs={{0,4},{4,8},{8,12},{12,0},{1,5},{5,9},{9,13},{13,1},{2,6},{6,10},{... | collective-permute-start | bytes 147464 | tf_op jit(solution)/shard_map/ppermute | solution.py:23
  2.8 2.3 %collective-permute-start.1 = (bf16[32,768]{1,0:T(8,128)(2,1)}, bf16[32,768]{1,0:T(8,128)(2,1)S(1)}, u32[]{:S(2)}, u32[]{:S(2)}) collective-permute-start(bf16[32,768]{1,0:T(8,128)(2,1)} %param.4), channel_id=1, source_target_pairs={{0,8},{4,12},{8,0},{12,4},{1,9},{5,13},{9,1},{13,5},{2,10},{6,14},... | collective-permute-start | bytes 147464 | tf_op jit(solution)/shard_map/ppermute | solution.py:23
  5.1 1.1 %collective-permute-start.2 = (bf16[32,768]{1,0:T(8,128)(2,1)}, bf16[32,768]{1,0:T(8,128)(2,1)S(1)}, u32[]{:S(2)}, u32[]{:S(2)}) collective-permute-start(bf16[32,768]{1,0:T(8,128)(2,1)} %param.4), channel_id=1, source_target_pairs={{0,12},{4,0},{8,4},{12,8},{1,13},{5,1},{9,5},{13,9},{2,14},{6,2},{... | collective-permute-start | bytes 147464 | tf_op jit(solution)/shard_map/ppermute | solution.py:23
  6.2 1.4 %fusion = f32[512]{0:T(512)S(1)} fusion(bf16[2048,768]{1,0:T(8,128)(2,1)} %param.6, s32[]{:T(128)S(6)} %select_n.3), kind=kLoop, calls=%fused_computation.3 | loop fusion | flops 1179136 | bytes 788484 | tf_op jit(solution)/shard_map/reduce_sum | solution.py:12
  7.6 1.3 %fusion.1 = bf16[512,768]{1,0:T(8,128)(2,1)S(1)} fusion(f32[512]{0:T(512)S(1)} %add_rsqrt_fusion.2, bf16[2048,768]{1,0:T(8,128)(2,1)} %param.6, s32[]{:T(128)S(6)} %select_n.3), kind=kLoop, calls=%fused_computation.4 | loop fusion | flops 1179648 | bytes 1574916 | tf_op jit(solution)/shard_map/convert_element_type | solution.py:46
  8.9 0.0 collective-permute-done
  8.9 0.0 collective-permute-done.1
  8.9 0.3 collective-permute-done.2
  9.3 0.0 copy-done.1
  9.3 2.7 %collective-permute-start.3 = (bf16[4,32,768]{2,1,0:T(8,128)(2,1)S(1)}, bf16[4,32,768]{2,1,0:T(8,128)(2,1)S(1)}, u32[]{:S(2)}, u32[]{:S(2)}) collective-permute-start(bf16[4,32,768]{2,1,0:T(8,128)(2,1)S(1)} %get-tuple-element.6), channel_id=1, source_target_pairs={{0,1},{1,2},{2,3},{3,0},{4,5},{5,6},{6,7},{7,4},{8,9},{9,10},{10,1... | collective-permute-start | bytes 589832 | tf_op jit(solution)/shard_map/ppermute | solution.py:23
  12.0 0.1 collective-permute-start.4
  12.1 0.3 collective-permute-start.5
  12.5 0.0 copy-done.2
  13.1 3.0 %collective-permute-done.3 = bf16[4,32,768]{2,1,0:T(8,128)(2,1)S(1)} collective-permute-done((bf16[4,32,768]{2,1,0:T(8,128)(2,1)S(1)}, bf16[4,32,768]{2,1,0:T(8,128)(2,1)S(1)}, u32[]{:S(2)}, u32[]{:S(2)}) %collective-permute-start.3) | collective-permute-done | bytes 196640 | tf_op jit(solution)/shard_map/ppermute | solution.py:23
  16.1 4.8 %collective-permute-done.4 = bf16[4,32,768]{2,1,0:T(8,128)(2,1)S(1)} collective-permute-done((bf16[4,32,768]{2,1,0:T(8,128)(2,1)S(1)}, bf16[4,32,768]{2,1,0:T(8,128)(2,1)S(1)}, u32[]{:S(2)}, u32[]{:S(2)}) %collective-permute-start.4) | collective-permute-done | bytes 196640 | tf_op jit(solution)/shard_map/ppermute | solution.py:23
  20.9 0.6 %collective-permute-done.5 = bf16[4,32,768]{2,1,0:T(8,128)(2,1)S(1)} collective-permute-done((bf16[4,32,768]{2,1,0:T(8,128)(2,1)S(1)}, bf16[4,32,768]{2,1,0:T(8,128)(2,1)S(1)}, u32[]{:S(2)}, u32[]{:S(2)}) %collective-permute-start.5) | collective-permute-done | bytes 196640 | tf_op jit(solution)/shard_map/ppermute | solution.py:23
  21.5 0.2 multiply_reduce_fusion.1
  21.7 0.1 maximum_convert_fusion
  21.9 0.1 rsqrt.32
  22.0 0.2 fusion.2
  22.1 0.7 %fusion.25 = (f32[512]{0:T(512)S(1)}, f32[512,512]{1,0:T(8,128)S(1)}) fusion(f32[]{:T(128)} %bitcast.86, bf16[512,768]{1,0:T(8,128)(2,1)S(1)} %fusion.2, bf16[512,768]{1,0:T(8,128)(2,1)S(1)} %fusion.1), kind=kOutput, calls=%fused_computation.67 | convolution fusion | flops 403176960 | bytes 2623492 | tf_op jit(solution)/shard_map/dot_general | solution.py:50
  22.8 0.1 stack_reshape.6
  22.9 0.3 exponential_reduce_fusion
  23.2 0.1 stack_reshape.7
  23.3 0.6 %collective-permute-start.6 = (f32[3,4,4,32]{3,2,1,0:T(4,128)S(1)}, f32[3,4,4,32]{3,2,1,0:T(4,128)S(1)}, u32[]{:S(2)}, u32[]{:S(2)}) collective-permute-start(f32[3,4,4,32]{3,2,1,0:T(4,128)S(1)} %get-tuple-element.12), channel_id=1, source_target_pairs={{0,4},{4,8},{8,12},{12,0},{1,5},{5,9},{9,13},{13,1},{2,6},{6,10},{... | collective-permute-start | bytes 18440 | tf_op jit(solution)/shard_map/ppermute | solution.py:23
  23.9 2.6 %collective-permute-start.7 = (f32[3,4,4,32]{3,2,1,0:T(4,128)S(1)}, f32[3,4,4,32]{3,2,1,0:T(4,128)S(1)}, u32[]{:S(2)}, u32[]{:S(2)}) collective-permute-start(f32[3,4,4,32]{3,2,1,0:T(4,128)S(1)} %get-tuple-element.12), channel_id=1, source_target_pairs={{0,8},{4,12},{8,0},{12,4},{1,9},{5,13},{9,1},{13,5},{2,10},{6,14},... | collective-permute-start | bytes 18440 | tf_op jit(solution)/shard_map/ppermute | solution.py:23
  26.5 0.1 collective-permute-start.8
  26.7 1.3 %collective-permute-done.6 = f32[3,4,4,32]{3,2,1,0:T(4,128)S(1)} collective-permute-done((f32[3,4,4,32]{3,2,1,0:T(4,128)S(1)}, f32[3,4,4,32]{3,2,1,0:T(4,128)S(1)}, u32[]{:S(2)}, u32[]{:S(2)}) %collective-permute-start.6) | collective-permute-done | bytes 6176 | tf_op jit(solution)/shard_map/ppermute | solution.py:23
  28.0 1.1 %collective-permute-done.7 = f32[3,4,4,32]{3,2,1,0:T(4,128)S(1)} collective-permute-done((f32[3,4,4,32]{3,2,1,0:T(4,128)S(1)}, f32[3,4,4,32]{3,2,1,0:T(4,128)S(1)}, u32[]{:S(2)}, u32[]{:S(2)}) %collective-permute-start.7) | collective-permute-done | bytes 6176 | tf_op jit(solution)/shard_map/ppermute | solution.py:23
  29.2 0.2 collective-permute-done.8
  29.5 1.5 %collective-permute-start.9 = (f32[3,4,4,32]{3,2,1,0:T(4,128)S(1)}, f32[3,4,4,32]{3,2,1,0:T(4,128)S(1)}, u32[]{:S(2)}, u32[]{:S(2)}) collective-permute-start(f32[3,4,4,32]{3,2,1,0:T(4,128)S(1)} %get-tuple-element.8), channel_id=1, source_target_pairs={{0,1},{1,2},{2,3},{3,0},{4,5},{5,6},{6,7},{7,4},{8,9},{9,10},{10,1... | collective-permute-start | bytes 18440 | tf_op jit(solution)/shard_map/ppermute | solution.py:23
  31.0 0.1 rsqrt.34
  31.1 1.2 %collective-permute-start.10 = (f32[3,4,4,32]{3,2,1,0:T(4,128)S(1)}, f32[3,4,4,32]{3,2,1,0:T(4,128)S(1)}, u32[]{:S(2)}, u32[]{:S(2)}) collective-permute-start(f32[3,4,4,32]{3,2,1,0:T(4,128)S(1)} %get-tuple-element.8), channel_id=1, source_target_pairs={{0,2},{1,3},{2,0},{3,1},{4,6},{5,7},{6,4},{7,5},{8,10},{9,11},{10,... | collective-permute-start | bytes 18440 | tf_op jit(solution)/shard_map/ppermute | solution.py:23
  32.3 0.0 collective-permute-start.11
  32.3 0.0 collective-permute-done.9
  32.3 1.5 %collective-permute-done.10 = f32[3,4,4,32]{3,2,1,0:T(4,128)S(1)} collective-permute-done((f32[3,4,4,32]{3,2,1,0:T(4,128)S(1)}, f32[3,4,4,32]{3,2,1,0:T(4,128)S(1)}, u32[]{:S(2)}, u32[]{:S(2)}) %collective-permute-start.10) | collective-permute-done | bytes 6176 | tf_op jit(solution)/shard_map/ppermute | solution.py:23
  33.8 1.7 %collective-permute-done.11 = f32[3,4,4,32]{3,2,1,0:T(4,128)S(1)} collective-permute-done((f32[3,4,4,32]{3,2,1,0:T(4,128)S(1)}, f32[3,4,4,32]{3,2,1,0:T(4,128)S(1)}, u32[]{:S(2)}, u32[]{:S(2)}) %collective-permute-start.11) | collective-permute-done | bytes 6176 | tf_op jit(solution)/shard_map/ppermute | solution.py:23
  35.7 0.1 add.63
  35.8 0.1 mul.81
  35.8 0.3 bitcast_reduce_fusion.2
  36.2 1.1 %convert_reduce_fusion = f32[512,768]{1,0:T(8,128)S(1)} fusion(bf16[4,128,512]{2,1,0:T(8,128)(2,1)S(1)} %bitcast.97, bf16[1,128,768]{2,1,0:T(8,128)(2,1)S(1)} %bitcast.96, bf16[1,128,768]{2,1,0:T(8,128)(2,1)S(1)} %bitcast.93, bf16[1,128,768]{2,1,0:T(8,128)(2,1)S(1)} %bitcast.90, bf16[1,128,768]{2,1,0:T(8,128)(2,1)S(1)} %bitcast.98, f32[4,128]{1,0:T(4,128)S(1)} %rsqrt.34), kind=kOutput, calls=%fused_computation | convolution fusion | flops 409337856 | bytes 2885632 | tf_op jit(solution)/shard_map/dot_general | solution.py:81
  37.2 0.0 copy-start
  37.3 0.4 %multiply_reduce_fusion = f32[512]{0:T(512)S(1)} fusion(f32[512,768]{1,0:T(8,128)S(1)} %convert_reduce_fusion, f32[512]{0:T(512)S(1)} %broadcast_add_fusion, bf16[512,768]{1,0:T(8,128)(2,1)S(1)} %fusion.1), kind=kLoop, calls=%fused_computation.8 | loop fusion | flops 1965568 | bytes 2363392 | tf_op jit(solution)/shard_map/reduce_sum | solution.py:12
  37.7 1.2 %multiply_convert_fusion = bf16[512,768]{1,0:T(8,128)(2,1)} fusion(f32[512]{0:T(512)S(1)} %add_rsqrt_fusion.1, f32[512,768]{1,0:T(8,128)S(1)} %convert_reduce_fusion, f32[512]{0:T(512)S(1)} %broadcast_add_fusion, bf16[512,768]{1,0:T(8,128)(2,1)S(1)} %fusion.1), kind=kLoop, calls=%fused_computation.7 | loop fusion | flops 1966080 | bytes 3149824 | tf_op jit(solution)/shard_map/convert_element_type | solution.py:89
  38.9 0.0 copy-done
  38.9 0.5 %fusion.18 = f32[32]{0:T(128)} fusion(f32[4,4,32]{2,1,0:T(4,128)S(1)} %bitcast.107, s32[32]{0:T(128)S(1)} %copy-done.2, f32[]{:T(128)} %bitcast.87), kind=kLoop, calls=%fused_computation.58 | loop fusion | flops 96 | bytes 388 | tf_op jit(solution)/shard_map/div | solution.py:92
  (34 shorter events, 0.5 us)
Async XLA Ops:
  0.6 8.6 %copy-start.1 = (bf16[32,768]{1,0:T(8,128)(2,1)S(1)}, bf16[32,768]{1,0:T(8,128)(2,1)}, u32[]{:S(2)}) copy-start(bf16[32,768]{1,0:T(8,128)(2,1)} %param.4) | copy-start | bytes 147460
  0.6 11.8 %copy-start.2 = (s32[32]{0:T(128)S(1)}, s32[32]{0:T(128)}, u32[]{:S(2)}) copy-start(s32[32]{0:T(128)} %param.5) | copy-start | bytes 388
  0.6 8.3 %collective-permute-start = (bf16[32,768]{1,0:T(8,128)(2,1)}, bf16[32,768]{1,0:T(8,128)(2,1)S(1)}, u32[]{:S(2)}, u32[]{:S(2)}) collective-permute-start(bf16[32,768]{1,0:T(8,128)(2,1)} %param.4), channel_id=1, source_target_pairs={{0,4},{4,8},{8,12},{12,0},{1,5},{5,9},{9,13},{13,1},{2,6},{6,10},{... | collective-permute-start | bytes 147464 | tf_op jit(solution)/shard_map/ppermute | solution.py:23
  2.8 6.1 %collective-permute-start.1 = (bf16[32,768]{1,0:T(8,128)(2,1)}, bf16[32,768]{1,0:T(8,128)(2,1)S(1)}, u32[]{:S(2)}, u32[]{:S(2)}) collective-permute-start(bf16[32,768]{1,0:T(8,128)(2,1)} %param.4), channel_id=1, source_target_pairs={{0,8},{4,12},{8,0},{12,4},{1,9},{5,13},{9,1},{13,5},{2,10},{6,14},... | collective-permute-start | bytes 147464 | tf_op jit(solution)/shard_map/ppermute | solution.py:23
  5.1 4.1 %collective-permute-start.2 = (bf16[32,768]{1,0:T(8,128)(2,1)}, bf16[32,768]{1,0:T(8,128)(2,1)S(1)}, u32[]{:S(2)}, u32[]{:S(2)}) collective-permute-start(bf16[32,768]{1,0:T(8,128)(2,1)} %param.4), channel_id=1, source_target_pairs={{0,12},{4,0},{8,4},{12,8},{1,13},{5,1},{9,5},{13,9},{2,14},{6,2},{... | collective-permute-start | bytes 147464 | tf_op jit(solution)/shard_map/ppermute | solution.py:23
  9.3 6.8 %collective-permute-start.3 = (bf16[4,32,768]{2,1,0:T(8,128)(2,1)S(1)}, bf16[4,32,768]{2,1,0:T(8,128)(2,1)S(1)}, u32[]{:S(2)}, u32[]{:S(2)}) collective-permute-start(bf16[4,32,768]{2,1,0:T(8,128)(2,1)S(1)} %get-tuple-element.6), channel_id=1, source_target_pairs={{0,1},{1,2},{2,3},{3,0},{4,5},{5,6},{6,7},{7,4},{8,9},{9,10},{10,1... | collective-permute-start | bytes 589832 | tf_op jit(solution)/shard_map/ppermute | solution.py:23
  12.0 8.9 %collective-permute-start.4 = (bf16[4,32,768]{2,1,0:T(8,128)(2,1)S(1)}, bf16[4,32,768]{2,1,0:T(8,128)(2,1)S(1)}, u32[]{:S(2)}, u32[]{:S(2)}) collective-permute-start(bf16[4,32,768]{2,1,0:T(8,128)(2,1)S(1)} %get-tuple-element.6), channel_id=1, source_target_pairs={{0,2},{1,3},{2,0},{3,1},{4,6},{5,7},{6,4},{7,5},{8,10},{9,11},{10,... | collective-permute-start | bytes 589832 | tf_op jit(solution)/shard_map/ppermute | solution.py:23
  12.1 9.4 %collective-permute-start.5 = (bf16[4,32,768]{2,1,0:T(8,128)(2,1)S(1)}, bf16[4,32,768]{2,1,0:T(8,128)(2,1)S(1)}, u32[]{:S(2)}, u32[]{:S(2)}) collective-permute-start(bf16[4,32,768]{2,1,0:T(8,128)(2,1)S(1)} %get-tuple-element.6), channel_id=1, source_target_pairs={{0,3},{1,0},{2,1},{3,2},{4,7},{5,4},{6,5},{7,6},{8,11},{9,8},{10,9... | collective-permute-start | bytes 589832 | tf_op jit(solution)/shard_map/ppermute | solution.py:23
  23.3 4.6 %collective-permute-start.6 = (f32[3,4,4,32]{3,2,1,0:T(4,128)S(1)}, f32[3,4,4,32]{3,2,1,0:T(4,128)S(1)}, u32[]{:S(2)}, u32[]{:S(2)}) collective-permute-start(f32[3,4,4,32]{3,2,1,0:T(4,128)S(1)} %get-tuple-element.12), channel_id=1, source_target_pairs={{0,4},{4,8},{8,12},{12,0},{1,5},{5,9},{9,13},{13,1},{2,6},{6,10},{... | collective-permute-start | bytes 18440 | tf_op jit(solution)/shard_map/ppermute | solution.py:23
  23.9 5.3 %collective-permute-start.7 = (f32[3,4,4,32]{3,2,1,0:T(4,128)S(1)}, f32[3,4,4,32]{3,2,1,0:T(4,128)S(1)}, u32[]{:S(2)}, u32[]{:S(2)}) collective-permute-start(f32[3,4,4,32]{3,2,1,0:T(4,128)S(1)} %get-tuple-element.12), channel_id=1, source_target_pairs={{0,8},{4,12},{8,0},{12,4},{1,9},{5,13},{9,1},{13,5},{2,10},{6,14},... | collective-permute-start | bytes 18440 | tf_op jit(solution)/shard_map/ppermute | solution.py:23
  26.5 2.8 %collective-permute-start.8 = (f32[3,4,4,32]{3,2,1,0:T(4,128)S(1)}, f32[3,4,4,32]{3,2,1,0:T(4,128)S(1)}, u32[]{:S(2)}, u32[]{:S(2)}) collective-permute-start(f32[3,4,4,32]{3,2,1,0:T(4,128)S(1)} %get-tuple-element.12), channel_id=1, source_target_pairs={{0,12},{4,0},{8,4},{12,8},{1,13},{5,1},{9,5},{13,9},{2,14},{6,2},{... | collective-permute-start | bytes 18440 | tf_op jit(solution)/shard_map/ppermute | solution.py:23
  29.5 2.8 %collective-permute-start.9 = (f32[3,4,4,32]{3,2,1,0:T(4,128)S(1)}, f32[3,4,4,32]{3,2,1,0:T(4,128)S(1)}, u32[]{:S(2)}, u32[]{:S(2)}) collective-permute-start(f32[3,4,4,32]{3,2,1,0:T(4,128)S(1)} %get-tuple-element.8), channel_id=1, source_target_pairs={{0,1},{1,2},{2,3},{3,0},{4,5},{5,6},{6,7},{7,4},{8,9},{9,10},{10,1... | collective-permute-start | bytes 18440 | tf_op jit(solution)/shard_map/ppermute | solution.py:23
  31.1 2.7 %collective-permute-start.10 = (f32[3,4,4,32]{3,2,1,0:T(4,128)S(1)}, f32[3,4,4,32]{3,2,1,0:T(4,128)S(1)}, u32[]{:S(2)}, u32[]{:S(2)}) collective-permute-start(f32[3,4,4,32]{3,2,1,0:T(4,128)S(1)} %get-tuple-element.8), channel_id=1, source_target_pairs={{0,2},{1,3},{2,0},{3,1},{4,6},{5,7},{6,4},{7,5},{8,10},{9,11},{10,... | collective-permute-start | bytes 18440 | tf_op jit(solution)/shard_map/ppermute | solution.py:23
  32.3 3.3 %collective-permute-start.11 = (f32[3,4,4,32]{3,2,1,0:T(4,128)S(1)}, f32[3,4,4,32]{3,2,1,0:T(4,128)S(1)}, u32[]{:S(2)}, u32[]{:S(2)}) collective-permute-start(f32[3,4,4,32]{3,2,1,0:T(4,128)S(1)} %get-tuple-element.8), channel_id=1, source_target_pairs={{0,3},{1,0},{2,1},{3,2},{4,7},{5,4},{6,5},{7,6},{8,11},{9,8},{10,9... | collective-permute-start | bytes 18440 | tf_op jit(solution)/shard_map/ppermute | solution.py:23
  37.2 1.7 %copy-start = (f32[512,768]{1,0:T(8,128)}, f32[512,768]{1,0:T(8,128)S(1)}, u32[]{:S(2)}) copy-start(f32[512,768]{1,0:T(8,128)S(1)} %convert_reduce_fusion) | copy-start | bytes 4718596

commit v5 on v4

--- a/solution.py
+++ b/solution.py
@@ -3,8 +3,7 @@
 from jax import lax
 from jax.sharding import PartitionSpec as P
 
-STAGES = ("cent", ("dp", "sub"))
-SHIFT_MAX = 4
+PART_AXES = ("cent", "dp", "sub")
 
 
 def normalize(values):
@@ -12,34 +11,43 @@
     return floats * lax.rsqrt(jnp.sum(floats * floats, axis=-1, keepdims=True) + 1e-06)
 
 
-def relative(name):
-    return lax.axis_size(name) <= SHIFT_MAX
+def exchange_stages():
+    stages = []
+    for name in PART_AXES:
+        size = lax.axis_size(name)
+        if size & (size - 1):
+            stages.append((name, 0))
+            continue
+        mask = 1
+        while mask < size:
+            stages.append((name, mask))
+            mask *= 2
+    return stages
 
 
-def gather_stage(value, name):
+def gather_stage(value, stage):
+    name, mask = stage
     size = lax.axis_size(name)
-    if relative(name):
-        parts = [value] + [
-            lax.ppermute(value, name, [(j, (j + q) % size) for j in range(size)]) for q in range(1, size)
-        ]
-        return jnp.stack(parts)
+    if mask:
+        return jnp.stack([value, lax.ppermute(value, name, [(j, j ^ mask) for j in range(size)])])
     return lax.all_gather(value, name, axis=0)
 
 
-def own_block(name):
-    return 0 if relative(name) else lax.axis_index(name)
+def own_block(stage):
+    name, mask = stage
+    return 0 if mask else lax.axis_index(name)
 
 
 def shards(embeddings, weights, centroids, inverse_temp):
     sharpness = inverse_temp[0]
     row_dev, width = embeddings.shape
-    sizes = {name: lax.axis_size(name) for name in STAGES}
-    n_groups = sizes[STAGES[1]]
+    stages = exchange_stages()
+    n_groups = lax.axis_size(("dp", "sub"))
     own_count = centroids.shape[0] // n_groups
 
     blocks = embeddings
-    for name in STAGES:
-        blocks = gather_stage(blocks, name)
+    for stage in stages:
+        blocks = gather_stage(blocks, stage)
     unit_rows = normalize(blocks.reshape(-1, width)).astype(jnp.bfloat16)
 
     offset = lax.axis_index(("dp", "sub")) * own_count
@@ -52,22 +60,19 @@
         )
         * sharpness
     )
-    block_shape = (n_groups, sizes["cent"], row_dev)
+    block_shape = blocks.shape[:-1]
     local_peak = jnp.max(scores, axis=1)
     local_total = jnp.sum(jnp.exp(scores - local_peak[:, None]), axis=1)
 
-    own_index = (own_block(STAGES[1]), own_block("cent"), 0)
+    own_index = tuple(own_block(stage) for stage in reversed(stages)) + (0,)
     known_weights = lax.dynamic_update_slice(
-        jnp.zeros(block_shape, jnp.float32), weights.astype(jnp.float32)[None, None], own_index
+        jnp.zeros(block_shape, jnp.float32), weights.astype(jnp.float32).reshape((1,) * len(stages) + (row_dev,)), own_index
     )
     stats = jnp.stack([local_peak.reshape(block_shape), local_total.reshape(block_shape), known_weights])
-    block_axis = {STAGES[1]: 1, "cent": 2}
-    for name in STAGES:
-        stacked = gather_stage(stats, name)
-        if relative(name):
-            stacked = jnp.stack(
-                [jnp.roll(stacked[q], q, axis=block_axis[name]) for q in range(sizes[name])]
-            )
+    for index, stage in enumerate(stages):
+        stacked = gather_stage(stats, stage)
+        if stage[1]:
+            stacked = jnp.stack([stacked[0], jnp.flip(stacked[1], axis=len(stages) - index)])
         peaks, totals = stacked[:, 0], stacked[:, 1]
         row_peak = jnp.max(peaks, axis=0)
         row_total = jnp.sum(totals * jnp.exp(peaks - row_peak[None]), axis=0)
@@ -88,7 +93,7 @@
     moved = own_cents.astype(jnp.float32) + centroid_sums / (own_mass + 1.0)[:, None]
     renormed = normalize(moved).astype(jnp.bfloat16)
 
-    own_log_sum = log_sum.reshape(block_shape)[own_index[:2]]
+    own_log_sum = log_sum.reshape(block_shape)[own_index[:-1]]
     objective = weights.astype(jnp.float32) * own_log_sum / sharpness
     return (centroid_sums, renormed, objective)
 

time: 39.7 us -> 41.5 us (1.045)
  the two profiles are of different devices: /device:TPU:1 before, /device:TPU:0 now
where the time goes in v5:
time: 41.5 us; the launch traced here: 41.3 us
  starting transfers between devices  15.1 us (36%)
  waiting for transfers between devices  14.9 us (36%)
  other arithmetic  7.41 us (18%)
  matrix products  1.76 us (4%)
  between operations  1.48 us (4%)
  local copies, waits for them, and re-layouts  0.61 us (1%)
    ppermute x8, starting transfers between devices, gather_stage(): lax.ppermute(value, name, [(j, j ^ mask) for j in range(size)])  15.1 us
    ppermute x8, waiting for transfers between devices, gather_stage(): lax.ppermute(value, name, [(j, j ^ mask) for j in range(size)])  14.9 us
    reduce_sum x3, other arithmetic, normalize(): jnp.sum(floats * floats, axis=-1, keepdims=True) + 1e-06  2.02 us
    convert_element_type x1, other arithmetic, shards(): normalize(lax.dynamic_slice_in_dim(centroids, offset, own_count, 0))  1.33 us
    convert_element_type x1, other arithmetic, shards(): renormed = normalize(moved).astype(jnp.bfloat16)  1.25 us
    dot_general x1, matrix products, shards(): lax.dot_general(grouped_resp, grouped_rows, (((1,), (1,)), ((0,), (0,))),...  1.08 us
    another operation x7, other arithmetic, gather_stage(): jnp.stack([value, lax.ppermute(value, name, [(j, j ^ mask) for j in range...  0.95 us
  transfers between devices with their start and end apart: 8, of which 7 were waited for; matrix products, arithmetic and copies ran while one was open for 7% of the time, Pallas kernels for 0%

profile of v5, /device:TPU:0, one launch (start us, length us, event | category | flops | bytes accessed | tf_op | source)
XLA Modules:
  0.0 41.3 jit_solution(7706922887369806341)
XLA Ops:
  0.6 3.1 %collective-permute-start = (bf16[32,768]{1,0:T(8,128)(2,1)}, bf16[32,768]{1,0:T(8,128)(2,1)S(1)}, u32[]{:S(2)}, u32[]{:S(2)}) collective-permute-start(bf16[32,768]{1,0:T(8,128)(2,1)} %param.4), channel_id=1, source_target_pairs={{0,4},{4,0},{8,12},{12,8},{1,5},{5,1},{9,13},{13,9},{2,6},{6,2},{1... | collective-permute-start | bytes 147464 | tf_op jit(solution)/shard_map/ppermute | solution.py:32
  3.7 2.3 %collective-permute-done = bf16[32,768]{1,0:T(8,128)(2,1)S(1)} collective-permute-done((bf16[32,768]{1,0:T(8,128)(2,1)}, bf16[32,768]{1,0:T(8,128)(2,1)S(1)}, u32[]{:S(2)}, u32[]{:S(2)}) %collective-permute-start) | collective-permute-done | bytes 49184 | tf_op jit(solution)/shard_map/ppermute | solution.py:32
  6.0 0.8 %fusion.31 = (bf16[1,2,32,768]{3,2,1,0:T(8,128)(2,1)S(1)}, bf16[2,32,768]{2,1,0:T(8,128)(2,1)S(1)}) fusion(bf16[1,32,768]{2,1,0:T(8,128)(2,1)S(1)} %bitcast.140, bf16[1,32,768]{2,1,0:T(8,128)(2,1)} %bitcast.139), kind=kLoop, calls=%fused_computation.92 | loop fusion | flops 49152 | bytes 294912 | tf_op jit(solution)/shard_map/stack | solution.py:32
  6.8 3.1 %collective-permute-start.1 = (bf16[2,32,768]{2,1,0:T(8,128)(2,1)S(1)}, bf16[2,32,768]{2,1,0:T(8,128)(2,1)S(1)}, u32[]{:S(2)}, u32[]{:S(2)}) collective-permute-start(bf16[2,32,768]{2,1,0:T(8,128)(2,1)S(1)} %get-tuple-element.18), channel_id=1, source_target_pairs={{0,8},{4,12},{8,0},{12,4},{1,9},{5,13},{9,1},{13,5},{2,10},{6,14},... | collective-permute-start | bytes 294920 | tf_op jit(solution)/shard_map/ppermute | solution.py:32
  9.9 1.4 %fusion = f32[512]{0:T(512)S(1)} fusion(bf16[2048,768]{1,0:T(8,128)(2,1)} %param.6, s32[]{:T(128)S(6)} %select_n.3), kind=kLoop, calls=%fused_computation.3 | loop fusion | flops 1179136 | bytes 788484 | tf_op jit(solution)/shard_map/reduce_sum | solution.py:11
  11.3 1.3 %collective-permute-done.1 = bf16[2,32,768]{2,1,0:T(8,128)(2,1)S(1)} collective-permute-done((bf16[2,32,768]{2,1,0:T(8,128)(2,1)S(1)}, bf16[2,32,768]{2,1,0:T(8,128)(2,1)S(1)}, u32[]{:S(2)}, u32[]{:S(2)}) %collective-permute-start.1) | collective-permute-done | bytes 98336 | tf_op jit(solution)/shard_map/ppermute | solution.py:32
  12.6 0.0 copy-start.1
  12.7 1.8 %collective-permute-start.2 = (bf16[2,2,32,768]{3,2,1,0:T(8,128)(2,1)S(1)}, bf16[2,2,32,768]{3,2,1,0:T(8,128)(2,1)S(1)}, u32[]{:S(2)}, u32[]{:S(2)}) collective-permute-start(bf16[2,2,32,768]{3,2,1,0:T(8,128)(2,1)S(1)} %get-tuple-element.16), channel_id=1, source_target_pairs={{0,2},{2,0},{1,3},{3,1},{4,6},{6,4},{5,7},{7,5},{8,10},{10,8},{9,1... | collective-permute-start | bytes 589832 | tf_op jit(solution)/shard_map/ppermute | solution.py:32
  14.4 3.9 %collective-permute-done.2 = bf16[2,2,32,768]{3,2,1,0:T(8,128)(2,1)S(1)} collective-permute-done((bf16[2,2,32,768]{3,2,1,0:T(8,128)(2,1)S(1)}, bf16[2,2,32,768]{3,2,1,0:T(8,128)(2,1)S(1)}, u32[]{:S(2)}, u32[]{:S(2)}) %collective-permute-start.2) | collective-permute-done | bytes 196640 | tf_op jit(solution)/shard_map/ppermute | solution.py:32
  18.4 0.1 fusion.33
  18.4 0.1 collective-permute-start.3
  18.5 1.3 %fusion.1 = bf16[512,768]{1,0:T(8,128)(2,1)S(1)} fusion(f32[512]{0:T(512)S(1)} %add_rsqrt_fusion.2, bf16[2048,768]{1,0:T(8,128)(2,1)} %param.6, s32[]{:T(128)S(6)} %select_n.3), kind=kLoop, calls=%fused_computation.4 | loop fusion | flops 1179648 | bytes 1574916 | tf_op jit(solution)/shard_map/convert_element_type | solution.py:54
  20.5 0.0 copy-done.1
  20.5 0.0 collective-permute-done.3
  20.6 0.2 multiply_reduce_fusion.1
  20.8 0.1 maximum_convert_fusion
  20.9 0.1 rsqrt.32
  21.0 0.2 fusion.2
  21.2 0.7 %fusion.38 = (f32[512]{0:T(512)S(1)}, f32[512,512]{1,0:T(8,128)S(1)}) fusion(f32[]{:T(128)} %bitcast.110, bf16[512,768]{1,0:T(8,128)(2,1)S(1)} %fusion.2, bf16[512,768]{1,0:T(8,128)(2,1)S(1)} %fusion.1), kind=kOutput, calls=%fused_computation.95 | convolution fusion | flops 403176960 | bytes 2623492 | tf_op jit(solution)/shard_map/dot_general | solution.py:58
  21.9 0.1 stack_reshape.6
  21.9 0.3 exponential_reduce_fusion
  22.2 0.1 stack_reshape.7
  22.4 2.0 %collective-permute-start.4 = (f32[3,2,2,2,2,32]{5,4,3,2,1,0:T(2,128)S(1)}, f32[3,2,2,2,2,32]{5,4,3,2,1,0:T(2,128)S(1)}, u32[]{:S(2)}, u32[]{:S(2)}) collective-permute-start(f32[3,2,2,2,2,32]{5,4,3,2,1,0:T(2,128)S(1)} %pad_maximum_fusion.3), channel_id=1, source_target_pairs={{0,4},{4,0},{8,12},{12,8},{1,5},{5,1},{9,13},{13,9},{2,6},{6,2},{1... | collective-permute-start | bytes 18440 | tf_op jit(solution)/shard_map/ppermute | solution.py:32
  24.4 0.1 rsqrt.34
  24.5 1.8 %collective-permute-done.4 = f32[3,2,2,2,2,32]{5,4,3,2,1,0:T(2,128)S(1)} collective-permute-done((f32[3,2,2,2,2,32]{5,4,3,2,1,0:T(2,128)S(1)}, f32[3,2,2,2,2,32]{5,4,3,2,1,0:T(2,128)S(1)}, u32[]{:S(2)}, u32[]{:S(2)}) %collective-permute-start.4) | collective-permute-done | bytes 6176 | tf_op jit(solution)/shard_map/ppermute | solution.py:32
  26.2 0.1 rev.16
  26.4 3.4 %collective-permute-start.5 = (f32[3,2,2,2,2,32]{5,4,3,2,1,0:T(2,128)S(1)}, f32[3,2,2,2,2,32]{5,4,3,2,1,0:T(2,128)S(1)}, u32[]{:S(2)}, u32[]{:S(2)}) collective-permute-start(f32[3,2,2,2,2,32]{5,4,3,2,1,0:T(2,128)S(1)} %pad_maximum_fusion.4), channel_id=1, source_target_pairs={{0,8},{4,12},{8,0},{12,4},{1,9},{5,13},{9,1},{13,5},{2,10},{6,14},... | collective-permute-start | bytes 18440 | tf_op jit(solution)/shard_map/ppermute | solution.py:32
  29.9 2.1 %collective-permute-done.5 = f32[3,2,2,2,2,32]{5,4,3,2,1,0:T(2,128)S(1)} collective-permute-done((f32[3,2,2,2,2,32]{5,4,3,2,1,0:T(2,128)S(1)}, f32[3,2,2,2,2,32]{5,4,3,2,1,0:T(2,128)S(1)}, u32[]{:S(2)}, u32[]{:S(2)}) %collective-permute-start.5) | collective-permute-done | bytes 6176 | tf_op jit(solution)/shard_map/ppermute | solution.py:32
  32.1 1.6 %collective-permute-start.6 = (f32[3,2,2,2,2,32]{5,4,3,2,1,0:T(2,128)S(1)}, f32[3,2,2,2,2,32]{5,4,3,2,1,0:T(2,128)S(1)}, u32[]{:S(2)}, u32[]{:S(2)}) collective-permute-start(f32[3,2,2,2,2,32]{5,4,3,2,1,0:T(2,128)S(1)} %pad_maximum_fusion.5), channel_id=1, source_target_pairs={{0,2},{2,0},{1,3},{3,1},{4,6},{6,4},{5,7},{7,5},{8,10},{10,8},{9,1... | collective-permute-start | bytes 18440 | tf_op jit(solution)/shard_map/ppermute | solution.py:32
  33.6 2.3 %collective-permute-done.6 = f32[3,2,2,2,2,32]{5,4,3,2,1,0:T(2,128)S(1)} collective-permute-done((f32[3,2,2,2,2,32]{5,4,3,2,1,0:T(2,128)S(1)}, f32[3,2,2,2,2,32]{5,4,3,2,1,0:T(2,128)S(1)}, u32[]{:S(2)}, u32[]{:S(2)}) %collective-permute-start.6) | collective-permute-done | bytes 6176 | tf_op jit(solution)/shard_map/ppermute | solution.py:32
  36.1 0.1 collective-permute-start.7
  36.2 1.2 %collective-permute-done.7 = f32[3,2,2,2,2,32]{5,4,3,2,1,0:T(2,128)S(1)} collective-permute-done((f32[3,2,2,2,2,32]{5,4,3,2,1,0:T(2,128)S(1)}, f32[3,2,2,2,2,32]{5,4,3,2,1,0:T(2,128)S(1)}, u32[]{:S(2)}, u32[]{:S(2)}) %collective-permute-start.7) | collective-permute-done | bytes 6176 | tf_op jit(solution)/shard_map/ppermute | solution.py:32
  37.4 0.1 mul.89
  37.5 0.1 add.63
  37.6 0.5 %fusion.30 = f32[32]{0:T(128)} fusion(f32[2,2,2,2,32]{4,3,2,1,0:T(2,128)S(1)} %log_add_fusion, s32[32]{0:T(128)S(1)} %copy-done.1, f32[]{:T(128)} %bitcast.111), kind=kLoop, calls=%fused_computation.89 | loop fusion | flops 96 | bytes 388 | tf_op jit(solution)/shard_map/div | solution.py:97
  38.1 0.3 bitcast_reduce_fusion.4
  38.5 1.1 %convert_reduce_fusion = f32[512,768]{1,0:T(8,128)S(1)} fusion(bf16[4,128,512]{2,1,0:T(8,128)(2,1)S(1)} %bitcast.113, f32[4,128,768]{2,1,0:T(8,128)S(1)} %bitcast.112, f32[4,128]{1,0:T(4,128)S(1)} %rsqrt.34), kind=kOutput, calls=%fused_computation | convolution fusion | flops 407764992 | bytes 3672064 | tf_op jit(solution)/shard_map/dot_general | solution.py:86
  39.6 0.0 copy-start
  39.6 0.4 %multiply_reduce_fusion = f32[512]{0:T(512)S(1)} fusion(f32[512,768]{1,0:T(8,128)S(1)} %convert_reduce_fusion, f32[512]{0:T(512)S(1)} %broadcast_add_fusion, bf16[512,768]{1,0:T(8,128)(2,1)S(1)} %fusion.1), kind=kLoop, calls=%fused_computation.8 | loop fusion | flops 1965568 | bytes 2363392 | tf_op jit(solution)/shard_map/reduce_sum | solution.py:11
  40.0 1.2 %multiply_convert_fusion = bf16[512,768]{1,0:T(8,128)(2,1)} fusion(f32[512]{0:T(512)S(1)} %add_rsqrt_fusion.1, f32[512,768]{1,0:T(8,128)S(1)} %convert_reduce_fusion, f32[512]{0:T(512)S(1)} %broadcast_add_fusion, bf16[512,768]{1,0:T(8,128)(2,1)S(1)} %fusion.1), kind=kLoop, calls=%fused_computation.7 | loop fusion | flops 1966080 | bytes 3149824 | tf_op jit(solution)/shard_map/convert_element_type | solution.py:94
  41.2 0.0 copy-done
  (32 shorter events, 0.6 us)
Async XLA Ops:
  0.6 5.4 %collective-permute-start = (bf16[32,768]{1,0:T(8,128)(2,1)}, bf16[32,768]{1,0:T(8,128)(2,1)S(1)}, u32[]{:S(2)}, u32[]{:S(2)}) collective-permute-start(bf16[32,768]{1,0:T(8,128)(2,1)} %param.4), channel_id=1, source_target_pairs={{0,4},{4,0},{8,12},{12,8},{1,5},{5,1},{9,13},{13,9},{2,6},{6,2},{1... | collective-permute-start | bytes 147464 | tf_op jit(solution)/shard_map/ppermute | solution.py:32
  6.8 5.8 %collective-permute-start.1 = (bf16[2,32,768]{2,1,0:T(8,128)(2,1)S(1)}, bf16[2,32,768]{2,1,0:T(8,128)(2,1)S(1)}, u32[]{:S(2)}, u32[]{:S(2)}) collective-permute-start(bf16[2,32,768]{2,1,0:T(8,128)(2,1)S(1)} %get-tuple-element.18), channel_id=1, source_target_pairs={{0,8},{4,12},{8,0},{12,4},{1,9},{5,13},{9,1},{13,5},{2,10},{6,14},... | collective-permute-start | bytes 294920 | tf_op jit(solution)/shard_map/ppermute | solution.py:32
  12.6 7.9 %copy-start.1 = (s32[32]{0:T(128)S(1)}, s32[32]{0:T(128)}, u32[]{:S(2)}) copy-start(s32[32]{0:T(128)} %param.5) | copy-start | bytes 388
  12.7 5.7 %collective-permute-start.2 = (bf16[2,2,32,768]{3,2,1,0:T(8,128)(2,1)S(1)}, bf16[2,2,32,768]{3,2,1,0:T(8,128)(2,1)S(1)}, u32[]{:S(2)}, u32[]{:S(2)}) collective-permute-start(bf16[2,2,32,768]{3,2,1,0:T(8,128)(2,1)S(1)} %get-tuple-element.16), channel_id=1, source_target_pairs={{0,2},{2,0},{1,3},{3,1},{4,6},{6,4},{5,7},{7,5},{8,10},{10,8},{9,1... | collective-permute-start | bytes 589832 | tf_op jit(solution)/shard_map/ppermute | solution.py:32
  18.4 2.1 %collective-permute-start.3 = (bf16[2,2,2,32,768]{4,3,2,1,0:T(8,128)(2,1)S(1)}, bf16[2,2,2,32,768]{4,3,2,1,0:T(8,128)(2,1)S(1)}, u32[]{:S(2)}, u32[]{:S(2)}) collective-permute-start(bf16[2,2,2,32,768]{4,3,2,1,0:T(8,128)(2,1)S(1)} %get-tuple-element.14), channel_id=1, source_target_pairs={{0,1},{1,0},{2,3},{3,2},{4,5},{5,4},{6,7},{7,6},{8,9},{9,8},{10,11... | collective-permute-start | bytes 1179656 | tf_op jit(solution)/shard_map/ppermute | solution.py:32
  22.4 3.9 %collective-permute-start.4 = (f32[3,2,2,2,2,32]{5,4,3,2,1,0:T(2,128)S(1)}, f32[3,2,2,2,2,32]{5,4,3,2,1,0:T(2,128)S(1)}, u32[]{:S(2)}, u32[]{:S(2)}) collective-permute-start(f32[3,2,2,2,2,32]{5,4,3,2,1,0:T(2,128)S(1)} %pad_maximum_fusion.3), channel_id=1, source_target_pairs={{0,4},{4,0},{8,12},{12,8},{1,5},{5,1},{9,13},{13,9},{2,6},{6,2},{1... | collective-permute-start | bytes 18440 | tf_op jit(solution)/shard_map/ppermute | solution.py:32
  26.4 5.5 %collective-permute-start.5 = (f32[3,2,2,2,2,32]{5,4,3,2,1,0:T(2,128)S(1)}, f32[3,2,2,2,2,32]{5,4,3,2,1,0:T(2,128)S(1)}, u32[]{:S(2)}, u32[]{:S(2)}) collective-permute-start(f32[3,2,2,2,2,32]{5,4,3,2,1,0:T(2,128)S(1)} %pad_maximum_fusion.4), channel_id=1, source_target_pairs={{0,8},{4,12},{8,0},{12,4},{1,9},{5,13},{9,1},{13,5},{2,10},{6,14},... | collective-permute-start | bytes 18440 | tf_op jit(solution)/shard_map/ppermute | solution.py:32
  32.1 3.9 %collective-permute-start.6 = (f32[3,2,2,2,2,32]{5,4,3,2,1,0:T(2,128)S(1)}, f32[3,2,2,2,2,32]{5,4,3,2,1,0:T(2,128)S(1)}, u32[]{:S(2)}, u32[]{:S(2)}) collective-permute-start(f32[3,2,2,2,2,32]{5,4,3,2,1,0:T(2,128)S(1)} %pad_maximum_fusion.5), channel_id=1, source_target_pairs={{0,2},{2,0},{1,3},{3,1},{4,6},{6,4},{5,7},{7,5},{8,10},{10,8},{9,1... | collective-permute-start | bytes 18440 | tf_op jit(solution)/shard_map/ppermute | solution.py:32
  36.1 1.3 %collective-permute-start.7 = (f32[3,2,2,2,2,32]{5,4,3,2,1,0:T(2,128)S(1)}, f32[3,2,2,2,2,32]{5,4,3,2,1,0:T(2,128)S(1)}, u32[]{:S(2)}, u32[]{:S(2)}) collective-permute-start(f32[3,2,2,2,2,32]{5,4,3,2,1,0:T(2,128)S(1)} %pad_maximum_fusion.6), channel_id=1, source_target_pairs={{0,1},{1,0},{2,3},{3,2},{4,5},{5,4},{6,7},{7,6},{8,9},{9,8},{10,11... | collective-permute-start | bytes 18440 | tf_op jit(solution)/shard_map/ppermute | solution.py:32
  39.6 1.7 %copy-start = (f32[512,768]{1,0:T(8,128)}, f32[512,768]{1,0:T(8,128)S(1)}, u32[]{:S(2)}) copy-start(f32[512,768]{1,0:T(8,128)S(1)} %convert_reduce_fusion) | copy-start | bytes 4718596

commit v6 on v3

--- a/solution.py
+++ b/solution.py
@@ -30,48 +30,66 @@
     return 0 if relative(name) else lax.axis_index(name)
 
 
+def merge_stats(stats, names, block_axis):
+    for name in names:
+        size = lax.axis_size(name)
+        stacked = gather_stage(stats, name)
+        if relative(name):
+            stacked = jnp.stack([jnp.roll(stacked[q], q, axis=block_axis[name]) for q in range(size)])
+        peaks, totals = stacked[:, 0], stacked[:, 1]
+        row_peak = jnp.max(peaks, axis=0)
+        row_total = jnp.sum(totals * jnp.exp(peaks - row_peak[None]), axis=0)
+        stats = jnp.stack([row_peak, row_total, jnp.max(stacked[:, 2], axis=0)])
+    return stats
+
+
 def shards(embeddings, weights, centroids, inverse_temp):
     sharpness = inverse_temp[0]
     row_dev, width = embeddings.shape
     sizes = {name: lax.axis_size(name) for name in STAGES}
     n_groups = sizes["dp"] * sizes["sub"]
-    own_count = centroids.shape[0] // n_groups
+    panel = centroids.shape[0]
+    own_count = panel // n_groups
+    n_rows = row_dev * sizes["cent"] * n_groups
+    full_panel = n_rows * panel * 4 <= (16 << 20)
 
-    blocks = embeddings
-    for name in STAGES:
-        blocks = gather_stage(blocks, name)
-    unit_rows = normalize(blocks.reshape(-1, width)).astype(jnp.bfloat16)
+    blocks = gather_stage(embeddings, "cent").reshape(-1, width)
+    cent_rows = blocks.shape[0]
+    weight_block = jnp.pad(weights.astype(jnp.bfloat16)[None, :], ((0, 15), (0, width - row_dev)))
+    payload = jnp.concatenate([blocks, weight_block], axis=0)
+    for name in STAGES[1:]:
+        payload = gather_stage(payload, name)
+    unit_rows = normalize(payload[:, :, :cent_rows].reshape(-1, width)).astype(jnp.bfloat16)
+    cent_weights = payload[:, :, cent_rows, :row_dev].astype(jnp.float32)
 
     offset = lax.axis_index(("dp", "sub")) * own_count
-    own_cents = normalize(lax.dynamic_slice_in_dim(centroids, offset, own_count, 0)).astype(jnp.bfloat16)
-    own_cents = lax.optimization_barrier(own_cents)
+    if full_panel:
+        panel_cents = lax.optimization_barrier(normalize(centroids).astype(jnp.bfloat16))
+        own_cents = lax.dynamic_slice_in_dim(panel_cents, offset, own_count, 0)
+        score_cents = panel_cents
+    else:
+        own_cents = normalize(lax.dynamic_slice_in_dim(centroids, offset, own_count, 0)).astype(jnp.bfloat16)
+        own_cents = lax.optimization_barrier(own_cents)
+        score_cents = own_cents
 
     scores = (
         lax.dot_general(
-            unit_rows, own_cents, (((1,), (1,)), ((), ())), preferred_element_type=jnp.float32
+            unit_rows, score_cents, (((1,), (1,)), ((), ())), preferred_element_type=jnp.float32
         )
         * sharpness
     )
     block_shape = (sizes["sub"], sizes["dp"], sizes["cent"], row_dev)
     local_peak = jnp.max(scores, axis=1)
     local_total = jnp.sum(jnp.exp(scores - local_peak[:, None]), axis=1)
+    if full_panel:
+        scores = lax.dynamic_slice_in_dim(scores, offset, own_count, 1)
 
-    own_index = (own_block("sub"), own_block("dp"), own_block("cent"), 0)
+    own_cent = own_block("cent")
     known_weights = lax.dynamic_update_slice(
-        jnp.zeros(block_shape, jnp.float32), weights.astype(jnp.float32)[None, None, None], own_index
+        jnp.zeros(block_shape, jnp.float32), cent_weights[:, :, None], (0, 0, own_cent, 0)
     )
     stats = jnp.stack([local_peak.reshape(block_shape), local_total.reshape(block_shape), known_weights])
-    block_axis = {"sub": 1, "dp": 2, "cent": 3}
-    for name in STAGES:
-        stacked = gather_stage(stats, name)
-        if relative(name):
-            stacked = jnp.stack(
-                [jnp.roll(stacked[q], q, axis=block_axis[name]) for q in range(sizes[name])]
-            )
-        peaks, totals = stacked[:, 0], stacked[:, 1]
-        row_peak = jnp.max(peaks, axis=0)
-        row_total = jnp.sum(totals * jnp.exp(peaks - row_peak[None]), axis=0)
-        stats = jnp.stack([row_peak, row_total, jnp.sum(stacked[:, 2], axis=0)])
+    stats = merge_stats(stats, STAGES[:1] if full_panel else STAGES, {"sub": 1, "dp": 2, "cent": 3})
     weight_float = stats[2].reshape(-1)
     log_sum = (stats[0] + jnp.log(stats[1])).reshape(-1)
 
@@ -88,7 +106,7 @@
     moved = own_cents.astype(jnp.float32) + centroid_sums / (own_mass + 1.0)[:, None]
     renormed = normalize(moved).astype(jnp.bfloat16)
 
-    own_log_sum = log_sum.reshape(block_shape)[own_index[:3]]
+    own_log_sum = log_sum.reshape(block_shape)[own_block("sub"), own_block("dp"), own_cent]
     objective = weights.astype(jnp.float32) * own_log_sum / sharpness
     return (centroid_sums, renormed, objective)
 

time: 38.4 us -> 45.5 us (1.18)
  other arithmetic: 7.24 us -> 17.9 us
  waiting for transfers between devices: 13 us -> 5.79 us
  matrix products: 1.77 us -> 6.05 us
  starting transfers between devices: 14.1 us -> 13.6 us
    ppermute x10 -> x8, waiting for transfers between devices: 13 us -> 5.79 us  [gather_stage(): lax.ppermute(value, name, [(j, (j + q) % size) for j in range(size)])]
    dot_general x1, matrix products: 0.69 us -> 3.76 us  [shards(): lax.dot_general(unit_rows, score_cents, (((1,), (1,)), ((), ())), preferr...]
    reduce_sum x1, other arithmetic: 0.3 us -> 2.9 us  [shards(): local_total = jnp.sum(jnp.exp(scores - local_peak[:, None]), axis=1)]
    reduce_sum x3, other arithmetic: 2.02 us -> 4.49 us  [normalize(): jnp.sum(floats * floats, axis=-1, keepdims=True) + 1e-06]
    convert_element_type x2 -> x3, other arithmetic: 1.48 us -> 3.43 us  [the longest x1 2.25 us: shards(): normalize(centroids).astype(jnp.bfloat16)]
    reduce_sum x1, other arithmetic: 0.29 us -> 1.51 us  [shards(): jnp.sum(grouped_resp.astype(jnp.float32), axis=1).astype(jnp.bfloat16)]
    dot_general x1, matrix products: 1.08 us -> 2.29 us  [shards(): lax.dot_general(grouped_resp, grouped_rows, (((1,), (1,)), ((0,), (0,))),...]
    convert_element_type x1, other arithmetic: 0.1 us -> 1.22 us  [normalize(): floats = values.astype(jnp.float32)]
  transfers between devices with their start and end apart: 10 -> 8, of which waited for: 8 -> 3; matrix products, arithmetic and copies ran while one was open for 7% -> 15% of each run, Pallas kernels for 0% -> 0%
where the time goes in v6:
time: 45.5 us; the launch traced here: 45.3 us
  other arithmetic  17.9 us (39%)
  starting transfers between devices  13.6 us (30%)
  matrix products  6.05 us (13%)
  waiting for transfers between devices  5.79 us (13%)
  between operations  1.49 us (3%)
    ppermute x8, starting transfers between devices, gather_stage(): lax.ppermute(value, name, [(j, (j + q) % size) for j in range(size)])  13.6 us
    ppermute x8, waiting for transfers between devices, gather_stage(): lax.ppermute(value, name, [(j, (j + q) % size) for j in range(size)])  5.79 us
    reduce_sum x3, other arithmetic, normalize(): jnp.sum(floats * floats, axis=-1, keepdims=True) + 1e-06  4.49 us
    dot_general x1, matrix products, shards(): lax.dot_general(unit_rows, score_cents, (((1,), (1,)), ((), ())), preferr...  3.76 us
    reduce_sum x1, other arithmetic, shards(): local_total = jnp.sum(jnp.exp(scores - local_peak[:, None]), axis=1)  2.9 us
    dot_general x1, matrix products, shards(): lax.dot_general(grouped_resp, grouped_rows, (((1,), (1,)), ((0,), (0,))),...  2.29 us
    convert_element_type x1, other arithmetic, shards(): normalize(centroids).astype(jnp.bfloat16)  2.25 us
    reduce_sum x1, other arithmetic, shards(): jnp.sum(grouped_resp.astype(jnp.float32), axis=1).astype(jnp.bfloat16)  1.51 us
  transfers between devices with their start and end apart: 8, of which 3 were waited for; matrix products, arithmetic and copies ran while one was open for 15% of the time, Pallas kernels for 0%

profile of v6, /device:TPU:0, one launch (start us, length us, event | category | flops | bytes accessed | tf_op | source)
XLA Modules:
  0.0 45.3 jit_solution(17199072910460830116)
XLA Ops:
  0.6 0.0 copy-start.4
  0.6 0.0 copy-start.1
  0.6 3.1 %collective-permute-start = (bf16[32,768]{1,0:T(8,128)(2,1)}, bf16[32,768]{1,0:T(8,128)(2,1)S(1)}, u32[]{:S(2)}, u32[]{:S(2)}) collective-permute-start(bf16[32,768]{1,0:T(8,128)(2,1)} %param.4), channel_id=1, source_target_pairs={{0,4},{4,8},{8,12},{12,0},{1,5},{5,9},{9,13},{13,1},{2,6},{6,10},{... | collective-permute-start | bytes 147464 | tf_op jit(solution)/shard_map/ppermute | solution.py:23
  3.7 2.1 %collective-permute-start.2 = (bf16[32,768]{1,0:T(8,128)(2,1)}, bf16[32,768]{1,0:T(8,128)(2,1)S(1)}, u32[]{:S(2)}, u32[]{:S(2)}) collective-permute-start(bf16[32,768]{1,0:T(8,128)(2,1)} %param.4), channel_id=1, source_target_pairs={{0,12},{4,0},{8,4},{12,8},{1,13},{5,1},{9,5},{13,9},{2,14},{6,2},{... | collective-permute-start | bytes 147464 | tf_op jit(solution)/shard_map/ppermute | solution.py:23
  5.8 0.9 %collective-permute-start.1 = (bf16[32,768]{1,0:T(8,128)(2,1)}, bf16[32,768]{1,0:T(8,128)(2,1)S(1)}, u32[]{:S(2)}, u32[]{:S(2)}) collective-permute-start(bf16[32,768]{1,0:T(8,128)(2,1)} %param.4), channel_id=1, source_target_pairs={{0,8},{4,12},{8,0},{12,4},{1,9},{5,13},{9,1},{13,5},{2,10},{6,14},... | collective-permute-start | bytes 147464 | tf_op jit(solution)/shard_map/ppermute | solution.py:23
  6.8 2.6 %fusion = f32[2048]{0:T(1024)S(1)} fusion(bf16[2048,768]{1,0:T(8,128)(2,1)} %param.6), kind=kLoop, calls=%fused_computation.2 | loop fusion | flops 4716544 | bytes 3153920 | tf_op jit(solution)/shard_map/reduce_sum | solution.py:12
  9.3 0.7 %convert_bitcast_fusion = bf16[1,32]{1,0:T(2,128)(2,1)S(1)} fusion(s32[32]{0:T(128)} %param.5), kind=kLoop, calls=%fused_computation.52 | loop fusion | flops 32 | bytes 192 | tf_op jit(solution)/shard_map/broadcast_in_dim | solution.py:58
  10.7 0.0 collective-permute-done
  10.7 0.0 collective-permute-done.2
  10.7 0.5 %collective-permute-done.1 = bf16[32,768]{1,0:T(8,128)(2,1)S(1)} collective-permute-done((bf16[32,768]{1,0:T(8,128)(2,1)}, bf16[32,768]{1,0:T(8,128)(2,1)S(1)}, u32[]{:S(2)}, u32[]{:S(2)}) %collective-permute-start.1) | collective-permute-done | bytes 49184 | tf_op jit(solution)/shard_map/ppermute | solution.py:23
  11.1 0.0 copy-done.4
  11.2 1.6 %collective-permute-start.3 = (bf16[144,768]{1,0:T(8,128)(2,1)S(1)}, bf16[144,768]{1,0:T(8,128)(2,1)S(1)}, u32[]{:S(2)}, u32[]{:S(2)}) collective-permute-start(bf16[144,768]{1,0:T(8,128)(2,1)S(1)} %get-tuple-element.8), channel_id=1, source_target_pairs={{0,2},{2,0},{1,3},{3,1},{4,6},{6,4},{5,7},{7,5},{8,10},{10,8},{9,1... | collective-permute-start | bytes 663560 | tf_op jit(solution)/shard_map/ppermute | solution.py:23
  12.8 4.6 %collective-permute-done.3 = bf16[144,768]{1,0:T(8,128)(2,1)S(1)} collective-permute-done((bf16[144,768]{1,0:T(8,128)(2,1)S(1)}, bf16[144,768]{1,0:T(8,128)(2,1)S(1)}, u32[]{:S(2)}, u32[]{:S(2)}) %collective-permute-start.3) | collective-permute-done | bytes 221216 | tf_op jit(solution)/shard_map/ppermute | solution.py:23
  17.4 1.0 %fusion.20 = (bf16[1,2,144,768]{3,2,1,0:T(8,128)(2,1)}, bf16[2,144,768]{2,1,0:T(8,128)(2,1)}) fusion(bf16[1,144,768]{2,1,0:T(8,128)(2,1)S(1)} %bitcast.72, bf16[1,144,768]{2,1,0:T(8,128)(2,1)S(1)} %get-tuple-element.7), kind=kLoop, calls=%fused_computation.56 | loop fusion | flops 221184 | bytes 1327104 | tf_op jit(solution)/shard_map/stack | solution.py:25
  18.4 0.0 collective-permute-start.4
  18.4 0.0 copy-done.1
  18.4 2.3 %fusion.1 = bf16[2048,768]{1,0:T(8,128)(2,1)} fusion(bf16[2048,768]{1,0:T(8,128)(2,1)S(1)} %copy-done.1, f32[2048]{0:T(1024)S(1)} %add_rsqrt_fusion), kind=kLoop, calls=%fused_computation.3 | loop fusion | flops 4718592 | bytes 6299648 | tf_op jit(solution)/shard_map/convert_element_type | solution.py:67
  20.6 0.0 collective-permute-done.4
  20.6 0.0 copy-start.2
  20.6 1.5 %multiply_reduce_fusion.1 = f32[2,2,128]{2,1,0:T(2,128)S(1)} fusion(bf16[1,2,144,768]{3,2,1,0:T(8,128)(2,1)} %bitcast.9, bf16[1,2,144,768]{3,2,1,0:T(8,128)(2,1)} %get-tuple-element.5), kind=kLoop, calls=%fused_computation.14 | loop fusion | flops 1572352 | bytes 886784 | tf_op jit(solution)/shard_map/reduce_sum | solution.py:12
  22.1 0.7 %fusion.15 = f32[1,2,2,4,32]{4,3,2,1,0:T(4,128)S(1)} fusion(bf16[1,2,144,768]{3,2,1,0:T(8,128)(2,1)} %bitcast.9, bf16[1,2,144,768]{3,2,1,0:T(8,128)(2,1)} %get-tuple-element.5), kind=kLoop, calls=%fused_computation.45 | loop fusion | flops 4096 | bytes 886784 | tf_op jit(solution)/shard_map/stack | solution.py:91
  22.8 1.2 %fusion.5 = f32[2,2,128,768]{3,2,1,0:T(8,128)S(1)} fusion(bf16[1,2,144,768]{3,2,1,0:T(8,128)(2,1)} %get-tuple-element.5, bf16[1,2,144,768]{3,2,1,0:T(8,128)(2,1)} %bitcast.9), kind=kLoop, calls=%fused_computation.19 | loop fusion | flops 786432 | bytes 2457600 | tf_op jit(solution)/shard_map/convert_element_type | solution.py:11
  24.1 0.1 fusion.3
  24.2 0.0 copy-done.2
  24.2 3.8 %fusion.22 = (f32[512]{0:T(512)S(1)}, f32[512,2048]{1,0:T(8,128)}) fusion(f32[]{:T(128)} %bitcast.68, bf16[512,768]{1,0:T(8,128)(2,1)S(1)} %fusion.3, bf16[2048,768]{1,0:T(8,128)(2,1)S(1)} %copy-done.2), kind=kOutput, calls=%fused_computation.58 | convolution fusion | flops 1612709376 | bytes 8128516 | tf_op jit(solution)/shard_map/dot_general | solution.py:76
  28.0 0.1 stack_reshape.6
  28.1 0.0 copy-start.5
  28.1 2.9 %exponential_reduce_fusion = f32[512]{0:T(512)S(1)} fusion(f32[512,2048]{1,0:T(8,128)} %get-tuple-element.14, f32[512]{0:T(512)S(1)} %get-tuple-element.13), kind=kLoop, calls=%fused_computation.5 | loop fusion | flops 2096640 | bytes 4198400 | tf_op jit(solution)/shard_map/reduce_sum | solution.py:83
  31.0 0.1 stack_reshape.7
  31.1 2.1 %collective-permute-start.6 = (f32[3,2,2,4,32]{4,3,2,1,0:T(4,128)S(1)}, f32[3,2,2,4,32]{4,3,2,1,0:T(4,128)S(1)}, u32[]{:S(2)}, u32[]{:S(2)}) collective-permute-start(f32[3,2,2,4,32]{4,3,2,1,0:T(4,128)S(1)} %get-tuple-element.10), channel_id=1, source_target_pairs={{0,8},{4,12},{8,0},{12,4},{1,9},{5,13},{9,1},{13,5},{2,10},{6,14},... | collective-permute-start | bytes 18440 | tf_op jit(solution)/shard_map/ppermute | solution.py:23
  33.2 1.3 %collective-permute-start.5 = (f32[3,2,2,4,32]{4,3,2,1,0:T(4,128)S(1)}, f32[3,2,2,4,32]{4,3,2,1,0:T(4,128)S(1)}, u32[]{:S(2)}, u32[]{:S(2)}) collective-permute-start(f32[3,2,2,4,32]{4,3,2,1,0:T(4,128)S(1)} %get-tuple-element.10), channel_id=1, source_target_pairs={{0,4},{4,8},{8,12},{12,0},{1,5},{5,9},{9,13},{13,1},{2,6},{6,10},{... | collective-permute-start | bytes 18440 | tf_op jit(solution)/shard_map/ppermute | solution.py:23
  34.5 2.5 %collective-permute-start.7 = (f32[3,2,2,4,32]{4,3,2,1,0:T(4,128)S(1)}, f32[3,2,2,4,32]{4,3,2,1,0:T(4,128)S(1)}, u32[]{:S(2)}, u32[]{:S(2)}) collective-permute-start(f32[3,2,2,4,32]{4,3,2,1,0:T(4,128)S(1)} %get-tuple-element.10), channel_id=1, source_target_pairs={{0,12},{4,0},{8,4},{12,8},{1,13},{5,1},{9,5},{13,9},{2,14},{6,2},{... | collective-permute-start | bytes 18440 | tf_op jit(solution)/shard_map/ppermute | solution.py:23
  37.0 1.0 %fusion.2 = bf16[4,128,768]{2,1,0:T(8,128)(2,1)} fusion(f32[2,2,128,768]{3,2,1,0:T(8,128)S(1)} %fusion.5, f32[4,128]{1,0:T(4,128)S(1)} %bitcast.83), kind=kLoop, calls=%fused_computation.8 | loop fusion | flops 786432 | bytes 2361344 | tf_op jit(solution)/shard_map/convert_element_type | solution.py:62
  38.0 0.0 copy-start.3
  38.0 0.0 collective-permute-done.6
  38.1 0.7 %collective-permute-done.5 = f32[3,2,2,4,32]{4,3,2,1,0:T(4,128)S(1)} collective-permute-done((f32[3,2,2,4,32]{4,3,2,1,0:T(4,128)S(1)}, f32[3,2,2,4,32]{4,3,2,1,0:T(4,128)S(1)}, u32[]{:S(2)}, u32[]{:S(2)}) %collective-permute-start.5) | collective-permute-done | bytes 6176 | tf_op jit(solution)/shard_map/ppermute | solution.py:23
  38.8 0.0 collective-permute-done.7
  39.0 0.1 mul.75
  39.1 0.1 add.70
  39.2 0.0 copy-done.5
  39.2 0.5 %fusion.17 = f32[32]{0:T(128)} fusion(f32[2,2,4,32]{3,2,1,0:T(4,128)S(1)} %bitcast.80, s32[32]{0:T(128)S(1)} %copy-done.5, f32[]{:T(128)} %bitcast.69), kind=kLoop, calls=%fused_computation.51 | loop fusion | flops 96 | bytes 388 | tf_op jit(solution)/shard_map/div | solution.py:110
  39.7 1.5 %bitcast_reduce_fusion.1 = (bf16[4,512]{1,0:T(4,128)(2,1)S(1)}, bf16[512,512]{1,0:T(8,128)(2,1)S(1)}) fusion(f32[512]{0:T(512)S(1)} %add.70, f32[512,2048]{1,0:T(8,128)} %get-tuple-element.14, s32[]{:T(128)S(6)} %select_n.4, f32[512]{0:T(512)S(1)} %mul.75), kind=kLoop, calls=%fused_computation.53 | loop fusion | flops 1046528 | bytes 1581060 | tf_op jit(solution)/shard_map/reduce_sum | solution.py:103
  41.3 2.3 %convert_reduce_fusion = f32[512,768]{1,0:T(8,128)S(1)} fusion(bf16[4,128,512]{2,1,0:T(8,128)(2,1)S(1)} %bitcast.70, bf16[4,128,768]{2,1,0:T(8,128)(2,1)} %fusion.2), kind=kOutput, calls=%fused_computation.4 | convolution fusion | flops 406978560 | bytes 2883584 | tf_op jit(solution)/shard_map/dot_general | solution.py:99
  43.6 0.0 copy-done.3
  43.6 0.0 copy-start
  43.6 0.4 multiply_reduce_fusion
  44.0 1.2 %multiply_convert_fusion = bf16[512,768]{1,0:T(8,128)(2,1)} fusion(f32[512]{0:T(512)S(1)} %add_rsqrt_fusion.1, f32[512,768]{1,0:T(8,128)S(1)} %convert_reduce_fusion, f32[512]{0:T(512)S(1)} %broadcast_add_fusion, bf16[2048,768]{1,0:T(8,128)(2,1)S(1)} %copy-done.3, s32[]{:T(128)S(6)} %select_n.4), kind=kLoop, calls=%fused_computation.11 | loop fusion | flops 1966080 | bytes 3149828 | tf_op jit(solution)/shard_map/convert_element_type | solution.py:107
  45.3 0.0 copy-done
  (20 shorter events, 0.3 us)
Async XLA Ops:
  0.6 10.5 %copy-start.4 = (bf16[32,768]{1,0:T(8,128)(2,1)S(1)}, bf16[32,768]{1,0:T(8,128)(2,1)}, u32[]{:S(2)}) copy-start(bf16[32,768]{1,0:T(8,128)(2,1)} %param.4) | copy-start | bytes 147460
  0.6 17.7 %copy-start.1 = (bf16[2048,768]{1,0:T(8,128)(2,1)S(1)}, bf16[2048,768]{1,0:T(8,128)(2,1)}, u32[]{:S(2)}) copy-start(bf16[2048,768]{1,0:T(8,128)(2,1)} %param.6) | copy-start | bytes 9437188
  0.6 10.0 %collective-permute-start = (bf16[32,768]{1,0:T(8,128)(2,1)}, bf16[32,768]{1,0:T(8,128)(2,1)S(1)}, u32[]{:S(2)}, u32[]{:S(2)}) collective-permute-start(bf16[32,768]{1,0:T(8,128)(2,1)} %param.4), channel_id=1, source_target_pairs={{0,4},{4,8},{8,12},{12,0},{1,5},{5,9},{9,13},{13,1},{2,6},{6,10},{... | collective-permute-start | bytes 147464 | tf_op jit(solution)/shard_map/ppermute | solution.py:23
  3.7 6.9 %collective-permute-start.2 = (bf16[32,768]{1,0:T(8,128)(2,1)}, bf16[32,768]{1,0:T(8,128)(2,1)S(1)}, u32[]{:S(2)}, u32[]{:S(2)}) collective-permute-start(bf16[32,768]{1,0:T(8,128)(2,1)} %param.4), channel_id=1, source_target_pairs={{0,12},{4,0},{8,4},{12,8},{1,13},{5,1},{9,5},{13,9},{2,14},{6,2},{... | collective-permute-start | bytes 147464 | tf_op jit(solution)/shard_map/ppermute | solution.py:23
  5.8 5.3 %collective-permute-start.1 = (bf16[32,768]{1,0:T(8,128)(2,1)}, bf16[32,768]{1,0:T(8,128)(2,1)S(1)}, u32[]{:S(2)}, u32[]{:S(2)}) collective-permute-start(bf16[32,768]{1,0:T(8,128)(2,1)} %param.4), channel_id=1, source_target_pairs={{0,8},{4,12},{8,0},{12,4},{1,9},{5,13},{9,1},{13,5},{2,10},{6,14},... | collective-permute-start | bytes 147464 | tf_op jit(solution)/shard_map/ppermute | solution.py:23
  11.2 6.2 %collective-permute-start.3 = (bf16[144,768]{1,0:T(8,128)(2,1)S(1)}, bf16[144,768]{1,0:T(8,128)(2,1)S(1)}, u32[]{:S(2)}, u32[]{:S(2)}) collective-permute-start(bf16[144,768]{1,0:T(8,128)(2,1)S(1)} %get-tuple-element.8), channel_id=1, source_target_pairs={{0,2},{2,0},{1,3},{3,1},{4,6},{6,4},{5,7},{7,5},{8,10},{10,8},{9,1... | collective-permute-start | bytes 663560 | tf_op jit(solution)/shard_map/ppermute | solution.py:23
  18.4 2.3 %collective-permute-start.4 = (bf16[2,144,768]{2,1,0:T(8,128)(2,1)}, bf16[2,144,768]{2,1,0:T(8,128)(2,1)}, u32[]{:S(2)}, u32[]{:S(2)}) collective-permute-start(bf16[2,144,768]{2,1,0:T(8,128)(2,1)} %get-tuple-element.6), channel_id=1, source_target_pairs={{0,1},{1,0},{2,3},{3,2},{4,5},{5,4},{6,7},{7,6},{8,9},{9,8},{10,11... | collective-permute-start | bytes 1327112 | tf_op jit(solution)/shard_map/ppermute | solution.py:23
  20.6 3.6 %copy-start.2 = (bf16[2048,768]{1,0:T(8,128)(2,1)S(1)}, bf16[2048,768]{1,0:T(8,128)(2,1)}, u32[]{:S(2)}) copy-start(bf16[2048,768]{1,0:T(8,128)(2,1)} %fusion.1) | copy-start | bytes 9437188
  28.1 11.1 %copy-start.5 = (s32[32]{0:T(128)S(1)}, s32[32]{0:T(128)}, u32[]{:S(2)}) copy-start(s32[32]{0:T(128)} %param.5) | copy-start | bytes 388
  31.1 7.0 %collective-permute-start.6 = (f32[3,2,2,4,32]{4,3,2,1,0:T(4,128)S(1)}, f32[3,2,2,4,32]{4,3,2,1,0:T(4,128)S(1)}, u32[]{:S(2)}, u32[]{:S(2)}) collective-permute-start(f32[3,2,2,4,32]{4,3,2,1,0:T(4,128)S(1)} %get-tuple-element.10), channel_id=1, source_target_pairs={{0,8},{4,12},{8,0},{12,4},{1,9},{5,13},{9,1},{13,5},{2,10},{6,14},... | collective-permute-start | bytes 18440 | tf_op jit(solution)/shard_map/ppermute | solution.py:23
  33.2 5.6 %collective-permute-start.5 = (f32[3,2,2,4,32]{4,3,2,1,0:T(4,128)S(1)}, f32[3,2,2,4,32]{4,3,2,1,0:T(4,128)S(1)}, u32[]{:S(2)}, u32[]{:S(2)}) collective-permute-start(f32[3,2,2,4,32]{4,3,2,1,0:T(4,128)S(1)} %get-tuple-element.10), channel_id=1, source_target_pairs={{0,4},{4,8},{8,12},{12,0},{1,5},{5,9},{9,13},{13,1},{2,6},{6,10},{... | collective-permute-start | bytes 18440 | tf_op jit(solution)/shard_map/ppermute | solution.py:23
  34.5 4.3 %collective-permute-start.7 = (f32[3,2,2,4,32]{4,3,2,1,0:T(4,128)S(1)}, f32[3,2,2,4,32]{4,3,2,1,0:T(4,128)S(1)}, u32[]{:S(2)}, u32[]{:S(2)}) collective-permute-start(f32[3,2,2,4,32]{4,3,2,1,0:T(4,128)S(1)} %get-tuple-element.10), channel_id=1, source_target_pairs={{0,12},{4,0},{8,4},{12,8},{1,13},{5,1},{9,5},{13,9},{2,14},{6,2},{... | collective-permute-start | bytes 18440 | tf_op jit(solution)/shard_map/ppermute | solution.py:23
  38.0 5.5 %copy-start.3 = (bf16[2048,768]{1,0:T(8,128)(2,1)S(1)}, bf16[2048,768]{1,0:T(8,128)(2,1)}, u32[]{:S(2)}) copy-start(bf16[2048,768]{1,0:T(8,128)(2,1)} %fusion.1) | copy-start | bytes 9437188
  43.6 1.7 %copy-start = (f32[512,768]{1,0:T(8,128)}, f32[512,768]{1,0:T(8,128)S(1)}, u32[]{:S(2)}) copy-start(f32[512,768]{1,0:T(8,128)S(1)} %convert_reduce_fusion) | copy-start | bytes 4718596

commit v7 on v3

--- a/solution.py
+++ b/solution.py
@@ -1,10 +1,12 @@
 import jax
 import jax.numpy as jnp
 from jax import lax
+from jax.experimental import pallas as pl
 from jax.sharding import PartitionSpec as P
 
 STAGES = ("cent", "dp", "sub")
 SHIFT_MAX = 4
+GROUP_ROWS = 128
 
 
 def normalize(values):
@@ -30,6 +32,26 @@
     return 0 if relative(name) else lax.axis_index(name)
 
 
+def update_kernel(scores_ref, log_sum_ref, weight_ref, rows_ref, cents_ref, sums_ref, renormed_ref):
+    n_groups = rows_ref.shape[0] // GROUP_ROWS
+    responsibility = (weight_ref[...] * jnp.exp(scores_ref[...] - log_sum_ref[...])).astype(jnp.bfloat16)
+    sums = jnp.zeros(sums_ref.shape, jnp.float32)
+    mass = jnp.zeros((sums_ref.shape[0], 1), jnp.float32)
+    for group in range(n_groups):
+        part = responsibility[:, group * GROUP_ROWS:(group + 1) * GROUP_ROWS]
+        partial_value = jnp.dot(
+            part, rows_ref[group * GROUP_ROWS:(group + 1) * GROUP_ROWS, :], preferred_element_type=jnp.float32
+        )
+        sums = sums + partial_value.astype(jnp.bfloat16).astype(jnp.float32)
+        group_mass = jnp.sum(part.astype(jnp.float32), axis=1, keepdims=True)
+        mass = mass + group_mass.astype(jnp.bfloat16).astype(jnp.float32)
+    sums_ref[...] = sums
+    moved = cents_ref[...].astype(jnp.float32) + sums / (mass + 1.0)
+    renormed_ref[...] = (moved * lax.rsqrt(jnp.sum(moved * moved, axis=1, keepdims=True) + 1e-06)).astype(
+        jnp.bfloat16
+    )
+
+
 def shards(embeddings, weights, centroids, inverse_temp):
     sharpness = inverse_temp[0]
     row_dev, width = embeddings.shape
@@ -48,13 +70,13 @@
 
     scores = (
         lax.dot_general(
-            unit_rows, own_cents, (((1,), (1,)), ((), ())), preferred_element_type=jnp.float32
+            own_cents, unit_rows, (((1,), (1,)), ((), ())), preferred_element_type=jnp.float32
         )
         * sharpness
     )
     block_shape = (sizes["sub"], sizes["dp"], sizes["cent"], row_dev)
-    local_peak = jnp.max(scores, axis=1)
-    local_total = jnp.sum(jnp.exp(scores - local_peak[:, None]), axis=1)
+    local_peak = jnp.max(scores, axis=0)
+    local_total = jnp.sum(jnp.exp(scores - local_peak[None, :]), axis=0)
 
     own_index = (own_block("sub"), own_block("dp"), own_block("cent"), 0)
     known_weights = lax.dynamic_update_slice(
@@ -75,18 +97,27 @@
     weight_float = stats[2].reshape(-1)
     log_sum = (stats[0] + jnp.log(stats[1])).reshape(-1)
 
-    responsibility = (weight_float[:, None] * jnp.exp(scores - log_sum[:, None])).astype(jnp.bfloat16)
-    grouped_resp = responsibility.reshape(n_groups, -1, own_count)
-    grouped_rows = unit_rows.reshape(n_groups, -1, width)
-    partial_value = lax.dot_general(
-        grouped_resp, grouped_rows, (((1,), (1,)), ((0,), (0,))), preferred_element_type=jnp.float32
-    ).astype(jnp.bfloat16)
-    centroid_sums = jnp.sum(partial_value.astype(jnp.float32), axis=0)
-    weight_mass = jnp.sum(grouped_resp.astype(jnp.float32), axis=1).astype(jnp.bfloat16)
-    own_mass = jnp.sum(weight_mass.astype(jnp.float32), axis=0)
-
-    moved = own_cents.astype(jnp.float32) + centroid_sums / (own_mass + 1.0)[:, None]
-    renormed = normalize(moved).astype(jnp.bfloat16)
+    n_rows = unit_rows.shape[0]
+    if n_rows == n_groups * GROUP_ROWS and n_rows * (own_count + width) * 4 <= (8 << 20):
+        centroid_sums, renormed = pl.pallas_call(
+            update_kernel,
+            out_shape=(
+                jax.ShapeDtypeStruct((own_count, width), jnp.float32),
+                jax.ShapeDtypeStruct((own_count, width), jnp.bfloat16),
+            ),
+        )(scores, log_sum[None, :], weight_float[None, :], unit_rows, own_cents)
+    else:
+        responsibility = (weight_float[None, :] * jnp.exp(scores - log_sum[None, :])).astype(jnp.bfloat16)
+        grouped_resp = responsibility.reshape(own_count, n_groups, -1)
+        grouped_rows = unit_rows.reshape(n_groups, -1, width)
+        partial_value = lax.dot_general(
+            grouped_resp, grouped_rows, (((2,), (1,)), ((1,), (0,))), preferred_element_type=jnp.float32
+        ).astype(jnp.bfloat16)
+        centroid_sums = jnp.sum(partial_value.astype(jnp.float32), axis=0)
+        weight_mass = jnp.sum(grouped_resp.astype(jnp.float32), axis=2).astype(jnp.bfloat16)
+        own_mass = jnp.sum(weight_mass.astype(jnp.float32), axis=1)
+        moved = own_cents.astype(jnp.float32) + centroid_sums / (own_mass + 1.0)[:, None]
+        renormed = normalize(moved).astype(jnp.bfloat16)
 
     own_log_sum = log_sum.reshape(block_shape)[own_index[:3]]
     objective = weights.astype(jnp.float32) * own_log_sum / sharpness

time: 38.4 us -> 40.8 us (1.062)
  Pallas kernels: 0 us -> 4.39 us
  other arithmetic: 7.24 us -> 5.14 us
  matrix products: 1.77 us -> 0.62 us
  local copies, waits for them, and re-layouts: 0.56 us -> 1.64 us
    pallas_call x0 -> x1, Pallas kernels: none -> 4.39 us  [shards(): pl.pallas_call(update_kernel, out_shape=(jax.ShapeDtypeStruct((own_count,...]
    convert_element_type x1 -> x0, other arithmetic: 1.25 us -> none  [shards(): renormed = normalize(moved).astype(jnp.bfloat16)]
    dot_general x2 -> x1, matrix products: 1.77 us -> 0.62 us  [shards(): lax.dot_general(own_cents, unit_rows, (((1,), (1,)), ((), ())), preferred...]
    another operation x0 -> x1, local copies, waits for them, and re-layouts: none -> 0.66 us  [shards(): weight_float[None, :]]
    add x1, local copies, waits for them, and re-layouts: 0.09 us -> 0.67 us  [shards(): log_sum = (stats[0] + jnp.log(stats[1])).reshape(-1)]
    reduce_sum x3 -> x2, other arithmetic: 2.02 us -> 1.59 us  [normalize(): jnp.sum(floats * floats, axis=-1, keepdims=True) + 1e-06]
    reduce_sum x3 -> x1, other arithmetic: 0.6 us -> 0.2 us  [shards(): local_total = jnp.sum(jnp.exp(scores - local_peak[None, :]), axis=0)]
where the time goes in v7:
time: 40.8 us; the launch traced here: 40.5 us
  starting transfers between devices  14.1 us (35%)
  waiting for transfers between devices  13.1 us (32%)
  other arithmetic  5.14 us (13%)
  Pallas kernels  4.39 us (11%)
  local copies, waits for them, and re-layouts  1.64 us (4%)
  between operations  1.52 us (4%)
  matrix products  0.62 us (2%)
    ppermute x10, starting transfers between devices, gather_stage(): lax.ppermute(value, name, [(j, (j + q) % size) for j in range(size)])  14.1 us
    ppermute x10, waiting for transfers between devices, gather_stage(): lax.ppermute(value, name, [(j, (j + q) % size) for j in range(size)])  13.1 us
    pallas_call x1, Pallas kernels, shards(): pl.pallas_call(update_kernel, out_shape=(jax.ShapeDtypeStruct((own_count,...  4.39 us
    reduce_sum x2, other arithmetic, normalize(): jnp.sum(floats * floats, axis=-1, keepdims=True) + 1e-06  1.59 us
    convert_element_type x1, other arithmetic, shards(): normalize(lax.dynamic_slice_in_dim(centroids, offset, own_count, 0))  1.33 us
    another operation x2, other arithmetic, gather_stage(): return jnp.stack(parts)  0.9 us
  transfers between devices with their start and end apart: 10, of which 8 were waited for; matrix products, arithmetic and copies ran while one was open for 7% of the time, Pallas kernels for 0%

profile of v7, /device:TPU:0, one launch (start us, length us, event | category | flops | bytes accessed | tf_op | source)
XLA Modules:
  0.0 40.5 jit_solution(16899909957106431322)
XLA Ops:
  0.6 3.1 %collective-permute-start = (bf16[32,768]{1,0:T(8,128)(2,1)}, bf16[32,768]{1,0:T(8,128)(2,1)S(1)}, u32[]{:S(2)}, u32[]{:S(2)}) collective-permute-start(bf16[32,768]{1,0:T(8,128)(2,1)} %param.4), channel_id=1, source_target_pairs={{0,4},{4,8},{8,12},{12,0},{1,5},{5,9},{9,13},{13,1},{2,6},{6,10},{... | collective-permute-start | bytes 147464 | tf_op jit(solution)/shard_map/ppermute | solution.py:25
  3.7 2.1 %collective-permute-start.2 = (bf16[32,768]{1,0:T(8,128)(2,1)}, bf16[32,768]{1,0:T(8,128)(2,1)S(1)}, u32[]{:S(2)}, u32[]{:S(2)}) collective-permute-start(bf16[32,768]{1,0:T(8,128)(2,1)} %param.4), channel_id=1, source_target_pairs={{0,12},{4,0},{8,4},{12,8},{1,13},{5,1},{9,5},{13,9},{2,14},{6,2},{... | collective-permute-start | bytes 147464 | tf_op jit(solution)/shard_map/ppermute | solution.py:25
  5.8 0.9 %collective-permute-start.1 = (bf16[32,768]{1,0:T(8,128)(2,1)}, bf16[32,768]{1,0:T(8,128)(2,1)S(1)}, u32[]{:S(2)}, u32[]{:S(2)}) collective-permute-start(bf16[32,768]{1,0:T(8,128)(2,1)} %param.4), channel_id=1, source_target_pairs={{0,8},{4,12},{8,0},{12,4},{1,9},{5,13},{9,1},{13,5},{2,10},{6,14},... | collective-permute-start | bytes 147464 | tf_op jit(solution)/shard_map/ppermute | solution.py:25
  6.7 1.4 %fusion = f32[512]{0:T(512)S(1)} fusion(bf16[2048,768]{1,0:T(8,128)(2,1)} %param.6, s32[]{:T(128)S(6)} %select_n.3), kind=kLoop, calls=%fused_computation.2 | loop fusion | flops 1179136 | bytes 788484 | tf_op jit(solution)/shard_map/reduce_sum | solution.py:14
  8.1 0.0 collective-permute-done
  8.1 0.4 %collective-permute-done.2 = bf16[32,768]{1,0:T(8,128)(2,1)S(1)} collective-permute-done((bf16[32,768]{1,0:T(8,128)(2,1)}, bf16[32,768]{1,0:T(8,128)(2,1)S(1)}, u32[]{:S(2)}, u32[]{:S(2)}) %collective-permute-start.2) | collective-permute-done | bytes 49184 | tf_op jit(solution)/shard_map/ppermute | solution.py:25
  8.5 2.6 %collective-permute-done.1 = bf16[32,768]{1,0:T(8,128)(2,1)S(1)} collective-permute-done((bf16[32,768]{1,0:T(8,128)(2,1)}, bf16[32,768]{1,0:T(8,128)(2,1)S(1)}, u32[]{:S(2)}, u32[]{:S(2)}) %collective-permute-start.1) | collective-permute-done | bytes 49184 | tf_op jit(solution)/shard_map/ppermute | solution.py:25
  11.1 0.0 copy-start.3
  11.1 0.8 %fusion.26 = (bf16[1,4,32,768]{3,2,1,0:T(8,128)(2,1)S(1)}, bf16[4,32,768]{2,1,0:T(8,128)(2,1)S(1)}) fusion(bf16[1,32,768]{2,1,0:T(8,128)(2,1)S(1)} %bitcast.108, bf16[1,32,768]{2,1,0:T(8,128)(2,1)S(1)} %bitcast.109, bf16[1,32,768]{2,1,0:T(8,128)(2,1)S(1)} %bitcast.107, bf16[1,32,768]{2,1,0:T(8,128)(2,1)} %bitcast.106), kind=kLoop, calls=%fused_computation.68 | loop fusion | flops 294912 | bytes 589824 | tf_op jit(solution)/shard_map/stack | solution.py:27
  12.0 1.6 %collective-permute-start.3 = (bf16[4,32,768]{2,1,0:T(8,128)(2,1)S(1)}, bf16[4,32,768]{2,1,0:T(8,128)(2,1)S(1)}, u32[]{:S(2)}, u32[]{:S(2)}) collective-permute-start(bf16[4,32,768]{2,1,0:T(8,128)(2,1)S(1)} %get-tuple-element.10), channel_id=1, source_target_pairs={{0,2},{2,0},{1,3},{3,1},{4,6},{6,4},{5,7},{7,5},{8,10},{10,8},{9,1... | collective-permute-start | bytes 589832 | tf_op jit(solution)/shard_map/ppermute | solution.py:25
  13.6 4.1 %collective-permute-done.3 = bf16[4,32,768]{2,1,0:T(8,128)(2,1)S(1)} collective-permute-done((bf16[4,32,768]{2,1,0:T(8,128)(2,1)S(1)}, bf16[4,32,768]{2,1,0:T(8,128)(2,1)S(1)}, u32[]{:S(2)}, u32[]{:S(2)}) %collective-permute-start.3) | collective-permute-done | bytes 196640 | tf_op jit(solution)/shard_map/ppermute | solution.py:25
  17.7 0.1 fusion.25
  17.8 0.1 collective-permute-start.4
  17.8 1.3 %fusion.1.cents_ref = bf16[512,768]{1,0:T(8,128)(2,1)S(1)} fusion(f32[512]{0:T(512)S(1)} %add_rsqrt_fusion.1, bf16[2048,768]{1,0:T(8,128)(2,1)} %param.6, s32[]{:T(128)S(6)} %select_n.3), kind=kLoop, calls=%fused_computation.3 | loop fusion | flops 1179648 | bytes 1574916 | tf_op jit(solution)/shard_map/convert_element_type | solution.py:68
  19.2 0.0 copy-start.1
  19.8 0.0 copy-done.3
  19.9 0.0 collective-permute-done.4
  19.9 0.2 multiply_reduce_fusion
  20.1 0.1 maximum_convert_fusion
  20.2 0.1 rsqrt.21
  20.3 0.2 fusion.2.rows_ref
  20.5 0.0 copy-start.2
  20.5 0.0 copy-done.1
  20.5 0.6 %fusion.30 = (f32[512]{0:T(512)S(1)}, f32[512,512]{1,0:T(8,128)S(1)}) fusion(f32[]{:T(128)} %bitcast.98, bf16[512,768]{1,0:T(8,128)(2,1)S(1)} %fusion.1.cents_ref, bf16[512,768]{1,0:T(8,128)(2,1)S(1)} %fusion.2.rows_ref), kind=kOutput, calls=%fused_computation.72 | convolution fusion | flops 403176960 | bytes 2623492 | tf_op jit(solution)/shard_map/dot_general | solution.py:72
  21.1 0.0 copy-start
  21.1 0.1 stack_reshape.6
  21.2 0.2 exponential_reduce_fusion
  21.4 0.0 copy-done.2
  21.4 0.1 stack_reshape.7
  21.5 0.9 %collective-permute-start.6 = (f32[3,2,2,4,32]{4,3,2,1,0:T(4,128)S(1)}, f32[3,2,2,4,32]{4,3,2,1,0:T(4,128)S(1)}, u32[]{:S(2)}, u32[]{:S(2)}) collective-permute-start(f32[3,2,2,4,32]{4,3,2,1,0:T(4,128)S(1)} %get-tuple-element.20), channel_id=1, source_target_pairs={{0,8},{4,12},{8,0},{12,4},{1,9},{5,13},{9,1},{13,5},{2,10},{6,14},... | collective-permute-start | bytes 18440 | tf_op jit(solution)/shard_map/ppermute | solution.py:25
  22.4 2.4 %collective-permute-start.5 = (f32[3,2,2,4,32]{4,3,2,1,0:T(4,128)S(1)}, f32[3,2,2,4,32]{4,3,2,1,0:T(4,128)S(1)}, u32[]{:S(2)}, u32[]{:S(2)}) collective-permute-start(f32[3,2,2,4,32]{4,3,2,1,0:T(4,128)S(1)} %get-tuple-element.20), channel_id=1, source_target_pairs={{0,4},{4,8},{8,12},{12,0},{1,5},{5,9},{9,13},{13,1},{2,6},{6,10},{... | collective-permute-start | bytes 18440 | tf_op jit(solution)/shard_map/ppermute | solution.py:25
  24.9 1.4 %collective-permute-start.7 = (f32[3,2,2,4,32]{4,3,2,1,0:T(4,128)S(1)}, f32[3,2,2,4,32]{4,3,2,1,0:T(4,128)S(1)}, u32[]{:S(2)}, u32[]{:S(2)}) collective-permute-start(f32[3,2,2,4,32]{4,3,2,1,0:T(4,128)S(1)} %get-tuple-element.20), channel_id=1, source_target_pairs={{0,12},{4,0},{8,4},{12,8},{1,13},{5,1},{9,5},{13,9},{2,14},{6,2},{... | collective-permute-start | bytes 18440 | tf_op jit(solution)/shard_map/ppermute | solution.py:25
  26.2 0.4 collective-permute-done.6
  26.7 1.4 %collective-permute-done.5 = f32[3,2,2,4,32]{4,3,2,1,0:T(4,128)S(1)} collective-permute-done((f32[3,2,2,4,32]{4,3,2,1,0:T(4,128)S(1)}, f32[3,2,2,4,32]{4,3,2,1,0:T(4,128)S(1)}, u32[]{:S(2)}, u32[]{:S(2)}) %collective-permute-start.5) | collective-permute-done | bytes 6176 | tf_op jit(solution)/shard_map/ppermute | solution.py:25
  28.1 0.6 %collective-permute-done.7 = f32[3,2,2,4,32]{4,3,2,1,0:T(4,128)S(1)} collective-permute-done((f32[3,2,2,4,32]{4,3,2,1,0:T(4,128)S(1)}, f32[3,2,2,4,32]{4,3,2,1,0:T(4,128)S(1)}, u32[]{:S(2)}, u32[]{:S(2)}) %collective-permute-start.7) | collective-permute-done | bytes 6176 | tf_op jit(solution)/shard_map/ppermute | solution.py:25
  28.9 1.6 %collective-permute-start.8 = (f32[3,2,2,4,32]{4,3,2,1,0:T(4,128)S(1)}, f32[3,2,2,4,32]{4,3,2,1,0:T(4,128)S(1)}, u32[]{:S(2)}, u32[]{:S(2)}) collective-permute-start(f32[3,2,2,4,32]{4,3,2,1,0:T(4,128)S(1)} %get-tuple-element.16), channel_id=1, source_target_pairs={{0,2},{2,0},{1,3},{3,1},{4,6},{6,4},{5,7},{7,5},{8,10},{10,8},{9,1... | collective-permute-start | bytes 18440 | tf_op jit(solution)/shard_map/ppermute | solution.py:25
  30.4 2.3 %collective-permute-done.8 = f32[3,2,2,4,32]{4,3,2,1,0:T(4,128)S(1)} collective-permute-done((f32[3,2,2,4,32]{4,3,2,1,0:T(4,128)S(1)}, f32[3,2,2,4,32]{4,3,2,1,0:T(4,128)S(1)}, u32[]{:S(2)}, u32[]{:S(2)}) %collective-permute-start.8) | collective-permute-done | bytes 6176 | tf_op jit(solution)/shard_map/ppermute | solution.py:25
  32.9 0.1 collective-permute-start.9
  32.9 1.2 %collective-permute-done.9 = f32[3,2,2,4,32]{4,3,2,1,0:T(4,128)S(1)} collective-permute-done((f32[3,2,2,4,32]{4,3,2,1,0:T(4,128)S(1)}, f32[3,2,2,4,32]{4,3,2,1,0:T(4,128)S(1)}, u32[]{:S(2)}, u32[]{:S(2)}) %collective-permute-start.9) | collective-permute-done | bytes 6176 | tf_op jit(solution)/shard_map/ppermute | solution.py:25
  34.2 0.7 %broadcast_in_dim_reshape_squeeze_stack.3.weight_ref = f32[1,512]{1,0:T(1,128)} reshape(f32[2,2,4,32]{3,2,1,0:T(4,128)S(1)} %fusion.16) | data formatting | bytes 4096 | tf_op jit(solution)/shard_map/broadcast_in_dim;reshape;squeeze;stack | solution.py:108
  34.9 0.7 %add.43.log_sum_ref = f32[1,512]{1,0:T(1,128)} reshape(f32[2,2,4,32]{3,2,1,0:T(4,128)S(1)} %bitcast.111) | data formatting | bytes 4096 | tf_op jit(solution)/shard_map/add | solution.py:98
  35.6 0.5 %fusion.21 = f32[32]{0:T(128)} fusion(f32[2,2,4,32]{3,2,1,0:T(4,128)S(1)} %bitcast.112, s32[32]{0:T(128)S(1)} %copy-done.3, f32[]{:T(128)} %bitcast.99), kind=kLoop, calls=%fused_computation.62 | loop fusion | flops 96 | bytes 388 | tf_op jit(solution)/shard_map/div | solution.py:123
  36.1 0.0 copy-done
  36.1 4.4 %shard_map.67 = (f32[512,768]{1,0:T(8,128)}, bf16[512,768]{1,0:T(8,128)(2,1)}) custom-call(f32[512,512]{1,0:T(8,128)} %copy-done, f32[1,512]{1,0:T(1,128)} %add.43.log_sum_ref, f32[1,512]{1,0:T(1,128)} %broadcast_in_dim_reshape_squeeze_stack.3.weight_ref, bf16[512,768]{1,0:T(8,128)(2,1)} %copy-done.2, bf16[512,768]{1,0:T(8,128)(2,1)} %copy-done.1), custom_call_target="tpu_custom_call" | custom-call | tf_op jit(solution)/shard_map/pallas_call | solution.py:102
  (29 shorter events, 0.4 us)
Async XLA Ops:
  0.6 7.5 %collective-permute-start = (bf16[32,768]{1,0:T(8,128)(2,1)}, bf16[32,768]{1,0:T(8,128)(2,1)S(1)}, u32[]{:S(2)}, u32[]{:S(2)}) collective-permute-start(bf16[32,768]{1,0:T(8,128)(2,1)} %param.4), channel_id=1, source_target_pairs={{0,4},{4,8},{8,12},{12,0},{1,5},{5,9},{9,13},{13,1},{2,6},{6,10},{... | collective-permute-start | bytes 147464 | tf_op jit(solution)/shard_map/ppermute | solution.py:25
  3.7 4.8 %collective-permute-start.2 = (bf16[32,768]{1,0:T(8,128)(2,1)}, bf16[32,768]{1,0:T(8,128)(2,1)S(1)}, u32[]{:S(2)}, u32[]{:S(2)}) collective-permute-start(bf16[32,768]{1,0:T(8,128)(2,1)} %param.4), channel_id=1, source_target_pairs={{0,12},{4,0},{8,4},{12,8},{1,13},{5,1},{9,5},{13,9},{2,14},{6,2},{... | collective-permute-start | bytes 147464 | tf_op jit(solution)/shard_map/ppermute | solution.py:25
  5.8 5.3 %collective-permute-start.1 = (bf16[32,768]{1,0:T(8,128)(2,1)}, bf16[32,768]{1,0:T(8,128)(2,1)S(1)}, u32[]{:S(2)}, u32[]{:S(2)}) collective-permute-start(bf16[32,768]{1,0:T(8,128)(2,1)} %param.4), channel_id=1, source_target_pairs={{0,8},{4,12},{8,0},{12,4},{1,9},{5,13},{9,1},{13,5},{2,10},{6,14},... | collective-permute-start | bytes 147464 | tf_op jit(solution)/shard_map/ppermute | solution.py:25
  11.1 8.7 %copy-start.3 = (s32[32]{0:T(128)S(1)}, s32[32]{0:T(128)}, u32[]{:S(2)}) copy-start(s32[32]{0:T(128)} %param.5) | copy-start | bytes 388
  12.0 5.7 %collective-permute-start.3 = (bf16[4,32,768]{2,1,0:T(8,128)(2,1)S(1)}, bf16[4,32,768]{2,1,0:T(8,128)(2,1)S(1)}, u32[]{:S(2)}, u32[]{:S(2)}) collective-permute-start(bf16[4,32,768]{2,1,0:T(8,128)(2,1)S(1)} %get-tuple-element.10), channel_id=1, source_target_pairs={{0,2},{2,0},{1,3},{3,1},{4,6},{6,4},{5,7},{7,5},{8,10},{10,8},{9,1... | collective-permute-start | bytes 589832 | tf_op jit(solution)/shard_map/ppermute | solution.py:25
  17.8 2.1 %collective-permute-start.4 = (bf16[2,4,32,768]{3,2,1,0:T(8,128)(2,1)S(1)}, bf16[2,4,32,768]{3,2,1,0:T(8,128)(2,1)S(1)}, u32[]{:S(2)}, u32[]{:S(2)}) collective-permute-start(bf16[2,4,32,768]{3,2,1,0:T(8,128)(2,1)S(1)} %get-tuple-element.8), channel_id=1, source_target_pairs={{0,1},{1,0},{2,3},{3,2},{4,5},{5,4},{6,7},{7,6},{8,9},{9,8},{10,11... | collective-permute-start | bytes 1179656 | tf_op jit(solution)/shard_map/ppermute | solution.py:25
  19.2 1.3 %copy-start.1 = (bf16[512,768]{1,0:T(8,128)(2,1)}, bf16[512,768]{1,0:T(8,128)(2,1)S(1)}, u32[]{:S(2)}) copy-start(bf16[512,768]{1,0:T(8,128)(2,1)S(1)} %fusion.1.cents_ref) | copy-start | bytes 2359300
  20.5 0.9 %copy-start.2 = (bf16[512,768]{1,0:T(8,128)(2,1)}, bf16[512,768]{1,0:T(8,128)(2,1)S(1)}, u32[]{:S(2)}) copy-start(bf16[512,768]{1,0:T(8,128)(2,1)S(1)} %fusion.2.rows_ref) | copy-start | bytes 2359300
  21.1 14.9 %copy-start = (f32[512,512]{1,0:T(8,128)}, f32[512,512]{1,0:T(8,128)S(1)}, u32[]{:S(2)}) copy-start(f32[512,512]{1,0:T(8,128)S(1)} %get-tuple-element.24.scores_ref) | copy-start | bytes 3145732
  21.5 5.1 %collective-permute-start.6 = (f32[3,2,2,4,32]{4,3,2,1,0:T(4,128)S(1)}, f32[3,2,2,4,32]{4,3,2,1,0:T(4,128)S(1)}, u32[]{:S(2)}, u32[]{:S(2)}) collective-permute-start(f32[3,2,2,4,32]{4,3,2,1,0:T(4,128)S(1)} %get-tuple-element.20), channel_id=1, source_target_pairs={{0,8},{4,12},{8,0},{12,4},{1,9},{5,13},{9,1},{13,5},{2,10},{6,14},... | collective-permute-start | bytes 18440 | tf_op jit(solution)/shard_map/ppermute | solution.py:25
  22.4 5.6 %collective-permute-start.5 = (f32[3,2,2,4,32]{4,3,2,1,0:T(4,128)S(1)}, f32[3,2,2,4,32]{4,3,2,1,0:T(4,128)S(1)}, u32[]{:S(2)}, u32[]{:S(2)}) collective-permute-start(f32[3,2,2,4,32]{4,3,2,1,0:T(4,128)S(1)} %get-tuple-element.20), channel_id=1, source_target_pairs={{0,4},{4,8},{8,12},{12,0},{1,5},{5,9},{9,13},{13,1},{2,6},{6,10},{... | collective-permute-start | bytes 18440 | tf_op jit(solution)/shard_map/ppermute | solution.py:25
  24.9 3.8 %collective-permute-start.7 = (f32[3,2,2,4,32]{4,3,2,1,0:T(4,128)S(1)}, f32[3,2,2,4,32]{4,3,2,1,0:T(4,128)S(1)}, u32[]{:S(2)}, u32[]{:S(2)}) collective-permute-start(f32[3,2,2,4,32]{4,3,2,1,0:T(4,128)S(1)} %get-tuple-element.20), channel_id=1, source_target_pairs={{0,12},{4,0},{8,4},{12,8},{1,13},{5,1},{9,5},{13,9},{2,14},{6,2},{... | collective-permute-start | bytes 18440 | tf_op jit(solution)/shard_map/ppermute | solution.py:25
  28.9 3.9 %collective-permute-start.8 = (f32[3,2,2,4,32]{4,3,2,1,0:T(4,128)S(1)}, f32[3,2,2,4,32]{4,3,2,1,0:T(4,128)S(1)}, u32[]{:S(2)}, u32[]{:S(2)}) collective-permute-start(f32[3,2,2,4,32]{4,3,2,1,0:T(4,128)S(1)} %get-tuple-element.16), channel_id=1, source_target_pairs={{0,2},{2,0},{1,3},{3,1},{4,6},{6,4},{5,7},{7,5},{8,10},{10,8},{9,1... | collective-permute-start | bytes 18440 | tf_op jit(solution)/shard_map/ppermute | solution.py:25
  32.9 1.3 %collective-permute-start.9 = (f32[3,2,2,4,32]{4,3,2,1,0:T(4,128)S(1)}, f32[3,2,2,4,32]{4,3,2,1,0:T(4,128)S(1)}, u32[]{:S(2)}, u32[]{:S(2)}) collective-permute-start(f32[3,2,2,4,32]{4,3,2,1,0:T(4,128)S(1)} %get-tuple-element.12), channel_id=1, source_target_pairs={{0,1},{1,0},{2,3},{3,2},{4,5},{5,4},{6,7},{7,6},{8,9},{9,8},{10,11... | collective-permute-start | bytes 18440 | tf_op jit(solution)/shard_map/ppermute | solution.py:25

commit v8 on v6

--- a/solution.py
+++ b/solution.py
@@ -51,7 +51,7 @@
     panel = centroids.shape[0]
     own_count = panel // n_groups
     n_rows = row_dev * sizes["cent"] * n_groups
-    full_panel = n_rows * panel * 4 <= (16 << 20)
+    dp_columns = n_rows * own_count * sizes["dp"] * 4 <= (16 << 20)
 
     blocks = gather_stage(embeddings, "cent").reshape(-1, width)
     cent_rows = blocks.shape[0]
@@ -63,10 +63,16 @@
     cent_weights = payload[:, :, cent_rows, :row_dev].astype(jnp.float32)
 
     offset = lax.axis_index(("dp", "sub")) * own_count
-    if full_panel:
-        panel_cents = lax.optimization_barrier(normalize(centroids).astype(jnp.bfloat16))
-        own_cents = lax.dynamic_slice_in_dim(panel_cents, offset, own_count, 0)
-        score_cents = panel_cents
+    if dp_columns:
+        dp_index, sub_index = lax.axis_index("dp"), lax.axis_index("sub")
+        slices = [
+            lax.dynamic_slice_in_dim(
+                centroids, ((dp_index + q) % sizes["dp"] * sizes["sub"] + sub_index) * own_count, own_count, 0
+            )
+            for q in range(sizes["dp"])
+        ]
+        score_cents = lax.optimization_barrier(normalize(jnp.concatenate(slices, axis=0)).astype(jnp.bfloat16))
+        own_cents = score_cents[:own_count]
     else:
         own_cents = normalize(lax.dynamic_slice_in_dim(centroids, offset, own_count, 0)).astype(jnp.bfloat16)
         own_cents = lax.optimization_barrier(own_cents)
@@ -81,15 +87,15 @@
     block_shape = (sizes["sub"], sizes["dp"], sizes["cent"], row_dev)
     local_peak = jnp.max(scores, axis=1)
     local_total = jnp.sum(jnp.exp(scores - local_peak[:, None]), axis=1)
-    if full_panel:
-        scores = lax.dynamic_slice_in_dim(scores, offset, own_count, 1)
+    if dp_columns:
+        scores = scores[:, :own_count]
 
     own_cent = own_block("cent")
     known_weights = lax.dynamic_update_slice(
         jnp.zeros(block_shape, jnp.float32), cent_weights[:, :, None], (0, 0, own_cent, 0)
     )
     stats = jnp.stack([local_peak.reshape(block_shape), local_total.reshape(block_shape), known_weights])
-    stats = merge_stats(stats, STAGES[:1] if full_panel else STAGES, {"sub": 1, "dp": 2, "cent": 3})
+    stats = merge_stats(stats, ("cent", "sub") if dp_columns else STAGES, {"sub": 1, "dp": 2, "cent": 3})
     weight_float = stats[2].reshape(-1)
     log_sum = (stats[0] + jnp.log(stats[1])).reshape(-1)
 

time: 45.5 us -> 39.3 us (0.86)
  other arithmetic: 17.9 us -> 9.84 us
  waiting for transfers between devices: 5.79 us -> 10 us
  matrix products: 6.05 us -> 3.4 us
  local copies, waits for them, and re-layouts: 0.4 us -> 1.86 us
  starting transfers between devices: 13.6 us -> 12.4 us
    ppermute x8 -> x9, waiting for transfers between devices: 5.79 us -> 10 us  [gather_stage(): lax.ppermute(value, name, [(j, (j + q) % size) for j in range(size)])]
    reduce_sum x3, other arithmetic: 4.49 us -> 1.03 us  [normalize(): jnp.sum(floats * floats, axis=-1, keepdims=True) + 1e-06]
    convert_element_type x1, other arithmetic: 2.25 us -> 0.32 us  [shards(): normalize(jnp.concatenate(slices, axis=0)).astype(jnp.bfloat16)]
    dynamic_slice x0 -> x1, local copies, waits for them, and re-layouts: none -> 1.47 us  [shards(): lax.dynamic_slice_in_dim(centroids, ((dp_index + q) % sizes['dp'] * sizes...]
    dot_general x1, matrix products: 3.76 us -> 2.37 us  [shards(): lax.dot_general(unit_rows, score_cents, (((1,), (1,)), ((), ())), preferr...]
    dot_general x1, matrix products: 2.29 us -> 1.02 us  [shards(): lax.dot_general(grouped_resp, grouped_rows, (((1,), (1,)), ((0,), (0,))),...]
    ppermute x8 -> x9, starting transfers between devices: 13.6 us -> 12.4 us  [gather_stage(): lax.ppermute(value, name, [(j, (j + q) % size) for j in range(size)])]
    convert_element_type x1, other arithmetic: 1.22 us -> 0.11 us  [normalize(): floats = values.astype(jnp.float32)]
  transfers between devices with their start and end apart: 8 -> 9, of which waited for: 3 -> 9; matrix products, arithmetic and copies ran while one was open for 15% -> 10% of each run, Pallas kernels for 0% -> 0%
where the time goes in v8:
time: 39.3 us; the launch traced here: 39 us
  starting transfers between devices  12.4 us (32%)
  waiting for transfers between devices  10 us (25%)
  other arithmetic  9.84 us (25%)
  matrix products  3.4 us (9%)
  local copies, waits for them, and re-layouts  1.86 us (5%)
  between operations  1.51 us (4%)
    ppermute x9, starting transfers between devices, gather_stage(): lax.ppermute(value, name, [(j, (j + q) % size) for j in range(size)])  12.4 us
    ppermute x9, waiting for transfers between devices, gather_stage(): lax.ppermute(value, name, [(j, (j + q) % size) for j in range(size)])  10 us
    dot_general x1, matrix products, shards(): lax.dot_general(unit_rows, score_cents, (((1,), (1,)), ((), ())), preferr...  2.37 us
    reduce_sum x1, other arithmetic, shards(): local_total = jnp.sum(jnp.exp(scores - local_peak[:, None]), axis=1)  2.04 us
    reduce_sum x1, other arithmetic, shards(): jnp.sum(grouped_resp.astype(jnp.float32), axis=1).astype(jnp.bfloat16)  1.51 us
    dynamic_slice x1, local copies, waits for them, and re-layouts, shards(): lax.dynamic_slice_in_dim(centroids, ((dp_index + q) % sizes['dp'] * sizes...  1.47 us
    convert_element_type x1, other arithmetic, shards(): renormed = normalize(moved).astype(jnp.bfloat16)  1.25 us
    convert_element_type x2, other arithmetic, shards(): normalize(payload[:, :, :cent_rows].reshape(-1, width)).astype(jnp.bfloat16)  1.18 us
  transfers between devices with their start and end apart: 9, of which 9 were waited for; matrix products, arithmetic and copies ran while one was open for 10% of the time, Pallas kernels for 0%

profile of v8, /device:TPU:0, one launch (start us, length us, event | category | flops | bytes accessed | tf_op | source)
XLA Modules:
  0.0 39.0 jit_solution(10546513250574373282)
XLA Ops:
  0.6 3.1 %collective-permute-start = (bf16[32,768]{1,0:T(8,128)(2,1)}, bf16[32,768]{1,0:T(8,128)(2,1)S(1)}, u32[]{:S(2)}, u32[]{:S(2)}) collective-permute-start(bf16[32,768]{1,0:T(8,128)(2,1)} %param.4), channel_id=1, source_target_pairs={{0,4},{4,8},{8,12},{12,0},{1,5},{5,9},{9,13},{13,1},{2,6},{6,10},{... | collective-permute-start | bytes 147464 | tf_op jit(solution)/shard_map/ppermute | solution.py:23
  3.7 2.1 %collective-permute-start.2 = (bf16[32,768]{1,0:T(8,128)(2,1)}, bf16[32,768]{1,0:T(8,128)(2,1)S(1)}, u32[]{:S(2)}, u32[]{:S(2)}) collective-permute-start(bf16[32,768]{1,0:T(8,128)(2,1)} %param.4), channel_id=1, source_target_pairs={{0,12},{4,0},{8,4},{12,8},{1,13},{5,1},{9,5},{13,9},{2,14},{6,2},{... | collective-permute-start | bytes 147464 | tf_op jit(solution)/shard_map/ppermute | solution.py:23
  5.8 0.9 %collective-permute-start.1 = (bf16[32,768]{1,0:T(8,128)(2,1)}, bf16[32,768]{1,0:T(8,128)(2,1)S(1)}, u32[]{:S(2)}, u32[]{:S(2)}) collective-permute-start(bf16[32,768]{1,0:T(8,128)(2,1)} %param.4), channel_id=1, source_target_pairs={{0,8},{4,12},{8,0},{12,4},{1,9},{5,13},{9,1},{13,5},{2,10},{6,14},... | collective-permute-start | bytes 147464 | tf_op jit(solution)/shard_map/ppermute | solution.py:23
  6.7 0.7 %convert_bitcast_fusion = bf16[1,32]{1,0:T(2,128)(2,1)S(1)} fusion(s32[32]{0:T(128)} %param.5), kind=kLoop, calls=%fused_computation.74 | loop fusion | flops 32 | bytes 192 | tf_op jit(solution)/shard_map/broadcast_in_dim | solution.py:58
  8.1 0.1 collective-permute-done
  8.1 0.4 %collective-permute-done.2 = bf16[32,768]{1,0:T(8,128)(2,1)S(1)} collective-permute-done((bf16[32,768]{1,0:T(8,128)(2,1)}, bf16[32,768]{1,0:T(8,128)(2,1)S(1)}, u32[]{:S(2)}, u32[]{:S(2)}) %collective-permute-start.2) | collective-permute-done | bytes 49184 | tf_op jit(solution)/shard_map/ppermute | solution.py:23
  8.5 2.6 %collective-permute-done.1 = bf16[32,768]{1,0:T(8,128)(2,1)S(1)} collective-permute-done((bf16[32,768]{1,0:T(8,128)(2,1)}, bf16[32,768]{1,0:T(8,128)(2,1)S(1)}, u32[]{:S(2)}, u32[]{:S(2)}) %collective-permute-start.1) | collective-permute-done | bytes 49184 | tf_op jit(solution)/shard_map/ppermute | solution.py:23
  11.1 0.8 %pad_maximum_fusion.2 = bf16[4,32,768]{2,1,0:T(8,128)(2,1)S(1)} fusion(bf16[1,32,768]{2,1,0:T(8,128)(2,1)S(1)} %bitcast.102, bf16[1,32,768]{2,1,0:T(8,128)(2,1)S(1)} %bitcast.103, bf16[1,32,768]{2,1,0:T(8,128)(2,1)S(1)} %bitcast.101, bf16[1,32,768]{2,1,0:T(8,128)(2,1)} %bitcast.100), kind=kLoop, calls=%fused_computation.28 | loop fusion | flops 294912 | bytes 393216 | tf_op jit(solution)/shard_map/stack | solution.py:25
  12.0 1.6 %collective-permute-start.3 = (bf16[144,768]{1,0:T(8,128)(2,1)S(1)}, bf16[144,768]{1,0:T(8,128)(2,1)S(1)}, u32[]{:S(2)}, u32[]{:S(2)}) collective-permute-start(bf16[144,768]{1,0:T(8,128)(2,1)S(1)} %get-tuple-element.10), channel_id=1, source_target_pairs={{0,2},{2,0},{1,3},{3,1},{4,6},{6,4},{5,7},{7,5},{8,10},{10,8},{9,1... | collective-permute-start | bytes 663560 | tf_op jit(solution)/shard_map/ppermute | solution.py:23
  13.6 1.5 %constant_dynamic-slice_fusion.1 = (bf16[512,768]{1,0:T(8,128)(2,1)S(1)}, bf16[512,768]{1,0:T(8,128)(2,1)S(1)}) fusion(bf16[2048,768]{1,0:T(8,128)(2,1)} %param.6, s32[]{:T(128)S(6)} %select_n.18, s32[]{:T(128)S(6)} %select_n.20), kind=kLoop, calls=%fused_computation.73 | loop fusion | bytes 3145736 | tf_op jit(solution)/shard_map/dynamic_slice | solution.py:69
  15.1 0.4 fusion
  15.4 2.7 %collective-permute-done.3 = bf16[144,768]{1,0:T(8,128)(2,1)S(1)} collective-permute-done((bf16[144,768]{1,0:T(8,128)(2,1)S(1)}, bf16[144,768]{1,0:T(8,128)(2,1)S(1)}, u32[]{:S(2)}, u32[]{:S(2)}) %collective-permute-start.3) | collective-permute-done | bytes 221216 | tf_op jit(solution)/shard_map/ppermute | solution.py:23
  18.2 0.1 fusion.31
  18.2 0.1 collective-permute-start.4
  18.3 0.3 fusion.1
  18.7 1.4 %collective-permute-done.4 = bf16[2,144,768]{2,1,0:T(8,128)(2,1)S(1)} collective-permute-done((bf16[2,144,768]{2,1,0:T(8,128)(2,1)S(1)}, bf16[2,144,768]{2,1,0:T(8,128)(2,1)S(1)}, u32[]{:S(2)}, u32[]{:S(2)}) %collective-permute-start.4) | collective-permute-done | bytes 442400 | tf_op jit(solution)/shard_map/ppermute | solution.py:23
  20.1 0.2 multiply_reduce_fusion.1
  20.3 0.1 fusion.8
  20.5 0.1 fusion.3
  20.6 2.4 %fusion.35 = (f32[512]{0:T(512)S(1)}, f32[512,1024]{1,0:T(8,128)}) fusion(f32[]{:T(128)} %bitcast.90, bf16[512,768]{1,0:T(8,128)(2,1)S(1)} %fusion.3, bf16[1024,768]{1,0:T(8,128)(2,1)S(1)} %fusion.1), kind=kOutput, calls=%fused_computation.82 | convolution fusion | flops 806354432 | bytes 4458500 | tf_op jit(solution)/shard_map/dot_general | solution.py:82
  23.0 0.1 stack_reshape.6
  23.1 2.0 %exponential_reduce_fusion = f32[512]{0:T(512)S(1)} fusion(f32[512,1024]{1,0:T(8,128)} %get-tuple-element.20, f32[512]{0:T(512)S(1)} %get-tuple-element.19), kind=kLoop, calls=%fused_computation.5 | loop fusion | flops 1048064 | bytes 2101248 | tf_op jit(solution)/shard_map/reduce_sum | solution.py:89
  25.1 0.1 stack_reshape.7
  25.2 0.7 %collective-permute-start.6 = (f32[3,2,2,4,32]{4,3,2,1,0:T(4,128)S(1)}, f32[3,2,2,4,32]{4,3,2,1,0:T(4,128)S(1)}, u32[]{:S(2)}, u32[]{:S(2)}) collective-permute-start(f32[3,2,2,4,32]{4,3,2,1,0:T(4,128)S(1)} %get-tuple-element.16), channel_id=1, source_target_pairs={{0,8},{4,12},{8,0},{12,4},{1,9},{5,13},{9,1},{13,5},{2,10},{6,14},... | collective-permute-start | bytes 18440 | tf_op jit(solution)/shard_map/ppermute | solution.py:23
  25.9 2.7 %collective-permute-start.5 = (f32[3,2,2,4,32]{4,3,2,1,0:T(4,128)S(1)}, f32[3,2,2,4,32]{4,3,2,1,0:T(4,128)S(1)}, u32[]{:S(2)}, u32[]{:S(2)}) collective-permute-start(f32[3,2,2,4,32]{4,3,2,1,0:T(4,128)S(1)} %get-tuple-element.16), channel_id=1, source_target_pairs={{0,4},{4,8},{8,12},{12,0},{1,5},{5,9},{9,13},{13,1},{2,6},{6,10},{... | collective-permute-start | bytes 18440 | tf_op jit(solution)/shard_map/ppermute | solution.py:23
  28.6 1.1 %collective-permute-start.7 = (f32[3,2,2,4,32]{4,3,2,1,0:T(4,128)S(1)}, f32[3,2,2,4,32]{4,3,2,1,0:T(4,128)S(1)}, u32[]{:S(2)}, u32[]{:S(2)}) collective-permute-start(f32[3,2,2,4,32]{4,3,2,1,0:T(4,128)S(1)} %get-tuple-element.16), channel_id=1, source_target_pairs={{0,12},{4,0},{8,4},{12,8},{1,13},{5,1},{9,5},{13,9},{2,14},{6,2},{... | collective-permute-start | bytes 18440 | tf_op jit(solution)/shard_map/ppermute | solution.py:23
  29.8 0.4 collective-permute-done.6
  30.2 1.4 %collective-permute-done.5 = f32[3,2,2,4,32]{4,3,2,1,0:T(4,128)S(1)} collective-permute-done((f32[3,2,2,4,32]{4,3,2,1,0:T(4,128)S(1)}, f32[3,2,2,4,32]{4,3,2,1,0:T(4,128)S(1)}, u32[]{:S(2)}, u32[]{:S(2)}) %collective-permute-start.5) | collective-permute-done | bytes 6176 | tf_op jit(solution)/shard_map/ppermute | solution.py:23
  31.6 0.9 %collective-permute-done.7 = f32[3,2,2,4,32]{4,3,2,1,0:T(4,128)S(1)} collective-permute-done((f32[3,2,2,4,32]{4,3,2,1,0:T(4,128)S(1)}, f32[3,2,2,4,32]{4,3,2,1,0:T(4,128)S(1)}, u32[]{:S(2)}, u32[]{:S(2)}) %collective-permute-start.7) | collective-permute-done | bytes 6176 | tf_op jit(solution)/shard_map/ppermute | solution.py:23
  32.5 0.0 copy-start.2
  32.7 0.1 collective-permute-start.8
  32.7 1.0 %fusion.2 = bf16[4,128,768]{2,1,0:T(8,128)(2,1)} fusion(f32[2,2,128,768]{3,2,1,0:T(8,128)S(1)} %fusion.8, f32[4,128]{1,0:T(4,128)S(1)} %bitcast.111), kind=kLoop, calls=%fused_computation.9 | loop fusion | flops 786432 | bytes 2361344 | tf_op jit(solution)/shard_map/convert_element_type | solution.py:62
  33.8 0.0 copy-start.1
  33.8 0.1 collective-permute-done.8
  34.0 0.1 mul.89
  34.1 0.1 add.90
  34.2 0.0 copy-done.2
  34.2 0.5 %fusion.27 = f32[32]{0:T(128)} fusion(f32[2,2,4,32]{3,2,1,0:T(4,128)S(1)} %bitcast.106, s32[32]{0:T(128)S(1)} %copy-done.2, f32[]{:T(128)} %bitcast.91), kind=kLoop, calls=%fused_computation.71 | loop fusion | flops 96 | bytes 388 | tf_op jit(solution)/shard_map/div | solution.py:116
  34.7 1.5 %bitcast_reduce_fusion.2 = (bf16[4,512]{1,0:T(4,128)(2,1)S(1)}, bf16[512,512]{1,0:T(8,128)(2,1)S(1)}) fusion(f32[512]{0:T(512)S(1)} %add.90, f32[512,1024]{1,0:T(8,128)} %get-tuple-element.20, f32[512]{0:T(512)S(1)} %mul.89), kind=kLoop, calls=%fused_computation.75 | loop fusion | flops 1046528 | bytes 1581056 | tf_op jit(solution)/shard_map/reduce_sum | solution.py:109
  36.3 0.0 copy-done.1
  36.3 1.0 %convert_reduce_fusion = f32[512,768]{1,0:T(8,128)S(1)} fusion(bf16[4,128,512]{2,1,0:T(8,128)(2,1)S(1)} %bitcast.95, bf16[4,128,768]{2,1,0:T(8,128)(2,1)S(1)} %copy-done.1), kind=kOutput, calls=%fused_computation | convolution fusion | flops 406978560 | bytes 2883584 | tf_op jit(solution)/shard_map/dot_general | solution.py:105
  37.3 0.0 copy-start
  37.3 0.4 %multiply_reduce_fusion = f32[512]{0:T(512)S(1)} fusion(f32[512,768]{1,0:T(8,128)S(1)} %convert_reduce_fusion, f32[512]{0:T(512)S(1)} %broadcast_add_fusion, bf16[1024,768]{1,0:T(8,128)(2,1)S(1)} %fusion.1), kind=kLoop, calls=%fused_computation.13 | loop fusion | flops 1965568 | bytes 2363392 | tf_op jit(solution)/shard_map/reduce_sum | solution.py:12
  37.7 1.3 %multiply_convert_fusion = bf16[512,768]{1,0:T(8,128)(2,1)} fusion(f32[512]{0:T(512)S(1)} %add_rsqrt_fusion.1, f32[512,768]{1,0:T(8,128)S(1)} %convert_reduce_fusion, f32[512]{0:T(512)S(1)} %broadcast_add_fusion, bf16[1024,768]{1,0:T(8,128)(2,1)S(1)} %fusion.1), kind=kLoop, calls=%fused_computation.12 | loop fusion | flops 1966080 | bytes 3149824 | tf_op jit(solution)/shard_map/convert_element_type | solution.py:113
  39.0 0.0 copy-done
  (26 shorter events, 0.4 us)
Async XLA Ops:
  0.6 7.5 %collective-permute-start = (bf16[32,768]{1,0:T(8,128)(2,1)}, bf16[32,768]{1,0:T(8,128)(2,1)S(1)}, u32[]{:S(2)}, u32[]{:S(2)}) collective-permute-start(bf16[32,768]{1,0:T(8,128)(2,1)} %param.4), channel_id=1, source_target_pairs={{0,4},{4,8},{8,12},{12,0},{1,5},{5,9},{9,13},{13,1},{2,6},{6,10},{... | collective-permute-start | bytes 147464 | tf_op jit(solution)/shard_map/ppermute | solution.py:23
  3.7 4.8 %collective-permute-start.2 = (bf16[32,768]{1,0:T(8,128)(2,1)}, bf16[32,768]{1,0:T(8,128)(2,1)S(1)}, u32[]{:S(2)}, u32[]{:S(2)}) collective-permute-start(bf16[32,768]{1,0:T(8,128)(2,1)} %param.4), channel_id=1, source_target_pairs={{0,12},{4,0},{8,4},{12,8},{1,13},{5,1},{9,5},{13,9},{2,14},{6,2},{... | collective-permute-start | bytes 147464 | tf_op jit(solution)/shard_map/ppermute | solution.py:23
  5.8 5.3 %collective-permute-start.1 = (bf16[32,768]{1,0:T(8,128)(2,1)}, bf16[32,768]{1,0:T(8,128)(2,1)S(1)}, u32[]{:S(2)}, u32[]{:S(2)}) collective-permute-start(bf16[32,768]{1,0:T(8,128)(2,1)} %param.4), channel_id=1, source_target_pairs={{0,8},{4,12},{8,0},{12,4},{1,9},{5,13},{9,1},{13,5},{2,10},{6,14},... | collective-permute-start | bytes 147464 | tf_op jit(solution)/shard_map/ppermute | solution.py:23
  12.0 6.2 %collective-permute-start.3 = (bf16[144,768]{1,0:T(8,128)(2,1)S(1)}, bf16[144,768]{1,0:T(8,128)(2,1)S(1)}, u32[]{:S(2)}, u32[]{:S(2)}) collective-permute-start(bf16[144,768]{1,0:T(8,128)(2,1)S(1)} %get-tuple-element.10), channel_id=1, source_target_pairs={{0,2},{2,0},{1,3},{3,1},{4,6},{6,4},{5,7},{7,5},{8,10},{10,8},{9,1... | collective-permute-start | bytes 663560 | tf_op jit(solution)/shard_map/ppermute | solution.py:23
  18.2 1.9 %collective-permute-start.4 = (bf16[2,144,768]{2,1,0:T(8,128)(2,1)S(1)}, bf16[2,144,768]{2,1,0:T(8,128)(2,1)S(1)}, u32[]{:S(2)}, u32[]{:S(2)}) collective-permute-start(bf16[2,144,768]{2,1,0:T(8,128)(2,1)S(1)} %get-tuple-element.8), channel_id=1, source_target_pairs={{0,1},{1,0},{2,3},{3,2},{4,5},{5,4},{6,7},{7,6},{8,9},{9,8},{10,11... | collective-permute-start | bytes 1327112 | tf_op jit(solution)/shard_map/ppermute | solution.py:23
  25.2 4.9 %collective-permute-start.6 = (f32[3,2,2,4,32]{4,3,2,1,0:T(4,128)S(1)}, f32[3,2,2,4,32]{4,3,2,1,0:T(4,128)S(1)}, u32[]{:S(2)}, u32[]{:S(2)}) collective-permute-start(f32[3,2,2,4,32]{4,3,2,1,0:T(4,128)S(1)} %get-tuple-element.16), channel_id=1, source_target_pairs={{0,8},{4,12},{8,0},{12,4},{1,9},{5,13},{9,1},{13,5},{2,10},{6,14},... | collective-permute-start | bytes 18440 | tf_op jit(solution)/shard_map/ppermute | solution.py:23
  25.9 5.6 %collective-permute-start.5 = (f32[3,2,2,4,32]{4,3,2,1,0:T(4,128)S(1)}, f32[3,2,2,4,32]{4,3,2,1,0:T(4,128)S(1)}, u32[]{:S(2)}, u32[]{:S(2)}) collective-permute-start(f32[3,2,2,4,32]{4,3,2,1,0:T(4,128)S(1)} %get-tuple-element.16), channel_id=1, source_target_pairs={{0,4},{4,8},{8,12},{12,0},{1,5},{5,9},{9,13},{13,1},{2,6},{6,10},{... | collective-permute-start | bytes 18440 | tf_op jit(solution)/shard_map/ppermute | solution.py:23
  28.6 3.8 %collective-permute-start.7 = (f32[3,2,2,4,32]{4,3,2,1,0:T(4,128)S(1)}, f32[3,2,2,4,32]{4,3,2,1,0:T(4,128)S(1)}, u32[]{:S(2)}, u32[]{:S(2)}) collective-permute-start(f32[3,2,2,4,32]{4,3,2,1,0:T(4,128)S(1)} %get-tuple-element.16), channel_id=1, source_target_pairs={{0,12},{4,0},{8,4},{12,8},{1,13},{5,1},{9,5},{13,9},{2,14},{6,2},{... | collective-permute-start | bytes 18440 | tf_op jit(solution)/shard_map/ppermute | solution.py:23
  32.5 1.7 %copy-start.2 = (s32[32]{0:T(128)S(1)}, s32[32]{0:T(128)}, u32[]{:S(2)}) copy-start(s32[32]{0:T(128)} %param.5) | copy-start | bytes 388
  32.7 1.3 %collective-permute-start.8 = (f32[3,2,2,4,32]{4,3,2,1,0:T(4,128)S(1)}, f32[3,2,2,4,32]{4,3,2,1,0:T(4,128)S(1)}, u32[]{:S(2)}, u32[]{:S(2)}) collective-permute-start(f32[3,2,2,4,32]{4,3,2,1,0:T(4,128)S(1)} %get-tuple-element.12), channel_id=1, source_target_pairs={{0,1},{1,0},{2,3},{3,2},{4,5},{5,4},{6,7},{7,6},{8,9},{9,8},{10,11... | collective-permute-start | bytes 18440 | tf_op jit(solution)/shard_map/ppermute | solution.py:23
  33.8 2.5 %copy-start.1 = (bf16[4,128,768]{2,1,0:T(8,128)(2,1)S(1)}, bf16[4,128,768]{2,1,0:T(8,128)(2,1)}, u32[]{:S(2)}) copy-start(bf16[4,128,768]{2,1,0:T(8,128)(2,1)} %fusion.2) | copy-start | bytes 2359300
  37.3 1.7 %copy-start = (f32[512,768]{1,0:T(8,128)}, f32[512,768]{1,0:T(8,128)S(1)}, u32[]{:S(2)}) copy-start(f32[512,768]{1,0:T(8,128)S(1)} %convert_reduce_fusion) | copy-start | bytes 4718596

commit v9 on v8

--- a/solution.py
+++ b/solution.py
@@ -65,30 +65,32 @@
     offset = lax.axis_index(("dp", "sub")) * own_count
     if dp_columns:
         dp_index, sub_index = lax.axis_index("dp"), lax.axis_index("sub")
-        slices = [
-            lax.dynamic_slice_in_dim(
-                centroids, ((dp_index + q) % sizes["dp"] * sizes["sub"] + sub_index) * own_count, own_count, 0
+        score_cents = [
+            lax.optimization_barrier(
+                normalize(
+                    lax.dynamic_slice_in_dim(
+                        centroids, ((dp_index + q) % sizes["dp"] * sizes["sub"] + sub_index) * own_count, own_count, 0
+                    )
+                ).astype(jnp.bfloat16)
             )
             for q in range(sizes["dp"])
         ]
-        score_cents = lax.optimization_barrier(normalize(jnp.concatenate(slices, axis=0)).astype(jnp.bfloat16))
-        own_cents = score_cents[:own_count]
     else:
         own_cents = normalize(lax.dynamic_slice_in_dim(centroids, offset, own_count, 0)).astype(jnp.bfloat16)
-        own_cents = lax.optimization_barrier(own_cents)
-        score_cents = own_cents
+        score_cents = [lax.optimization_barrier(own_cents)]
+    own_cents = score_cents[0]
 
-    scores = (
-        lax.dot_general(
-            unit_rows, score_cents, (((1,), (1,)), ((), ())), preferred_element_type=jnp.float32
-        )
+    score_blocks = [
+        lax.dot_general(unit_rows, cents, (((1,), (1,)), ((), ())), preferred_element_type=jnp.float32)
         * sharpness
-    )
+        for cents in score_cents
+    ]
+    scores = score_blocks[0]
     block_shape = (sizes["sub"], sizes["dp"], sizes["cent"], row_dev)
-    local_peak = jnp.max(scores, axis=1)
-    local_total = jnp.sum(jnp.exp(scores - local_peak[:, None]), axis=1)
-    if dp_columns:
-        scores = scores[:, :own_count]
+    local_peak = score_blocks[0].max(axis=1)
+    for block in score_blocks[1:]:
+        local_peak = jnp.maximum(local_peak, block.max(axis=1))
+    local_total = sum(jnp.sum(jnp.exp(block - local_peak[:, None]), axis=1) for block in score_blocks)
 
     own_cent = own_block("cent")
     known_weights = lax.dynamic_update_slice(

time: 39.3 us -> 37.6 us (0.957)
  local copies, waits for them, and re-layouts: 1.86 us -> 0.39 us
  waiting for transfers between devices: 10 us -> 8.74 us
  other arithmetic: 9.84 us -> 11 us
    dynamic_slice x1 -> x0, local copies, waits for them, and re-layouts: 1.47 us -> none  [shards(): lax.dynamic_slice_in_dim(centroids, ((dp_index + q) % sizes['dp'] * sizes...]
    reduce_sum x3, other arithmetic: 1.03 us -> 2.41 us  [normalize(): jnp.sum(floats * floats, axis=-1, keepdims=True) + 1e-06]
    convert_element_type x1, other arithmetic: 0.32 us -> 1.7 us  [shards(): score_cents = [lax.optimization_barrier(normalize(lax.dynamic_slice_in_di...]
    ppermute x9, waiting for transfers between devices: 10 us -> 8.74 us  [gather_stage(): lax.ppermute(value, name, [(j, (j + q) % size) for j in range(size)])]
    reduce_sum x1, other arithmetic: 1.51 us -> 0.28 us  [shards(): jnp.sum(grouped_resp.astype(jnp.float32), axis=1).astype(jnp.bfloat16)]
    dot_general x1 -> x2, matrix products: 2.37 us -> 2.27 us  [shards(): lax.dot_general(unit_rows, cents, (((1,), (1,)), ((), ())), preferred_ele...]
  transfers between devices with their start and end apart: 9 -> 9, of which waited for: 9 -> 9; matrix products, arithmetic and copies ran while one was open for 10% -> 14% of each run, Pallas kernels for 0% -> 0%
where the time goes in v9:
time: 37.6 us; the launch traced here: 37.3 us
  starting transfers between devices  12.4 us (33%)
  other arithmetic  11 us (29%)
  waiting for transfers between devices  8.74 us (23%)
  matrix products  3.29 us (9%)
  between operations  1.51 us (4%)
  local copies, waits for them, and re-layouts  0.39 us (1%)
    ppermute x9, starting transfers between devices, gather_stage(): lax.ppermute(value, name, [(j, (j + q) % size) for j in range(size)])  12.4 us
    ppermute x9, waiting for transfers between devices, gather_stage(): lax.ppermute(value, name, [(j, (j + q) % size) for j in range(size)])  8.74 us
    reduce_sum x3, other arithmetic, normalize(): jnp.sum(floats * floats, axis=-1, keepdims=True) + 1e-06  2.41 us
    dot_general x2, matrix products, shards(): lax.dot_general(unit_rows, cents, (((1,), (1,)), ((), ())), preferred_ele...  2.27 us
    convert_element_type x1, other arithmetic, shards(): score_cents = [lax.optimization_barrier(normalize(lax.dynamic_slice_in_di...  1.7 us
    reduce_sum x1, other arithmetic, shards(): jnp.sum(jnp.exp(block - local_peak[:, None]), axis=1)  1.67 us
    convert_element_type x1, other arithmetic, shards(): renormed = normalize(moved).astype(jnp.bfloat16)  1.25 us
    convert_element_type x2, other arithmetic, shards(): normalize(payload[:, :, :cent_rows].reshape(-1, width)).astype(jnp.bfloat16)  1.18 us
  transfers between devices with their start and end apart: 9, of which 9 were waited for; matrix products, arithmetic and copies ran while one was open for 14% of the time, Pallas kernels for 0%

profile of v9, /device:TPU:0, one launch (start us, length us, event | category | flops | bytes accessed | tf_op | source)
XLA Modules:
  0.0 37.3 jit_solution(11494495939024717036)
XLA Ops:
  0.6 3.1 %collective-permute-start = (bf16[32,768]{1,0:T(8,128)(2,1)}, bf16[32,768]{1,0:T(8,128)(2,1)S(1)}, u32[]{:S(2)}, u32[]{:S(2)}) collective-permute-start(bf16[32,768]{1,0:T(8,128)(2,1)} %param.4), channel_id=1, source_target_pairs={{0,4},{4,8},{8,12},{12,0},{1,5},{5,9},{9,13},{13,1},{2,6},{6,10},{... | collective-permute-start | bytes 147464 | tf_op jit(solution)/shard_map/ppermute | solution.py:23
  3.7 2.1 %collective-permute-start.2 = (bf16[32,768]{1,0:T(8,128)(2,1)}, bf16[32,768]{1,0:T(8,128)(2,1)S(1)}, u32[]{:S(2)}, u32[]{:S(2)}) collective-permute-start(bf16[32,768]{1,0:T(8,128)(2,1)} %param.4), channel_id=1, source_target_pairs={{0,12},{4,0},{8,4},{12,8},{1,13},{5,1},{9,5},{13,9},{2,14},{6,2},{... | collective-permute-start | bytes 147464 | tf_op jit(solution)/shard_map/ppermute | solution.py:23
  5.8 0.9 %collective-permute-start.1 = (bf16[32,768]{1,0:T(8,128)(2,1)}, bf16[32,768]{1,0:T(8,128)(2,1)S(1)}, u32[]{:S(2)}, u32[]{:S(2)}) collective-permute-start(bf16[32,768]{1,0:T(8,128)(2,1)} %param.4), channel_id=1, source_target_pairs={{0,8},{4,12},{8,0},{12,4},{1,9},{5,13},{9,1},{13,5},{2,10},{6,14},... | collective-permute-start | bytes 147464 | tf_op jit(solution)/shard_map/ppermute | solution.py:23
  6.7 0.7 %convert_bitcast_fusion = bf16[1,32]{1,0:T(2,128)(2,1)S(1)} fusion(s32[32]{0:T(128)} %param.5), kind=kLoop, calls=%fused_computation.75 | loop fusion | flops 32 | bytes 192 | tf_op jit(solution)/shard_map/broadcast_in_dim | solution.py:58
  7.4 0.7 %collective-permute-done = bf16[32,768]{1,0:T(8,128)(2,1)S(1)} collective-permute-done((bf16[32,768]{1,0:T(8,128)(2,1)}, bf16[32,768]{1,0:T(8,128)(2,1)S(1)}, u32[]{:S(2)}, u32[]{:S(2)}) %collective-permute-start) | collective-permute-done | bytes 49184 | tf_op jit(solution)/shard_map/ppermute | solution.py:23
  8.1 0.4 %collective-permute-done.2 = bf16[32,768]{1,0:T(8,128)(2,1)S(1)} collective-permute-done((bf16[32,768]{1,0:T(8,128)(2,1)}, bf16[32,768]{1,0:T(8,128)(2,1)S(1)}, u32[]{:S(2)}, u32[]{:S(2)}) %collective-permute-start.2) | collective-permute-done | bytes 49184 | tf_op jit(solution)/shard_map/ppermute | solution.py:23
  8.5 2.6 %collective-permute-done.1 = bf16[32,768]{1,0:T(8,128)(2,1)S(1)} collective-permute-done((bf16[32,768]{1,0:T(8,128)(2,1)}, bf16[32,768]{1,0:T(8,128)(2,1)S(1)}, u32[]{:S(2)}, u32[]{:S(2)}) %collective-permute-start.1) | collective-permute-done | bytes 49184 | tf_op jit(solution)/shard_map/ppermute | solution.py:23
  11.1 0.8 %pad_maximum_fusion.1 = bf16[4,32,768]{2,1,0:T(8,128)(2,1)S(1)} fusion(bf16[1,32,768]{2,1,0:T(8,128)(2,1)S(1)} %bitcast.105, bf16[1,32,768]{2,1,0:T(8,128)(2,1)S(1)} %bitcast.106, bf16[1,32,768]{2,1,0:T(8,128)(2,1)S(1)} %bitcast.104, bf16[1,32,768]{2,1,0:T(8,128)(2,1)} %bitcast.103), kind=kLoop, calls=%fused_computation.30 | loop fusion | flops 294912 | bytes 393216 | tf_op jit(solution)/shard_map/stack | solution.py:25
  12.0 1.6 %collective-permute-start.3 = (bf16[144,768]{1,0:T(8,128)(2,1)S(1)}, bf16[144,768]{1,0:T(8,128)(2,1)S(1)}, u32[]{:S(2)}, u32[]{:S(2)}) collective-permute-start(bf16[144,768]{1,0:T(8,128)(2,1)S(1)} %get-tuple-element.14), channel_id=1, source_target_pairs={{0,2},{2,0},{1,3},{3,1},{4,6},{6,4},{5,7},{7,5},{8,10},{10,8},{9,1... | collective-permute-start | bytes 663560 | tf_op jit(solution)/shard_map/ppermute | solution.py:23
  14.2 1.8 %fusion.2 = (f32[512]{0:T(512)S(1)}, f32[512]{0:T(512)S(1)}) fusion(bf16[2048,768]{1,0:T(8,128)(2,1)} %param.6, s32[]{:T(128)S(6)} %select_n.20, s32[]{:T(128)S(6)} %select_n.18), kind=kLoop, calls=%fused_computation.7 | loop fusion | flops 2358272 | bytes 1576968 | tf_op jit(solution)/shard_map/reduce_sum | solution.py:12
  16.0 2.2 %collective-permute-done.3 = bf16[144,768]{1,0:T(8,128)(2,1)S(1)} collective-permute-done((bf16[144,768]{1,0:T(8,128)(2,1)S(1)}, bf16[144,768]{1,0:T(8,128)(2,1)S(1)}, u32[]{:S(2)}, u32[]{:S(2)}) %collective-permute-start.3) | collective-permute-done | bytes 221216 | tf_op jit(solution)/shard_map/ppermute | solution.py:23
  18.2 0.1 pad_maximum_fusion
  18.2 0.1 collective-permute-start.4
  18.3 1.7 %fusion.3 = (bf16[512,768]{1,0:T(8,128)(2,1)S(1)}, bf16[512,768]{1,0:T(8,128)(2,1)S(1)}) fusion(f32[512]{0:T(512)S(1)} %get-tuple-element.27, bf16[2048,768]{1,0:T(8,128)(2,1)} %param.6, s32[]{:T(128)S(6)} %select_n.20, f32[512]{0:T(512)S(1)} %get-tuple-element.28, s32[]{:T(128)S(6)} %select_n.18), kind=kLoop, calls=%fused_computation.8 | loop fusion | flops 2359296 | bytes 3149832 | tf_op jit(solution)/shard_map/convert_element_type | solution.py:74
  20.0 0.1 collective-permute-done.4
  20.1 0.2 multiply_reduce_fusion.1
  20.3 0.1 fusion.7
  20.5 0.1 fusion.5
  20.6 1.6 %fusion.34 = (f32[512]{0:T(512)S(1)}, f32[512,512]{1,0:T(8,128)}) fusion(f32[]{:T(128)} %bitcast.94, bf16[512,768]{1,0:T(8,128)(2,1)S(1)} %fusion.5, bf16[512,768]{1,0:T(8,128)(2,1)S(1)} %get-tuple-element.9), kind=kOutput, calls=%fused_computation.84 | convolution fusion | flops 403176960 | bytes 2623492 | tf_op jit(solution)/shard_map/dot_general | solution.py:84
  22.2 0.7 %fusion.33 = (f32[512]{0:T(512)S(1)}, f32[512,512]{1,0:T(8,128)S(1)}) fusion(f32[]{:T(128)} %bitcast.92, bf16[512,768]{1,0:T(8,128)(2,1)S(1)} %fusion.5, bf16[512,768]{1,0:T(8,128)(2,1)S(1)} %get-tuple-element.10), kind=kOutput, calls=%fused_computation.83 | convolution fusion | flops 403176960 | bytes 2623492 | tf_op jit(solution)/shard_map/dot_general | solution.py:84
  22.9 0.1 max.18
  23.0 1.7 %exponential_reduce_fusion = (f32[512]{0:T(512)S(1)}, f32[512]{0:T(512)S(1)}) fusion(f32[512,512]{1,0:T(8,128)} %get-tuple-element.26, f32[512]{0:T(512)S(1)} %max.17, f32[512,512]{1,0:T(8,128)S(1)} %get-tuple-element.24), kind=kLoop, calls=%fused_computation.20 | loop fusion | flops 1047552 | bytes 2103296 | tf_op jit(solution)/shard_map/reduce_sum | solution.py:93
  24.7 0.1 add.108
  24.8 0.7 %collective-permute-start.6 = (f32[3,2,2,4,32]{4,3,2,1,0:T(4,128)S(1)}, f32[3,2,2,4,32]{4,3,2,1,0:T(4,128)S(1)}, u32[]{:S(2)}, u32[]{:S(2)}) collective-permute-start(f32[3,2,2,4,32]{4,3,2,1,0:T(4,128)S(1)} %get-tuple-element.20), channel_id=1, source_target_pairs={{0,8},{4,12},{8,0},{12,4},{1,9},{5,13},{9,1},{13,5},{2,10},{6,14},... | collective-permute-start | bytes 18440 | tf_op jit(solution)/shard_map/ppermute | solution.py:23
  25.5 2.7 %collective-permute-start.5 = (f32[3,2,2,4,32]{4,3,2,1,0:T(4,128)S(1)}, f32[3,2,2,4,32]{4,3,2,1,0:T(4,128)S(1)}, u32[]{:S(2)}, u32[]{:S(2)}) collective-permute-start(f32[3,2,2,4,32]{4,3,2,1,0:T(4,128)S(1)} %get-tuple-element.20), channel_id=1, source_target_pairs={{0,4},{4,8},{8,12},{12,0},{1,5},{5,9},{9,13},{13,1},{2,6},{6,10},{... | collective-permute-start | bytes 18440 | tf_op jit(solution)/shard_map/ppermute | solution.py:23
  28.2 1.1 %collective-permute-start.7 = (f32[3,2,2,4,32]{4,3,2,1,0:T(4,128)S(1)}, f32[3,2,2,4,32]{4,3,2,1,0:T(4,128)S(1)}, u32[]{:S(2)}, u32[]{:S(2)}) collective-permute-start(f32[3,2,2,4,32]{4,3,2,1,0:T(4,128)S(1)} %get-tuple-element.20), channel_id=1, source_target_pairs={{0,12},{4,0},{8,4},{12,8},{1,13},{5,1},{9,5},{13,9},{2,14},{6,2},{... | collective-permute-start | bytes 18440 | tf_op jit(solution)/shard_map/ppermute | solution.py:23
  29.3 0.5 %collective-permute-done.6 = f32[3,2,2,4,32]{4,3,2,1,0:T(4,128)S(1)} collective-permute-done((f32[3,2,2,4,32]{4,3,2,1,0:T(4,128)S(1)}, f32[3,2,2,4,32]{4,3,2,1,0:T(4,128)S(1)}, u32[]{:S(2)}, u32[]{:S(2)}) %collective-permute-start.6) | collective-permute-done | bytes 6176 | tf_op jit(solution)/shard_map/ppermute | solution.py:23
  29.9 1.3 %collective-permute-done.5 = f32[3,2,2,4,32]{4,3,2,1,0:T(4,128)S(1)} collective-permute-done((f32[3,2,2,4,32]{4,3,2,1,0:T(4,128)S(1)}, f32[3,2,2,4,32]{4,3,2,1,0:T(4,128)S(1)}, u32[]{:S(2)}, u32[]{:S(2)}) %collective-permute-start.5) | collective-permute-done | bytes 6176 | tf_op jit(solution)/shard_map/ppermute | solution.py:23
  31.2 0.8 %collective-permute-done.7 = f32[3,2,2,4,32]{4,3,2,1,0:T(4,128)S(1)} collective-permute-done((f32[3,2,2,4,32]{4,3,2,1,0:T(4,128)S(1)}, f32[3,2,2,4,32]{4,3,2,1,0:T(4,128)S(1)}, u32[]{:S(2)}, u32[]{:S(2)}) %collective-permute-start.7) | collective-permute-done | bytes 6176 | tf_op jit(solution)/shard_map/ppermute | solution.py:23
  32.0 0.0 copy-start.2
  32.2 0.1 collective-permute-start.8
  32.3 1.0 %fusion.4 = bf16[4,128,768]{2,1,0:T(8,128)(2,1)} fusion(f32[2,2,128,768]{3,2,1,0:T(8,128)S(1)} %fusion.7, f32[4,128]{1,0:T(4,128)S(1)} %bitcast.114), kind=kLoop, calls=%fused_computation.10 | loop fusion | flops 786432 | bytes 2361344 | tf_op jit(solution)/shard_map/convert_element_type | solution.py:62
  33.3 0.0 copy-start.1
  33.3 0.1 collective-permute-done.8
  33.5 0.1 mul.108
  33.6 0.1 add.110
  33.7 0.0 copy-done.2
  33.7 0.5 %fusion.26 = f32[32]{0:T(128)} fusion(f32[2,2,4,32]{3,2,1,0:T(4,128)S(1)} %bitcast.109, s32[32]{0:T(128)S(1)} %copy-done.2, f32[]{:T(128)} %bitcast.93), kind=kLoop, calls=%fused_computation.74 | loop fusion | flops 96 | bytes 388 | tf_op jit(solution)/shard_map/div | solution.py:118
  34.2 0.3 bitcast_reduce_fusion.2
  34.6 0.0 copy-done.1
  34.6 1.0 %convert_reduce_fusion = f32[512,768]{1,0:T(8,128)S(1)} fusion(bf16[4,128,512]{2,1,0:T(8,128)(2,1)S(1)} %bitcast.98, bf16[4,128,768]{2,1,0:T(8,128)(2,1)S(1)} %copy-done.1), kind=kOutput, calls=%fused_computation | convolution fusion | flops 406978560 | bytes 2883584 | tf_op jit(solution)/shard_map/dot_general | solution.py:107
  35.6 0.0 copy-start
  35.6 0.4 %multiply_reduce_fusion = f32[512]{0:T(512)S(1)} fusion(f32[512,768]{1,0:T(8,128)S(1)} %convert_reduce_fusion, f32[512]{0:T(512)S(1)} %broadcast_add_fusion, bf16[512,768]{1,0:T(8,128)(2,1)S(1)} %get-tuple-element.10), kind=kLoop, calls=%fused_computation.14 | loop fusion | flops 1965568 | bytes 2363392 | tf_op jit(solution)/shard_map/reduce_sum | solution.py:12
  36.1 1.3 %multiply_convert_fusion = bf16[512,768]{1,0:T(8,128)(2,1)} fusion(f32[512]{0:T(512)S(1)} %add_rsqrt_fusion, f32[512,768]{1,0:T(8,128)S(1)} %convert_reduce_fusion, f32[512]{0:T(512)S(1)} %broadcast_add_fusion, bf16[512,768]{1,0:T(8,128)(2,1)S(1)} %get-tuple-element.10), kind=kLoop, calls=%fused_computation.13 | loop fusion | flops 1966080 | bytes 3149824 | tf_op jit(solution)/shard_map/convert_element_type | solution.py:115
  37.3 0.0 copy-done
  (28 shorter events, 0.4 us)
Async XLA Ops:
  0.6 7.5 %collective-permute-start = (bf16[32,768]{1,0:T(8,128)(2,1)}, bf16[32,768]{1,0:T(8,128)(2,1)S(1)}, u32[]{:S(2)}, u32[]{:S(2)}) collective-permute-start(bf16[32,768]{1,0:T(8,128)(2,1)} %param.4), channel_id=1, source_target_pairs={{0,4},{4,8},{8,12},{12,0},{1,5},{5,9},{9,13},{13,1},{2,6},{6,10},{... | collective-permute-start | bytes 147464 | tf_op jit(solution)/shard_map/ppermute | solution.py:23
  3.7 4.8 %collective-permute-start.2 = (bf16[32,768]{1,0:T(8,128)(2,1)}, bf16[32,768]{1,0:T(8,128)(2,1)S(1)}, u32[]{:S(2)}, u32[]{:S(2)}) collective-permute-start(bf16[32,768]{1,0:T(8,128)(2,1)} %param.4), channel_id=1, source_target_pairs={{0,12},{4,0},{8,4},{12,8},{1,13},{5,1},{9,5},{13,9},{2,14},{6,2},{... | collective-permute-start | bytes 147464 | tf_op jit(solution)/shard_map/ppermute | solution.py:23
  5.8 5.3 %collective-permute-start.1 = (bf16[32,768]{1,0:T(8,128)(2,1)}, bf16[32,768]{1,0:T(8,128)(2,1)S(1)}, u32[]{:S(2)}, u32[]{:S(2)}) collective-permute-start(bf16[32,768]{1,0:T(8,128)(2,1)} %param.4), channel_id=1, source_target_pairs={{0,8},{4,12},{8,0},{12,4},{1,9},{5,13},{9,1},{13,5},{2,10},{6,14},... | collective-permute-start | bytes 147464 | tf_op jit(solution)/shard_map/ppermute | solution.py:23
  12.0 6.2 %collective-permute-start.3 = (bf16[144,768]{1,0:T(8,128)(2,1)S(1)}, bf16[144,768]{1,0:T(8,128)(2,1)S(1)}, u32[]{:S(2)}, u32[]{:S(2)}) collective-permute-start(bf16[144,768]{1,0:T(8,128)(2,1)S(1)} %get-tuple-element.14), channel_id=1, source_target_pairs={{0,2},{2,0},{1,3},{3,1},{4,6},{6,4},{5,7},{7,5},{8,10},{10,8},{9,1... | collective-permute-start | bytes 663560 | tf_op jit(solution)/shard_map/ppermute | solution.py:23
  18.2 1.9 %collective-permute-start.4 = (bf16[2,144,768]{2,1,0:T(8,128)(2,1)S(1)}, bf16[2,144,768]{2,1,0:T(8,128)(2,1)S(1)}, u32[]{:S(2)}, u32[]{:S(2)}) collective-permute-start(bf16[2,144,768]{2,1,0:T(8,128)(2,1)S(1)} %get-tuple-element.11), channel_id=1, source_target_pairs={{0,1},{1,0},{2,3},{3,2},{4,5},{5,4},{6,7},{7,6},{8,9},{9,8},{10,11... | collective-permute-start | bytes 1327112 | tf_op jit(solution)/shard_map/ppermute | solution.py:23
  24.8 5.1 %collective-permute-start.6 = (f32[3,2,2,4,32]{4,3,2,1,0:T(4,128)S(1)}, f32[3,2,2,4,32]{4,3,2,1,0:T(4,128)S(1)}, u32[]{:S(2)}, u32[]{:S(2)}) collective-permute-start(f32[3,2,2,4,32]{4,3,2,1,0:T(4,128)S(1)} %get-tuple-element.20), channel_id=1, source_target_pairs={{0,8},{4,12},{8,0},{12,4},{1,9},{5,13},{9,1},{13,5},{2,10},{6,14},... | collective-permute-start | bytes 18440 | tf_op jit(solution)/shard_map/ppermute | solution.py:23
  25.5 5.7 %collective-permute-start.5 = (f32[3,2,2,4,32]{4,3,2,1,0:T(4,128)S(1)}, f32[3,2,2,4,32]{4,3,2,1,0:T(4,128)S(1)}, u32[]{:S(2)}, u32[]{:S(2)}) collective-permute-start(f32[3,2,2,4,32]{4,3,2,1,0:T(4,128)S(1)} %get-tuple-element.20), channel_id=1, source_target_pairs={{0,4},{4,8},{8,12},{12,0},{1,5},{5,9},{9,13},{13,1},{2,6},{6,10},{... | collective-permute-start | bytes 18440 | tf_op jit(solution)/shard_map/ppermute | solution.py:23
  28.2 3.8 %collective-permute-start.7 = (f32[3,2,2,4,32]{4,3,2,1,0:T(4,128)S(1)}, f32[3,2,2,4,32]{4,3,2,1,0:T(4,128)S(1)}, u32[]{:S(2)}, u32[]{:S(2)}) collective-permute-start(f32[3,2,2,4,32]{4,3,2,1,0:T(4,128)S(1)} %get-tuple-element.20), channel_id=1, source_target_pairs={{0,12},{4,0},{8,4},{12,8},{1,13},{5,1},{9,5},{13,9},{2,14},{6,2},{... | collective-permute-start | bytes 18440 | tf_op jit(solution)/shard_map/ppermute | solution.py:23
  32.0 1.7 %copy-start.2 = (s32[32]{0:T(128)S(1)}, s32[32]{0:T(128)}, u32[]{:S(2)}) copy-start(s32[32]{0:T(128)} %param.5) | copy-start | bytes 388
  32.2 1.3 %collective-permute-start.8 = (f32[3,2,2,4,32]{4,3,2,1,0:T(4,128)S(1)}, f32[3,2,2,4,32]{4,3,2,1,0:T(4,128)S(1)}, u32[]{:S(2)}, u32[]{:S(2)}) collective-permute-start(f32[3,2,2,4,32]{4,3,2,1,0:T(4,128)S(1)} %get-tuple-element.16), channel_id=1, source_target_pairs={{0,1},{1,0},{2,3},{3,2},{4,5},{5,4},{6,7},{7,6},{8,9},{9,8},{10,11... | collective-permute-start | bytes 18440 | tf_op jit(solution)/shard_map/ppermute | solution.py:23
  33.3 1.3 %copy-start.1 = (bf16[4,128,768]{2,1,0:T(8,128)(2,1)S(1)}, bf16[4,128,768]{2,1,0:T(8,128)(2,1)}, u32[]{:S(2)}) copy-start(bf16[4,128,768]{2,1,0:T(8,128)(2,1)} %fusion.4) | copy-start | bytes 2359300
  35.6 1.7 %copy-start = (f32[512,768]{1,0:T(8,128)}, f32[512,768]{1,0:T(8,128)S(1)}, u32[]{:S(2)}) copy-start(f32[512,768]{1,0:T(8,128)S(1)} %convert_reduce_fusion) | copy-start | bytes 4718596

commit v10 on v9

--- a/solution.py
+++ b/solution.py
@@ -59,7 +59,9 @@
     payload = jnp.concatenate([blocks, weight_block], axis=0)
     for name in STAGES[1:]:
         payload = gather_stage(payload, name)
-    unit_rows = normalize(payload[:, :, :cent_rows].reshape(-1, width)).astype(jnp.bfloat16)
+    halves = [
+        normalize(payload[half, :, :cent_rows].reshape(-1, width)).astype(jnp.bfloat16) for half in range(sizes["sub"])
+    ]
     cent_weights = payload[:, :, cent_rows, :row_dev].astype(jnp.float32)
 
     offset = lax.axis_index(("dp", "sub")) * own_count
@@ -81,16 +83,22 @@
     own_cents = score_cents[0]
 
     score_blocks = [
-        lax.dot_general(unit_rows, cents, (((1,), (1,)), ((), ())), preferred_element_type=jnp.float32)
-        * sharpness
-        for cents in score_cents
+        [
+            lax.dot_general(rows, cents, (((1,), (1,)), ((), ())), preferred_element_type=jnp.float32) * sharpness
+            for cents in score_cents
+        ]
+        for rows in halves
     ]
-    scores = score_blocks[0]
     block_shape = (sizes["sub"], sizes["dp"], sizes["cent"], row_dev)
-    local_peak = score_blocks[0].max(axis=1)
-    for block in score_blocks[1:]:
-        local_peak = jnp.maximum(local_peak, block.max(axis=1))
-    local_total = sum(jnp.sum(jnp.exp(block - local_peak[:, None]), axis=1) for block in score_blocks)
+    peaks, totals = [], []
+    for blocks_of_half in score_blocks:
+        half_peak = blocks_of_half[0].max(axis=1)
+        for block in blocks_of_half[1:]:
+            half_peak = jnp.maximum(half_peak, block.max(axis=1))
+        peaks.append(half_peak)
+        totals.append(sum(jnp.sum(jnp.exp(block - half_peak[:, None]), axis=1) for block in blocks_of_half))
+    local_peak = jnp.concatenate(peaks)
+    local_total = jnp.concatenate(totals)
 
     own_cent = own_block("cent")
     known_weights = lax.dynamic_update_slice(
@@ -101,15 +109,22 @@
     weight_float = stats[2].reshape(-1)
     log_sum = (stats[0] + jnp.log(stats[1])).reshape(-1)
 
-    responsibility = (weight_float[:, None] * jnp.exp(scores - log_sum[:, None])).astype(jnp.bfloat16)
-    grouped_resp = responsibility.reshape(n_groups, -1, own_count)
-    grouped_rows = unit_rows.reshape(n_groups, -1, width)
-    partial_value = lax.dot_general(
-        grouped_resp, grouped_rows, (((1,), (1,)), ((0,), (0,))), preferred_element_type=jnp.float32
-    ).astype(jnp.bfloat16)
-    centroid_sums = jnp.sum(partial_value.astype(jnp.float32), axis=0)
-    weight_mass = jnp.sum(grouped_resp.astype(jnp.float32), axis=1).astype(jnp.bfloat16)
-    own_mass = jnp.sum(weight_mass.astype(jnp.float32), axis=0)
+    half_log_sum = log_sum.reshape(sizes["sub"], -1)
+    half_weight = weight_float.reshape(sizes["sub"], -1)
+    centroid_sums = jnp.zeros((own_count, width), jnp.float32)
+    own_mass = jnp.zeros((own_count,), jnp.float32)
+    for half, rows in enumerate(halves):
+        responsibility = (
+            half_weight[half][:, None] * jnp.exp(score_blocks[half][0] - half_log_sum[half][:, None])
+        ).astype(jnp.bfloat16)
+        grouped_resp = responsibility.reshape(sizes["dp"], -1, own_count)
+        grouped_rows = rows.reshape(sizes["dp"], -1, width)
+        partial_value = lax.dot_general(
+            grouped_resp, grouped_rows, (((1,), (1,)), ((0,), (0,))), preferred_element_type=jnp.float32
+        ).astype(jnp.bfloat16)
+        centroid_sums = centroid_sums + jnp.sum(partial_value.astype(jnp.float32), axis=0)
+        weight_mass = jnp.sum(grouped_resp.astype(jnp.float32), axis=1).astype(jnp.bfloat16)
+        own_mass = own_mass + jnp.sum(weight_mass.astype(jnp.float32), axis=0)
 
     moved = own_cents.astype(jnp.float32) + centroid_sums / (own_mass + 1.0)[:, None]
     renormed = normalize(moved).astype(jnp.bfloat16)

time: 37.6 us -> 34.9 us (0.928)
  other arithmetic: 11 us -> 7.94 us
    reduce_sum x2 -> x4, other arithmetic: 1.69 us -> 0.66 us  [the longest x2 0.62 us: shards(): jnp.sum(jnp.exp(block - half_peak[:, None]), axis=1)]
    convert_element_type x2, other arithmetic: 1.18 us -> 0.22 us  [shards(): normalize(payload[half, :, :cent_rows].reshape(-1, width))]
    another operation x3, other arithmetic: 0.91 us -> 0.12 us  [gather_stage(): return jnp.stack(parts)]
    broadcast_in_dim x1, other arithmetic: 0.66 us -> 0.01 us  [shards(): weights.astype(jnp.bfloat16)[None, :]]
    dot_general x2 -> x4, matrix products: 2.27 us -> 1.94 us  [shards(): lax.dot_general(rows, cents, (((1,), (1,)), ((), ())), preferred_element_...]
    dot_general x1 -> x2, matrix products: 1.02 us -> 1.3 us  [shards(): lax.dot_general(grouped_resp, grouped_rows, (((1,), (1,)), ((0,), (0,))),...]
    reduce_sum x3 -> x4, other arithmetic: 2.41 us -> 2.55 us  [normalize(): jnp.sum(floats * floats, axis=-1, keepdims=True) + 1e-06]
  transfers between devices with their start and end apart: 9 -> 9, of which waited for: 9 -> 7; matrix products, arithmetic and copies ran while one was open for 14% -> 14% of each run, Pallas kernels for 0% -> 0%
where the time goes in v10:
time: 34.9 us; the launch traced here: 34.7 us
  starting transfers between devices  12.4 us (36%)
  waiting for transfers between devices  9 us (26%)
  other arithmetic  7.94 us (23%)
  matrix products  3.24 us (9%)
  between operations  1.6 us (5%)
  local copies, waits for them, and re-layouts  0.55 us (2%)
    ppermute x9, starting transfers between devices, gather_stage(): lax.ppermute(value, name, [(j, (j + q) % size) for j in range(size)])  12.4 us
    ppermute x9, waiting for transfers between devices, gather_stage(): lax.ppermute(value, name, [(j, (j + q) % size) for j in range(size)])  9 us
    reduce_sum x4, other arithmetic, normalize(): jnp.sum(floats * floats, axis=-1, keepdims=True) + 1e-06  2.55 us
    dot_general x4, matrix products, shards(): lax.dot_general(rows, cents, (((1,), (1,)), ((), ())), preferred_element_...  1.94 us
    convert_element_type x1, other arithmetic, shards(): score_cents = [lax.optimization_barrier(normalize(lax.dynamic_slice_in_di...  1.69 us
    convert_element_type x1, other arithmetic, shards(): renormed = normalize(moved).astype(jnp.bfloat16)  1.38 us
    dot_general x2, matrix products, shards(): lax.dot_general(grouped_resp, grouped_rows, (((1,), (1,)), ((0,), (0,))),...  1.3 us
  transfers between devices with their start and end apart: 9, of which 7 were waited for; matrix products, arithmetic and copies ran while one was open for 14% of the time, Pallas kernels for 0%

profile of v10, /device:TPU:0, one launch (start us, length us, event | category | flops | bytes accessed | tf_op | source)
XLA Modules:
  0.0 34.7 jit_solution(1985019195054996596)
XLA Ops:
  0.6 0.0 copy-start.1
  0.6 3.1 %collective-permute-start = (bf16[32,768]{1,0:T(8,128)(2,1)}, bf16[32,768]{1,0:T(8,128)(2,1)S(1)}, u32[]{:S(2)}, u32[]{:S(2)}) collective-permute-start(bf16[32,768]{1,0:T(8,128)(2,1)} %param.4), channel_id=1, source_target_pairs={{0,4},{4,8},{8,12},{12,0},{1,5},{5,9},{9,13},{13,1},{2,6},{6,10},{... | collective-permute-start | bytes 147464 | tf_op jit(solution)/shard_map/ppermute | solution.py:23
  3.7 2.1 %collective-permute-start.2 = (bf16[32,768]{1,0:T(8,128)(2,1)}, bf16[32,768]{1,0:T(8,128)(2,1)S(1)}, u32[]{:S(2)}, u32[]{:S(2)}) collective-permute-start(bf16[32,768]{1,0:T(8,128)(2,1)} %param.4), channel_id=1, source_target_pairs={{0,12},{4,0},{8,4},{12,8},{1,13},{5,1},{9,5},{13,9},{2,14},{6,2},{... | collective-permute-start | bytes 147464 | tf_op jit(solution)/shard_map/ppermute | solution.py:23
  5.8 0.9 %collective-permute-start.1 = (bf16[32,768]{1,0:T(8,128)(2,1)}, bf16[32,768]{1,0:T(8,128)(2,1)S(1)}, u32[]{:S(2)}, u32[]{:S(2)}) collective-permute-start(bf16[32,768]{1,0:T(8,128)(2,1)} %param.4), channel_id=1, source_target_pairs={{0,8},{4,12},{8,0},{12,4},{1,9},{5,13},{9,1},{13,5},{2,10},{6,14},... | collective-permute-start | bytes 147464 | tf_op jit(solution)/shard_map/ppermute | solution.py:23
  6.8 1.7 %fusion.2 = (f32[512]{0:T(512)S(1)}, f32[512]{0:T(512)S(1)}) fusion(bf16[2048,768]{1,0:T(8,128)(2,1)} %param.6, s32[]{:T(128)S(6)} %select_n.20, s32[]{:T(128)S(6)} %select_n.18), kind=kLoop, calls=%fused_computation.10 | loop fusion | flops 2358272 | bytes 1576968 | tf_op jit(solution)/shard_map/reduce_sum | solution.py:12
  9.2 0.0 collective-permute-done
  9.2 0.0 collective-permute-done.2
  9.2 1.9 %collective-permute-done.1 = bf16[32,768]{1,0:T(8,128)(2,1)S(1)} collective-permute-done((bf16[32,768]{1,0:T(8,128)(2,1)}, bf16[32,768]{1,0:T(8,128)(2,1)S(1)}, u32[]{:S(2)}, u32[]{:S(2)}) %collective-permute-start.1) | collective-permute-done | bytes 49184 | tf_op jit(solution)/shard_map/ppermute | solution.py:23
  11.2 1.6 %collective-permute-start.3 = (bf16[144,768]{1,0:T(8,128)(2,1)S(1)}, bf16[144,768]{1,0:T(8,128)(2,1)S(1)}, u32[]{:S(2)}, u32[]{:S(2)}) collective-permute-start(bf16[144,768]{1,0:T(8,128)(2,1)S(1)} %get-tuple-element.20), channel_id=1, source_target_pairs={{0,2},{2,0},{1,3},{3,1},{4,6},{6,4},{5,7},{7,5},{8,10},{10,8},{9,1... | collective-permute-start | bytes 663560 | tf_op jit(solution)/shard_map/ppermute | solution.py:23
  12.8 1.7 %fusion.3 = (bf16[512,768]{1,0:T(8,128)(2,1)S(1)}, bf16[512,768]{1,0:T(8,128)(2,1)S(1)}) fusion(f32[512]{0:T(512)S(1)} %get-tuple-element.45, bf16[2048,768]{1,0:T(8,128)(2,1)} %param.6, s32[]{:T(128)S(6)} %select_n.20, f32[512]{0:T(512)S(1)} %get-tuple-element.46, s32[]{:T(128)S(6)} %select_n.18), kind=kLoop, calls=%fused_computation.11 | loop fusion | flops 2359296 | bytes 3149832 | tf_op jit(solution)/shard_map/convert_element_type | solution.py:76
  14.5 2.9 %collective-permute-done.3 = bf16[144,768]{1,0:T(8,128)(2,1)S(1)} collective-permute-done((bf16[144,768]{1,0:T(8,128)(2,1)S(1)}, bf16[144,768]{1,0:T(8,128)(2,1)S(1)}, u32[]{:S(2)}, u32[]{:S(2)}) %collective-permute-start.3) | collective-permute-done | bytes 221216 | tf_op jit(solution)/shard_map/ppermute | solution.py:23
  17.4 0.1 pad_maximum_fusion
  17.5 0.2 multiply_reduce_fusion.2
  17.6 0.1 slice_convert_fusion.1
  17.7 0.1 collective-permute-start.4
  17.8 0.1 fusion.7
  17.9 0.5 %fusion.44 = (f32[256]{0:T(256)S(1)}, f32[256,512]{1,0:T(8,128)S(1)}) fusion(f32[]{:T(128)} %bitcast.114, bf16[256,768]{1,0:T(8,128)(2,1)S(1)} %fusion.7, bf16[512,768]{1,0:T(8,128)(2,1)S(1)} %get-tuple-element.15), kind=kOutput, calls=%fused_computation.108 | convolution fusion | flops 201588480 | bytes 1704964 | tf_op jit(solution)/shard_map/dot_general | solution.py:87
  18.4 0.5 %fusion.43 = (f32[256]{0:T(256)S(1)}, f32[256,512]{1,0:T(8,128)S(1)}) fusion(f32[]{:T(128)} %bitcast.110, bf16[256,768]{1,0:T(8,128)(2,1)S(1)} %fusion.7, bf16[512,768]{1,0:T(8,128)(2,1)S(1)} %get-tuple-element.16), kind=kOutput, calls=%fused_computation.107 | convolution fusion | flops 201588480 | bytes 1704964 | tf_op jit(solution)/shard_map/dot_general | solution.py:87
  18.9 0.3 exponential_reduce_fusion.2
  19.2 0.4 %collective-permute-done.4 = bf16[2,144,768]{2,1,0:T(8,128)(2,1)S(1)} collective-permute-done((bf16[2,144,768]{2,1,0:T(8,128)(2,1)S(1)}, bf16[2,144,768]{2,1,0:T(8,128)(2,1)S(1)}, u32[]{:S(2)}, u32[]{:S(2)}) %collective-permute-start.4) | collective-permute-done | bytes 442400 | tf_op jit(solution)/shard_map/ppermute | solution.py:23
  19.5 0.2 multiply_reduce_fusion.1
  19.7 0.1 slice_convert_fusion
  19.8 0.1 fusion.6
  19.9 0.5 %fusion.42 = (f32[256]{0:T(256)S(1)}, f32[256,512]{1,0:T(8,128)S(1)}) fusion(f32[]{:T(128)} %bitcast.112, bf16[256,768]{1,0:T(8,128)(2,1)S(1)} %fusion.6, bf16[512,768]{1,0:T(8,128)(2,1)S(1)} %get-tuple-element.15), kind=kOutput, calls=%fused_computation.106 | convolution fusion | flops 201588480 | bytes 1704964 | tf_op jit(solution)/shard_map/dot_general | solution.py:87
  20.4 0.5 %fusion.41 = (f32[256]{0:T(256)S(1)}, f32[256,512]{1,0:T(8,128)S(1)}) fusion(f32[]{:T(128)} %bitcast.113, bf16[256,768]{1,0:T(8,128)(2,1)S(1)} %fusion.6, bf16[512,768]{1,0:T(8,128)(2,1)S(1)} %get-tuple-element.16), kind=kOutput, calls=%fused_computation.105 | convolution fusion | flops 201588480 | bytes 1704964 | tf_op jit(solution)/shard_map/dot_general | solution.py:87
  20.9 0.3 exponential_reduce_fusion
  21.2 0.1 stack_reshape.7
  21.3 0.1 stack_reshape.6
  21.4 0.7 %collective-permute-start.6 = (f32[3,2,2,4,32]{4,3,2,1,0:T(4,128)S(1)}, f32[3,2,2,4,32]{4,3,2,1,0:T(4,128)S(1)}, u32[]{:S(2)}, u32[]{:S(2)}) collective-permute-start(f32[3,2,2,4,32]{4,3,2,1,0:T(4,128)S(1)} %get-tuple-element.26), channel_id=1, source_target_pairs={{0,8},{4,12},{8,0},{12,4},{1,9},{5,13},{9,1},{13,5},{2,10},{6,14},... | collective-permute-start | bytes 18440 | tf_op jit(solution)/shard_map/ppermute | solution.py:23
  22.1 2.7 %collective-permute-start.5 = (f32[3,2,2,4,32]{4,3,2,1,0:T(4,128)S(1)}, f32[3,2,2,4,32]{4,3,2,1,0:T(4,128)S(1)}, u32[]{:S(2)}, u32[]{:S(2)}) collective-permute-start(f32[3,2,2,4,32]{4,3,2,1,0:T(4,128)S(1)} %get-tuple-element.26), channel_id=1, source_target_pairs={{0,4},{4,8},{8,12},{12,0},{1,5},{5,9},{9,13},{13,1},{2,6},{6,10},{... | collective-permute-start | bytes 18440 | tf_op jit(solution)/shard_map/ppermute | solution.py:23
  24.8 1.1 %collective-permute-start.7 = (f32[3,2,2,4,32]{4,3,2,1,0:T(4,128)S(1)}, f32[3,2,2,4,32]{4,3,2,1,0:T(4,128)S(1)}, u32[]{:S(2)}, u32[]{:S(2)}) collective-permute-start(f32[3,2,2,4,32]{4,3,2,1,0:T(4,128)S(1)} %get-tuple-element.26), channel_id=1, source_target_pairs={{0,12},{4,0},{8,4},{12,8},{1,13},{5,1},{9,5},{13,9},{2,14},{6,2},{... | collective-permute-start | bytes 18440 | tf_op jit(solution)/shard_map/ppermute | solution.py:23
  26.0 0.4 %collective-permute-done.6 = f32[3,2,2,4,32]{4,3,2,1,0:T(4,128)S(1)} collective-permute-done((f32[3,2,2,4,32]{4,3,2,1,0:T(4,128)S(1)}, f32[3,2,2,4,32]{4,3,2,1,0:T(4,128)S(1)}, u32[]{:S(2)}, u32[]{:S(2)}) %collective-permute-start.6) | collective-permute-done | bytes 6176 | tf_op jit(solution)/shard_map/ppermute | solution.py:23
  26.4 1.4 %collective-permute-done.5 = f32[3,2,2,4,32]{4,3,2,1,0:T(4,128)S(1)} collective-permute-done((f32[3,2,2,4,32]{4,3,2,1,0:T(4,128)S(1)}, f32[3,2,2,4,32]{4,3,2,1,0:T(4,128)S(1)}, u32[]{:S(2)}, u32[]{:S(2)}) %collective-permute-start.5) | collective-permute-done | bytes 6176 | tf_op jit(solution)/shard_map/ppermute | solution.py:23
  27.8 0.9 %collective-permute-done.7 = f32[3,2,2,4,32]{4,3,2,1,0:T(4,128)S(1)} collective-permute-done((f32[3,2,2,4,32]{4,3,2,1,0:T(4,128)S(1)}, f32[3,2,2,4,32]{4,3,2,1,0:T(4,128)S(1)}, u32[]{:S(2)}, u32[]{:S(2)}) %collective-permute-start.7) | collective-permute-done | bytes 6176 | tf_op jit(solution)/shard_map/ppermute | solution.py:23
  28.8 0.1 collective-permute-start.8
  28.9 1.2 %collective-permute-done.8 = f32[3,2,2,4,32]{4,3,2,1,0:T(4,128)S(1)} collective-permute-done((f32[3,2,2,4,32]{4,3,2,1,0:T(4,128)S(1)}, f32[3,2,2,4,32]{4,3,2,1,0:T(4,128)S(1)}, u32[]{:S(2)}, u32[]{:S(2)}) %collective-permute-start.8) | collective-permute-done | bytes 6176 | tf_op jit(solution)/shard_map/ppermute | solution.py:23
  30.2 0.5 %fusion.30 = f32[32]{0:T(128)} fusion(f32[2,2,4,32]{3,2,1,0:T(4,128)S(1)} %bitcast.131, s32[32]{0:T(128)S(1)} %copy-done.2, f32[]{:T(128)} %bitcast.111), kind=kLoop, calls=%fused_computation.91 | loop fusion | flops 96 | bytes 388 | tf_op jit(solution)/shard_map/div | solution.py:133
  30.7 0.1 sub.77
  30.8 0.1 mul.154
  30.9 0.2 bitcast_reduce_fusion.2
  31.1 0.1 mul.148
  31.2 0.1 sub.74
  31.3 0.2 bitcast_reduce_fusion.3
  31.5 0.6 %convert_reduce_fusion.1 = f32[512,768]{1,0:T(8,128)S(1)} fusion(bf16[2,128,512]{2,1,0:T(8,128)(2,1)S(1)} %bitcast.120, f32[2,128]{1,0:T(2,128)S(1)} %get-tuple-element.35, bf16[1,2,144,768]{3,2,1,0:T(8,128)(2,1)S(1)} %get-tuple-element.18), kind=kOutput, calls=%fused_computation.1 | convolution fusion | flops 203882496 | bytes 2229248 | tf_op jit(solution)/shard_map/dot_general | solution.py:122
  32.2 0.6 %convert_reduce_fusion = f32[512,768]{1,0:T(8,128)S(1)} fusion(bf16[2,128,512]{2,1,0:T(8,128)(2,1)S(1)} %bitcast.119, f32[2,128]{1,0:T(2,128)S(1)} %get-tuple-element.33, bf16[1,2,144,768]{3,2,1,0:T(8,128)(2,1)S(1)} %bitcast.118), kind=kOutput, calls=%fused_computation | convolution fusion | flops 203882496 | bytes 2229248 | tf_op jit(solution)/shard_map/dot_general | solution.py:122
  32.8 0.5 %multiply_reduce_fusion = (f32[512]{0:T(512)S(1)}, f32[512,768]{1,0:T(8,128)S(1)}) fusion(f32[512]{0:T(512)S(1)} %add_add_fusion, bf16[512,768]{1,0:T(8,128)(2,1)S(1)} %get-tuple-element.16, f32[512,768]{1,0:T(8,128)S(1)} %convert_reduce_fusion.1, f32[512,768]{1,0:T(8,128)S(1)} %convert_reduce_fusion), kind=kLoop, calls=%fused_computation.13 | loop fusion | flops 2358784 | bytes 5509120 | tf_op jit(solution)/shard_map/reduce_sum | solution.py:12
  33.3 1.4 %multiply_convert_fusion = bf16[512,768]{1,0:T(8,128)(2,1)} fusion(f32[512]{0:T(512)S(1)} %add_rsqrt_fusion, f32[512,768]{1,0:T(8,128)S(1)} %get-tuple-element.10, f32[512]{0:T(512)S(1)} %add_add_fusion, bf16[512,768]{1,0:T(8,128)(2,1)S(1)} %get-tuple-element.16), kind=kLoop, calls=%fused_computation.12 | loop fusion | flops 1966080 | bytes 3149824 | tf_op jit(solution)/shard_map/convert_element_type | solution.py:130
  34.7 0.0 copy-done
  (42 shorter events, 0.5 us)
Async XLA Ops:
  0.6 10.5 %copy-start.1 = (bf16[32,768]{1,0:T(8,128)(2,1)S(1)}, bf16[32,768]{1,0:T(8,128)(2,1)}, u32[]{:S(2)}) copy-start(bf16[32,768]{1,0:T(8,128)(2,1)} %param.4) | copy-start | bytes 147460
  0.6 7.9 %copy-start.2 = (s32[32]{0:T(128)S(1)}, s32[32]{0:T(128)}, u32[]{:S(2)}) copy-start(s32[32]{0:T(128)} %param.5) | copy-start | bytes 388
  0.6 8.6 %collective-permute-start = (bf16[32,768]{1,0:T(8,128)(2,1)}, bf16[32,768]{1,0:T(8,128)(2,1)S(1)}, u32[]{:S(2)}, u32[]{:S(2)}) collective-permute-start(bf16[32,768]{1,0:T(8,128)(2,1)} %param.4), channel_id=1, source_target_pairs={{0,4},{4,8},{8,12},{12,0},{1,5},{5,9},{9,13},{13,1},{2,6},{6,10},{... | collective-permute-start | bytes 147464 | tf_op jit(solution)/shard_map/ppermute | solution.py:23
  3.7 5.5 %collective-permute-start.2 = (bf16[32,768]{1,0:T(8,128)(2,1)}, bf16[32,768]{1,0:T(8,128)(2,1)S(1)}, u32[]{:S(2)}, u32[]{:S(2)}) collective-permute-start(bf16[32,768]{1,0:T(8,128)(2,1)} %param.4), channel_id=1, source_target_pairs={{0,12},{4,0},{8,4},{12,8},{1,13},{5,1},{9,5},{13,9},{2,14},{6,2},{... | collective-permute-start | bytes 147464 | tf_op jit(solution)/shard_map/ppermute | solution.py:23
  5.8 5.3 %collective-permute-start.1 = (bf16[32,768]{1,0:T(8,128)(2,1)}, bf16[32,768]{1,0:T(8,128)(2,1)S(1)}, u32[]{:S(2)}, u32[]{:S(2)}) collective-permute-start(bf16[32,768]{1,0:T(8,128)(2,1)} %param.4), channel_id=1, source_target_pairs={{0,8},{4,12},{8,0},{12,4},{1,9},{5,13},{9,1},{13,5},{2,10},{6,14},... | collective-permute-start | bytes 147464 | tf_op jit(solution)/shard_map/ppermute | solution.py:23
  11.2 6.2 %collective-permute-start.3 = (bf16[144,768]{1,0:T(8,128)(2,1)S(1)}, bf16[144,768]{1,0:T(8,128)(2,1)S(1)}, u32[]{:S(2)}, u32[]{:S(2)}) collective-permute-start(bf16[144,768]{1,0:T(8,128)(2,1)S(1)} %get-tuple-element.20), channel_id=1, source_target_pairs={{0,2},{2,0},{1,3},{3,1},{4,6},{6,4},{5,7},{7,5},{8,10},{10,8},{9,1... | collective-permute-start | bytes 663560 | tf_op jit(solution)/shard_map/ppermute | solution.py:23
  17.7 1.9 %collective-permute-start.4 = (bf16[2,144,768]{2,1,0:T(8,128)(2,1)S(1)}, bf16[2,144,768]{2,1,0:T(8,128)(2,1)S(1)}, u32[]{:S(2)}, u32[]{:S(2)}) collective-permute-start(bf16[2,144,768]{2,1,0:T(8,128)(2,1)S(1)} %get-tuple-element.17), channel_id=1, source_target_pairs={{0,1},{1,0},{2,3},{3,2},{4,5},{5,4},{6,7},{7,6},{8,9},{9,8},{10,11... | collective-permute-start | bytes 1327112 | tf_op jit(solution)/shard_map/ppermute | solution.py:23
  21.4 4.9 %collective-permute-start.6 = (f32[3,2,2,4,32]{4,3,2,1,0:T(4,128)S(1)}, f32[3,2,2,4,32]{4,3,2,1,0:T(4,128)S(1)}, u32[]{:S(2)}, u32[]{:S(2)}) collective-permute-start(f32[3,2,2,4,32]{4,3,2,1,0:T(4,128)S(1)} %get-tuple-element.26), channel_id=1, source_target_pairs={{0,8},{4,12},{8,0},{12,4},{1,9},{5,13},{9,1},{13,5},{2,10},{6,14},... | collective-permute-start | bytes 18440 | tf_op jit(solution)/shard_map/ppermute | solution.py:23
  22.1 5.6 %collective-permute-start.5 = (f32[3,2,2,4,32]{4,3,2,1,0:T(4,128)S(1)}, f32[3,2,2,4,32]{4,3,2,1,0:T(4,128)S(1)}, u32[]{:S(2)}, u32[]{:S(2)}) collective-permute-start(f32[3,2,2,4,32]{4,3,2,1,0:T(4,128)S(1)} %get-tuple-element.26), channel_id=1, source_target_pairs={{0,4},{4,8},{8,12},{12,0},{1,5},{5,9},{9,13},{13,1},{2,6},{6,10},{... | collective-permute-start | bytes 18440 | tf_op jit(solution)/shard_map/ppermute | solution.py:23
  24.8 3.8 %collective-permute-start.7 = (f32[3,2,2,4,32]{4,3,2,1,0:T(4,128)S(1)}, f32[3,2,2,4,32]{4,3,2,1,0:T(4,128)S(1)}, u32[]{:S(2)}, u32[]{:S(2)}) collective-permute-start(f32[3,2,2,4,32]{4,3,2,1,0:T(4,128)S(1)} %get-tuple-element.26), channel_id=1, source_target_pairs={{0,12},{4,0},{8,4},{12,8},{1,13},{5,1},{9,5},{13,9},{2,14},{6,2},{... | collective-permute-start | bytes 18440 | tf_op jit(solution)/shard_map/ppermute | solution.py:23
  28.8 1.3 %collective-permute-start.8 = (f32[3,2,2,4,32]{4,3,2,1,0:T(4,128)S(1)}, f32[3,2,2,4,32]{4,3,2,1,0:T(4,128)S(1)}, u32[]{:S(2)}, u32[]{:S(2)}) collective-permute-start(f32[3,2,2,4,32]{4,3,2,1,0:T(4,128)S(1)} %get-tuple-element.22), channel_id=1, source_target_pairs={{0,1},{1,0},{2,3},{3,2},{4,5},{5,4},{6,7},{7,6},{8,9},{9,8},{10,11... | collective-permute-start | bytes 18440 | tf_op jit(solution)/shard_map/ppermute | solution.py:23
  33.3 1.4 %copy-start = (f32[512,768]{1,0:T(8,128)}, f32[512,768]{1,0:T(8,128)S(1)}, u32[]{:S(2)}) copy-start(f32[512,768]{1,0:T(8,128)S(1)} %get-tuple-element.10) | copy-start | bytes 4718596

commit v11 on v10

--- a/solution.py
+++ b/solution.py
@@ -1,4 +1,5 @@
 import jax
+import numpy as np
 import jax.numpy as jnp
 from jax import lax
 from jax.sharding import PartitionSpec as P
@@ -16,14 +17,26 @@
     return lax.axis_size(name) <= SHIFT_MAX
 
 
+def partner(index, step, size):
+    if size & (size - 1):
+        return (index + step) % size
+    return index ^ step
+
+
 def gather_stage(value, name):
     size = lax.axis_size(name)
     if relative(name):
         parts = [value] + [
-            lax.ppermute(value, name, [(j, (j + q) % size) for j in range(size)]) for q in range(1, size)
+            lax.ppermute(value, name, [(j, partner(j, q, size)) for j in range(size)]) for q in range(1, size)
         ]
         return jnp.stack(parts)
     return lax.all_gather(value, name, axis=0)
+
+
+def align(received, step, size, axis):
+    if size & (size - 1):
+        return jnp.roll(received, step, axis=axis)
+    return jnp.take(received, np.array([p ^ step for p in range(size)]), axis=axis)
 
 
 def own_block(name):
@@ -35,7 +48,7 @@
         size = lax.axis_size(name)
         stacked = gather_stage(stats, name)
         if relative(name):
-            stacked = jnp.stack([jnp.roll(stacked[q], q, axis=block_axis[name]) for q in range(size)])
+            stacked = jnp.stack([align(stacked[q], q, size, block_axis[name]) for q in range(size)])
         peaks, totals = stacked[:, 0], stacked[:, 1]
         row_peak = jnp.max(peaks, axis=0)
         row_total = jnp.sum(totals * jnp.exp(peaks - row_peak[None]), axis=0)
@@ -129,8 +142,8 @@
     moved = own_cents.astype(jnp.float32) + centroid_sums / (own_mass + 1.0)[:, None]
     renormed = normalize(moved).astype(jnp.bfloat16)
 
-    own_log_sum = log_sum.reshape(block_shape)[own_block("sub"), own_block("dp"), own_cent]
-    objective = weights.astype(jnp.float32) * own_log_sum / sharpness
+    own_rows = (own_block("sub"), own_block("dp"), own_cent)
+    objective = (weight_float.reshape(block_shape)[own_rows] * log_sum.reshape(block_shape)[own_rows]) / sharpness
     return (centroid_sums, renormed, objective)
 
 

time: 34.9 us -> 45.3 us (1.30)
  other arithmetic: 7.94 us -> 16.1 us
  local copies, waits for them, and re-layouts: 0.55 us -> 4.96 us
  waiting for transfers between devices: 9 us -> 7.29 us
  starting transfers between devices: 12.4 us -> 11.8 us
    gather x0 -> x6, local copies, waits for them, and re-layouts: none -> 3.49 us  [align(): jnp.take(received, np.array([p ^ step for p in range(size)]), axis=axis)]
    another operation x3 -> x4, other arithmetic: 0.12 us -> 2.84 us  [gather_stage(): return jnp.stack(parts)]
    gather x0 -> x6, other arithmetic: none -> 2 us
    ppermute x9, waiting for transfers between devices: 9 us -> 7.29 us  [gather_stage(): lax.ppermute(value, name, [(j, partner(j, q, size)) for j in range(size)])]
    convert_element_type x2 -> x4, other arithmetic: 0.22 us -> 1.74 us  [shards(): normalize(payload[half, :, :cent_rows].reshape(-1, width))]
    another operation x0 -> x4, local copies, waits for them, and re-layouts: none -> 0.69 us  [the longest x2 0.68 us: gather_stage(): return jnp.stack(parts)]
    broadcast_in_dim x1, other arithmetic: 0.01 us -> 0.66 us  [shards(): weights.astype(jnp.bfloat16)[None, :]]
    reduce_sum x4, other arithmetic: 2.55 us -> 3.19 us  [normalize(): jnp.sum(floats * floats, axis=-1, keepdims=True) + 1e-06]
  transfers between devices with their start and end apart: 9 -> 9, of which waited for: 7 -> 5; matrix products, arithmetic and copies ran while one was open for 14% -> 24% of each run, Pallas kernels for 0% -> 0%
where the time goes in v11:
time: 45.3 us; the launch traced here: 45 us
  other arithmetic  16.1 us (36%)
  starting transfers between devices  11.8 us (26%)
  waiting for transfers between devices  7.29 us (16%)
  local copies, waits for them, and re-layouts  4.96 us (11%)
  matrix products  3.17 us (7%)
  between operations  1.68 us (4%)
    ppermute x9, starting transfers between devices, gather_stage(): lax.ppermute(value, name, [(j, partner(j, q, size)) for j in range(size)])  11.8 us
    ppermute x9, waiting for transfers between devices, gather_stage(): lax.ppermute(value, name, [(j, partner(j, q, size)) for j in range(size)])  7.29 us
    gather x6, local copies, waits for them, and re-layouts, align(): jnp.take(received, np.array([p ^ step for p in range(size)]), axis=axis)  3.49 us
    reduce_sum x4, other arithmetic, normalize(): jnp.sum(floats * floats, axis=-1, keepdims=True) + 1e-06  3.19 us
    another operation x4, other arithmetic, gather_stage(): return jnp.stack(parts)  2.84 us
    gather x6, other arithmetic  2 us
    dot_general x4, matrix products, shards(): lax.dot_general(rows, cents, (((1,), (1,)), ((), ())), preferred_element_...  1.94 us
    convert_element_type x4, other arithmetic, shards(): normalize(payload[half, :, :cent_rows].reshape(-1, width))  1.74 us
  transfers between devices with their start and end apart: 9, of which 5 were waited for; matrix products, arithmetic and copies ran while one was open for 24% of the time, Pallas kernels for 0%

profile of v11, /device:TPU:0, one launch (start us, length us, event | category | flops | bytes accessed | tf_op | source)
XLA Modules:
  0.0 45.0 jit_solution(17912078901306499104)
XLA Ops:
  0.6 3.1 %collective-permute-start = (bf16[32,768]{1,0:T(8,128)(2,1)}, bf16[32,768]{1,0:T(8,128)(2,1)S(1)}, u32[]{:S(2)}, u32[]{:S(2)}) collective-permute-start(bf16[32,768]{1,0:T(8,128)(2,1)} %param.14), channel_id=1, source_target_pairs={{0,4},{4,0},{8,12},{12,8},{1,5},{5,1},{9,13},{13,9},{2,6},{6,2},{1... | collective-permute-start | bytes 147464 | tf_op jit(solution)/shard_map/ppermute | solution.py:30
  3.7 2.5 %collective-permute-start.2 = (bf16[32,768]{1,0:T(8,128)(2,1)}, bf16[32,768]{1,0:T(8,128)(2,1)S(1)}, u32[]{:S(2)}, u32[]{:S(2)}) collective-permute-start(bf16[32,768]{1,0:T(8,128)(2,1)} %param.14), channel_id=1, source_target_pairs={{0,12},{4,8},{8,4},{12,0},{1,13},{5,9},{9,5},{13,1},{2,14},{6,10},... | collective-permute-start | bytes 147464 | tf_op jit(solution)/shard_map/ppermute | solution.py:30
  6.2 0.1 collective-permute-start.1
  6.3 0.7 %convert_bitcast_fusion = bf16[1,32]{1,0:T(2,128)(2,1)S(1)} fusion(s32[32]{0:T(128)} %param.15), kind=kLoop, calls=%fused_computation.105 | loop fusion | flops 32 | bytes 192 | tf_op jit(solution)/shard_map/broadcast_in_dim | solution.py:71
  7.0 0.7 %pad_clamp_fusion.4 = s32[1024]{0:T(1024)S(1)} fusion(s32[4]{0:T(128)} %constant.120), kind=kLoop, calls=%fused_computation.91 | loop fusion | flops 1024 | bytes 4112 | tf_op gather
  7.7 0.7 %pad_clamp_fusion.3 = s32[1024]{0:T(1024)S(1)} fusion(s32[4]{0:T(128)} %constant.121), kind=kLoop, calls=%fused_computation.90 | loop fusion | flops 1024 | bytes 4112 | tf_op gather
  8.3 0.7 %pad_clamp_fusion.2 = s32[1024]{0:T(1024)S(1)} fusion(s32[4]{0:T(128)} %constant.122), kind=kLoop, calls=%fused_computation.89 | loop fusion | flops 1024 | bytes 4112 | tf_op gather
  9.0 1.7 %fusion.2 = (f32[512]{0:T(512)S(1)}, f32[512]{0:T(512)S(1)}) fusion(bf16[2048,768]{1,0:T(8,128)(2,1)} %param.16, s32[]{:T(128)S(6)} %select_n.34, s32[]{:T(128)S(6)} %select_n.32), kind=kLoop, calls=%fused_computation.16 | loop fusion | flops 2358272 | bytes 1576968 | tf_op jit(solution)/shard_map/reduce_sum | solution.py:13
  10.8 1.7 %fusion.3 = (bf16[512,768]{1,0:T(8,128)(2,1)S(1)}, bf16[512,768]{1,0:T(8,128)(2,1)S(1)}) fusion(f32[512]{0:T(512)S(1)} %get-tuple-element.33, bf16[2048,768]{1,0:T(8,128)(2,1)} %param.16, s32[]{:T(128)S(6)} %select_n.34, f32[512]{0:T(512)S(1)} %get-tuple-element.34, s32[]{:T(128)S(6)} %select_n.32), kind=kLoop, calls=%fused_computation.17 | loop fusion | flops 2359296 | bytes 3149832 | tf_op jit(solution)/shard_map/convert_element_type | solution.py:89
  13.3 1.6 %collective-permute-start.3 = (bf16[144,768]{1,0:T(8,128)(2,1)S(1)}, bf16[144,768]{1,0:T(8,128)(2,1)S(1)}, u32[]{:S(2)}, u32[]{:S(2)}) collective-permute-start(bf16[144,768]{1,0:T(8,128)(2,1)S(1)} %get-tuple-element.20), channel_id=1, source_target_pairs={{0,2},{2,0},{1,3},{3,1},{4,6},{6,4},{5,7},{7,5},{8,10},{10,8},{9,1... | collective-permute-start | bytes 663560 | tf_op jit(solution)/shard_map/ppermute | solution.py:30
  14.8 0.3 copy.141
  15.2 4.8 %collective-permute-done.3 = bf16[144,768]{1,0:T(8,128)(2,1)S(1)} collective-permute-done((bf16[144,768]{1,0:T(8,128)(2,1)S(1)}, bf16[144,768]{1,0:T(8,128)(2,1)S(1)}, u32[]{:S(2)}, u32[]{:S(2)}) %collective-permute-start.3) | collective-permute-done | bytes 221216 | tf_op jit(solution)/shard_map/ppermute | solution.py:30
  19.9 0.3 copy.142
  20.3 1.0 %fusion.45 = bf16[1,2,144,768]{3,1,2,0:T(2,128)(2,1)S(1)} fusion(bf16[1,144,768]{2,0,1:T(2,128)(2,1)S(1)} %copy.142, bf16[1,144,768]{2,0,1:T(2,128)(2,1)S(1)} %copy.141), kind=kLoop, calls=%fused_computation.118 | loop fusion | flops 884736 | bytes 884736 | tf_op jit(solution)/shard_map/stack | solution.py:32
  21.3 1.8 %pad_maximum_fusion = bf16[2,144,768]{2,0,1:T(2,128)(2,1)} fusion(bf16[1,144,768]{2,0,1:T(2,128)(2,1)S(1)} %copy.142, bf16[1,144,768]{2,0,1:T(2,128)(2,1)S(1)} %copy.141), kind=kLoop, calls=%fused_computation.42 | loop fusion | flops 884736 | bytes 884736 | tf_op jit(solution)/shard_map/stack | solution.py:32
  23.1 0.5 %multiply_reduce_fusion.2 = f32[2,128]{0,1:T(8,128)S(1)} fusion(bf16[1,2,144,768]{3,1,2,0:T(2,128)(2,1)S(1)} %fusion.45), kind=kLoop, calls=%fused_computation.34 | loop fusion | flops 589568 | bytes 394240 | tf_op jit(solution)/shard_map/reduce_sum | solution.py:13
  23.5 0.3 slice_convert_fusion.1
  24.1 0.5 %fusion.34 = (f32[256]{0:T(256)S(1)}, f32[256,512]{1,0:T(8,128)S(1)}) fusion(f32[]{:T(128)} %bitcast.120, bf16[256,768]{1,0:T(8,128)(2,1)S(1)} %fusion.7, bf16[512,768]{1,0:T(8,128)(2,1)S(1)} %get-tuple-element.17), kind=kOutput, calls=%fused_computation.117 | convolution fusion | flops 201588480 | bytes 1704964 | tf_op jit(solution)/shard_map/dot_general | solution.py:100
  24.6 0.5 %fusion.33 = (f32[256]{0:T(256)S(1)}, f32[256,512]{1,0:T(8,128)S(1)}) fusion(f32[]{:T(128)} %bitcast.116, bf16[256,768]{1,0:T(8,128)(2,1)S(1)} %fusion.7, bf16[512,768]{1,0:T(8,128)(2,1)S(1)} %get-tuple-element.18), kind=kOutput, calls=%fused_computation.116 | convolution fusion | flops 201588480 | bytes 1704964 | tf_op jit(solution)/shard_map/dot_general | solution.py:100
  25.1 0.3 exponential_reduce_fusion.2
  25.4 0.4 fusion.5
  25.8 0.1 collective-permute-done.4
  25.9 0.5 %multiply_reduce_fusion.1 = f32[2,128]{0,1:T(8,128)S(1)} fusion(bf16[1,2,144,768]{3,1,2,0:T(2,128)(2,1)S(1)} %bitcast.122), kind=kLoop, calls=%fused_computation.33 | loop fusion | flops 589568 | bytes 394240 | tf_op jit(solution)/shard_map/reduce_sum | solution.py:13
  26.5 1.1 %fusion.4 = bf16[2,128,768]{2,0,1:T(2,128)(2,1)} fusion(f32[2,128]{0,1:T(8,128)S(1)} %add_rsqrt_fusion, bf16[1,2,144,768]{3,1,2,0:T(2,128)(2,1)S(1)} %bitcast.123), kind=kLoop, calls=%fused_computation.26 | loop fusion | flops 589824 | bytes 787456 | tf_op jit(solution)/shard_map/convert_element_type | solution.py:76
  27.7 0.3 slice_convert_fusion
  28.0 0.1 fusion.6
  28.1 0.5 %fusion.32 = (f32[256]{0:T(256)S(1)}, f32[256,512]{1,0:T(8,128)S(1)}) fusion(f32[]{:T(128)} %bitcast.118, bf16[256,768]{1,0:T(8,128)(2,1)S(1)} %fusion.6, bf16[512,768]{1,0:T(8,128)(2,1)S(1)} %get-tuple-element.17), kind=kOutput, calls=%fused_computation.115 | convolution fusion | flops 201588480 | bytes 1704964 | tf_op jit(solution)/shard_map/dot_general | solution.py:100
  28.6 0.5 %fusion.31 = (f32[256]{0:T(256)S(1)}, f32[256,512]{1,0:T(8,128)S(1)}) fusion(f32[]{:T(128)} %bitcast.119, bf16[256,768]{1,0:T(8,128)(2,1)S(1)} %fusion.6, bf16[512,768]{1,0:T(8,128)(2,1)S(1)} %get-tuple-element.18), kind=kOutput, calls=%fused_computation.114 | convolution fusion | flops 201588480 | bytes 1704964 | tf_op jit(solution)/shard_map/dot_general | solution.py:100
  29.1 0.3 exponential_reduce_fusion
  29.6 2.7 %collective-permute-start.7 = (f32[3,2,2,4,32]{4,2,3,1,0:T(2,128)S(1)}, f32[3,2,2,4,32]{4,2,3,1,0:T(2,128)S(1)}, u32[]{:S(2)}, u32[]{:S(2)}) collective-permute-start(f32[3,2,2,4,32]{4,2,3,1,0:T(2,128)S(1)} %pad_maximum_fusion.3), channel_id=1, source_target_pairs={{0,12},{4,8},{8,4},{12,0},{1,13},{5,9},{9,5},{13,1},{2,14},{6,10},... | collective-permute-start | bytes 18440 | tf_op jit(solution)/shard_map/ppermute | solution.py:30
  32.4 0.3 collective-permute-start.6
  32.7 1.4 %collective-permute-start.5 = (f32[3,2,2,4,32]{4,2,3,1,0:T(2,128)S(1)}, f32[3,2,2,4,32]{4,2,3,1,0:T(2,128)S(1)}, u32[]{:S(2)}, u32[]{:S(2)}) collective-permute-start(f32[3,2,2,4,32]{4,2,3,1,0:T(2,128)S(1)} %pad_maximum_fusion.3), channel_id=1, source_target_pairs={{0,4},{4,0},{8,12},{12,8},{1,5},{5,1},{9,13},{13,9},{2,6},{6,2},{1... | collective-permute-start | bytes 18440 | tf_op jit(solution)/shard_map/ppermute | solution.py:30
  34.1 0.6 %gather_fusion = f32[4,3,2,2,32]{4,3,2,1,0:T(2,128)S(1)} fusion(f32[3,2,2,4,32]{4,2,3,1,0:T(2,128)S(1)} %pad_maximum_fusion.3, s32[1024]{0:T(1024)S(1)} %pad_clamp_fusion.5), kind=kCustom, calls=%fused_computation.clone | custom fusion | bytes 12304 | tf_op jit(solution)/shard_map/jit(_take)/gather | solution.py:39
  34.8 0.6 %collective-permute-done.7 = f32[3,2,2,4,32]{4,2,3,1,0:T(2,128)S(1)} collective-permute-done((f32[3,2,2,4,32]{4,2,3,1,0:T(2,128)S(1)}, f32[3,2,2,4,32]{4,2,3,1,0:T(2,128)S(1)}, u32[]{:S(2)}, u32[]{:S(2)}) %collective-permute-start.7) | collective-permute-done | bytes 6176 | tf_op jit(solution)/shard_map/ppermute | solution.py:30
  35.4 0.6 %gather_fusion.3 = f32[4,3,2,2,32]{4,3,2,1,0:T(2,128)S(1)} fusion(f32[3,2,2,4,32]{4,2,3,1,0:T(2,128)S(1)} %collective-permute-done.7, s32[1024]{0:T(1024)S(1)} %pad_clamp_fusion.2), kind=kCustom, calls=%fused_computation.4.clone | custom fusion | bytes 12304 | tf_op jit(solution)/shard_map/jit(_take)/gather | solution.py:39
  36.0 1.3 %collective-permute-done.6 = f32[3,2,2,4,32]{4,2,3,1,0:T(2,128)S(1)} collective-permute-done((f32[3,2,2,4,32]{4,2,3,1,0:T(2,128)S(1)}, f32[3,2,2,4,32]{4,2,3,1,0:T(2,128)S(1)}, u32[]{:S(2)}, u32[]{:S(2)}) %collective-permute-start.6) | collective-permute-done | bytes 6176 | tf_op jit(solution)/shard_map/ppermute | solution.py:30
  37.2 0.6 %gather_fusion.2 = f32[4,3,2,2,32]{4,3,2,1,0:T(2,128)S(1)} fusion(f32[3,2,2,4,32]{4,2,3,1,0:T(2,128)S(1)} %collective-permute-done.6, s32[1024]{0:T(1024)S(1)} %pad_clamp_fusion.3), kind=kCustom, calls=%fused_computation.3.clone | custom fusion | bytes 12304 | tf_op jit(solution)/shard_map/jit(_take)/gather | solution.py:39
  37.8 0.6 %gather_fusion.1 = f32[4,3,2,2,32]{4,3,2,1,0:T(2,128)S(1)} fusion(f32[3,2,2,4,32]{4,2,3,1,0:T(2,128)S(1)} %collective-permute-done.5, s32[1024]{0:T(1024)S(1)} %pad_clamp_fusion.4), kind=kCustom, calls=%fused_computation.2.clone | custom fusion | bytes 12304 | tf_op jit(solution)/shard_map/jit(_take)/gather | solution.py:39
  38.7 0.6 %gather_fusion.4 = f32[2,3,2,4,32]{4,3,2,1,0:T(4,128)S(1)} fusion(f32[3,2,2,4,32]{4,3,2,1,0:T(4,128)S(1)} %pad_maximum_fusion.4, s32[1024]{0:T(1024)S(1)} %pad_clamp_fusion.1), kind=kCustom, calls=%fused_computation.1.clone | custom fusion | bytes 12296 | tf_op jit(solution)/shard_map/jit(_take)/gather | solution.py:39
  39.4 0.5 %collective-permute-done.8 = f32[3,2,2,4,32]{4,3,2,1,0:T(4,128)S(1)} collective-permute-done((f32[3,2,2,4,32]{4,3,2,1,0:T(4,128)S(1)}, f32[3,2,2,4,32]{4,3,2,1,0:T(4,128)S(1)}, u32[]{:S(2)}, u32[]{:S(2)}) %collective-permute-start.8) | collective-permute-done | bytes 6176 | tf_op jit(solution)/shard_map/ppermute | solution.py:30
  39.9 0.6 %gather_fusion.5 = f32[2,3,2,4,32]{4,3,2,1,0:T(4,128)S(1)} fusion(f32[3,2,2,4,32]{4,3,2,1,0:T(4,128)S(1)} %collective-permute-done.8, s32[1024]{0:T(1024)S(1)} %pad_clamp_fusion), kind=kCustom, calls=%fused_computation.5.clone | custom fusion | bytes 12296 | tf_op jit(solution)/shard_map/jit(_take)/gather | solution.py:39
  40.6 0.5 %fusion.27 = f32[32]{0:T(128)} fusion(f32[2,2,4,32]{3,1,2,0:T(2,128)S(1)} %fusion.24, f32[2,2,4,32]{3,2,1,0:T(4,128)S(1)} %fusion.17, f32[]{:T(128)} %bitcast.117), kind=kLoop, calls=%fused_computation.106 | loop fusion | flops 64 | bytes 388 | tf_op jit(solution)/shard_map/div | solution.py:146
  41.3 0.2 bitcast_reduce_fusion.2
  41.7 0.2 bitcast_reduce_fusion.3
  41.9 0.6 %convert_reduce_fusion.1 = f32[512,768]{1,0:T(8,128)S(1)} fusion(bf16[2,128,512]{2,1,0:T(8,128)(2,1)S(1)} %bitcast.126, bf16[2,128,768]{2,0,1:T(2,128)(2,1)S(1)} %fusion.5), kind=kOutput, calls=%fused_computation.7 | convolution fusion | flops 203292672 | bytes 2228224 | tf_op jit(solution)/shard_map/dot_general | solution.py:135
  42.5 0.6 %convert_reduce_fusion = f32[512,768]{1,0:T(8,128)S(1)} fusion(bf16[2,128,512]{2,1,0:T(8,128)(2,1)S(1)} %bitcast.125, bf16[2,128,768]{2,0,1:T(2,128)(2,1)S(1)} %copy-done.1), kind=kOutput, calls=%fused_computation.6 | convolution fusion | flops 203292672 | bytes 2228224 | tf_op jit(solution)/shard_map/dot_general | solution.py:135
  43.1 0.5 %multiply_reduce_fusion = (f32[512]{0:T(512)S(1)}, f32[512,768]{1,0:T(8,128)S(1)}) fusion(f32[512]{0:T(512)S(1)} %add_add_fusion, bf16[512,768]{1,0:T(8,128)(2,1)S(1)} %get-tuple-element.18, f32[512,768]{1,0:T(8,128)S(1)} %convert_reduce_fusion.1, f32[512,768]{1,0:T(8,128)S(1)} %convert_reduce_fusion), kind=kLoop, calls=%fused_computation.19 | loop fusion | flops 2358784 | bytes 5509120 | tf_op jit(solution)/shard_map/reduce_sum | solution.py:13
  43.6 1.4 %multiply_convert_fusion = bf16[512,768]{1,0:T(8,128)(2,1)} fusion(f32[512]{0:T(512)S(1)} %add_rsqrt_fusion.2, f32[512,768]{1,0:T(8,128)S(1)} %get-tuple-element.12, f32[512]{0:T(512)S(1)} %add_add_fusion, bf16[512,768]{1,0:T(8,128)(2,1)S(1)} %get-tuple-element.18), kind=kLoop, calls=%fused_computation.18 | loop fusion | flops 1966080 | bytes 3149824 | tf_op jit(solution)/shard_map/convert_element_type | solution.py:143
  (69 shorter events, 1.6 us)
Async XLA Ops:
  0.6 12.5 %collective-permute-start = (bf16[32,768]{1,0:T(8,128)(2,1)}, bf16[32,768]{1,0:T(8,128)(2,1)S(1)}, u32[]{:S(2)}, u32[]{:S(2)}) collective-permute-start(bf16[32,768]{1,0:T(8,128)(2,1)} %param.14), channel_id=1, source_target_pairs={{0,4},{4,0},{8,12},{12,8},{1,5},{5,1},{9,13},{13,9},{2,6},{6,2},{1... | collective-permute-start | bytes 147464 | tf_op jit(solution)/shard_map/ppermute | solution.py:30
  3.7 9.4 %collective-permute-start.2 = (bf16[32,768]{1,0:T(8,128)(2,1)}, bf16[32,768]{1,0:T(8,128)(2,1)S(1)}, u32[]{:S(2)}, u32[]{:S(2)}) collective-permute-start(bf16[32,768]{1,0:T(8,128)(2,1)} %param.14), channel_id=1, source_target_pairs={{0,12},{4,8},{8,4},{12,0},{1,13},{5,9},{9,5},{13,1},{2,14},{6,10},... | collective-permute-start | bytes 147464 | tf_op jit(solution)/shard_map/ppermute | solution.py:30
  6.2 7.0 %collective-permute-start.1 = (bf16[32,768]{1,0:T(8,128)(2,1)}, bf16[32,768]{1,0:T(8,128)(2,1)S(1)}, u32[]{:S(2)}, u32[]{:S(2)}) collective-permute-start(bf16[32,768]{1,0:T(8,128)(2,1)} %param.14), channel_id=1, source_target_pairs={{0,8},{4,12},{8,0},{12,4},{1,9},{5,13},{9,1},{13,5},{2,10},{6,14},... | collective-permute-start | bytes 147464 | tf_op jit(solution)/shard_map/ppermute | solution.py:30
  10.8 2.4 %copy-start.2 = (bf16[32,768]{1,0:T(8,128)(2,1)S(1)}, bf16[32,768]{1,0:T(8,128)(2,1)}, u32[]{:S(2)}) copy-start(bf16[32,768]{1,0:T(8,128)(2,1)} %param.14) | copy-start | bytes 147460
  10.8 4.1 %copy-start.3 = (s32[2]{0:T(128)S(1)}, s32[2]{0:T(128)}, u32[]{:S(2)}) copy-start(s32[2]{0:T(128)} %constant.123) | copy-start | bytes 28
  13.3 6.7 %collective-permute-start.3 = (bf16[144,768]{1,0:T(8,128)(2,1)S(1)}, bf16[144,768]{1,0:T(8,128)(2,1)S(1)}, u32[]{:S(2)}, u32[]{:S(2)}) collective-permute-start(bf16[144,768]{1,0:T(8,128)(2,1)S(1)} %get-tuple-element.20), channel_id=1, source_target_pairs={{0,2},{2,0},{1,3},{3,1},{4,6},{6,4},{5,7},{7,5},{8,10},{10,8},{9,1... | collective-permute-start | bytes 663560 | tf_op jit(solution)/shard_map/ppermute | solution.py:30
  23.9 2.0 %collective-permute-start.4 = (bf16[2,144,768]{2,0,1:T(2,128)(2,1)}, bf16[2,144,768]{2,0,1:T(2,128)(2,1)S(1)}, u32[]{:S(2)}, u32[]{:S(2)}) collective-permute-start(bf16[2,144,768]{2,0,1:T(2,128)(2,1)} %pad_maximum_fusion), channel_id=1, source_target_pairs={{0,1},{1,0},{2,3},{3,2},{4,5},{5,4},{6,7},{7,6},{8,9},{9,8},{10,11... | collective-permute-start | bytes 1327112 | tf_op jit(solution)/shard_map/ppermute | solution.py:30
  29.6 5.7 %collective-permute-start.7 = (f32[3,2,2,4,32]{4,2,3,1,0:T(2,128)S(1)}, f32[3,2,2,4,32]{4,2,3,1,0:T(2,128)S(1)}, u32[]{:S(2)}, u32[]{:S(2)}) collective-permute-start(f32[3,2,2,4,32]{4,2,3,1,0:T(2,128)S(1)} %pad_maximum_fusion.3), channel_id=1, source_target_pairs={{0,12},{4,8},{8,4},{12,0},{1,13},{5,9},{9,5},{13,1},{2,14},{6,10},... | collective-permute-start | bytes 18440 | tf_op jit(solution)/shard_map/ppermute | solution.py:30
  32.4 4.9 %collective-permute-start.6 = (f32[3,2,2,4,32]{4,2,3,1,0:T(2,128)S(1)}, f32[3,2,2,4,32]{4,2,3,1,0:T(2,128)S(1)}, u32[]{:S(2)}, u32[]{:S(2)}) collective-permute-start(f32[3,2,2,4,32]{4,2,3,1,0:T(2,128)S(1)} %pad_maximum_fusion.3), channel_id=1, source_target_pairs={{0,8},{4,12},{8,0},{12,4},{1,9},{5,13},{9,1},{13,5},{2,10},{6,14},... | collective-permute-start | bytes 18440 | tf_op jit(solution)/shard_map/ppermute | solution.py:30
  32.7 5.1 %collective-permute-start.5 = (f32[3,2,2,4,32]{4,2,3,1,0:T(2,128)S(1)}, f32[3,2,2,4,32]{4,2,3,1,0:T(2,128)S(1)}, u32[]{:S(2)}, u32[]{:S(2)}) collective-permute-start(f32[3,2,2,4,32]{4,2,3,1,0:T(2,128)S(1)} %pad_maximum_fusion.3), channel_id=1, source_target_pairs={{0,4},{4,0},{8,12},{12,8},{1,5},{5,1},{9,13},{13,9},{2,6},{6,2},{1... | collective-permute-start | bytes 18440 | tf_op jit(solution)/shard_map/ppermute | solution.py:30
  38.6 1.3 %collective-permute-start.8 = (f32[3,2,2,4,32]{4,3,2,1,0:T(4,128)S(1)}, f32[3,2,2,4,32]{4,3,2,1,0:T(4,128)S(1)}, u32[]{:S(2)}, u32[]{:S(2)}) collective-permute-start(f32[3,2,2,4,32]{4,3,2,1,0:T(4,128)S(1)} %pad_maximum_fusion.4), channel_id=1, source_target_pairs={{0,1},{1,0},{2,3},{3,2},{4,5},{5,4},{6,7},{7,6},{8,9},{9,8},{10,11... | collective-permute-start | bytes 18440 | tf_op jit(solution)/shard_map/ppermute | solution.py:30
  41.5 1.0 %copy-start.1 = (bf16[2,128,768]{2,0,1:T(2,128)(2,1)S(1)}, bf16[2,128,768]{2,0,1:T(2,128)(2,1)}, u32[]{:S(2)}) copy-start(bf16[2,128,768]{2,0,1:T(2,128)(2,1)} %fusion.4) | copy-start | bytes 1179652
  43.6 1.4 %copy-start = (f32[512,768]{1,0:T(8,128)}, f32[512,768]{1,0:T(8,128)S(1)}, u32[]{:S(2)}) copy-start(f32[512,768]{1,0:T(8,128)S(1)} %get-tuple-element.12) | copy-start | bytes 4718596

commit v12 on v10

--- a/solution.py
+++ b/solution.py
@@ -129,8 +129,8 @@
     moved = own_cents.astype(jnp.float32) + centroid_sums / (own_mass + 1.0)[:, None]
     renormed = normalize(moved).astype(jnp.bfloat16)
 
-    own_log_sum = log_sum.reshape(block_shape)[own_block("sub"), own_block("dp"), own_cent]
-    objective = weights.astype(jnp.float32) * own_log_sum / sharpness
+    own_rows = (own_block("sub"), own_block("dp"), own_cent)
+    objective = (weight_float.reshape(block_shape)[own_rows] * log_sum.reshape(block_shape)[own_rows]) / sharpness
     return (centroid_sums, renormed, objective)
 
 

time: 34.9 us -> 34.9 us (level)
  no operation moved by 1% of the time
where the time goes in v12:
time: 34.9 us; the launch traced here: 34.7 us
  starting transfers between devices  12.4 us (36%)
  waiting for transfers between devices  9 us (26%)
  other arithmetic  7.94 us (23%)
  matrix products  3.23 us (9%)
  between operations  1.61 us (5%)
  local copies, waits for them, and re-layouts  0.55 us (2%)
    ppermute x9, starting transfers between devices, gather_stage(): lax.ppermute(value, name, [(j, (j + q) % size) for j in range(size)])  12.4 us
    ppermute x9, waiting for transfers between devices, gather_stage(): lax.ppermute(value, name, [(j, (j + q) % size) for j in range(size)])  9 us
    reduce_sum x4, other arithmetic, normalize(): jnp.sum(floats * floats, axis=-1, keepdims=True) + 1e-06  2.55 us
    dot_general x4, matrix products, shards(): lax.dot_general(rows, cents, (((1,), (1,)), ((), ())), preferred_element_...  1.94 us
    convert_element_type x1, other arithmetic, shards(): score_cents = [lax.optimization_barrier(normalize(lax.dynamic_slice_in_di...  1.69 us
    convert_element_type x1, other arithmetic, shards(): renormed = normalize(moved).astype(jnp.bfloat16)  1.38 us
    dot_general x2, matrix products, shards(): lax.dot_general(grouped_resp, grouped_rows, (((1,), (1,)), ((0,), (0,))),...  1.29 us
  transfers between devices with their start and end apart: 9, of which 7 were waited for; matrix products, arithmetic and copies ran while one was open for 14% of the time, Pallas kernels for 0%

profile of v12, /device:TPU:0, one launch (start us, length us, event | category | flops | bytes accessed | tf_op | source)
XLA Modules:
  0.0 34.7 jit_solution(3033888001144939252)
XLA Ops:
  0.6 0.0 copy-start.1
  0.6 0.0 copy-start.2
  0.6 3.1 %collective-permute-start = (bf16[32,768]{1,0:T(8,128)(2,1)}, bf16[32,768]{1,0:T(8,128)(2,1)S(1)}, u32[]{:S(2)}, u32[]{:S(2)}) collective-permute-start(bf16[32,768]{1,0:T(8,128)(2,1)} %param.4), channel_id=1, source_target_pairs={{0,4},{4,8},{8,12},{12,0},{1,5},{5,9},{9,13},{13,1},{2,6},{6,10},{... | collective-permute-start | bytes 147464 | tf_op jit(solution)/shard_map/ppermute | solution.py:23
  3.7 2.1 %collective-permute-start.2 = (bf16[32,768]{1,0:T(8,128)(2,1)}, bf16[32,768]{1,0:T(8,128)(2,1)S(1)}, u32[]{:S(2)}, u32[]{:S(2)}) collective-permute-start(bf16[32,768]{1,0:T(8,128)(2,1)} %param.4), channel_id=1, source_target_pairs={{0,12},{4,0},{8,4},{12,8},{1,13},{5,1},{9,5},{13,9},{2,14},{6,2},{... | collective-permute-start | bytes 147464 | tf_op jit(solution)/shard_map/ppermute | solution.py:23
  5.8 0.9 %collective-permute-start.1 = (bf16[32,768]{1,0:T(8,128)(2,1)}, bf16[32,768]{1,0:T(8,128)(2,1)S(1)}, u32[]{:S(2)}, u32[]{:S(2)}) collective-permute-start(bf16[32,768]{1,0:T(8,128)(2,1)} %param.4), channel_id=1, source_target_pairs={{0,8},{4,12},{8,0},{12,4},{1,9},{5,13},{9,1},{13,5},{2,10},{6,14},... | collective-permute-start | bytes 147464 | tf_op jit(solution)/shard_map/ppermute | solution.py:23
  6.8 1.7 %fusion.2 = (f32[512]{0:T(512)S(1)}, f32[512]{0:T(512)S(1)}) fusion(bf16[2048,768]{1,0:T(8,128)(2,1)} %param.6, s32[]{:T(128)S(6)} %select_n.20, s32[]{:T(128)S(6)} %select_n.18), kind=kLoop, calls=%fused_computation.10 | loop fusion | flops 2358272 | bytes 1576968 | tf_op jit(solution)/shard_map/reduce_sum | solution.py:12
  9.2 0.0 collective-permute-done
  9.2 0.0 collective-permute-done.2
  9.2 1.9 %collective-permute-done.1 = bf16[32,768]{1,0:T(8,128)(2,1)S(1)} collective-permute-done((bf16[32,768]{1,0:T(8,128)(2,1)}, bf16[32,768]{1,0:T(8,128)(2,1)S(1)}, u32[]{:S(2)}, u32[]{:S(2)}) %collective-permute-start.1) | collective-permute-done | bytes 49184 | tf_op jit(solution)/shard_map/ppermute | solution.py:23
  11.2 1.6 %collective-permute-start.3 = (bf16[144,768]{1,0:T(8,128)(2,1)S(1)}, bf16[144,768]{1,0:T(8,128)(2,1)S(1)}, u32[]{:S(2)}, u32[]{:S(2)}) collective-permute-start(bf16[144,768]{1,0:T(8,128)(2,1)S(1)} %get-tuple-element.20), channel_id=1, source_target_pairs={{0,2},{2,0},{1,3},{3,1},{4,6},{6,4},{5,7},{7,5},{8,10},{10,8},{9,1... | collective-permute-start | bytes 663560 | tf_op jit(solution)/shard_map/ppermute | solution.py:23
  12.8 1.7 %fusion.3 = (bf16[512,768]{1,0:T(8,128)(2,1)S(1)}, bf16[512,768]{1,0:T(8,128)(2,1)S(1)}) fusion(f32[512]{0:T(512)S(1)} %get-tuple-element.45, bf16[2048,768]{1,0:T(8,128)(2,1)} %param.6, s32[]{:T(128)S(6)} %select_n.20, f32[512]{0:T(512)S(1)} %get-tuple-element.46, s32[]{:T(128)S(6)} %select_n.18), kind=kLoop, calls=%fused_computation.11 | loop fusion | flops 2359296 | bytes 3149832 | tf_op jit(solution)/shard_map/convert_element_type | solution.py:76
  14.5 2.9 %collective-permute-done.3 = bf16[144,768]{1,0:T(8,128)(2,1)S(1)} collective-permute-done((bf16[144,768]{1,0:T(8,128)(2,1)S(1)}, bf16[144,768]{1,0:T(8,128)(2,1)S(1)}, u32[]{:S(2)}, u32[]{:S(2)}) %collective-permute-start.3) | collective-permute-done | bytes 221216 | tf_op jit(solution)/shard_map/ppermute | solution.py:23
  17.4 0.1 pad_maximum_fusion
  17.5 0.2 multiply_reduce_fusion.2
  17.6 0.1 slice_convert_fusion.1
  17.7 0.1 collective-permute-start.4
  17.8 0.1 fusion.7
  17.9 0.5 %fusion.44 = (f32[256]{0:T(256)S(1)}, f32[256,512]{1,0:T(8,128)S(1)}) fusion(f32[]{:T(128)} %bitcast.110, bf16[256,768]{1,0:T(8,128)(2,1)S(1)} %fusion.7, bf16[512,768]{1,0:T(8,128)(2,1)S(1)} %get-tuple-element.15), kind=kOutput, calls=%fused_computation.108 | convolution fusion | flops 201588480 | bytes 1704964 | tf_op jit(solution)/shard_map/dot_general | solution.py:87
  18.4 0.5 %fusion.43 = (f32[256]{0:T(256)S(1)}, f32[256,512]{1,0:T(8,128)S(1)}) fusion(f32[]{:T(128)} %bitcast.106, bf16[256,768]{1,0:T(8,128)(2,1)S(1)} %fusion.7, bf16[512,768]{1,0:T(8,128)(2,1)S(1)} %get-tuple-element.16), kind=kOutput, calls=%fused_computation.107 | convolution fusion | flops 201588480 | bytes 1704964 | tf_op jit(solution)/shard_map/dot_general | solution.py:87
  18.9 0.3 exponential_reduce_fusion.2
  19.2 0.4 %collective-permute-done.4 = bf16[2,144,768]{2,1,0:T(8,128)(2,1)S(1)} collective-permute-done((bf16[2,144,768]{2,1,0:T(8,128)(2,1)S(1)}, bf16[2,144,768]{2,1,0:T(8,128)(2,1)S(1)}, u32[]{:S(2)}, u32[]{:S(2)}) %collective-permute-start.4) | collective-permute-done | bytes 442400 | tf_op jit(solution)/shard_map/ppermute | solution.py:23
  19.5 0.2 multiply_reduce_fusion.1
  19.7 0.1 slice_convert_fusion
  19.8 0.1 fusion.6
  19.9 0.5 %fusion.42 = (f32[256]{0:T(256)S(1)}, f32[256,512]{1,0:T(8,128)S(1)}) fusion(f32[]{:T(128)} %bitcast.108, bf16[256,768]{1,0:T(8,128)(2,1)S(1)} %fusion.6, bf16[512,768]{1,0:T(8,128)(2,1)S(1)} %get-tuple-element.15), kind=kOutput, calls=%fused_computation.106 | convolution fusion | flops 201588480 | bytes 1704964 | tf_op jit(solution)/shard_map/dot_general | solution.py:87
  20.4 0.5 %fusion.41 = (f32[256]{0:T(256)S(1)}, f32[256,512]{1,0:T(8,128)S(1)}) fusion(f32[]{:T(128)} %bitcast.109, bf16[256,768]{1,0:T(8,128)(2,1)S(1)} %fusion.6, bf16[512,768]{1,0:T(8,128)(2,1)S(1)} %get-tuple-element.16), kind=kOutput, calls=%fused_computation.105 | convolution fusion | flops 201588480 | bytes 1704964 | tf_op jit(solution)/shard_map/dot_general | solution.py:87
  20.9 0.3 exponential_reduce_fusion
  21.2 0.1 stack_reshape.7
  21.3 0.1 stack_reshape.6
  21.4 0.7 %collective-permute-start.6 = (f32[3,2,2,4,32]{4,3,2,1,0:T(4,128)S(1)}, f32[3,2,2,4,32]{4,3,2,1,0:T(4,128)S(1)}, u32[]{:S(2)}, u32[]{:S(2)}) collective-permute-start(f32[3,2,2,4,32]{4,3,2,1,0:T(4,128)S(1)} %get-tuple-element.26), channel_id=1, source_target_pairs={{0,8},{4,12},{8,0},{12,4},{1,9},{5,13},{9,1},{13,5},{2,10},{6,14},... | collective-permute-start | bytes 18440 | tf_op jit(solution)/shard_map/ppermute | solution.py:23
  22.1 2.7 %collective-permute-start.5 = (f32[3,2,2,4,32]{4,3,2,1,0:T(4,128)S(1)}, f32[3,2,2,4,32]{4,3,2,1,0:T(4,128)S(1)}, u32[]{:S(2)}, u32[]{:S(2)}) collective-permute-start(f32[3,2,2,4,32]{4,3,2,1,0:T(4,128)S(1)} %get-tuple-element.26), channel_id=1, source_target_pairs={{0,4},{4,8},{8,12},{12,0},{1,5},{5,9},{9,13},{13,1},{2,6},{6,10},{... | collective-permute-start | bytes 18440 | tf_op jit(solution)/shard_map/ppermute | solution.py:23
  24.8 1.1 %collective-permute-start.7 = (f32[3,2,2,4,32]{4,3,2,1,0:T(4,128)S(1)}, f32[3,2,2,4,32]{4,3,2,1,0:T(4,128)S(1)}, u32[]{:S(2)}, u32[]{:S(2)}) collective-permute-start(f32[3,2,2,4,32]{4,3,2,1,0:T(4,128)S(1)} %get-tuple-element.26), channel_id=1, source_target_pairs={{0,12},{4,0},{8,4},{12,8},{1,13},{5,1},{9,5},{13,9},{2,14},{6,2},{... | collective-permute-start | bytes 18440 | tf_op jit(solution)/shard_map/ppermute | solution.py:23
  26.0 0.4 %collective-permute-done.6 = f32[3,2,2,4,32]{4,3,2,1,0:T(4,128)S(1)} collective-permute-done((f32[3,2,2,4,32]{4,3,2,1,0:T(4,128)S(1)}, f32[3,2,2,4,32]{4,3,2,1,0:T(4,128)S(1)}, u32[]{:S(2)}, u32[]{:S(2)}) %collective-permute-start.6) | collective-permute-done | bytes 6176 | tf_op jit(solution)/shard_map/ppermute | solution.py:23
  26.4 1.4 %collective-permute-done.5 = f32[3,2,2,4,32]{4,3,2,1,0:T(4,128)S(1)} collective-permute-done((f32[3,2,2,4,32]{4,3,2,1,0:T(4,128)S(1)}, f32[3,2,2,4,32]{4,3,2,1,0:T(4,128)S(1)}, u32[]{:S(2)}, u32[]{:S(2)}) %collective-permute-start.5) | collective-permute-done | bytes 6176 | tf_op jit(solution)/shard_map/ppermute | solution.py:23
  27.8 0.9 %collective-permute-done.7 = f32[3,2,2,4,32]{4,3,2,1,0:T(4,128)S(1)} collective-permute-done((f32[3,2,2,4,32]{4,3,2,1,0:T(4,128)S(1)}, f32[3,2,2,4,32]{4,3,2,1,0:T(4,128)S(1)}, u32[]{:S(2)}, u32[]{:S(2)}) %collective-permute-start.7) | collective-permute-done | bytes 6176 | tf_op jit(solution)/shard_map/ppermute | solution.py:23
  28.8 0.1 collective-permute-start.8
  28.9 1.2 %collective-permute-done.8 = f32[3,2,2,4,32]{4,3,2,1,0:T(4,128)S(1)} collective-permute-done((f32[3,2,2,4,32]{4,3,2,1,0:T(4,128)S(1)}, f32[3,2,2,4,32]{4,3,2,1,0:T(4,128)S(1)}, u32[]{:S(2)}, u32[]{:S(2)}) %collective-permute-start.8) | collective-permute-done | bytes 6176 | tf_op jit(solution)/shard_map/ppermute | solution.py:23
  30.2 0.5 %fusion.30 = f32[32]{0:T(128)} fusion(f32[2,2,4,32]{3,2,1,0:T(4,128)S(1)} %bitcast.127, f32[2,2,4,32]{3,2,1,0:T(4,128)S(1)} %fusion.19, f32[]{:T(128)} %bitcast.107), kind=kLoop, calls=%fused_computation.92 | loop fusion | flops 64 | bytes 388 | tf_op jit(solution)/shard_map/div | solution.py:133
  30.7 0.1 mul.155
  30.8 0.1 sub.77
  30.9 0.2 bitcast_reduce_fusion.2
  31.1 0.1 sub.74
  31.2 0.1 mul.149
  31.3 0.2 bitcast_reduce_fusion.3
  31.5 0.6 %convert_reduce_fusion.1 = f32[512,768]{1,0:T(8,128)S(1)} fusion(bf16[2,128,512]{2,1,0:T(8,128)(2,1)S(1)} %bitcast.116, f32[2,128]{1,0:T(2,128)S(1)} %get-tuple-element.35, bf16[1,2,144,768]{3,2,1,0:T(8,128)(2,1)S(1)} %get-tuple-element.18), kind=kOutput, calls=%fused_computation.1 | convolution fusion | flops 203882496 | bytes 2229248 | tf_op jit(solution)/shard_map/dot_general | solution.py:122
  32.2 0.6 %convert_reduce_fusion = f32[512,768]{1,0:T(8,128)S(1)} fusion(bf16[2,128,512]{2,1,0:T(8,128)(2,1)S(1)} %bitcast.115, f32[2,128]{1,0:T(2,128)S(1)} %get-tuple-element.33, bf16[1,2,144,768]{3,2,1,0:T(8,128)(2,1)S(1)} %bitcast.114), kind=kOutput, calls=%fused_computation | convolution fusion | flops 203882496 | bytes 2229248 | tf_op jit(solution)/shard_map/dot_general | solution.py:122
  32.8 0.5 %multiply_reduce_fusion = (f32[512]{0:T(512)S(1)}, f32[512,768]{1,0:T(8,128)S(1)}) fusion(f32[512]{0:T(512)S(1)} %add_add_fusion, bf16[512,768]{1,0:T(8,128)(2,1)S(1)} %get-tuple-element.16, f32[512,768]{1,0:T(8,128)S(1)} %convert_reduce_fusion.1, f32[512,768]{1,0:T(8,128)S(1)} %convert_reduce_fusion), kind=kLoop, calls=%fused_computation.13 | loop fusion | flops 2358784 | bytes 5509120 | tf_op jit(solution)/shard_map/reduce_sum | solution.py:12
  33.3 1.4 %multiply_convert_fusion = bf16[512,768]{1,0:T(8,128)(2,1)} fusion(f32[512]{0:T(512)S(1)} %add_rsqrt_fusion, f32[512,768]{1,0:T(8,128)S(1)} %get-tuple-element.10, f32[512]{0:T(512)S(1)} %add_add_fusion, bf16[512,768]{1,0:T(8,128)(2,1)S(1)} %get-tuple-element.16), kind=kLoop, calls=%fused_computation.12 | loop fusion | flops 1966080 | bytes 3149824 | tf_op jit(solution)/shard_map/convert_element_type | solution.py:130
  (42 shorter events, 0.5 us)
Async XLA Ops:
  0.6 10.5 %copy-start.1 = (bf16[32,768]{1,0:T(8,128)(2,1)S(1)}, bf16[32,768]{1,0:T(8,128)(2,1)}, u32[]{:S(2)}) copy-start(bf16[32,768]{1,0:T(8,128)(2,1)} %param.4) | copy-start | bytes 147460
  0.6 7.9 %copy-start.2 = (s32[32]{0:T(128)S(1)}, s32[32]{0:T(128)}, u32[]{:S(2)}) copy-start(s32[32]{0:T(128)} %param.5) | copy-start | bytes 388
  0.6 8.6 %collective-permute-start = (bf16[32,768]{1,0:T(8,128)(2,1)}, bf16[32,768]{1,0:T(8,128)(2,1)S(1)}, u32[]{:S(2)}, u32[]{:S(2)}) collective-permute-start(bf16[32,768]{1,0:T(8,128)(2,1)} %param.4), channel_id=1, source_target_pairs={{0,4},{4,8},{8,12},{12,0},{1,5},{5,9},{9,13},{13,1},{2,6},{6,10},{... | collective-permute-start | bytes 147464 | tf_op jit(solution)/shard_map/ppermute | solution.py:23
  3.7 5.5 %collective-permute-start.2 = (bf16[32,768]{1,0:T(8,128)(2,1)}, bf16[32,768]{1,0:T(8,128)(2,1)S(1)}, u32[]{:S(2)}, u32[]{:S(2)}) collective-permute-start(bf16[32,768]{1,0:T(8,128)(2,1)} %param.4), channel_id=1, source_target_pairs={{0,12},{4,0},{8,4},{12,8},{1,13},{5,1},{9,5},{13,9},{2,14},{6,2},{... | collective-permute-start | bytes 147464 | tf_op jit(solution)/shard_map/ppermute | solution.py:23
  5.8 5.3 %collective-permute-start.1 = (bf16[32,768]{1,0:T(8,128)(2,1)}, bf16[32,768]{1,0:T(8,128)(2,1)S(1)}, u32[]{:S(2)}, u32[]{:S(2)}) collective-permute-start(bf16[32,768]{1,0:T(8,128)(2,1)} %param.4), channel_id=1, source_target_pairs={{0,8},{4,12},{8,0},{12,4},{1,9},{5,13},{9,1},{13,5},{2,10},{6,14},... | collective-permute-start | bytes 147464 | tf_op jit(solution)/shard_map/ppermute | solution.py:23
  11.2 6.2 %collective-permute-start.3 = (bf16[144,768]{1,0:T(8,128)(2,1)S(1)}, bf16[144,768]{1,0:T(8,128)(2,1)S(1)}, u32[]{:S(2)}, u32[]{:S(2)}) collective-permute-start(bf16[144,768]{1,0:T(8,128)(2,1)S(1)} %get-tuple-element.20), channel_id=1, source_target_pairs={{0,2},{2,0},{1,3},{3,1},{4,6},{6,4},{5,7},{7,5},{8,10},{10,8},{9,1... | collective-permute-start | bytes 663560 | tf_op jit(solution)/shard_map/ppermute | solution.py:23
  17.7 1.9 %collective-permute-start.4 = (bf16[2,144,768]{2,1,0:T(8,128)(2,1)S(1)}, bf16[2,144,768]{2,1,0:T(8,128)(2,1)S(1)}, u32[]{:S(2)}, u32[]{:S(2)}) collective-permute-start(bf16[2,144,768]{2,1,0:T(8,128)(2,1)S(1)} %get-tuple-element.17), channel_id=1, source_target_pairs={{0,1},{1,0},{2,3},{3,2},{4,5},{5,4},{6,7},{7,6},{8,9},{9,8},{10,11... | collective-permute-start | bytes 1327112 | tf_op jit(solution)/shard_map/ppermute | solution.py:23
  21.4 4.9 %collective-permute-start.6 = (f32[3,2,2,4,32]{4,3,2,1,0:T(4,128)S(1)}, f32[3,2,2,4,32]{4,3,2,1,0:T(4,128)S(1)}, u32[]{:S(2)}, u32[]{:S(2)}) collective-permute-start(f32[3,2,2,4,32]{4,3,2,1,0:T(4,128)S(1)} %get-tuple-element.26), channel_id=1, source_target_pairs={{0,8},{4,12},{8,0},{12,4},{1,9},{5,13},{9,1},{13,5},{2,10},{6,14},... | collective-permute-start | bytes 18440 | tf_op jit(solution)/shard_map/ppermute | solution.py:23
  22.1 5.6 %collective-permute-start.5 = (f32[3,2,2,4,32]{4,3,2,1,0:T(4,128)S(1)}, f32[3,2,2,4,32]{4,3,2,1,0:T(4,128)S(1)}, u32[]{:S(2)}, u32[]{:S(2)}) collective-permute-start(f32[3,2,2,4,32]{4,3,2,1,0:T(4,128)S(1)} %get-tuple-element.26), channel_id=1, source_target_pairs={{0,4},{4,8},{8,12},{12,0},{1,5},{5,9},{9,13},{13,1},{2,6},{6,10},{... | collective-permute-start | bytes 18440 | tf_op jit(solution)/shard_map/ppermute | solution.py:23
  24.8 3.8 %collective-permute-start.7 = (f32[3,2,2,4,32]{4,3,2,1,0:T(4,128)S(1)}, f32[3,2,2,4,32]{4,3,2,1,0:T(4,128)S(1)}, u32[]{:S(2)}, u32[]{:S(2)}) collective-permute-start(f32[3,2,2,4,32]{4,3,2,1,0:T(4,128)S(1)} %get-tuple-element.26), channel_id=1, source_target_pairs={{0,12},{4,0},{8,4},{12,8},{1,13},{5,1},{9,5},{13,9},{2,14},{6,2},{... | collective-permute-start | bytes 18440 | tf_op jit(solution)/shard_map/ppermute | solution.py:23
  28.8 1.3 %collective-permute-start.8 = (f32[3,2,2,4,32]{4,3,2,1,0:T(4,128)S(1)}, f32[3,2,2,4,32]{4,3,2,1,0:T(4,128)S(1)}, u32[]{:S(2)}, u32[]{:S(2)}) collective-permute-start(f32[3,2,2,4,32]{4,3,2,1,0:T(4,128)S(1)} %get-tuple-element.22), channel_id=1, source_target_pairs={{0,1},{1,0},{2,3},{3,2},{4,5},{5,4},{6,7},{7,6},{8,9},{9,8},{10,11... | collective-permute-start | bytes 18440 | tf_op jit(solution)/shard_map/ppermute | solution.py:23
  33.3 1.4 %copy-start = (f32[512,768]{1,0:T(8,128)}, f32[512,768]{1,0:T(8,128)S(1)}, u32[]{:S(2)}) copy-start(f32[512,768]{1,0:T(8,128)S(1)} %get-tuple-element.10) | copy-start | bytes 4718596

commit v13 on v12

--- a/solution.py
+++ b/solution.py
@@ -57,12 +57,20 @@
     cent_rows = blocks.shape[0]
     weight_block = jnp.pad(weights.astype(jnp.bfloat16)[None, :], ((0, 15), (0, width - row_dev)))
     payload = jnp.concatenate([blocks, weight_block], axis=0)
-    for name in STAGES[1:]:
-        payload = gather_stage(payload, name)
-    halves = [
-        normalize(payload[half, :, :cent_rows].reshape(-1, width)).astype(jnp.bfloat16) for half in range(sizes["sub"])
+    if sizes["dp"] == 2 and sizes["sub"] == 2:
+        from_dp = gather_stage(payload, "dp")[1]
+        from_sub = gather_stage(payload, "sub")[1]
+        from_diagonal = gather_stage(from_dp, "sub")[1]
+        pieces = [payload, from_dp, from_sub, from_diagonal]
+    else:
+        for name in STAGES[1:]:
+            payload = gather_stage(payload, name)
+        pieces = [payload[half] for half in range(sizes["sub"])]
+    chunks = [
+        normalize(piece[..., :cent_rows, :].reshape(-1, width)).astype(jnp.bfloat16) for piece in pieces
     ]
-    cent_weights = payload[:, :, cent_rows, :row_dev].astype(jnp.float32)
+    cent_weights = jnp.stack([piece[..., cent_rows, :row_dev] for piece in pieces]).astype(jnp.float32)
+    cent_weights = cent_weights.reshape(sizes["sub"], sizes["dp"], row_dev)
 
     offset = lax.axis_index(("dp", "sub")) * own_count
     if dp_columns:
@@ -87,7 +95,7 @@
             lax.dot_general(rows, cents, (((1,), (1,)), ((), ())), preferred_element_type=jnp.float32) * sharpness
             for cents in score_cents
         ]
-        for rows in halves
+        for rows in chunks
     ]
     block_shape = (sizes["sub"], sizes["dp"], sizes["cent"], row_dev)
     peaks, totals = [], []
@@ -109,22 +117,17 @@
     weight_float = stats[2].reshape(-1)
     log_sum = (stats[0] + jnp.log(stats[1])).reshape(-1)
 
-    half_log_sum = log_sum.reshape(sizes["sub"], -1)
-    half_weight = weight_float.reshape(sizes["sub"], -1)
-    centroid_sums = jnp.zeros((own_count, width), jnp.float32)
-    own_mass = jnp.zeros((own_count,), jnp.float32)
-    for half, rows in enumerate(halves):
-        responsibility = (
-            half_weight[half][:, None] * jnp.exp(score_blocks[half][0] - half_log_sum[half][:, None])
-        ).astype(jnp.bfloat16)
-        grouped_resp = responsibility.reshape(sizes["dp"], -1, own_count)
-        grouped_rows = rows.reshape(sizes["dp"], -1, width)
-        partial_value = lax.dot_general(
-            grouped_resp, grouped_rows, (((1,), (1,)), ((0,), (0,))), preferred_element_type=jnp.float32
-        ).astype(jnp.bfloat16)
-        centroid_sums = centroid_sums + jnp.sum(partial_value.astype(jnp.float32), axis=0)
-        weight_mass = jnp.sum(grouped_resp.astype(jnp.float32), axis=1).astype(jnp.bfloat16)
-        own_mass = own_mass + jnp.sum(weight_mass.astype(jnp.float32), axis=0)
+    own_scores = jnp.stack([blocks_of_chunk[0] for blocks_of_chunk in score_blocks]).reshape(n_groups, -1, own_count)
+    grouped_rows = jnp.stack(chunks).reshape(n_groups, -1, width)
+    grouped_resp = (
+        weight_float.reshape(n_groups, -1, 1) * jnp.exp(own_scores - log_sum.reshape(n_groups, -1, 1))
+    ).astype(jnp.bfloat16)
+    partial_value = lax.dot_general(
+        grouped_resp, grouped_rows, (((1,), (1,)), ((0,), (0,))), preferred_element_type=jnp.float32
+    ).astype(jnp.bfloat16)
+    centroid_sums = jnp.sum(partial_value.astype(jnp.float32), axis=0)
+    weight_mass = jnp.sum(grouped_resp.astype(jnp.float32), axis=1).astype(jnp.bfloat16)
+    own_mass = jnp.sum(weight_mass.astype(jnp.float32), axis=0)
 
     moved = own_cents.astype(jnp.float32) + centroid_sums / (own_mass + 1.0)[:, None]
     renormed = normalize(moved).astype(jnp.bfloat16)

time: 34.9 us -> 38.2 us (1.095)
  matrix products: 3.23 us -> 4.9 us
  starting transfers between devices: 12.4 us -> 13.7 us
    dot_general x4 -> x8, matrix products: 1.94 us -> 3.86 us  [shards(): lax.dot_general(rows, cents, (((1,), (1,)), ((), ())), preferred_element_...]
    ppermute x9 -> x10, starting transfers between devices: 12.4 us -> 13.7 us  [gather_stage(): lax.ppermute(value, name, [(j, (j + q) % size) for j in range(size)])]
    reduce_sum x2 -> x4, other arithmetic: 0.62 us -> 0.94 us  [shards(): jnp.sum(jnp.exp(block - half_peak[:, None]), axis=1)]
    dot_general x2 -> x1, matrix products: 1.29 us -> 1.04 us  [shards(): lax.dot_general(grouped_resp, grouped_rows, (((1,), (1,)), ((0,), (0,))),...]
    reduce_sum x4 -> x6, other arithmetic: 2.55 us -> 2.65 us  [normalize(): jnp.sum(floats * floats, axis=-1, keepdims=True) + 1e-06]
    ppermute x9 -> x10, waiting for transfers between devices: 9 us -> 9.1 us  [gather_stage(): lax.ppermute(value, name, [(j, (j + q) % size) for j in range(size)])]
  transfers between devices with their start and end apart: 9 -> 10, of which waited for: 7 -> 5; matrix products, arithmetic and copies ran while one was open for 14% -> 14% of each run, Pallas kernels for 0% -> 0%
where the time goes in v13:
time: 38.2 us; the launch traced here: 38 us
  starting transfers between devices  13.7 us (36%)
  waiting for transfers between devices  9.1 us (24%)
  other arithmetic  8.22 us (22%)
  matrix products  4.9 us (13%)
  between operations  1.65 us (4%)
  local copies, waits for them, and re-layouts  0.49 us (1%)
    ppermute x10, starting transfers between devices, gather_stage(): lax.ppermute(value, name, [(j, (j + q) % size) for j in range(size)])  13.7 us
    ppermute x10, waiting for transfers between devices, gather_stage(): lax.ppermute(value, name, [(j, (j + q) % size) for j in range(size)])  9.1 us
    dot_general x8, matrix products, shards(): lax.dot_general(rows, cents, (((1,), (1,)), ((), ())), preferred_element_...  3.86 us
    reduce_sum x6, other arithmetic, normalize(): jnp.sum(floats * floats, axis=-1, keepdims=True) + 1e-06  2.65 us
    convert_element_type x1, other arithmetic, shards(): score_cents = [lax.optimization_barrier(normalize(lax.dynamic_slice_in_di...  1.7 us
    convert_element_type x1, other arithmetic, shards(): renormed = normalize(moved).astype(jnp.bfloat16)  1.25 us
    dot_general x1, matrix products, shards(): lax.dot_general(grouped_resp, grouped_rows, (((1,), (1,)), ((0,), (0,))),...  1.04 us
    reduce_sum x4, other arithmetic, shards(): jnp.sum(jnp.exp(block - half_peak[:, None]), axis=1)  0.94 us
  transfers between devices with their start and end apart: 10, of which 5 were waited for; matrix products, arithmetic and copies ran while one was open for 14% of the time, Pallas kernels for 0%

profile of v13, /device:TPU:0, one launch (start us, length us, event | category | flops | bytes accessed | tf_op | source)
XLA Modules:
  0.0 38.0 jit_solution(7297801628044814807)
XLA Ops:
  0.6 3.1 %collective-permute-start = (bf16[32,768]{1,0:T(8,128)(2,1)}, bf16[32,768]{1,0:T(8,128)(2,1)S(1)}, u32[]{:S(2)}, u32[]{:S(2)}) collective-permute-start(bf16[32,768]{1,0:T(8,128)(2,1)} %param.4), channel_id=1, source_target_pairs={{0,4},{4,8},{8,12},{12,0},{1,5},{5,9},{9,13},{13,1},{2,6},{6,10},{... | collective-permute-start | bytes 147464 | tf_op jit(solution)/shard_map/ppermute | solution.py:23
  3.7 2.1 %collective-permute-start.2 = (bf16[32,768]{1,0:T(8,128)(2,1)}, bf16[32,768]{1,0:T(8,128)(2,1)S(1)}, u32[]{:S(2)}, u32[]{:S(2)}) collective-permute-start(bf16[32,768]{1,0:T(8,128)(2,1)} %param.4), channel_id=1, source_target_pairs={{0,12},{4,0},{8,4},{12,8},{1,13},{5,1},{9,5},{13,9},{2,14},{6,2},{... | collective-permute-start | bytes 147464 | tf_op jit(solution)/shard_map/ppermute | solution.py:23
  5.8 0.9 %collective-permute-start.1 = (bf16[32,768]{1,0:T(8,128)(2,1)}, bf16[32,768]{1,0:T(8,128)(2,1)S(1)}, u32[]{:S(2)}, u32[]{:S(2)}) collective-permute-start(bf16[32,768]{1,0:T(8,128)(2,1)} %param.4), channel_id=1, source_target_pairs={{0,8},{4,12},{8,0},{12,4},{1,9},{5,13},{9,1},{13,5},{2,10},{6,14},... | collective-permute-start | bytes 147464 | tf_op jit(solution)/shard_map/ppermute | solution.py:23
  6.7 1.7 %fusion.2 = (f32[512]{0:T(512)S(1)}, f32[512]{0:T(512)S(1)}) fusion(bf16[2048,768]{1,0:T(8,128)(2,1)} %param.6, s32[]{:T(128)S(6)} %select_n.20, s32[]{:T(128)S(6)} %select_n.18), kind=kLoop, calls=%fused_computation.7 | loop fusion | flops 2358272 | bytes 1576968 | tf_op jit(solution)/shard_map/reduce_sum | solution.py:12
  8.5 1.7 %fusion.1 = (bf16[512,768]{1,0:T(8,128)(2,1)S(1)}, bf16[512,768]{1,0:T(8,128)(2,1)S(1)}) fusion(f32[512]{0:T(512)S(1)} %get-tuple-element.44, bf16[2048,768]{1,0:T(8,128)(2,1)} %param.6, s32[]{:T(128)S(6)} %select_n.18, f32[512]{0:T(512)S(1)} %get-tuple-element.43, s32[]{:T(128)S(6)} %select_n.20), kind=kLoop, calls=%fused_computation.6 | loop fusion | flops 2359296 | bytes 3149832 | tf_op jit(solution)/shard_map/convert_element_type | solution.py:84
  10.9 0.2 collective-permute-done.1
  11.2 0.1 multiply_reduce_fusion.1
  11.3 0.1 collective-permute-start.4
  11.4 1.6 %collective-permute-start.3 = (bf16[144,768]{1,0:T(8,128)(2,1)S(1)}, bf16[144,768]{1,0:T(8,128)(2,1)S(1)}, u32[]{:S(2)}, u32[]{:S(2)}) collective-permute-start(bf16[144,768]{1,0:T(8,128)(2,1)S(1)} %fusion.22), channel_id=1, source_target_pairs={{0,2},{2,0},{1,3},{3,1},{4,6},{6,4},{5,7},{7,5},{8,10},{10,8},{9,1... | collective-permute-start | bytes 663560 | tf_op jit(solution)/shard_map/ppermute | solution.py:23
  13.0 0.1 rsqrt.60
  13.1 0.5 %fusion.59 = (f32[128]{0:T(128)S(1)}, f32[128,512]{1,0:T(8,128)S(1)}) fusion(f32[]{:T(128)} %bitcast.95, bf16[512,768]{1,0:T(8,128)(2,1)S(1)} %get-tuple-element.18, bf16[128,768]{1,0:T(8,128)(2,1)S(1)} %bitcast.97, f32[128]{0:T(128)S(1)} %rsqrt.60), kind=kOutput, calls=%fused_computation.122 | convolution fusion | flops 101089152 | bytes 1246212 | tf_op jit(solution)/shard_map/dot_general | solution.py:95
  13.6 0.5 %fusion.58 = (f32[128]{0:T(128)S(1)}, f32[128,512]{1,0:T(8,128)S(1)}) fusion(f32[]{:T(128)} %bitcast.87, bf16[512,768]{1,0:T(8,128)(2,1)S(1)} %get-tuple-element.17, bf16[128,768]{1,0:T(8,128)(2,1)S(1)} %bitcast.98, f32[128]{0:T(128)S(1)} %rsqrt.60), kind=kOutput, calls=%fused_computation.121 | convolution fusion | flops 101089152 | bytes 1246212 | tf_op jit(solution)/shard_map/dot_general | solution.py:95
  14.1 0.2 exponential_reduce_fusion.6
  14.3 0.1 fusion.21
  14.4 0.1 fusion.17
  14.5 4.7 %collective-permute-done.3 = bf16[144,768]{1,0:T(8,128)(2,1)S(1)} collective-permute-done((bf16[144,768]{1,0:T(8,128)(2,1)S(1)}, bf16[144,768]{1,0:T(8,128)(2,1)S(1)}, u32[]{:S(2)}, u32[]{:S(2)}) %collective-permute-start.3) | collective-permute-done | bytes 221216 | tf_op jit(solution)/shard_map/ppermute | solution.py:23
  19.2 0.1 fusion.15
  19.4 0.5 %fusion.55 = (f32[128]{0:T(128)S(1)}, f32[128,512]{1,0:T(8,128)S(1)}) fusion(f32[]{:T(128)} %bitcast.91, bf16[512,768]{1,0:T(8,128)(2,1)S(1)} %get-tuple-element.18, f32[128]{0:T(128)S(1)} %add_rsqrt_fusion.5, bf16[144,768]{1,0:T(8,128)(2,1)S(1)} %collective-permute-done.4), kind=kOutput, calls=%fused_computation.118 | convolution fusion | flops 101089152 | bytes 1246212 | tf_op jit(solution)/shard_map/dot_general | solution.py:95
  19.9 0.5 %fusion.54 = (f32[128]{0:T(128)S(1)}, f32[128,512]{1,0:T(8,128)S(1)}) fusion(f32[]{:T(128)} %bitcast.92, bf16[512,768]{1,0:T(8,128)(2,1)S(1)} %get-tuple-element.17, f32[128]{0:T(128)S(1)} %add_rsqrt_fusion.5, bf16[144,768]{1,0:T(8,128)(2,1)S(1)} %collective-permute-done.4), kind=kOutput, calls=%fused_computation.117 | convolution fusion | flops 101089152 | bytes 1246212 | tf_op jit(solution)/shard_map/dot_general | solution.py:95
  20.3 0.2 exponential_reduce_fusion.2
  20.6 0.5 %fusion.57 = (f32[128]{0:T(128)S(1)}, f32[128,512]{1,0:T(8,128)S(1)}) fusion(f32[]{:T(128)} %bitcast.93, bf16[512,768]{1,0:T(8,128)(2,1)S(1)} %get-tuple-element.18, f32[128]{0:T(128)S(1)} %add_rsqrt_fusion.6, bf16[144,768]{1,0:T(8,128)(2,1)S(1)} %collective-permute-done.3), kind=kOutput, calls=%fused_computation.120 | convolution fusion | flops 101089152 | bytes 1246212 | tf_op jit(solution)/shard_map/dot_general | solution.py:95
  21.1 0.5 %fusion.56 = (f32[128]{0:T(128)S(1)}, f32[128,512]{1,0:T(8,128)S(1)}) fusion(f32[]{:T(128)} %bitcast.94, bf16[512,768]{1,0:T(8,128)(2,1)S(1)} %get-tuple-element.17, f32[128]{0:T(128)S(1)} %add_rsqrt_fusion.6, bf16[144,768]{1,0:T(8,128)(2,1)S(1)} %collective-permute-done.3), kind=kOutput, calls=%fused_computation.119 | convolution fusion | flops 101089152 | bytes 1246212 | tf_op jit(solution)/shard_map/dot_general | solution.py:95
  21.6 0.2 exponential_reduce_fusion.4
  21.8 0.1 collective-permute-start.5
  21.9 0.1 fusion.41
  22.0 1.4 %collective-permute-done.5 = bf16[144,768]{1,0:T(8,128)(2,1)S(1)} collective-permute-done((bf16[144,768]{1,0:T(8,128)(2,1)S(1)}, bf16[144,768]{1,0:T(8,128)(2,1)S(1)}, u32[]{:S(2)}, u32[]{:S(2)}) %collective-permute-start.5) | collective-permute-done | bytes 221216 | tf_op jit(solution)/shard_map/ppermute | solution.py:23
  23.4 0.1 fusion.19
  23.6 0.5 %fusion.53 = (f32[128]{0:T(128)S(1)}, f32[128,512]{1,0:T(8,128)S(1)}) fusion(f32[]{:T(128)} %bitcast.89, bf16[512,768]{1,0:T(8,128)(2,1)S(1)} %get-tuple-element.18, f32[128]{0:T(128)S(1)} %add_rsqrt_fusion.4, bf16[144,768]{1,0:T(8,128)(2,1)S(1)} %collective-permute-done.5), kind=kOutput, calls=%fused_computation.116 | convolution fusion | flops 101089152 | bytes 1246212 | tf_op jit(solution)/shard_map/dot_general | solution.py:95
  24.0 0.5 %fusion.52 = (f32[128]{0:T(128)S(1)}, f32[128,512]{1,0:T(8,128)S(1)}) fusion(f32[]{:T(128)} %bitcast.90, bf16[512,768]{1,0:T(8,128)(2,1)S(1)} %get-tuple-element.17, f32[128]{0:T(128)S(1)} %add_rsqrt_fusion.4, bf16[144,768]{1,0:T(8,128)(2,1)S(1)} %collective-permute-done.5), kind=kOutput, calls=%fused_computation.115 | convolution fusion | flops 101089152 | bytes 1246212 | tf_op jit(solution)/shard_map/dot_general | solution.py:95
  24.6 0.2 exponential_reduce_fusion
  24.8 0.1 stack_reshape.7
  24.9 0.1 stack_reshape.6
  25.0 1.9 %collective-permute-start.7 = (f32[3,2,2,4,32]{4,3,2,1,0:T(4,128)S(1)}, f32[3,2,2,4,32]{4,3,2,1,0:T(4,128)S(1)}, u32[]{:S(2)}, u32[]{:S(2)}) collective-permute-start(f32[3,2,2,4,32]{4,3,2,1,0:T(4,128)S(1)} %get-tuple-element.24), channel_id=1, source_target_pairs={{0,8},{4,12},{8,0},{12,4},{1,9},{5,13},{9,1},{13,5},{2,10},{6,14},... | collective-permute-start | bytes 18440 | tf_op jit(solution)/shard_map/ppermute | solution.py:23
  26.9 0.1 fusion.44
  27.0 1.1 %collective-permute-start.6 = (f32[3,2,2,4,32]{4,3,2,1,0:T(4,128)S(1)}, f32[3,2,2,4,32]{4,3,2,1,0:T(4,128)S(1)}, u32[]{:S(2)}, u32[]{:S(2)}) collective-permute-start(f32[3,2,2,4,32]{4,3,2,1,0:T(4,128)S(1)} %get-tuple-element.24), channel_id=1, source_target_pairs={{0,4},{4,8},{8,12},{12,0},{1,5},{5,9},{9,13},{13,1},{2,6},{6,10},{... | collective-permute-start | bytes 18440 | tf_op jit(solution)/shard_map/ppermute | solution.py:23
  28.1 2.8 %collective-permute-start.8 = (f32[3,2,2,4,32]{4,3,2,1,0:T(4,128)S(1)}, f32[3,2,2,4,32]{4,3,2,1,0:T(4,128)S(1)}, u32[]{:S(2)}, u32[]{:S(2)}) collective-permute-start(f32[3,2,2,4,32]{4,3,2,1,0:T(4,128)S(1)} %get-tuple-element.24), channel_id=1, source_target_pairs={{0,12},{4,0},{8,4},{12,8},{1,13},{5,1},{9,5},{13,9},{2,14},{6,2},{... | collective-permute-start | bytes 18440 | tf_op jit(solution)/shard_map/ppermute | solution.py:23
  30.9 1.8 %collective-permute-done.6 = f32[3,2,2,4,32]{4,3,2,1,0:T(4,128)S(1)} collective-permute-done((f32[3,2,2,4,32]{4,3,2,1,0:T(4,128)S(1)}, f32[3,2,2,4,32]{4,3,2,1,0:T(4,128)S(1)}, u32[]{:S(2)}, u32[]{:S(2)}) %collective-permute-start.6) | collective-permute-done | bytes 6176 | tf_op jit(solution)/shard_map/ppermute | solution.py:23
  32.9 0.1 collective-permute-start.9
  33.0 0.1 fusion.38
  33.1 1.1 %collective-permute-done.9 = f32[3,2,2,4,32]{4,3,2,1,0:T(4,128)S(1)} collective-permute-done((f32[3,2,2,4,32]{4,3,2,1,0:T(4,128)S(1)}, f32[3,2,2,4,32]{4,3,2,1,0:T(4,128)S(1)}, u32[]{:S(2)}, u32[]{:S(2)}) %collective-permute-start.9) | collective-permute-done | bytes 6176 | tf_op jit(solution)/shard_map/ppermute | solution.py:23
  34.2 0.1 mul.187
  34.4 0.1 add.136
  34.4 0.5 %fusion.34 = f32[32]{0:T(128)} fusion(f32[2,2,4,32]{3,2,1,0:T(4,128)S(1)} %bitcast.112, f32[2,2,4,32]{3,2,1,0:T(4,128)S(1)} %fusion.28, f32[]{:T(128)} %bitcast.88), kind=kLoop, calls=%fused_computation.104 | loop fusion | flops 64 | bytes 388 | tf_op jit(solution)/shard_map/div | solution.py:136
  35.0 0.3 fusion.47
  35.3 1.0 %convert_reduce_fusion = f32[512,768]{1,0:T(8,128)S(1)} fusion(bf16[4,128,512]{2,1,0:T(8,128)(2,1)S(1)} %get-tuple-element.14, bf16[1,128,768]{2,1,0:T(8,128)(2,1)S(1)} %fusion.38, bf16[1,128,768]{2,1,0:T(8,128)(2,1)S(1)} %fusion.41, bf16[1,128,768]{2,1,0:T(8,128)(2,1)S(1)} %fusion.44, bf16[1,128,768]{2,1,0:T(8,128)(2,1)S(1)} %fusion.21), kind=kOutput, calls=%fused_computation | convolution fusion | flops 408158208 | bytes 2883584 | tf_op jit(solution)/shard_map/dot_general | solution.py:125
  36.3 0.0 copy-start
  36.3 0.4 %multiply_reduce_fusion = f32[512]{0:T(512)S(1)} fusion(f32[512,768]{1,0:T(8,128)S(1)} %convert_reduce_fusion, f32[512]{0:T(512)S(1)} %broadcast_add_fusion, bf16[512,768]{1,0:T(8,128)(2,1)S(1)} %get-tuple-element.17), kind=kLoop, calls=%fused_computation.10 | loop fusion | flops 1965568 | bytes 2363392 | tf_op jit(solution)/shard_map/reduce_sum | solution.py:12
  36.8 1.2 %multiply_convert_fusion = bf16[512,768]{1,0:T(8,128)(2,1)} fusion(f32[512]{0:T(512)S(1)} %add_rsqrt_fusion, f32[512,768]{1,0:T(8,128)S(1)} %convert_reduce_fusion, f32[512]{0:T(512)S(1)} %broadcast_add_fusion, bf16[512,768]{1,0:T(8,128)(2,1)S(1)} %get-tuple-element.17), kind=kLoop, calls=%fused_computation.9 | loop fusion | flops 1966080 | bytes 3149824 | tf_op jit(solution)/shard_map/convert_element_type | solution.py:133
  (56 shorter events, 0.6 us)
Async XLA Ops:
  0.6 10.3 %collective-permute-start = (bf16[32,768]{1,0:T(8,128)(2,1)}, bf16[32,768]{1,0:T(8,128)(2,1)S(1)}, u32[]{:S(2)}, u32[]{:S(2)}) collective-permute-start(bf16[32,768]{1,0:T(8,128)(2,1)} %param.4), channel_id=1, source_target_pairs={{0,4},{4,8},{8,12},{12,0},{1,5},{5,9},{9,13},{13,1},{2,6},{6,10},{... | collective-permute-start | bytes 147464 | tf_op jit(solution)/shard_map/ppermute | solution.py:23
  3.7 7.2 %collective-permute-start.2 = (bf16[32,768]{1,0:T(8,128)(2,1)}, bf16[32,768]{1,0:T(8,128)(2,1)S(1)}, u32[]{:S(2)}, u32[]{:S(2)}) collective-permute-start(bf16[32,768]{1,0:T(8,128)(2,1)} %param.4), channel_id=1, source_target_pairs={{0,12},{4,0},{8,4},{12,8},{1,13},{5,1},{9,5},{13,9},{2,14},{6,2},{... | collective-permute-start | bytes 147464 | tf_op jit(solution)/shard_map/ppermute | solution.py:23
  5.8 5.3 %collective-permute-start.1 = (bf16[32,768]{1,0:T(8,128)(2,1)}, bf16[32,768]{1,0:T(8,128)(2,1)S(1)}, u32[]{:S(2)}, u32[]{:S(2)}) collective-permute-start(bf16[32,768]{1,0:T(8,128)(2,1)} %param.4), channel_id=1, source_target_pairs={{0,8},{4,12},{8,0},{12,4},{1,9},{5,13},{9,1},{13,5},{2,10},{6,14},... | collective-permute-start | bytes 147464 | tf_op jit(solution)/shard_map/ppermute | solution.py:23
  8.5 1.7 %copy-start.2 = (s32[32]{0:T(128)S(1)}, s32[32]{0:T(128)}, u32[]{:S(2)}) copy-start(s32[32]{0:T(128)} %param.5) | copy-start | bytes 388
  8.5 2.6 %copy-start.1 = (bf16[32,768]{1,0:T(8,128)(2,1)S(1)}, bf16[32,768]{1,0:T(8,128)(2,1)}, u32[]{:S(2)}) copy-start(bf16[32,768]{1,0:T(8,128)(2,1)} %param.4) | copy-start | bytes 147460
  11.3 3.1 %collective-permute-start.4 = (bf16[144,768]{1,0:T(8,128)(2,1)S(1)}, bf16[144,768]{1,0:T(8,128)(2,1)S(1)}, u32[]{:S(2)}, u32[]{:S(2)}) collective-permute-start(bf16[144,768]{1,0:T(8,128)(2,1)S(1)} %fusion.22), channel_id=1, source_target_pairs={{0,1},{1,0},{2,3},{3,2},{4,5},{5,4},{6,7},{7,6},{8,9},{9,8},{10,11... | collective-permute-start | bytes 663560 | tf_op jit(solution)/shard_map/ppermute | solution.py:23
  11.4 7.8 %collective-permute-start.3 = (bf16[144,768]{1,0:T(8,128)(2,1)S(1)}, bf16[144,768]{1,0:T(8,128)(2,1)S(1)}, u32[]{:S(2)}, u32[]{:S(2)}) collective-permute-start(bf16[144,768]{1,0:T(8,128)(2,1)S(1)} %fusion.22), channel_id=1, source_target_pairs={{0,2},{2,0},{1,3},{3,1},{4,6},{6,4},{5,7},{7,5},{8,10},{10,8},{9,1... | collective-permute-start | bytes 663560 | tf_op jit(solution)/shard_map/ppermute | solution.py:23
  21.8 1.5 %collective-permute-start.5 = (bf16[144,768]{1,0:T(8,128)(2,1)S(1)}, bf16[144,768]{1,0:T(8,128)(2,1)S(1)}, u32[]{:S(2)}, u32[]{:S(2)}) collective-permute-start(bf16[144,768]{1,0:T(8,128)(2,1)S(1)} %collective-permute-done.3), channel_id=1, source_target_pairs={{0,1},{1,0},{2,3},{3,2},{4,5},{5,4},{6,7},{7,6},{8,9},{9,8},{10,11... | collective-permute-start | bytes 663560 | tf_op jit(solution)/shard_map/ppermute | solution.py:23
  25.0 5.9 %collective-permute-start.7 = (f32[3,2,2,4,32]{4,3,2,1,0:T(4,128)S(1)}, f32[3,2,2,4,32]{4,3,2,1,0:T(4,128)S(1)}, u32[]{:S(2)}, u32[]{:S(2)}) collective-permute-start(f32[3,2,2,4,32]{4,3,2,1,0:T(4,128)S(1)} %get-tuple-element.24), channel_id=1, source_target_pairs={{0,8},{4,12},{8,0},{12,4},{1,9},{5,13},{9,1},{13,5},{2,10},{6,14},... | collective-permute-start | bytes 18440 | tf_op jit(solution)/shard_map/ppermute | solution.py:23
  27.0 5.7 %collective-permute-start.6 = (f32[3,2,2,4,32]{4,3,2,1,0:T(4,128)S(1)}, f32[3,2,2,4,32]{4,3,2,1,0:T(4,128)S(1)}, u32[]{:S(2)}, u32[]{:S(2)}) collective-permute-start(f32[3,2,2,4,32]{4,3,2,1,0:T(4,128)S(1)} %get-tuple-element.24), channel_id=1, source_target_pairs={{0,4},{4,8},{8,12},{12,0},{1,5},{5,9},{9,13},{13,1},{2,6},{6,10},{... | collective-permute-start | bytes 18440 | tf_op jit(solution)/shard_map/ppermute | solution.py:23
  28.1 4.6 %collective-permute-start.8 = (f32[3,2,2,4,32]{4,3,2,1,0:T(4,128)S(1)}, f32[3,2,2,4,32]{4,3,2,1,0:T(4,128)S(1)}, u32[]{:S(2)}, u32[]{:S(2)}) collective-permute-start(f32[3,2,2,4,32]{4,3,2,1,0:T(4,128)S(1)} %get-tuple-element.24), channel_id=1, source_target_pairs={{0,12},{4,0},{8,4},{12,8},{1,13},{5,1},{9,5},{13,9},{2,14},{6,2},{... | collective-permute-start | bytes 18440 | tf_op jit(solution)/shard_map/ppermute | solution.py:23
  32.9 1.3 %collective-permute-start.9 = (f32[3,2,2,4,32]{4,3,2,1,0:T(4,128)S(1)}, f32[3,2,2,4,32]{4,3,2,1,0:T(4,128)S(1)}, u32[]{:S(2)}, u32[]{:S(2)}) collective-permute-start(f32[3,2,2,4,32]{4,3,2,1,0:T(4,128)S(1)} %get-tuple-element.20), channel_id=1, source_target_pairs={{0,1},{1,0},{2,3},{3,2},{4,5},{5,4},{6,7},{7,6},{8,9},{9,8},{10,11... | collective-permute-start | bytes 18440 | tf_op jit(solution)/shard_map/ppermute | solution.py:23
  36.3 1.7 %copy-start = (f32[512,768]{1,0:T(8,128)}, f32[512,768]{1,0:T(8,128)S(1)}, u32[]{:S(2)}) copy-start(f32[512,768]{1,0:T(8,128)S(1)} %convert_reduce_fusion) | copy-start | bytes 4718596

commit v14 on v10

--- a/solution.py
+++ b/solution.py
@@ -109,22 +109,35 @@
     weight_float = stats[2].reshape(-1)
     log_sum = (stats[0] + jnp.log(stats[1])).reshape(-1)
 
-    half_log_sum = log_sum.reshape(sizes["sub"], -1)
-    half_weight = weight_float.reshape(sizes["sub"], -1)
-    centroid_sums = jnp.zeros((own_count, width), jnp.float32)
-    own_mass = jnp.zeros((own_count,), jnp.float32)
-    for half, rows in enumerate(halves):
-        responsibility = (
-            half_weight[half][:, None] * jnp.exp(score_blocks[half][0] - half_log_sum[half][:, None])
+    if sum(rows.size for rows in halves) * 2 <= (4 << 20):
+        own_scores = jnp.stack([blocks_of_half[0] for blocks_of_half in score_blocks]).reshape(n_groups, -1, own_count)
+        grouped_rows = jnp.stack(halves).reshape(n_groups, -1, width)
+        grouped_resp = (
+            weight_float.reshape(n_groups, -1, 1) * jnp.exp(own_scores - log_sum.reshape(n_groups, -1, 1))
         ).astype(jnp.bfloat16)
-        grouped_resp = responsibility.reshape(sizes["dp"], -1, own_count)
-        grouped_rows = rows.reshape(sizes["dp"], -1, width)
         partial_value = lax.dot_general(
             grouped_resp, grouped_rows, (((1,), (1,)), ((0,), (0,))), preferred_element_type=jnp.float32
         ).astype(jnp.bfloat16)
-        centroid_sums = centroid_sums + jnp.sum(partial_value.astype(jnp.float32), axis=0)
+        centroid_sums = jnp.sum(partial_value.astype(jnp.float32), axis=0)
         weight_mass = jnp.sum(grouped_resp.astype(jnp.float32), axis=1).astype(jnp.bfloat16)
-        own_mass = own_mass + jnp.sum(weight_mass.astype(jnp.float32), axis=0)
+        own_mass = jnp.sum(weight_mass.astype(jnp.float32), axis=0)
+    else:
+        half_log_sum = log_sum.reshape(sizes["sub"], -1)
+        half_weight = weight_float.reshape(sizes["sub"], -1)
+        centroid_sums = jnp.zeros((own_count, width), jnp.float32)
+        own_mass = jnp.zeros((own_count,), jnp.float32)
+        for half, rows in enumerate(halves):
+            responsibility = (
+                half_weight[half][:, None] * jnp.exp(score_blocks[half][0] - half_log_sum[half][:, None])
+            ).astype(jnp.bfloat16)
+            grouped_resp = responsibility.reshape(sizes["dp"], -1, own_count)
+            grouped_rows = rows.reshape(sizes["dp"], -1, width)
+            partial_value = lax.dot_general(
+                grouped_resp, grouped_rows, (((1,), (1,)), ((0,), (0,))), preferred_element_type=jnp.float32
+            ).astype(jnp.bfloat16)
+            centroid_sums = centroid_sums + jnp.sum(partial_value.astype(jnp.float32), axis=0)
+            weight_mass = jnp.sum(grouped_resp.astype(jnp.float32), axis=1).astype(jnp.bfloat16)
+            own_mass = own_mass + jnp.sum(weight_mass.astype(jnp.float32), axis=0)
 
     moved = own_cents.astype(jnp.float32) + centroid_sums / (own_mass + 1.0)[:, None]
     renormed = normalize(moved).astype(jnp.bfloat16)

time: 34.9 us -> 36.3 us (1.040)
  other arithmetic: 7.94 us -> 10.6 us
  waiting for transfers between devices: 9 us -> 7.75 us
    another operation x0 -> x2, other arithmetic: none -> 2.02 us  [the longest x1 1.95 us: shards(): grouped_rows = jnp.stack(halves).reshape(n_groups, -1, width)]
    ppermute x9, waiting for transfers between devices: 9 us -> 7.75 us  [gather_stage(): lax.ppermute(value, name, [(j, (j + q) % size) for j in range(size)])]
    convert_element_type x2 -> x3, other arithmetic: 0.22 us -> 1.1 us  [shards(): normalize(payload[half, :, :cent_rows].reshape(-1, width))]
    dot_general x2 -> x1, matrix products: 1.3 us -> 0.98 us  [shards(): lax.dot_general(grouped_resp, grouped_rows, (((1,), (1,)), ((0,), (0,))),...]
  transfers between devices with their start and end apart: 9 -> 9, of which waited for: 7 -> 6; matrix products, arithmetic and copies ran while one was open for 14% -> 20% of each run, Pallas kernels for 0% -> 0%
where the time goes in v14:
time: 36.3 us; the launch traced here: 36 us
  starting transfers between devices  12.4 us (34%)
  other arithmetic  10.6 us (29%)
  waiting for transfers between devices  7.75 us (21%)
  matrix products  2.92 us (8%)
  between operations  1.62 us (4%)
  local copies, waits for them, and re-layouts  0.72 us (2%)
    ppermute x9, starting transfers between devices, gather_stage(): lax.ppermute(value, name, [(j, (j + q) % size) for j in range(size)])  12.4 us
    ppermute x9, waiting for transfers between devices, gather_stage(): lax.ppermute(value, name, [(j, (j + q) % size) for j in range(size)])  7.75 us
    reduce_sum x4, other arithmetic, normalize(): jnp.sum(floats * floats, axis=-1, keepdims=True) + 1e-06  2.49 us
    another operation x1, other arithmetic, shards(): grouped_rows = jnp.stack(halves).reshape(n_groups, -1, width)  1.95 us
    dot_general x4, matrix products, shards(): lax.dot_general(rows, cents, (((1,), (1,)), ((), ())), preferred_element_...  1.94 us
    convert_element_type x1, other arithmetic, shards(): score_cents = [lax.optimization_barrier(normalize(lax.dynamic_slice_in_di...  1.69 us
    convert_element_type x1, other arithmetic, shards(): renormed = normalize(moved).astype(jnp.bfloat16)  1.25 us
    convert_element_type x3, other arithmetic, shards(): normalize(payload[half, :, :cent_rows].reshape(-1, width))  1.1 us
  transfers between devices with their start and end apart: 9, of which 6 were waited for; matrix products, arithmetic and copies ran while one was open for 20% of the time, Pallas kernels for 0%

profile of v14, /device:TPU:0, one launch (start us, length us, event | category | flops | bytes accessed | tf_op | source)
XLA Modules:
  0.0 36.0 jit_solution(12856673429690578162)
XLA Ops:
  0.6 3.1 %collective-permute-start = (bf16[32,768]{1,0:T(8,128)(2,1)}, bf16[32,768]{1,0:T(8,128)(2,1)S(1)}, u32[]{:S(2)}, u32[]{:S(2)}) collective-permute-start(bf16[32,768]{1,0:T(8,128)(2,1)} %param.4), channel_id=1, source_target_pairs={{0,4},{4,8},{8,12},{12,0},{1,5},{5,9},{9,13},{13,1},{2,6},{6,10},{... | collective-permute-start | bytes 147464 | tf_op jit(solution)/shard_map/ppermute | solution.py:23
  3.7 2.1 %collective-permute-start.2 = (bf16[32,768]{1,0:T(8,128)(2,1)}, bf16[32,768]{1,0:T(8,128)(2,1)S(1)}, u32[]{:S(2)}, u32[]{:S(2)}) collective-permute-start(bf16[32,768]{1,0:T(8,128)(2,1)} %param.4), channel_id=1, source_target_pairs={{0,12},{4,0},{8,4},{12,8},{1,13},{5,1},{9,5},{13,9},{2,14},{6,2},{... | collective-permute-start | bytes 147464 | tf_op jit(solution)/shard_map/ppermute | solution.py:23
  5.8 0.9 %collective-permute-start.1 = (bf16[32,768]{1,0:T(8,128)(2,1)}, bf16[32,768]{1,0:T(8,128)(2,1)S(1)}, u32[]{:S(2)}, u32[]{:S(2)}) collective-permute-start(bf16[32,768]{1,0:T(8,128)(2,1)} %param.4), channel_id=1, source_target_pairs={{0,8},{4,12},{8,0},{12,4},{1,9},{5,13},{9,1},{13,5},{2,10},{6,14},... | collective-permute-start | bytes 147464 | tf_op jit(solution)/shard_map/ppermute | solution.py:23
  6.8 1.7 %fusion.2 = (f32[512]{0:T(512)S(1)}, f32[512]{0:T(512)S(1)}) fusion(bf16[2048,768]{1,0:T(8,128)(2,1)} %param.6, s32[]{:T(128)S(6)} %select_n.20, s32[]{:T(128)S(6)} %select_n.18), kind=kLoop, calls=%fused_computation.7 | loop fusion | flops 2358272 | bytes 1576968 | tf_op jit(solution)/shard_map/reduce_sum | solution.py:12
  9.2 0.0 collective-permute-done
  9.2 0.0 collective-permute-done.2
  9.2 1.9 %collective-permute-done.1 = bf16[32,768]{1,0:T(8,128)(2,1)S(1)} collective-permute-done((bf16[32,768]{1,0:T(8,128)(2,1)}, bf16[32,768]{1,0:T(8,128)(2,1)S(1)}, u32[]{:S(2)}, u32[]{:S(2)}) %collective-permute-start.1) | collective-permute-done | bytes 49184 | tf_op jit(solution)/shard_map/ppermute | solution.py:23
  11.2 1.6 %collective-permute-start.3 = (bf16[144,768]{1,0:T(8,128)(2,1)S(1)}, bf16[144,768]{1,0:T(8,128)(2,1)S(1)}, u32[]{:S(2)}, u32[]{:S(2)}) collective-permute-start(bf16[144,768]{1,0:T(8,128)(2,1)S(1)} %get-tuple-element.14), channel_id=1, source_target_pairs={{0,2},{2,0},{1,3},{3,1},{4,6},{6,4},{5,7},{7,5},{8,10},{10,8},{9,1... | collective-permute-start | bytes 663560 | tf_op jit(solution)/shard_map/ppermute | solution.py:23
  12.8 1.7 %fusion.3 = (bf16[512,768]{1,0:T(8,128)(2,1)S(1)}, bf16[512,768]{1,0:T(8,128)(2,1)S(1)}) fusion(f32[512]{0:T(512)S(1)} %get-tuple-element.33, bf16[2048,768]{1,0:T(8,128)(2,1)} %param.6, s32[]{:T(128)S(6)} %select_n.20, f32[512]{0:T(512)S(1)} %get-tuple-element.34, s32[]{:T(128)S(6)} %select_n.18), kind=kLoop, calls=%fused_computation.8 | loop fusion | flops 2359296 | bytes 3149832 | tf_op jit(solution)/shard_map/convert_element_type | solution.py:76
  14.5 2.9 %collective-permute-done.3 = bf16[144,768]{1,0:T(8,128)(2,1)S(1)} collective-permute-done((bf16[144,768]{1,0:T(8,128)(2,1)S(1)}, bf16[144,768]{1,0:T(8,128)(2,1)S(1)}, u32[]{:S(2)}, u32[]{:S(2)}) %collective-permute-start.3) | collective-permute-done | bytes 221216 | tf_op jit(solution)/shard_map/ppermute | solution.py:23
  17.4 0.1 fusion.31
  17.5 0.2 multiply_reduce_fusion.2
  17.6 0.1 slice_convert_fusion.1
  17.7 0.1 collective-permute-start.4
  17.8 0.1 fusion.7
  17.9 0.5 %fusion.37 = (f32[256]{0:T(256)S(1)}, f32[256,512]{1,0:T(8,128)S(1)}) fusion(f32[]{:T(128)} %bitcast.111, bf16[256,768]{1,0:T(8,128)(2,1)S(1)} %fusion.7, bf16[512,768]{1,0:T(8,128)(2,1)S(1)} %get-tuple-element.9), kind=kOutput, calls=%fused_computation.98 | convolution fusion | flops 201588480 | bytes 1704964 | tf_op jit(solution)/shard_map/dot_general | solution.py:87
  18.4 0.5 %fusion.36 = (f32[256]{0:T(256)S(1)}, f32[256,512]{1,0:T(8,128)S(1)}) fusion(f32[]{:T(128)} %bitcast.107, bf16[256,768]{1,0:T(8,128)(2,1)S(1)} %fusion.7, bf16[512,768]{1,0:T(8,128)(2,1)S(1)} %get-tuple-element.10), kind=kOutput, calls=%fused_computation.97 | convolution fusion | flops 201588480 | bytes 1704964 | tf_op jit(solution)/shard_map/dot_general | solution.py:87
  18.9 0.3 exponential_reduce_fusion.2
  19.2 0.4 %collective-permute-done.4 = bf16[2,144,768]{2,1,0:T(8,128)(2,1)S(1)} collective-permute-done((bf16[2,144,768]{2,1,0:T(8,128)(2,1)S(1)}, bf16[2,144,768]{2,1,0:T(8,128)(2,1)S(1)}, u32[]{:S(2)}, u32[]{:S(2)}) %collective-permute-start.4) | collective-permute-done | bytes 442400 | tf_op jit(solution)/shard_map/ppermute | solution.py:23
  19.5 0.2 multiply_reduce_fusion.1
  19.7 0.1 slice_convert_fusion
  19.8 0.1 fusion.6
  19.9 0.9 %fusion.4 = (bf16[1,256,768]{2,1,0:T(8,128)(2,1)S(1)}, bf16[1,256,768]{2,1,0:T(8,128)(2,1)}) fusion(f32[1,2,128,768]{3,2,1,0:T(8,128)S(1)} %slice_convert_fusion, f32[256]{0:T(256)S(1)} %rsqrt_bitcast_fusion, f32[256]{0:T(256)S(1)} %rsqrt_bitcast_fusion.1, f32[1,2,128,768]{3,2,1,0:T(8,128)S(1)} %slice_convert_fusion.1), kind=kLoop, calls=%fused_computation.20 | loop fusion | flops 786432 | bytes 2361344 | tf_op jit(solution)/shard_map/convert_element_type | solution.py:63
  20.8 0.5 %fusion.35 = (f32[256]{0:T(256)S(1)}, f32[256,512]{1,0:T(8,128)S(1)}) fusion(f32[]{:T(128)} %bitcast.109, bf16[256,768]{1,0:T(8,128)(2,1)S(1)} %fusion.6, bf16[512,768]{1,0:T(8,128)(2,1)S(1)} %get-tuple-element.9), kind=kOutput, calls=%fused_computation.96 | convolution fusion | flops 201588480 | bytes 1704964 | tf_op jit(solution)/shard_map/dot_general | solution.py:87
  21.3 0.5 %fusion.34 = (f32[256]{0:T(256)S(1)}, f32[256,512]{1,0:T(8,128)S(1)}) fusion(f32[]{:T(128)} %bitcast.110, bf16[256,768]{1,0:T(8,128)(2,1)S(1)} %fusion.6, bf16[512,768]{1,0:T(8,128)(2,1)S(1)} %get-tuple-element.10), kind=kOutput, calls=%fused_computation.95 | convolution fusion | flops 201588480 | bytes 1704964 | tf_op jit(solution)/shard_map/dot_general | solution.py:87
  21.8 0.3 exponential_reduce_fusion
  22.1 0.1 stack_reshape.7
  22.2 0.1 stack_reshape.6
  22.3 0.7 %collective-permute-start.6 = (f32[3,2,2,4,32]{4,3,2,1,0:T(4,128)S(1)}, f32[3,2,2,4,32]{4,3,2,1,0:T(4,128)S(1)}, u32[]{:S(2)}, u32[]{:S(2)}) collective-permute-start(f32[3,2,2,4,32]{4,3,2,1,0:T(4,128)S(1)} %get-tuple-element.20), channel_id=1, source_target_pairs={{0,8},{4,12},{8,0},{12,4},{1,9},{5,13},{9,1},{13,5},{2,10},{6,14},... | collective-permute-start | bytes 18440 | tf_op jit(solution)/shard_map/ppermute | solution.py:23
  23.0 2.7 %collective-permute-start.5 = (f32[3,2,2,4,32]{4,3,2,1,0:T(4,128)S(1)}, f32[3,2,2,4,32]{4,3,2,1,0:T(4,128)S(1)}, u32[]{:S(2)}, u32[]{:S(2)}) collective-permute-start(f32[3,2,2,4,32]{4,3,2,1,0:T(4,128)S(1)} %get-tuple-element.20), channel_id=1, source_target_pairs={{0,4},{4,8},{8,12},{12,0},{1,5},{5,9},{9,13},{13,1},{2,6},{6,10},{... | collective-permute-start | bytes 18440 | tf_op jit(solution)/shard_map/ppermute | solution.py:23
  25.7 1.1 %collective-permute-start.7 = (f32[3,2,2,4,32]{4,3,2,1,0:T(4,128)S(1)}, f32[3,2,2,4,32]{4,3,2,1,0:T(4,128)S(1)}, u32[]{:S(2)}, u32[]{:S(2)}) collective-permute-start(f32[3,2,2,4,32]{4,3,2,1,0:T(4,128)S(1)} %get-tuple-element.20), channel_id=1, source_target_pairs={{0,12},{4,0},{8,4},{12,8},{1,13},{5,1},{9,5},{13,9},{2,14},{6,2},{... | collective-permute-start | bytes 18440 | tf_op jit(solution)/shard_map/ppermute | solution.py:23
  26.8 0.1 pad_maximum_fusion
  26.9 0.3 collective-permute-done.6
  27.3 1.4 %collective-permute-done.5 = f32[3,2,2,4,32]{4,3,2,1,0:T(4,128)S(1)} collective-permute-done((f32[3,2,2,4,32]{4,3,2,1,0:T(4,128)S(1)}, f32[3,2,2,4,32]{4,3,2,1,0:T(4,128)S(1)}, u32[]{:S(2)}, u32[]{:S(2)}) %collective-permute-start.5) | collective-permute-done | bytes 6176 | tf_op jit(solution)/shard_map/ppermute | solution.py:23
  28.7 0.9 %collective-permute-done.7 = f32[3,2,2,4,32]{4,3,2,1,0:T(4,128)S(1)} collective-permute-done((f32[3,2,2,4,32]{4,3,2,1,0:T(4,128)S(1)}, f32[3,2,2,4,32]{4,3,2,1,0:T(4,128)S(1)}, u32[]{:S(2)}, u32[]{:S(2)}) %collective-permute-start.7) | collective-permute-done | bytes 6176 | tf_op jit(solution)/shard_map/ppermute | solution.py:23
  29.7 0.1 collective-permute-start.8
  29.8 1.9 %pad_maximum_fusion.1 = bf16[2,256,768]{2,1,0:T(8,128)(2,1)} fusion(bf16[1,256,768]{2,1,0:T(8,128)(2,1)S(1)} %get-tuple-element.31, bf16[1,256,768]{2,1,0:T(8,128)(2,1)} %get-tuple-element.32), kind=kLoop, calls=%fused_computation.18 | loop fusion | flops 393216 | bytes 1572864 | tf_op jit(solution)/shard_map/stack | solution.py:114
  31.7 0.3 copy.12
  32.1 0.0 copy-start.1
  32.1 0.0 collective-permute-done.8
  32.2 0.1 mul.150
  32.3 0.1 add.111
  32.4 0.5 %fusion.27 = f32[32]{0:T(128)} fusion(f32[2,2,4,32]{3,2,1,0:T(4,128)S(1)} %bitcast.129, s32[32]{0:T(128)S(1)} %copy-done.3, f32[]{:T(128)} %bitcast.108), kind=kLoop, calls=%fused_computation.87 | loop fusion | flops 96 | bytes 388 | tf_op jit(solution)/shard_map/div | solution.py:146
  32.9 0.4 fusion.10
  33.3 1.0 %convert_reduce_fusion = f32[512,768]{1,0:T(8,128)S(1)} fusion(bf16[4,128,768]{2,1,0:T(8,128)(2,1)S(1)} %bitcast.118, f32[4,128,512]{1,2,0:T(8,128)S(1)} %copy.12, f32[4,128]{1,0:T(4,128)S(1)} %add.111, f32[4,128]{1,0:T(4,128)S(1)} %mul.150), kind=kOutput, calls=%fused_computation | convolution fusion | flops 407764992 | bytes 3411968 | tf_op jit(solution)/shard_map/dot_general | solution.py:118
  34.3 0.0 copy-start
  34.3 0.4 %multiply_reduce_fusion = f32[512]{0:T(512)S(1)} fusion(f32[512,768]{1,0:T(8,128)S(1)} %convert_reduce_fusion, f32[512]{0:T(512)S(1)} %broadcast_add_fusion, bf16[512,768]{1,0:T(8,128)(2,1)S(1)} %get-tuple-element.10), kind=kLoop, calls=%fused_computation.10 | loop fusion | flops 1965568 | bytes 2363392 | tf_op jit(solution)/shard_map/reduce_sum | solution.py:12
  34.7 1.2 %multiply_convert_fusion = bf16[512,768]{1,0:T(8,128)(2,1)} fusion(f32[512]{0:T(512)S(1)} %add_rsqrt_fusion, f32[512,768]{1,0:T(8,128)S(1)} %convert_reduce_fusion, f32[512]{0:T(512)S(1)} %broadcast_add_fusion, bf16[512,768]{1,0:T(8,128)(2,1)S(1)} %get-tuple-element.10), kind=kLoop, calls=%fused_computation.9 | loop fusion | flops 1966080 | bytes 3149824 | tf_op jit(solution)/shard_map/convert_element_type | solution.py:143
  (41 shorter events, 0.5 us)
Async XLA Ops:
  0.6 10.5 %copy-start.2 = (bf16[32,768]{1,0:T(8,128)(2,1)S(1)}, bf16[32,768]{1,0:T(8,128)(2,1)}, u32[]{:S(2)}) copy-start(bf16[32,768]{1,0:T(8,128)(2,1)} %param.4) | copy-start | bytes 147460
  0.6 7.9 %copy-start.3 = (s32[32]{0:T(128)S(1)}, s32[32]{0:T(128)}, u32[]{:S(2)}) copy-start(s32[32]{0:T(128)} %param.5) | copy-start | bytes 388
  0.6 8.6 %collective-permute-start = (bf16[32,768]{1,0:T(8,128)(2,1)}, bf16[32,768]{1,0:T(8,128)(2,1)S(1)}, u32[]{:S(2)}, u32[]{:S(2)}) collective-permute-start(bf16[32,768]{1,0:T(8,128)(2,1)} %param.4), channel_id=1, source_target_pairs={{0,4},{4,8},{8,12},{12,0},{1,5},{5,9},{9,13},{13,1},{2,6},{6,10},{... | collective-permute-start | bytes 147464 | tf_op jit(solution)/shard_map/ppermute | solution.py:23
  3.7 5.5 %collective-permute-start.2 = (bf16[32,768]{1,0:T(8,128)(2,1)}, bf16[32,768]{1,0:T(8,128)(2,1)S(1)}, u32[]{:S(2)}, u32[]{:S(2)}) collective-permute-start(bf16[32,768]{1,0:T(8,128)(2,1)} %param.4), channel_id=1, source_target_pairs={{0,12},{4,0},{8,4},{12,8},{1,13},{5,1},{9,5},{13,9},{2,14},{6,2},{... | collective-permute-start | bytes 147464 | tf_op jit(solution)/shard_map/ppermute | solution.py:23
  5.8 5.3 %collective-permute-start.1 = (bf16[32,768]{1,0:T(8,128)(2,1)}, bf16[32,768]{1,0:T(8,128)(2,1)S(1)}, u32[]{:S(2)}, u32[]{:S(2)}) collective-permute-start(bf16[32,768]{1,0:T(8,128)(2,1)} %param.4), channel_id=1, source_target_pairs={{0,8},{4,12},{8,0},{12,4},{1,9},{5,13},{9,1},{13,5},{2,10},{6,14},... | collective-permute-start | bytes 147464 | tf_op jit(solution)/shard_map/ppermute | solution.py:23
  11.2 6.2 %collective-permute-start.3 = (bf16[144,768]{1,0:T(8,128)(2,1)S(1)}, bf16[144,768]{1,0:T(8,128)(2,1)S(1)}, u32[]{:S(2)}, u32[]{:S(2)}) collective-permute-start(bf16[144,768]{1,0:T(8,128)(2,1)S(1)} %get-tuple-element.14), channel_id=1, source_target_pairs={{0,2},{2,0},{1,3},{3,1},{4,6},{6,4},{5,7},{7,5},{8,10},{10,8},{9,1... | collective-permute-start | bytes 663560 | tf_op jit(solution)/shard_map/ppermute | solution.py:23
  17.7 1.9 %collective-permute-start.4 = (bf16[2,144,768]{2,1,0:T(8,128)(2,1)S(1)}, bf16[2,144,768]{2,1,0:T(8,128)(2,1)S(1)}, u32[]{:S(2)}, u32[]{:S(2)}) collective-permute-start(bf16[2,144,768]{2,1,0:T(8,128)(2,1)S(1)} %get-tuple-element.12), channel_id=1, source_target_pairs={{0,1},{1,0},{2,3},{3,2},{4,5},{5,4},{6,7},{7,6},{8,9},{9,8},{10,11... | collective-permute-start | bytes 1327112 | tf_op jit(solution)/shard_map/ppermute | solution.py:23
  22.3 4.9 %collective-permute-start.6 = (f32[3,2,2,4,32]{4,3,2,1,0:T(4,128)S(1)}, f32[3,2,2,4,32]{4,3,2,1,0:T(4,128)S(1)}, u32[]{:S(2)}, u32[]{:S(2)}) collective-permute-start(f32[3,2,2,4,32]{4,3,2,1,0:T(4,128)S(1)} %get-tuple-element.20), channel_id=1, source_target_pairs={{0,8},{4,12},{8,0},{12,4},{1,9},{5,13},{9,1},{13,5},{2,10},{6,14},... | collective-permute-start | bytes 18440 | tf_op jit(solution)/shard_map/ppermute | solution.py:23
  23.0 5.6 %collective-permute-start.5 = (f32[3,2,2,4,32]{4,3,2,1,0:T(4,128)S(1)}, f32[3,2,2,4,32]{4,3,2,1,0:T(4,128)S(1)}, u32[]{:S(2)}, u32[]{:S(2)}) collective-permute-start(f32[3,2,2,4,32]{4,3,2,1,0:T(4,128)S(1)} %get-tuple-element.20), channel_id=1, source_target_pairs={{0,4},{4,8},{8,12},{12,0},{1,5},{5,9},{9,13},{13,1},{2,6},{6,10},{... | collective-permute-start | bytes 18440 | tf_op jit(solution)/shard_map/ppermute | solution.py:23
  25.7 3.8 %collective-permute-start.7 = (f32[3,2,2,4,32]{4,3,2,1,0:T(4,128)S(1)}, f32[3,2,2,4,32]{4,3,2,1,0:T(4,128)S(1)}, u32[]{:S(2)}, u32[]{:S(2)}) collective-permute-start(f32[3,2,2,4,32]{4,3,2,1,0:T(4,128)S(1)} %get-tuple-element.20), channel_id=1, source_target_pairs={{0,12},{4,0},{8,4},{12,8},{1,13},{5,1},{9,5},{13,9},{2,14},{6,2},{... | collective-permute-start | bytes 18440 | tf_op jit(solution)/shard_map/ppermute | solution.py:23
  29.7 2.4 %collective-permute-start.8 = (f32[3,2,2,4,32]{4,3,2,1,0:T(4,128)S(1)}, f32[3,2,2,4,32]{4,3,2,1,0:T(4,128)S(1)}, u32[]{:S(2)}, u32[]{:S(2)}) collective-permute-start(f32[3,2,2,4,32]{4,3,2,1,0:T(4,128)S(1)} %get-tuple-element.16), channel_id=1, source_target_pairs={{0,1},{1,0},{2,3},{3,2},{4,5},{5,4},{6,7},{7,6},{8,9},{9,8},{10,11... | collective-permute-start | bytes 18440 | tf_op jit(solution)/shard_map/ppermute | solution.py:23
  32.1 1.2 %copy-start.1 = (bf16[2,256,768]{2,1,0:T(8,128)(2,1)S(1)}, bf16[2,256,768]{2,1,0:T(8,128)(2,1)}, u32[]{:S(2)}) copy-start(bf16[2,256,768]{2,1,0:T(8,128)(2,1)} %pad_maximum_fusion.1) | copy-start | bytes 2359300
  34.3 1.7 %copy-start = (f32[512,768]{1,0:T(8,128)}, f32[512,768]{1,0:T(8,128)S(1)}, u32[]{:S(2)}) copy-start(f32[512,768]{1,0:T(8,128)S(1)} %convert_reduce_fusion) | copy-start | bytes 4718596

commit v15 on v10

--- a/solution.py
+++ b/solution.py
@@ -67,36 +67,28 @@
     offset = lax.axis_index(("dp", "sub")) * own_count
     if dp_columns:
         dp_index, sub_index = lax.axis_index("dp"), lax.axis_index("sub")
-        score_cents = [
-            lax.optimization_barrier(
-                normalize(
-                    lax.dynamic_slice_in_dim(
-                        centroids, ((dp_index + q) % sizes["dp"] * sizes["sub"] + sub_index) * own_count, own_count, 0
-                    )
-                ).astype(jnp.bfloat16)
+        slices = [
+            lax.dynamic_slice_in_dim(
+                centroids, ((dp_index + q) % sizes["dp"] * sizes["sub"] + sub_index) * own_count, own_count, 0
             )
             for q in range(sizes["dp"])
         ]
+        score_cents = lax.optimization_barrier(normalize(jnp.concatenate(slices, axis=0)).astype(jnp.bfloat16))
     else:
         own_cents = normalize(lax.dynamic_slice_in_dim(centroids, offset, own_count, 0)).astype(jnp.bfloat16)
-        score_cents = [lax.optimization_barrier(own_cents)]
-    own_cents = score_cents[0]
+        score_cents = lax.optimization_barrier(own_cents)
+    own_cents = score_cents[:own_count]
 
     score_blocks = [
-        [
-            lax.dot_general(rows, cents, (((1,), (1,)), ((), ())), preferred_element_type=jnp.float32) * sharpness
-            for cents in score_cents
-        ]
+        lax.dot_general(rows, score_cents, (((1,), (1,)), ((), ())), preferred_element_type=jnp.float32) * sharpness
         for rows in halves
     ]
     block_shape = (sizes["sub"], sizes["dp"], sizes["cent"], row_dev)
     peaks, totals = [], []
-    for blocks_of_half in score_blocks:
-        half_peak = blocks_of_half[0].max(axis=1)
-        for block in blocks_of_half[1:]:
-            half_peak = jnp.maximum(half_peak, block.max(axis=1))
+    for block in score_blocks:
+        half_peak = block.max(axis=1)
         peaks.append(half_peak)
-        totals.append(sum(jnp.sum(jnp.exp(block - half_peak[:, None]), axis=1) for block in blocks_of_half))
+        totals.append(jnp.sum(jnp.exp(block - half_peak[:, None]), axis=1))
     local_peak = jnp.concatenate(peaks)
     local_total = jnp.concatenate(totals)
 
@@ -115,7 +107,7 @@
     own_mass = jnp.zeros((own_count,), jnp.float32)
     for half, rows in enumerate(halves):
         responsibility = (
-            half_weight[half][:, None] * jnp.exp(score_blocks[half][0] - half_log_sum[half][:, None])
+            half_weight[half][:, None] * jnp.exp(score_blocks[half][:, :own_count] - half_log_sum[half][:, None])
         ).astype(jnp.bfloat16)
         grouped_resp = responsibility.reshape(sizes["dp"], -1, own_count)
         grouped_rows = rows.reshape(sizes["dp"], -1, width)

time: 34.9 us -> 37.6 us (1.077)
  local copies, waits for them, and re-layouts: 0.55 us -> 3.31 us
  waiting for transfers between devices: 9 us -> 10.3 us
  other arithmetic: 7.94 us -> 6.77 us
  matrix products: 3.24 us -> 2.67 us
    reduce_sum x2, other arithmetic: 0.37 us -> 2.09 us  [shards(): jnp.sum(grouped_resp.astype(jnp.float32), axis=1).astype(jnp.bfloat16)]
    dynamic_slice x0 -> x1, local copies, waits for them, and re-layouts: none -> 1.47 us  [shards(): lax.dynamic_slice_in_dim(centroids, ((dp_index + q) % sizes['dp'] * sizes...]
    reduce_sum x4, other arithmetic: 2.55 us -> 1.17 us  [normalize(): jnp.sum(floats * floats, axis=-1, keepdims=True) + 1e-06]
    convert_element_type x1, other arithmetic: 1.69 us -> 0.32 us  [shards(): normalize(jnp.concatenate(slices, axis=0)).astype(jnp.bfloat16)]
    ppermute x9, waiting for transfers between devices: 9 us -> 10.3 us  [gather_stage(): lax.ppermute(value, name, [(j, (j + q) % size) for j in range(size)])]
    unnamed x6 -> x10, local copies, waits for them, and re-layouts: 0.01 us -> 1.3 us
    dot_general x4 -> x2, matrix products: 1.94 us -> 1.37 us  [shards(): lax.dot_general(rows, score_cents, (((1,), (1,)), ((), ())), preferred_el...]
  transfers between devices with their start and end apart: 9 -> 9, of which waited for: 7 -> 7; matrix products, arithmetic and copies ran while one was open for 14% -> 8% of each run, Pallas kernels for 0% -> 0%
where the time goes in v15:
time: 37.6 us; the launch traced here: 37.3 us
  starting transfers between devices  12.7 us (34%)
  waiting for transfers between devices  10.3 us (27%)
  other arithmetic  6.77 us (18%)
  local copies, waits for them, and re-layouts  3.31 us (9%)
  matrix products  2.67 us (7%)
  between operations  1.59 us (4%)
    ppermute x9, starting transfers between devices, gather_stage(): lax.ppermute(value, name, [(j, (j + q) % size) for j in range(size)])  12.7 us
    ppermute x9, waiting for transfers between devices, gather_stage(): lax.ppermute(value, name, [(j, (j + q) % size) for j in range(size)])  10.3 us
    reduce_sum x2, other arithmetic, shards(): jnp.sum(grouped_resp.astype(jnp.float32), axis=1).astype(jnp.bfloat16)  2.09 us
    dynamic_slice x1, local copies, waits for them, and re-layouts, shards(): lax.dynamic_slice_in_dim(centroids, ((dp_index + q) % sizes['dp'] * sizes...  1.47 us
    convert_element_type x1, other arithmetic, shards(): renormed = normalize(moved).astype(jnp.bfloat16)  1.38 us
    dot_general x2, matrix products, shards(): lax.dot_general(rows, score_cents, (((1,), (1,)), ((), ())), preferred_el...  1.37 us
    unnamed x10, local copies, waits for them, and re-layouts  1.3 us
    dot_general x2, matrix products, shards(): lax.dot_general(grouped_resp, grouped_rows, (((1,), (1,)), ((0,), (0,))),...  1.29 us
  transfers between devices with their start and end apart: 9, of which 7 were waited for; matrix products, arithmetic and copies ran while one was open for 8% of the time, Pallas kernels for 0%

profile of v15, /device:TPU:0, one launch (start us, length us, event | category | flops | bytes accessed | tf_op | source)
XLA Modules:
  0.0 37.3 jit_solution(15530868988077616401)
XLA Ops:
  0.6 3.1 %collective-permute-start = (bf16[32,768]{1,0:T(8,128)(2,1)}, bf16[32,768]{1,0:T(8,128)(2,1)S(1)}, u32[]{:S(2)}, u32[]{:S(2)}) collective-permute-start(bf16[32,768]{1,0:T(8,128)(2,1)} %param.4), channel_id=1, source_target_pairs={{0,4},{4,8},{8,12},{12,0},{1,5},{5,9},{9,13},{13,1},{2,6},{6,10},{... | collective-permute-start | bytes 147464 | tf_op jit(solution)/shard_map/ppermute | solution.py:23
  3.7 2.1 %collective-permute-start.2 = (bf16[32,768]{1,0:T(8,128)(2,1)}, bf16[32,768]{1,0:T(8,128)(2,1)S(1)}, u32[]{:S(2)}, u32[]{:S(2)}) collective-permute-start(bf16[32,768]{1,0:T(8,128)(2,1)} %param.4), channel_id=1, source_target_pairs={{0,12},{4,0},{8,4},{12,8},{1,13},{5,1},{9,5},{13,9},{2,14},{6,2},{... | collective-permute-start | bytes 147464 | tf_op jit(solution)/shard_map/ppermute | solution.py:23
  5.8 0.9 %collective-permute-start.1 = (bf16[32,768]{1,0:T(8,128)(2,1)}, bf16[32,768]{1,0:T(8,128)(2,1)S(1)}, u32[]{:S(2)}, u32[]{:S(2)}) collective-permute-start(bf16[32,768]{1,0:T(8,128)(2,1)} %param.4), channel_id=1, source_target_pairs={{0,8},{4,12},{8,0},{12,4},{1,9},{5,13},{9,1},{13,5},{2,10},{6,14},... | collective-permute-start | bytes 147464 | tf_op jit(solution)/shard_map/ppermute | solution.py:23
  6.7 1.5 %constant_dynamic-slice_fusion.1 = (bf16[512,768]{1,0:T(8,128)(2,1)S(1)}, bf16[512,768]{1,0:T(8,128)(2,1)S(1)}) fusion(bf16[2048,768]{1,0:T(8,128)(2,1)} %param.6, s32[]{:T(128)S(6)} %select_n.18, s32[]{:T(128)S(6)} %select_n.20), kind=kLoop, calls=%fused_computation.91 | loop fusion | bytes 3145736 | tf_op jit(solution)/shard_map/dynamic_slice | solution.py:71
  8.2 0.0 copy-start.4
  8.2 0.0 copy-start.3
  8.2 0.4 %fusion = f32[1024]{0:T(1024)S(1)} fusion(bf16[512,768]{1,0:T(8,128)(2,1)S(1)} %get-tuple-element.10, bf16[512,768]{1,0:T(8,128)(2,1)S(1)} %get-tuple-element.9), kind=kLoop, calls=%fused_computation.2 | loop fusion | flops 4717568 | bytes 1576960 | tf_op jit(solution)/shard_map/reduce_sum | solution.py:12
  8.6 0.2 copy-done.4
  9.5 0.0 collective-permute-done.2
  9.6 1.6 %collective-permute-done.1 = bf16[32,768]{1,0:T(8,128)(2,1)S(1)} collective-permute-done((bf16[32,768]{1,0:T(8,128)(2,1)}, bf16[32,768]{1,0:T(8,128)(2,1)S(1)}, u32[]{:S(2)}, u32[]{:S(2)}) %collective-permute-start.1) | collective-permute-done | bytes 49184 | tf_op jit(solution)/shard_map/ppermute | solution.py:23
  11.2 1.6 %collective-permute-start.3 = (bf16[144,768]{1,0:T(8,128)(2,1)S(1)}, bf16[144,768]{1,0:T(8,128)(2,1)S(1)}, u32[]{:S(2)}, u32[]{:S(2)}) collective-permute-start(bf16[144,768]{1,0:T(8,128)(2,1)S(1)} %get-tuple-element.14), channel_id=1, source_target_pairs={{0,2},{2,0},{1,3},{3,1},{4,6},{6,4},{5,7},{7,5},{8,10},{10,8},{9,1... | collective-permute-start | bytes 663560 | tf_op jit(solution)/shard_map/ppermute | solution.py:23
  12.8 0.3 fusion.1
  13.1 4.3 %collective-permute-done.3 = bf16[144,768]{1,0:T(8,128)(2,1)S(1)} collective-permute-done((bf16[144,768]{1,0:T(8,128)(2,1)S(1)}, bf16[144,768]{1,0:T(8,128)(2,1)S(1)}, u32[]{:S(2)}, u32[]{:S(2)}) %collective-permute-start.3) | collective-permute-done | bytes 221216 | tf_op jit(solution)/shard_map/ppermute | solution.py:23
  17.4 0.1 fusion.40
  17.4 0.2 multiply_reduce_fusion.2
  17.6 0.1 slice_convert_fusion.1
  17.7 0.1 collective-permute-start.4
  17.7 0.1 fusion.5
  17.9 0.7 %fusion.48 = (f32[256]{0:T(256)S(1)}, f32[256,1024]{1,0:T(8,128)S(1)}) fusion(f32[]{:T(128)} %bitcast.106, bf16[256,768]{1,0:T(8,128)(2,1)S(1)} %fusion.5, bf16[1024,768]{1,0:T(8,128)(2,1)S(1)} %fusion.1), kind=kOutput, calls=%fused_computation.106 | convolution fusion | flops 403177216 | bytes 3015684 | tf_op jit(solution)/shard_map/dot_general | solution.py:83
  18.6 1.0 %collective-permute-done.4 = bf16[2,144,768]{2,1,0:T(8,128)(2,1)S(1)} collective-permute-done((bf16[2,144,768]{2,1,0:T(8,128)(2,1)S(1)}, bf16[2,144,768]{2,1,0:T(8,128)(2,1)S(1)}, u32[]{:S(2)}, u32[]{:S(2)}) %collective-permute-start.4) | collective-permute-done | bytes 442400 | tf_op jit(solution)/shard_map/ppermute | solution.py:23
  19.5 0.2 multiply_reduce_fusion.1
  19.7 0.1 slice_convert_fusion
  19.8 0.1 fusion.4
  19.9 0.7 %fusion.47 = (f32[256]{0:T(256)S(1)}, f32[256,1024]{1,0:T(8,128)S(1)}) fusion(f32[]{:T(128)} %bitcast.108, bf16[256,768]{1,0:T(8,128)(2,1)S(1)} %fusion.4, bf16[1024,768]{1,0:T(8,128)(2,1)S(1)} %fusion.1), kind=kOutput, calls=%fused_computation.105 | convolution fusion | flops 403177216 | bytes 3015684 | tf_op jit(solution)/shard_map/dot_general | solution.py:83
  20.6 1.0 %copy-done = f32[256,1024]{1,0:T(8,128)} copy-done((f32[256,1024]{1,0:T(8,128)}, f32[256,1024]{1,0:T(8,128)S(1)}, u32[]{:S(2)}) %copy-start) | copy-done | bytes 1048600
  21.6 0.5 %exponential_reduce_fusion = (f32[256]{0:T(256)S(1)}, f32[256]{0:T(256)S(1)}) fusion(f32[256,1024]{1,0:T(8,128)S(1)} %get-tuple-element.32, f32[256]{0:T(256)S(1)} %get-tuple-element.31, f32[256,1024]{1,0:T(8,128)S(1)} %get-tuple-element.34, f32[256]{0:T(256)S(1)} %get-tuple-element.33), kind=kLoop, calls=%fused_computation.14 | loop fusion | flops 1048064 | bytes 2101248 | tf_op jit(solution)/shard_map/reduce_sum | solution.py:91
  22.1 0.1 stack_reshape.7
  22.1 0.1 stack_reshape.6
  22.2 1.0 %collective-permute-start.6 = (f32[3,2,2,4,32]{4,3,2,1,0:T(4,128)S(1)}, f32[3,2,2,4,32]{4,3,2,1,0:T(4,128)S(1)}, u32[]{:S(2)}, u32[]{:S(2)}) collective-permute-start(f32[3,2,2,4,32]{4,3,2,1,0:T(4,128)S(1)} %get-tuple-element.20), channel_id=1, source_target_pairs={{0,8},{4,12},{8,0},{12,4},{1,9},{5,13},{9,1},{13,5},{2,10},{6,14},... | collective-permute-start | bytes 18440 | tf_op jit(solution)/shard_map/ppermute | solution.py:23
  23.2 2.4 %collective-permute-start.5 = (f32[3,2,2,4,32]{4,3,2,1,0:T(4,128)S(1)}, f32[3,2,2,4,32]{4,3,2,1,0:T(4,128)S(1)}, u32[]{:S(2)}, u32[]{:S(2)}) collective-permute-start(f32[3,2,2,4,32]{4,3,2,1,0:T(4,128)S(1)} %get-tuple-element.20), channel_id=1, source_target_pairs={{0,4},{4,8},{8,12},{12,0},{1,5},{5,9},{9,13},{13,1},{2,6},{6,10},{... | collective-permute-start | bytes 18440 | tf_op jit(solution)/shard_map/ppermute | solution.py:23
  25.7 1.4 %collective-permute-start.7 = (f32[3,2,2,4,32]{4,3,2,1,0:T(4,128)S(1)}, f32[3,2,2,4,32]{4,3,2,1,0:T(4,128)S(1)}, u32[]{:S(2)}, u32[]{:S(2)}) collective-permute-start(f32[3,2,2,4,32]{4,3,2,1,0:T(4,128)S(1)} %get-tuple-element.20), channel_id=1, source_target_pairs={{0,12},{4,0},{8,4},{12,8},{1,13},{5,1},{9,5},{13,9},{2,14},{6,2},{... | collective-permute-start | bytes 18440 | tf_op jit(solution)/shard_map/ppermute | solution.py:23
  27.1 0.1 collective-permute-done.6
  27.2 1.7 %collective-permute-done.5 = f32[3,2,2,4,32]{4,3,2,1,0:T(4,128)S(1)} collective-permute-done((f32[3,2,2,4,32]{4,3,2,1,0:T(4,128)S(1)}, f32[3,2,2,4,32]{4,3,2,1,0:T(4,128)S(1)}, u32[]{:S(2)}, u32[]{:S(2)}) %collective-permute-start.5) | collective-permute-done | bytes 6176 | tf_op jit(solution)/shard_map/ppermute | solution.py:23
  28.9 0.6 %collective-permute-done.7 = f32[3,2,2,4,32]{4,3,2,1,0:T(4,128)S(1)} collective-permute-done((f32[3,2,2,4,32]{4,3,2,1,0:T(4,128)S(1)}, f32[3,2,2,4,32]{4,3,2,1,0:T(4,128)S(1)}, u32[]{:S(2)}, u32[]{:S(2)}) %collective-permute-start.7) | collective-permute-done | bytes 6176 | tf_op jit(solution)/shard_map/ppermute | solution.py:23
  29.7 0.1 collective-permute-start.8
  29.8 1.2 %collective-permute-done.8 = f32[3,2,2,4,32]{4,3,2,1,0:T(4,128)S(1)} collective-permute-done((f32[3,2,2,4,32]{4,3,2,1,0:T(4,128)S(1)}, f32[3,2,2,4,32]{4,3,2,1,0:T(4,128)S(1)}, u32[]{:S(2)}, u32[]{:S(2)}) %collective-permute-start.8) | collective-permute-done | bytes 6176 | tf_op jit(solution)/shard_map/ppermute | solution.py:23
  31.1 0.5 %fusion.34 = f32[32]{0:T(128)} fusion(f32[2,2,4,32]{3,2,1,0:T(4,128)S(1)} %bitcast.125, s32[32]{0:T(128)S(1)} %copy-done.4, f32[]{:T(128)} %bitcast.107), kind=kLoop, calls=%fused_computation.89 | loop fusion | flops 96 | bytes 388 | tf_op jit(solution)/shard_map/div | solution.py:125
  31.6 0.1 sub.63
  31.7 0.1 mul.130
  31.7 1.9 %bitcast_reduce_fusion.2 = (bf16[2,512]{1,0:T(2,128)(2,1)S(1)}, bf16[256,512]{1,0:T(8,128)(2,1)}) fusion(f32[256]{0:T(256)S(1)} %sub.63, f32[256,1024]{1,0:T(8,128)} %copy-done, f32[256]{0:T(256)S(1)} %mul.130), kind=kLoop, calls=%fused_computation.93 | loop fusion | flops 523264 | bytes 790528 | tf_op jit(solution)/shard_map/reduce_sum | solution.py:118
  33.7 0.1 mul.124
  33.8 0.1 sub.60
  33.8 0.2 bitcast_reduce_fusion.3
  34.1 0.6 %convert_reduce_fusion.1 = f32[512,768]{1,0:T(8,128)S(1)} fusion(bf16[2,128,512]{2,1,0:T(8,128)(2,1)S(1)} %bitcast.114, f32[2,128]{1,0:T(2,128)S(1)} %get-tuple-element.29, bf16[1,2,144,768]{3,2,1,0:T(8,128)(2,1)S(1)} %get-tuple-element.11), kind=kOutput, calls=%fused_computation.5 | convolution fusion | flops 203882496 | bytes 2229248 | tf_op jit(solution)/shard_map/dot_general | solution.py:114
  34.7 0.1 copy-done.2
  34.8 0.6 %convert_reduce_fusion = f32[512,768]{1,0:T(8,128)S(1)} fusion(bf16[2,128,512]{2,1,0:T(8,128)(2,1)S(1)} %bitcast.113, f32[2,128]{1,0:T(2,128)S(1)} %get-tuple-element.27, bf16[1,2,144,768]{3,2,1,0:T(8,128)(2,1)S(1)} %bitcast.112), kind=kOutput, calls=%fused_computation.4 | convolution fusion | flops 203882496 | bytes 2229248 | tf_op jit(solution)/shard_map/dot_general | solution.py:114
  35.4 0.5 %multiply_reduce_fusion = (f32[512]{0:T(512)S(1)}, f32[512,768]{1,0:T(8,128)S(1)}) fusion(f32[512]{0:T(512)S(1)} %add_add_fusion, bf16[1024,768]{1,0:T(8,128)(2,1)S(1)} %fusion.1, f32[512,768]{1,0:T(8,128)S(1)} %convert_reduce_fusion.1, f32[512,768]{1,0:T(8,128)S(1)} %convert_reduce_fusion), kind=kLoop, calls=%fused_computation.10 | loop fusion | flops 2358784 | bytes 5509120 | tf_op jit(solution)/shard_map/reduce_sum | solution.py:12
  36.0 1.4 %multiply_convert_fusion = bf16[512,768]{1,0:T(8,128)(2,1)} fusion(f32[512]{0:T(512)S(1)} %add_rsqrt_fusion.1, f32[512,768]{1,0:T(8,128)S(1)} %get-tuple-element.4, f32[512]{0:T(512)S(1)} %add_add_fusion, bf16[1024,768]{1,0:T(8,128)(2,1)S(1)} %fusion.1), kind=kLoop, calls=%fused_computation.9 | loop fusion | flops 1966080 | bytes 3149824 | tf_op jit(solution)/shard_map/convert_element_type | solution.py:122
  (40 shorter events, 0.5 us)
Async XLA Ops:
  0.6 8.9 %collective-permute-start = (bf16[32,768]{1,0:T(8,128)(2,1)}, bf16[32,768]{1,0:T(8,128)(2,1)S(1)}, u32[]{:S(2)}, u32[]{:S(2)}) collective-permute-start(bf16[32,768]{1,0:T(8,128)(2,1)} %param.4), channel_id=1, source_target_pairs={{0,4},{4,8},{8,12},{12,0},{1,5},{5,9},{9,13},{13,1},{2,6},{6,10},{... | collective-permute-start | bytes 147464 | tf_op jit(solution)/shard_map/ppermute | solution.py:23
  3.7 5.8 %collective-permute-start.2 = (bf16[32,768]{1,0:T(8,128)(2,1)}, bf16[32,768]{1,0:T(8,128)(2,1)S(1)}, u32[]{:S(2)}, u32[]{:S(2)}) collective-permute-start(bf16[32,768]{1,0:T(8,128)(2,1)} %param.4), channel_id=1, source_target_pairs={{0,12},{4,0},{8,4},{12,8},{1,13},{5,1},{9,5},{13,9},{2,14},{6,2},{... | collective-permute-start | bytes 147464 | tf_op jit(solution)/shard_map/ppermute | solution.py:23
  5.8 5.3 %collective-permute-start.1 = (bf16[32,768]{1,0:T(8,128)(2,1)}, bf16[32,768]{1,0:T(8,128)(2,1)S(1)}, u32[]{:S(2)}, u32[]{:S(2)}) collective-permute-start(bf16[32,768]{1,0:T(8,128)(2,1)} %param.4), channel_id=1, source_target_pairs={{0,8},{4,12},{8,0},{12,4},{1,9},{5,13},{9,1},{13,5},{2,10},{6,14},... | collective-permute-start | bytes 147464 | tf_op jit(solution)/shard_map/ppermute | solution.py:23
  8.2 0.7 %copy-start.4 = (s32[32]{0:T(128)S(1)}, s32[32]{0:T(128)}, u32[]{:S(2)}) copy-start(s32[32]{0:T(128)} %param.5) | copy-start | bytes 388
  8.2 2.9 %copy-start.3 = (bf16[32,768]{1,0:T(8,128)(2,1)S(1)}, bf16[32,768]{1,0:T(8,128)(2,1)}, u32[]{:S(2)}) copy-start(bf16[32,768]{1,0:T(8,128)(2,1)} %param.4) | copy-start | bytes 147460
  11.2 6.2 %collective-permute-start.3 = (bf16[144,768]{1,0:T(8,128)(2,1)S(1)}, bf16[144,768]{1,0:T(8,128)(2,1)S(1)}, u32[]{:S(2)}, u32[]{:S(2)}) collective-permute-start(bf16[144,768]{1,0:T(8,128)(2,1)S(1)} %get-tuple-element.14), channel_id=1, source_target_pairs={{0,2},{2,0},{1,3},{3,1},{4,6},{6,4},{5,7},{7,5},{8,10},{10,8},{9,1... | collective-permute-start | bytes 663560 | tf_op jit(solution)/shard_map/ppermute | solution.py:23
  17.7 1.9 %collective-permute-start.4 = (bf16[2,144,768]{2,1,0:T(8,128)(2,1)S(1)}, bf16[2,144,768]{2,1,0:T(8,128)(2,1)S(1)}, u32[]{:S(2)}, u32[]{:S(2)}) collective-permute-start(bf16[2,144,768]{2,1,0:T(8,128)(2,1)S(1)} %get-tuple-element.12), channel_id=1, source_target_pairs={{0,1},{1,0},{2,3},{3,2},{4,5},{5,4},{6,7},{7,6},{8,9},{9,8},{10,11... | collective-permute-start | bytes 1327112 | tf_op jit(solution)/shard_map/ppermute | solution.py:23
  20.6 1.0 %copy-start = (f32[256,1024]{1,0:T(8,128)}, f32[256,1024]{1,0:T(8,128)S(1)}, u32[]{:S(2)}) copy-start(f32[256,1024]{1,0:T(8,128)S(1)} %get-tuple-element.32) | copy-start | bytes 3145732
  22.2 4.9 %collective-permute-start.6 = (f32[3,2,2,4,32]{4,3,2,1,0:T(4,128)S(1)}, f32[3,2,2,4,32]{4,3,2,1,0:T(4,128)S(1)}, u32[]{:S(2)}, u32[]{:S(2)}) collective-permute-start(f32[3,2,2,4,32]{4,3,2,1,0:T(4,128)S(1)} %get-tuple-element.20), channel_id=1, source_target_pairs={{0,8},{4,12},{8,0},{12,4},{1,9},{5,13},{9,1},{13,5},{2,10},{6,14},... | collective-permute-start | bytes 18440 | tf_op jit(solution)/shard_map/ppermute | solution.py:23
  23.2 5.6 %collective-permute-start.5 = (f32[3,2,2,4,32]{4,3,2,1,0:T(4,128)S(1)}, f32[3,2,2,4,32]{4,3,2,1,0:T(4,128)S(1)}, u32[]{:S(2)}, u32[]{:S(2)}) collective-permute-start(f32[3,2,2,4,32]{4,3,2,1,0:T(4,128)S(1)} %get-tuple-element.20), channel_id=1, source_target_pairs={{0,4},{4,8},{8,12},{12,0},{1,5},{5,9},{9,13},{13,1},{2,6},{6,10},{... | collective-permute-start | bytes 18440 | tf_op jit(solution)/shard_map/ppermute | solution.py:23
  25.7 3.8 %collective-permute-start.7 = (f32[3,2,2,4,32]{4,3,2,1,0:T(4,128)S(1)}, f32[3,2,2,4,32]{4,3,2,1,0:T(4,128)S(1)}, u32[]{:S(2)}, u32[]{:S(2)}) collective-permute-start(f32[3,2,2,4,32]{4,3,2,1,0:T(4,128)S(1)} %get-tuple-element.20), channel_id=1, source_target_pairs={{0,12},{4,0},{8,4},{12,8},{1,13},{5,1},{9,5},{13,9},{2,14},{6,2},{... | collective-permute-start | bytes 18440 | tf_op jit(solution)/shard_map/ppermute | solution.py:23
  29.7 1.3 %collective-permute-start.8 = (f32[3,2,2,4,32]{4,3,2,1,0:T(4,128)S(1)}, f32[3,2,2,4,32]{4,3,2,1,0:T(4,128)S(1)}, u32[]{:S(2)}, u32[]{:S(2)}) collective-permute-start(f32[3,2,2,4,32]{4,3,2,1,0:T(4,128)S(1)} %get-tuple-element.16), channel_id=1, source_target_pairs={{0,1},{1,0},{2,3},{3,2},{4,5},{5,4},{6,7},{7,6},{8,9},{9,8},{10,11... | collective-permute-start | bytes 18440 | tf_op jit(solution)/shard_map/ppermute | solution.py:23
  33.8 1.0 %copy-start.2 = (bf16[256,512]{1,0:T(8,128)(2,1)S(1)}, bf16[256,512]{1,0:T(8,128)(2,1)}, u32[]{:S(2)}) copy-start(bf16[256,512]{1,0:T(8,128)(2,1)} %get-tuple-element.6) | copy-start | bytes 786436
  35.9 1.4 %copy-start.1 = (f32[512,768]{1,0:T(8,128)}, f32[512,768]{1,0:T(8,128)S(1)}, u32[]{:S(2)}) copy-start(f32[512,768]{1,0:T(8,128)S(1)} %get-tuple-element.4) | copy-start | bytes 4718596

commit v16 on v10

--- a/solution.py
+++ b/solution.py
@@ -126,7 +126,7 @@
         weight_mass = jnp.sum(grouped_resp.astype(jnp.float32), axis=1).astype(jnp.bfloat16)
         own_mass = own_mass + jnp.sum(weight_mass.astype(jnp.float32), axis=0)
 
-    moved = own_cents.astype(jnp.float32) + centroid_sums / (own_mass + 1.0)[:, None]
+    moved = lax.optimization_barrier(own_cents.astype(jnp.float32) + centroid_sums / (own_mass + 1.0)[:, None])
     renormed = normalize(moved).astype(jnp.bfloat16)
 
     own_log_sum = log_sum.reshape(block_shape)[own_block("sub"), own_block("dp"), own_cent]

time: 34.9 us -> 35.7 us (1.023)
  other arithmetic: 7.94 us -> 8.8 us
    add x0 -> x1, other arithmetic: none -> 1.5 us  [shards(): own_cents.astype(jnp.float32) + centroid_sums / (own_mass + 1.0)[:, None]]
where the time goes in v16:
time: 35.7 us; the launch traced here: 35.5 us
  starting transfers between devices  12.4 us (35%)
  waiting for transfers between devices  9 us (25%)
  other arithmetic  8.8 us (25%)
  matrix products  3.24 us (9%)
  between operations  1.59 us (4%)
  local copies, waits for them, and re-layouts  0.54 us (2%)
    ppermute x9, starting transfers between devices, gather_stage(): lax.ppermute(value, name, [(j, (j + q) % size) for j in range(size)])  12.4 us
    ppermute x9, waiting for transfers between devices, gather_stage(): lax.ppermute(value, name, [(j, (j + q) % size) for j in range(size)])  9 us
    reduce_sum x4, other arithmetic, normalize(): jnp.sum(floats * floats, axis=-1, keepdims=True) + 1e-06  2.24 us
    dot_general x4, matrix products, shards(): lax.dot_general(rows, cents, (((1,), (1,)), ((), ())), preferred_element_...  1.94 us
    convert_element_type x1, other arithmetic, shards(): score_cents = [lax.optimization_barrier(normalize(lax.dynamic_slice_in_di...  1.69 us
    add x1, other arithmetic, shards(): own_cents.astype(jnp.float32) + centroid_sums / (own_mass + 1.0)[:, None]  1.5 us
    dot_general x2, matrix products, shards(): lax.dot_general(grouped_resp, grouped_rows, (((1,), (1,)), ((0,), (0,))),...  1.3 us
    convert_element_type x1, other arithmetic, shards(): renormed = normalize(moved).astype(jnp.bfloat16)  1.04 us
  transfers between devices with their start and end apart: 9, of which 7 were waited for; matrix products, arithmetic and copies ran while one was open for 14% of the time, Pallas kernels for 0%

profile of v16, /device:TPU:0, one launch (start us, length us, event | category | flops | bytes accessed | tf_op | source)
XLA Modules:
  0.0 35.5 jit_solution(13564234156148248873)
XLA Ops:
  0.6 3.1 %collective-permute-start = (bf16[32,768]{1,0:T(8,128)(2,1)}, bf16[32,768]{1,0:T(8,128)(2,1)S(1)}, u32[]{:S(2)}, u32[]{:S(2)}) collective-permute-start(bf16[32,768]{1,0:T(8,128)(2,1)} %param.4), channel_id=1, source_target_pairs={{0,4},{4,8},{8,12},{12,0},{1,5},{5,9},{9,13},{13,1},{2,6},{6,10},{... | collective-permute-start | bytes 147464 | tf_op jit(solution)/shard_map/ppermute | solution.py:23
  3.7 2.1 %collective-permute-start.2 = (bf16[32,768]{1,0:T(8,128)(2,1)}, bf16[32,768]{1,0:T(8,128)(2,1)S(1)}, u32[]{:S(2)}, u32[]{:S(2)}) collective-permute-start(bf16[32,768]{1,0:T(8,128)(2,1)} %param.4), channel_id=1, source_target_pairs={{0,12},{4,0},{8,4},{12,8},{1,13},{5,1},{9,5},{13,9},{2,14},{6,2},{... | collective-permute-start | bytes 147464 | tf_op jit(solution)/shard_map/ppermute | solution.py:23
  5.8 0.9 %collective-permute-start.1 = (bf16[32,768]{1,0:T(8,128)(2,1)}, bf16[32,768]{1,0:T(8,128)(2,1)S(1)}, u32[]{:S(2)}, u32[]{:S(2)}) collective-permute-start(bf16[32,768]{1,0:T(8,128)(2,1)} %param.4), channel_id=1, source_target_pairs={{0,8},{4,12},{8,0},{12,4},{1,9},{5,13},{9,1},{13,5},{2,10},{6,14},... | collective-permute-start | bytes 147464 | tf_op jit(solution)/shard_map/ppermute | solution.py:23
  6.8 1.7 %fusion.2 = (f32[512]{0:T(512)S(1)}, f32[512]{0:T(512)S(1)}) fusion(bf16[2048,768]{1,0:T(8,128)(2,1)} %param.6, s32[]{:T(128)S(6)} %select_n.20, s32[]{:T(128)S(6)} %select_n.18), kind=kLoop, calls=%fused_computation.10 | loop fusion | flops 2358272 | bytes 1576968 | tf_op jit(solution)/shard_map/reduce_sum | solution.py:12
  8.5 0.0 copy-done.1
  9.2 0.0 collective-permute-done
  9.2 0.0 collective-permute-done.2
  9.2 1.9 %collective-permute-done.1 = bf16[32,768]{1,0:T(8,128)(2,1)S(1)} collective-permute-done((bf16[32,768]{1,0:T(8,128)(2,1)}, bf16[32,768]{1,0:T(8,128)(2,1)S(1)}, u32[]{:S(2)}, u32[]{:S(2)}) %collective-permute-start.1) | collective-permute-done | bytes 49184 | tf_op jit(solution)/shard_map/ppermute | solution.py:23
  11.2 1.6 %collective-permute-start.3 = (bf16[144,768]{1,0:T(8,128)(2,1)S(1)}, bf16[144,768]{1,0:T(8,128)(2,1)S(1)}, u32[]{:S(2)}, u32[]{:S(2)}) collective-permute-start(bf16[144,768]{1,0:T(8,128)(2,1)S(1)} %get-tuple-element.20), channel_id=1, source_target_pairs={{0,2},{2,0},{1,3},{3,1},{4,6},{6,4},{5,7},{7,5},{8,10},{10,8},{9,1... | collective-permute-start | bytes 663560 | tf_op jit(solution)/shard_map/ppermute | solution.py:23
  12.8 1.7 %fusion.3 = (bf16[512,768]{1,0:T(8,128)(2,1)S(1)}, bf16[512,768]{1,0:T(8,128)(2,1)S(1)}) fusion(f32[512]{0:T(512)S(1)} %get-tuple-element.45, bf16[2048,768]{1,0:T(8,128)(2,1)} %param.6, s32[]{:T(128)S(6)} %select_n.20, f32[512]{0:T(512)S(1)} %get-tuple-element.46, s32[]{:T(128)S(6)} %select_n.18), kind=kLoop, calls=%fused_computation.11 | loop fusion | flops 2359296 | bytes 3149832 | tf_op jit(solution)/shard_map/convert_element_type | solution.py:76
  14.5 2.9 %collective-permute-done.3 = bf16[144,768]{1,0:T(8,128)(2,1)S(1)} collective-permute-done((bf16[144,768]{1,0:T(8,128)(2,1)S(1)}, bf16[144,768]{1,0:T(8,128)(2,1)S(1)}, u32[]{:S(2)}, u32[]{:S(2)}) %collective-permute-start.3) | collective-permute-done | bytes 221216 | tf_op jit(solution)/shard_map/ppermute | solution.py:23
  17.4 0.1 pad_maximum_fusion
  17.5 0.2 multiply_reduce_fusion.2
  17.6 0.1 slice_convert_fusion.1
  17.7 0.1 collective-permute-start.4
  17.8 0.1 fusion.7
  17.9 0.5 %fusion.44 = (f32[256]{0:T(256)S(1)}, f32[256,512]{1,0:T(8,128)S(1)}) fusion(f32[]{:T(128)} %bitcast.114, bf16[256,768]{1,0:T(8,128)(2,1)S(1)} %fusion.7, bf16[512,768]{1,0:T(8,128)(2,1)S(1)} %get-tuple-element.15), kind=kOutput, calls=%fused_computation.108 | convolution fusion | flops 201588480 | bytes 1704964 | tf_op jit(solution)/shard_map/dot_general | solution.py:87
  18.4 0.5 %fusion.43 = (f32[256]{0:T(256)S(1)}, f32[256,512]{1,0:T(8,128)S(1)}) fusion(f32[]{:T(128)} %bitcast.110, bf16[256,768]{1,0:T(8,128)(2,1)S(1)} %fusion.7, bf16[512,768]{1,0:T(8,128)(2,1)S(1)} %get-tuple-element.16), kind=kOutput, calls=%fused_computation.107 | convolution fusion | flops 201588480 | bytes 1704964 | tf_op jit(solution)/shard_map/dot_general | solution.py:87
  18.9 0.3 exponential_reduce_fusion.2
  19.2 0.4 %collective-permute-done.4 = bf16[2,144,768]{2,1,0:T(8,128)(2,1)S(1)} collective-permute-done((bf16[2,144,768]{2,1,0:T(8,128)(2,1)S(1)}, bf16[2,144,768]{2,1,0:T(8,128)(2,1)S(1)}, u32[]{:S(2)}, u32[]{:S(2)}) %collective-permute-start.4) | collective-permute-done | bytes 442400 | tf_op jit(solution)/shard_map/ppermute | solution.py:23
  19.5 0.2 multiply_reduce_fusion.1
  19.7 0.1 slice_convert_fusion
  19.8 0.1 fusion.6
  19.9 0.5 %fusion.42 = (f32[256]{0:T(256)S(1)}, f32[256,512]{1,0:T(8,128)S(1)}) fusion(f32[]{:T(128)} %bitcast.112, bf16[256,768]{1,0:T(8,128)(2,1)S(1)} %fusion.6, bf16[512,768]{1,0:T(8,128)(2,1)S(1)} %get-tuple-element.15), kind=kOutput, calls=%fused_computation.106 | convolution fusion | flops 201588480 | bytes 1704964 | tf_op jit(solution)/shard_map/dot_general | solution.py:87
  20.4 0.5 %fusion.41 = (f32[256]{0:T(256)S(1)}, f32[256,512]{1,0:T(8,128)S(1)}) fusion(f32[]{:T(128)} %bitcast.113, bf16[256,768]{1,0:T(8,128)(2,1)S(1)} %fusion.6, bf16[512,768]{1,0:T(8,128)(2,1)S(1)} %get-tuple-element.16), kind=kOutput, calls=%fused_computation.105 | convolution fusion | flops 201588480 | bytes 1704964 | tf_op jit(solution)/shard_map/dot_general | solution.py:87
  20.9 0.3 exponential_reduce_fusion
  21.2 0.1 stack_reshape.7
  21.3 0.1 stack_reshape.6
  21.4 0.7 %collective-permute-start.6 = (f32[3,2,2,4,32]{4,3,2,1,0:T(4,128)S(1)}, f32[3,2,2,4,32]{4,3,2,1,0:T(4,128)S(1)}, u32[]{:S(2)}, u32[]{:S(2)}) collective-permute-start(f32[3,2,2,4,32]{4,3,2,1,0:T(4,128)S(1)} %get-tuple-element.26), channel_id=1, source_target_pairs={{0,8},{4,12},{8,0},{12,4},{1,9},{5,13},{9,1},{13,5},{2,10},{6,14},... | collective-permute-start | bytes 18440 | tf_op jit(solution)/shard_map/ppermute | solution.py:23
  22.1 2.7 %collective-permute-start.5 = (f32[3,2,2,4,32]{4,3,2,1,0:T(4,128)S(1)}, f32[3,2,2,4,32]{4,3,2,1,0:T(4,128)S(1)}, u32[]{:S(2)}, u32[]{:S(2)}) collective-permute-start(f32[3,2,2,4,32]{4,3,2,1,0:T(4,128)S(1)} %get-tuple-element.26), channel_id=1, source_target_pairs={{0,4},{4,8},{8,12},{12,0},{1,5},{5,9},{9,13},{13,1},{2,6},{6,10},{... | collective-permute-start | bytes 18440 | tf_op jit(solution)/shard_map/ppermute | solution.py:23
  24.8 1.1 %collective-permute-start.7 = (f32[3,2,2,4,32]{4,3,2,1,0:T(4,128)S(1)}, f32[3,2,2,4,32]{4,3,2,1,0:T(4,128)S(1)}, u32[]{:S(2)}, u32[]{:S(2)}) collective-permute-start(f32[3,2,2,4,32]{4,3,2,1,0:T(4,128)S(1)} %get-tuple-element.26), channel_id=1, source_target_pairs={{0,12},{4,0},{8,4},{12,8},{1,13},{5,1},{9,5},{13,9},{2,14},{6,2},{... | collective-permute-start | bytes 18440 | tf_op jit(solution)/shard_map/ppermute | solution.py:23
  26.0 0.4 %collective-permute-done.6 = f32[3,2,2,4,32]{4,3,2,1,0:T(4,128)S(1)} collective-permute-done((f32[3,2,2,4,32]{4,3,2,1,0:T(4,128)S(1)}, f32[3,2,2,4,32]{4,3,2,1,0:T(4,128)S(1)}, u32[]{:S(2)}, u32[]{:S(2)}) %collective-permute-start.6) | collective-permute-done | bytes 6176 | tf_op jit(solution)/shard_map/ppermute | solution.py:23
  26.4 1.4 %collective-permute-done.5 = f32[3,2,2,4,32]{4,3,2,1,0:T(4,128)S(1)} collective-permute-done((f32[3,2,2,4,32]{4,3,2,1,0:T(4,128)S(1)}, f32[3,2,2,4,32]{4,3,2,1,0:T(4,128)S(1)}, u32[]{:S(2)}, u32[]{:S(2)}) %collective-permute-start.5) | collective-permute-done | bytes 6176 | tf_op jit(solution)/shard_map/ppermute | solution.py:23
  27.8 0.9 %collective-permute-done.7 = f32[3,2,2,4,32]{4,3,2,1,0:T(4,128)S(1)} collective-permute-done((f32[3,2,2,4,32]{4,3,2,1,0:T(4,128)S(1)}, f32[3,2,2,4,32]{4,3,2,1,0:T(4,128)S(1)}, u32[]{:S(2)}, u32[]{:S(2)}) %collective-permute-start.7) | collective-permute-done | bytes 6176 | tf_op jit(solution)/shard_map/ppermute | solution.py:23
  28.8 0.1 collective-permute-start.8
  28.9 1.2 %collective-permute-done.8 = f32[3,2,2,4,32]{4,3,2,1,0:T(4,128)S(1)} collective-permute-done((f32[3,2,2,4,32]{4,3,2,1,0:T(4,128)S(1)}, f32[3,2,2,4,32]{4,3,2,1,0:T(4,128)S(1)}, u32[]{:S(2)}, u32[]{:S(2)}) %collective-permute-start.8) | collective-permute-done | bytes 6176 | tf_op jit(solution)/shard_map/ppermute | solution.py:23
  30.2 0.5 %fusion.30 = f32[32]{0:T(128)} fusion(f32[2,2,4,32]{3,2,1,0:T(4,128)S(1)} %bitcast.131, s32[32]{0:T(128)S(1)} %copy-done.1, f32[]{:T(128)} %bitcast.111), kind=kLoop, calls=%fused_computation.91 | loop fusion | flops 96 | bytes 388 | tf_op jit(solution)/shard_map/div | solution.py:133
  30.7 0.1 sub.77
  30.8 0.1 mul.154
  30.9 0.2 bitcast_reduce_fusion.2
  31.1 0.1 mul.148
  31.2 0.1 sub.74
  31.3 0.2 bitcast_reduce_fusion.3
  31.5 0.6 %convert_reduce_fusion.1 = f32[512,768]{1,0:T(8,128)S(1)} fusion(bf16[2,128,512]{2,1,0:T(8,128)(2,1)S(1)} %bitcast.120, f32[2,128]{1,0:T(2,128)S(1)} %get-tuple-element.35, bf16[1,2,144,768]{3,2,1,0:T(8,128)(2,1)S(1)} %get-tuple-element.18), kind=kOutput, calls=%fused_computation.1 | convolution fusion | flops 203882496 | bytes 2229248 | tf_op jit(solution)/shard_map/dot_general | solution.py:122
  32.2 0.6 %convert_reduce_fusion = f32[512,768]{1,0:T(8,128)S(1)} fusion(bf16[2,128,512]{2,1,0:T(8,128)(2,1)S(1)} %bitcast.119, f32[2,128]{1,0:T(2,128)S(1)} %get-tuple-element.33, bf16[1,2,144,768]{3,2,1,0:T(8,128)(2,1)S(1)} %bitcast.118), kind=kOutput, calls=%fused_computation | convolution fusion | flops 203882496 | bytes 2229248 | tf_op jit(solution)/shard_map/dot_general | solution.py:122
  32.8 1.5 %divide_add_fusion = (f32[512,768]{1,0:T(8,128)S(1)}, f32[512,768]{1,0:T(8,128)}) fusion(bf16[512,768]{1,0:T(8,128)(2,1)S(1)} %get-tuple-element.16, f32[512]{0:T(512)S(1)} %add_add_fusion, f32[512,768]{1,0:T(8,128)S(1)} %convert_reduce_fusion.1, f32[512,768]{1,0:T(8,128)S(1)} %convert_reduce_fusion), kind=kLoop, calls=%fused_computation.14 | loop fusion | flops 1572864 | bytes 7079936 | tf_op jit(solution)/shard_map/add | solution.py:129
  34.3 0.2 multiply_reduce_fusion
  34.5 1.0 %multiply_convert_fusion = bf16[512,768]{1,0:T(8,128)(2,1)} fusion(f32[512,768]{1,0:T(8,128)S(1)} %get-tuple-element.9, f32[512]{0:T(512)S(1)} %add_rsqrt_fusion), kind=kLoop, calls=%fused_computation.12 | loop fusion | flops 786432 | bytes 2361344 | tf_op jit(solution)/shard_map/convert_element_type | solution.py:130
  (41 shorter events, 0.5 us)
Async XLA Ops:
  0.6 10.5 %copy-start = (bf16[32,768]{1,0:T(8,128)(2,1)S(1)}, bf16[32,768]{1,0:T(8,128)(2,1)}, u32[]{:S(2)}) copy-start(bf16[32,768]{1,0:T(8,128)(2,1)} %param.4) | copy-start | bytes 147460
  0.6 7.9 %copy-start.1 = (s32[32]{0:T(128)S(1)}, s32[32]{0:T(128)}, u32[]{:S(2)}) copy-start(s32[32]{0:T(128)} %param.5) | copy-start | bytes 388
  0.6 8.6 %collective-permute-start = (bf16[32,768]{1,0:T(8,128)(2,1)}, bf16[32,768]{1,0:T(8,128)(2,1)S(1)}, u32[]{:S(2)}, u32[]{:S(2)}) collective-permute-start(bf16[32,768]{1,0:T(8,128)(2,1)} %param.4), channel_id=1, source_target_pairs={{0,4},{4,8},{8,12},{12,0},{1,5},{5,9},{9,13},{13,1},{2,6},{6,10},{... | collective-permute-start | bytes 147464 | tf_op jit(solution)/shard_map/ppermute | solution.py:23
  3.7 5.5 %collective-permute-start.2 = (bf16[32,768]{1,0:T(8,128)(2,1)}, bf16[32,768]{1,0:T(8,128)(2,1)S(1)}, u32[]{:S(2)}, u32[]{:S(2)}) collective-permute-start(bf16[32,768]{1,0:T(8,128)(2,1)} %param.4), channel_id=1, source_target_pairs={{0,12},{4,0},{8,4},{12,8},{1,13},{5,1},{9,5},{13,9},{2,14},{6,2},{... | collective-permute-start | bytes 147464 | tf_op jit(solution)/shard_map/ppermute | solution.py:23
  5.8 5.3 %collective-permute-start.1 = (bf16[32,768]{1,0:T(8,128)(2,1)}, bf16[32,768]{1,0:T(8,128)(2,1)S(1)}, u32[]{:S(2)}, u32[]{:S(2)}) collective-permute-start(bf16[32,768]{1,0:T(8,128)(2,1)} %param.4), channel_id=1, source_target_pairs={{0,8},{4,12},{8,0},{12,4},{1,9},{5,13},{9,1},{13,5},{2,10},{6,14},... | collective-permute-start | bytes 147464 | tf_op jit(solution)/shard_map/ppermute | solution.py:23
  11.2 6.2 %collective-permute-start.3 = (bf16[144,768]{1,0:T(8,128)(2,1)S(1)}, bf16[144,768]{1,0:T(8,128)(2,1)S(1)}, u32[]{:S(2)}, u32[]{:S(2)}) collective-permute-start(bf16[144,768]{1,0:T(8,128)(2,1)S(1)} %get-tuple-element.20), channel_id=1, source_target_pairs={{0,2},{2,0},{1,3},{3,1},{4,6},{6,4},{5,7},{7,5},{8,10},{10,8},{9,1... | collective-permute-start | bytes 663560 | tf_op jit(solution)/shard_map/ppermute | solution.py:23
  17.7 1.9 %collective-permute-start.4 = (bf16[2,144,768]{2,1,0:T(8,128)(2,1)S(1)}, bf16[2,144,768]{2,1,0:T(8,128)(2,1)S(1)}, u32[]{:S(2)}, u32[]{:S(2)}) collective-permute-start(bf16[2,144,768]{2,1,0:T(8,128)(2,1)S(1)} %get-tuple-element.17), channel_id=1, source_target_pairs={{0,1},{1,0},{2,3},{3,2},{4,5},{5,4},{6,7},{7,6},{8,9},{9,8},{10,11... | collective-permute-start | bytes 1327112 | tf_op jit(solution)/shard_map/ppermute | solution.py:23
  21.4 4.9 %collective-permute-start.6 = (f32[3,2,2,4,32]{4,3,2,1,0:T(4,128)S(1)}, f32[3,2,2,4,32]{4,3,2,1,0:T(4,128)S(1)}, u32[]{:S(2)}, u32[]{:S(2)}) collective-permute-start(f32[3,2,2,4,32]{4,3,2,1,0:T(4,128)S(1)} %get-tuple-element.26), channel_id=1, source_target_pairs={{0,8},{4,12},{8,0},{12,4},{1,9},{5,13},{9,1},{13,5},{2,10},{6,14},... | collective-permute-start | bytes 18440 | tf_op jit(solution)/shard_map/ppermute | solution.py:23
  22.1 5.6 %collective-permute-start.5 = (f32[3,2,2,4,32]{4,3,2,1,0:T(4,128)S(1)}, f32[3,2,2,4,32]{4,3,2,1,0:T(4,128)S(1)}, u32[]{:S(2)}, u32[]{:S(2)}) collective-permute-start(f32[3,2,2,4,32]{4,3,2,1,0:T(4,128)S(1)} %get-tuple-element.26), channel_id=1, source_target_pairs={{0,4},{4,8},{8,12},{12,0},{1,5},{5,9},{9,13},{13,1},{2,6},{6,10},{... | collective-permute-start | bytes 18440 | tf_op jit(solution)/shard_map/ppermute | solution.py:23
  24.8 3.8 %collective-permute-start.7 = (f32[3,2,2,4,32]{4,3,2,1,0:T(4,128)S(1)}, f32[3,2,2,4,32]{4,3,2,1,0:T(4,128)S(1)}, u32[]{:S(2)}, u32[]{:S(2)}) collective-permute-start(f32[3,2,2,4,32]{4,3,2,1,0:T(4,128)S(1)} %get-tuple-element.26), channel_id=1, source_target_pairs={{0,12},{4,0},{8,4},{12,8},{1,13},{5,1},{9,5},{13,9},{2,14},{6,2},{... | collective-permute-start | bytes 18440 | tf_op jit(solution)/shard_map/ppermute | solution.py:23
  28.8 1.3 %collective-permute-start.8 = (f32[3,2,2,4,32]{4,3,2,1,0:T(4,128)S(1)}, f32[3,2,2,4,32]{4,3,2,1,0:T(4,128)S(1)}, u32[]{:S(2)}, u32[]{:S(2)}) collective-permute-start(f32[3,2,2,4,32]{4,3,2,1,0:T(4,128)S(1)} %get-tuple-element.22), channel_id=1, source_target_pairs={{0,1},{1,0},{2,3},{3,2},{4,5},{5,4},{6,7},{7,6},{8,9},{9,8},{10,11... | collective-permute-start | bytes 18440 | tf_op jit(solution)/shard_map/ppermute | solution.py:23

commit v17 on v11

--- a/solution.py
+++ b/solution.py
@@ -1,5 +1,4 @@
 import jax
-import numpy as np
 import jax.numpy as jnp
 from jax import lax
 from jax.sharding import PartitionSpec as P
@@ -36,7 +35,14 @@
 def align(received, step, size, axis):
     if size & (size - 1):
         return jnp.roll(received, step, axis=axis)
-    return jnp.take(received, np.array([p ^ step for p in range(size)]), axis=axis)
+    shape = received.shape
+    bit = 1
+    while bit < size:
+        if step & bit:
+            split = shape[:axis] + (size // (2 * bit), 2, bit) + shape[axis + 1:]
+            received = jnp.flip(received.reshape(split), axis=axis + 1).reshape(shape)
+        bit *= 2
+    return received
 
 
 def own_block(name):
@@ -142,8 +148,8 @@
     moved = own_cents.astype(jnp.float32) + centroid_sums / (own_mass + 1.0)[:, None]
     renormed = normalize(moved).astype(jnp.bfloat16)
 
-    own_rows = (own_block("sub"), own_block("dp"), own_cent)
-    objective = (weight_float.reshape(block_shape)[own_rows] * log_sum.reshape(block_shape)[own_rows]) / sharpness
+    own_log_sum = log_sum.reshape(block_shape)[own_block("sub"), own_block("dp"), own_cent]
+    objective = weights.astype(jnp.float32) * own_log_sum / sharpness
     return (centroid_sums, renormed, objective)
 
 

time: 45.3 us -> 37.3 us (0.82)
  other arithmetic: 16.1 us -> 7.88 us
  waiting for transfers between devices: 7.29 us -> 11.9 us
  local copies, waits for them, and re-layouts: 4.96 us -> 0.66 us
    ppermute x9, waiting for transfers between devices: 7.29 us -> 11.9 us  [gather_stage(): lax.ppermute(value, name, [(j, partner(j, q, size)) for j in range(size)])]
    gather x6 -> x0, local copies, waits for them, and re-layouts: 3.49 us -> none  [align(): jnp.take(received, np.array([p ^ step for p in range(size)]), axis=axis)]
    another operation x4 -> x5, other arithmetic: 2.84 us -> 0.14 us  [gather_stage(): return jnp.stack(parts)]
    gather x6 -> x0, other arithmetic: 2 us -> none
    convert_element_type x4 -> x2, other arithmetic: 1.74 us -> 0.22 us  [shards(): normalize(payload[half, :, :cent_rows].reshape(-1, width))]
    another operation x4 -> x1, local copies, waits for them, and re-layouts: 0.69 us -> 0.01 us  [merge_stats(): jnp.stack([align(stacked[q], q, size, block_axis[name]) for q in range(si...]
    broadcast_in_dim x1, other arithmetic: 0.66 us -> 0.01 us  [shards(): weights.astype(jnp.bfloat16)[None, :]]
    reduce_sum x4, other arithmetic: 3.19 us -> 2.55 us  [normalize(): jnp.sum(floats * floats, axis=-1, keepdims=True) + 1e-06]
  transfers between devices with their start and end apart: 9 -> 9, of which waited for: 5 -> 8; matrix products, arithmetic and copies ran while one was open for 24% -> 13% of each run, Pallas kernels for 0% -> 0%
where the time goes in v17:
time: 37.3 us; the launch traced here: 37.1 us
  waiting for transfers between devices  11.9 us (32%)
  starting transfers between devices  11.8 us (32%)
  other arithmetic  7.88 us (21%)
  matrix products  3.23 us (9%)
  between operations  1.57 us (4%)
  local copies, waits for them, and re-layouts  0.66 us (2%)
    ppermute x9, waiting for transfers between devices, gather_stage(): lax.ppermute(value, name, [(j, partner(j, q, size)) for j in range(size)])  11.9 us
    ppermute x9, starting transfers between devices, gather_stage(): lax.ppermute(value, name, [(j, partner(j, q, size)) for j in range(size)])  11.8 us
    reduce_sum x4, other arithmetic, normalize(): jnp.sum(floats * floats, axis=-1, keepdims=True) + 1e-06  2.55 us
    dot_general x4, matrix products, shards(): lax.dot_general(rows, cents, (((1,), (1,)), ((), ())), preferred_element_...  1.94 us
    convert_element_type x1, other arithmetic, shards(): score_cents = [lax.optimization_barrier(normalize(lax.dynamic_slice_in_di...  1.69 us
    convert_element_type x1, other arithmetic, shards(): renormed = normalize(moved).astype(jnp.bfloat16)  1.38 us
    dot_general x2, matrix products, shards(): lax.dot_general(grouped_resp, grouped_rows, (((1,), (1,)), ((0,), (0,))),...  1.29 us
  transfers between devices with their start and end apart: 9, of which 8 were waited for; matrix products, arithmetic and copies ran while one was open for 13% of the time, Pallas kernels for 0%

profile of v17, /device:TPU:0, one launch (start us, length us, event | category | flops | bytes accessed | tf_op | source)
XLA Modules:
  0.0 37.1 jit_solution(8051509650957604070)
XLA Ops:
  0.6 3.1 %collective-permute-start = (bf16[32,768]{1,0:T(8,128)(2,1)}, bf16[32,768]{1,0:T(8,128)(2,1)S(1)}, u32[]{:S(2)}, u32[]{:S(2)}) collective-permute-start(bf16[32,768]{1,0:T(8,128)(2,1)} %param.4), channel_id=1, source_target_pairs={{0,4},{4,0},{8,12},{12,8},{1,5},{5,1},{9,13},{13,9},{2,6},{6,2},{1... | collective-permute-start | bytes 147464 | tf_op jit(solution)/shard_map/ppermute | solution.py:29
  3.7 2.5 %collective-permute-start.2 = (bf16[32,768]{1,0:T(8,128)(2,1)}, bf16[32,768]{1,0:T(8,128)(2,1)S(1)}, u32[]{:S(2)}, u32[]{:S(2)}) collective-permute-start(bf16[32,768]{1,0:T(8,128)(2,1)} %param.4), channel_id=1, source_target_pairs={{0,12},{4,8},{8,4},{12,0},{1,13},{5,9},{9,5},{13,1},{2,14},{6,10},... | collective-permute-start | bytes 147464 | tf_op jit(solution)/shard_map/ppermute | solution.py:29
  6.2 0.1 collective-permute-start.1
  6.3 1.7 %fusion.2 = (f32[512]{0:T(512)S(1)}, f32[512]{0:T(512)S(1)}) fusion(bf16[2048,768]{1,0:T(8,128)(2,1)} %param.6, s32[]{:T(128)S(6)} %select_n.20, s32[]{:T(128)S(6)} %select_n.18), kind=kLoop, calls=%fused_computation.10 | loop fusion | flops 2358272 | bytes 1576968 | tf_op jit(solution)/shard_map/reduce_sum | solution.py:12
  8.8 0.0 collective-permute-done
  8.8 1.7 %collective-permute-done.2 = bf16[32,768]{1,0:T(8,128)(2,1)S(1)} collective-permute-done((bf16[32,768]{1,0:T(8,128)(2,1)}, bf16[32,768]{1,0:T(8,128)(2,1)S(1)}, u32[]{:S(2)}, u32[]{:S(2)}) %collective-permute-start.2) | collective-permute-done | bytes 49184 | tf_op jit(solution)/shard_map/ppermute | solution.py:29
  10.5 1.5 %collective-permute-done.1 = bf16[32,768]{1,0:T(8,128)(2,1)S(1)} collective-permute-done((bf16[32,768]{1,0:T(8,128)(2,1)}, bf16[32,768]{1,0:T(8,128)(2,1)S(1)}, u32[]{:S(2)}, u32[]{:S(2)}) %collective-permute-start.1) | collective-permute-done | bytes 49184 | tf_op jit(solution)/shard_map/ppermute | solution.py:29
  12.0 1.6 %collective-permute-start.3 = (bf16[144,768]{1,0:T(8,128)(2,1)S(1)}, bf16[144,768]{1,0:T(8,128)(2,1)S(1)}, u32[]{:S(2)}, u32[]{:S(2)}) collective-permute-start(bf16[144,768]{1,0:T(8,128)(2,1)S(1)} %get-tuple-element.20), channel_id=1, source_target_pairs={{0,2},{2,0},{1,3},{3,1},{4,6},{6,4},{5,7},{7,5},{8,10},{10,8},{9,1... | collective-permute-start | bytes 663560 | tf_op jit(solution)/shard_map/ppermute | solution.py:29
  13.6 1.7 %fusion.3 = (bf16[512,768]{1,0:T(8,128)(2,1)S(1)}, bf16[512,768]{1,0:T(8,128)(2,1)S(1)}) fusion(f32[512]{0:T(512)S(1)} %get-tuple-element.41, bf16[2048,768]{1,0:T(8,128)(2,1)} %param.6, s32[]{:T(128)S(6)} %select_n.20, f32[512]{0:T(512)S(1)} %get-tuple-element.42, s32[]{:T(128)S(6)} %select_n.18), kind=kLoop, calls=%fused_computation.11 | loop fusion | flops 2359296 | bytes 3149832 | tf_op jit(solution)/shard_map/convert_element_type | solution.py:95
  15.3 2.8 %collective-permute-done.3 = bf16[144,768]{1,0:T(8,128)(2,1)S(1)} collective-permute-done((bf16[144,768]{1,0:T(8,128)(2,1)S(1)}, bf16[144,768]{1,0:T(8,128)(2,1)S(1)}, u32[]{:S(2)}, u32[]{:S(2)}) %collective-permute-start.3) | collective-permute-done | bytes 221216 | tf_op jit(solution)/shard_map/ppermute | solution.py:29
  18.1 0.1 pad_maximum_fusion
  18.1 0.2 multiply_reduce_fusion.2
  18.3 0.1 slice_convert_fusion.1
  18.4 0.1 collective-permute-start.4
  18.4 0.1 fusion.7
  18.6 0.5 %fusion.42 = (f32[256]{0:T(256)S(1)}, f32[256,512]{1,0:T(8,128)S(1)}) fusion(f32[]{:T(128)} %bitcast.114, bf16[256,768]{1,0:T(8,128)(2,1)S(1)} %fusion.7, bf16[512,768]{1,0:T(8,128)(2,1)S(1)} %get-tuple-element.15), kind=kOutput, calls=%fused_computation.103 | convolution fusion | flops 201588480 | bytes 1704964 | tf_op jit(solution)/shard_map/dot_general | solution.py:106
  19.0 0.5 %fusion.41 = (f32[256]{0:T(256)S(1)}, f32[256,512]{1,0:T(8,128)S(1)}) fusion(f32[]{:T(128)} %bitcast.110, bf16[256,768]{1,0:T(8,128)(2,1)S(1)} %fusion.7, bf16[512,768]{1,0:T(8,128)(2,1)S(1)} %get-tuple-element.16), kind=kOutput, calls=%fused_computation.102 | convolution fusion | flops 201588480 | bytes 1704964 | tf_op jit(solution)/shard_map/dot_general | solution.py:106
  19.5 0.3 exponential_reduce_fusion.2
  19.9 0.4 collective-permute-done.4
  20.2 0.2 multiply_reduce_fusion.1
  20.4 0.1 slice_convert_fusion
  20.5 0.1 fusion.6
  20.6 0.5 %fusion.40 = (f32[256]{0:T(256)S(1)}, f32[256,512]{1,0:T(8,128)S(1)}) fusion(f32[]{:T(128)} %bitcast.112, bf16[256,768]{1,0:T(8,128)(2,1)S(1)} %fusion.6, bf16[512,768]{1,0:T(8,128)(2,1)S(1)} %get-tuple-element.15), kind=kOutput, calls=%fused_computation.101 | convolution fusion | flops 201588480 | bytes 1704964 | tf_op jit(solution)/shard_map/dot_general | solution.py:106
  21.1 0.5 %fusion.39 = (f32[256]{0:T(256)S(1)}, f32[256,512]{1,0:T(8,128)S(1)}) fusion(f32[]{:T(128)} %bitcast.113, bf16[256,768]{1,0:T(8,128)(2,1)S(1)} %fusion.6, bf16[512,768]{1,0:T(8,128)(2,1)S(1)} %get-tuple-element.16), kind=kOutput, calls=%fused_computation.100 | convolution fusion | flops 201588480 | bytes 1704964 | tf_op jit(solution)/shard_map/dot_general | solution.py:106
  21.6 0.3 exponential_reduce_fusion
  21.9 0.1 stack_reshape.19
  22.0 0.1 stack_reshape.18
  22.1 0.7 %collective-permute-start.6 = (f32[3,2,2,4,32]{4,3,2,1,0:T(4,128)S(1)}, f32[3,2,2,4,32]{4,3,2,1,0:T(4,128)S(1)}, u32[]{:S(2)}, u32[]{:S(2)}) collective-permute-start(f32[3,2,2,4,32]{4,3,2,1,0:T(4,128)S(1)} %get-tuple-element.24), channel_id=1, source_target_pairs={{0,8},{4,12},{8,0},{12,4},{1,9},{5,13},{9,1},{13,5},{2,10},{6,14},... | collective-permute-start | bytes 18440 | tf_op jit(solution)/shard_map/ppermute | solution.py:29
  22.8 2.6 %collective-permute-start.5 = (f32[3,2,2,4,32]{4,3,2,1,0:T(4,128)S(1)}, f32[3,2,2,4,32]{4,3,2,1,0:T(4,128)S(1)}, u32[]{:S(2)}, u32[]{:S(2)}) collective-permute-start(f32[3,2,2,4,32]{4,3,2,1,0:T(4,128)S(1)} %get-tuple-element.24), channel_id=1, source_target_pairs={{0,4},{4,0},{8,12},{12,8},{1,5},{5,1},{9,13},{13,9},{2,6},{6,2},{1... | collective-permute-start | bytes 18440 | tf_op jit(solution)/shard_map/ppermute | solution.py:29
  25.4 1.1 %collective-permute-start.7 = (f32[3,2,2,4,32]{4,3,2,1,0:T(4,128)S(1)}, f32[3,2,2,4,32]{4,3,2,1,0:T(4,128)S(1)}, u32[]{:S(2)}, u32[]{:S(2)}) collective-permute-start(f32[3,2,2,4,32]{4,3,2,1,0:T(4,128)S(1)} %get-tuple-element.24), channel_id=1, source_target_pairs={{0,12},{4,8},{8,4},{12,0},{1,13},{5,9},{9,5},{13,1},{2,14},{6,10},... | collective-permute-start | bytes 18440 | tf_op jit(solution)/shard_map/ppermute | solution.py:29
  26.5 0.4 %collective-permute-done.6 = f32[3,2,2,4,32]{4,3,2,1,0:T(4,128)S(1)} collective-permute-done((f32[3,2,2,4,32]{4,3,2,1,0:T(4,128)S(1)}, f32[3,2,2,4,32]{4,3,2,1,0:T(4,128)S(1)}, u32[]{:S(2)}, u32[]{:S(2)}) %collective-permute-start.6) | collective-permute-done | bytes 6176 | tf_op jit(solution)/shard_map/ppermute | solution.py:29
  27.0 0.3 collective-permute-done.5
  27.2 0.1 rev.16
  27.3 3.8 %collective-permute-done.7 = f32[3,2,2,4,32]{4,3,2,1,0:T(4,128)S(1)} collective-permute-done((f32[3,2,2,4,32]{4,3,2,1,0:T(4,128)S(1)}, f32[3,2,2,4,32]{4,3,2,1,0:T(4,128)S(1)}, u32[]{:S(2)}, u32[]{:S(2)}) %collective-permute-start.7) | collective-permute-done | bytes 6176 | tf_op jit(solution)/shard_map/ppermute | solution.py:29
  31.1 0.1 rev.18
  31.3 0.1 collective-permute-start.8
  31.4 1.2 %collective-permute-done.8 = f32[3,2,2,4,32]{4,3,2,1,0:T(4,128)S(1)} collective-permute-done((f32[3,2,2,4,32]{4,3,2,1,0:T(4,128)S(1)}, f32[3,2,2,4,32]{4,3,2,1,0:T(4,128)S(1)}, u32[]{:S(2)}, u32[]{:S(2)}) %collective-permute-start.8) | collective-permute-done | bytes 6176 | tf_op jit(solution)/shard_map/ppermute | solution.py:29
  32.6 0.5 %fusion.30 = f32[32]{0:T(128)} fusion(f32[2,2,4,32]{3,2,1,0:T(4,128)S(1)} %bitcast.134, s32[32]{0:T(128)S(1)} %copy-done.2, f32[]{:T(128)} %bitcast.111), kind=kLoop, calls=%fused_computation.88 | loop fusion | flops 96 | bytes 388 | tf_op jit(solution)/shard_map/div | solution.py:152
  33.2 0.1 sub.77
  33.2 0.1 mul.154
  33.3 0.2 bitcast_reduce_fusion.2
  33.5 0.1 mul.148
  33.6 0.1 sub.74
  33.7 0.2 bitcast_reduce_fusion.3
  33.9 0.6 %convert_reduce_fusion.1 = f32[512,768]{1,0:T(8,128)S(1)} fusion(bf16[2,128,512]{2,1,0:T(8,128)(2,1)S(1)} %bitcast.120, f32[2,128]{1,0:T(2,128)S(1)} %get-tuple-element.31, bf16[1,2,144,768]{3,2,1,0:T(8,128)(2,1)S(1)} %get-tuple-element.18), kind=kOutput, calls=%fused_computation.1 | convolution fusion | flops 203882496 | bytes 2229248 | tf_op jit(solution)/shard_map/dot_general | solution.py:141
  34.6 0.6 %convert_reduce_fusion = f32[512,768]{1,0:T(8,128)S(1)} fusion(bf16[2,128,512]{2,1,0:T(8,128)(2,1)S(1)} %bitcast.119, f32[2,128]{1,0:T(2,128)S(1)} %get-tuple-element.29, bf16[1,2,144,768]{3,2,1,0:T(8,128)(2,1)S(1)} %bitcast.118), kind=kOutput, calls=%fused_computation | convolution fusion | flops 203882496 | bytes 2229248 | tf_op jit(solution)/shard_map/dot_general | solution.py:141
  35.2 0.5 %multiply_reduce_fusion = (f32[512]{0:T(512)S(1)}, f32[512,768]{1,0:T(8,128)S(1)}) fusion(f32[512]{0:T(512)S(1)} %add_add_fusion, bf16[512,768]{1,0:T(8,128)(2,1)S(1)} %get-tuple-element.16, f32[512,768]{1,0:T(8,128)S(1)} %convert_reduce_fusion.1, f32[512,768]{1,0:T(8,128)S(1)} %convert_reduce_fusion), kind=kLoop, calls=%fused_computation.13 | loop fusion | flops 2358784 | bytes 5509120 | tf_op jit(solution)/shard_map/reduce_sum | solution.py:12
  35.7 1.4 %multiply_convert_fusion = bf16[512,768]{1,0:T(8,128)(2,1)} fusion(f32[512]{0:T(512)S(1)} %add_rsqrt_fusion, f32[512,768]{1,0:T(8,128)S(1)} %get-tuple-element.10, f32[512]{0:T(512)S(1)} %add_add_fusion, bf16[512,768]{1,0:T(8,128)(2,1)S(1)} %get-tuple-element.16), kind=kLoop, calls=%fused_computation.12 | loop fusion | flops 1966080 | bytes 3149824 | tf_op jit(solution)/shard_map/convert_element_type | solution.py:149
  (38 shorter events, 0.4 us)
Async XLA Ops:
  0.6 11.3 %copy-start.1 = (bf16[32,768]{1,0:T(8,128)(2,1)S(1)}, bf16[32,768]{1,0:T(8,128)(2,1)}, u32[]{:S(2)}) copy-start(bf16[32,768]{1,0:T(8,128)(2,1)} %param.4) | copy-start | bytes 147460
  0.6 7.5 %copy-start.2 = (s32[32]{0:T(128)S(1)}, s32[32]{0:T(128)}, u32[]{:S(2)}) copy-start(s32[32]{0:T(128)} %param.5) | copy-start | bytes 388
  0.6 8.1 %collective-permute-start = (bf16[32,768]{1,0:T(8,128)(2,1)}, bf16[32,768]{1,0:T(8,128)(2,1)S(1)}, u32[]{:S(2)}, u32[]{:S(2)}) collective-permute-start(bf16[32,768]{1,0:T(8,128)(2,1)} %param.4), channel_id=1, source_target_pairs={{0,4},{4,0},{8,12},{12,8},{1,5},{5,1},{9,13},{13,9},{2,6},{6,2},{1... | collective-permute-start | bytes 147464 | tf_op jit(solution)/shard_map/ppermute | solution.py:29
  3.7 6.7 %collective-permute-start.2 = (bf16[32,768]{1,0:T(8,128)(2,1)}, bf16[32,768]{1,0:T(8,128)(2,1)S(1)}, u32[]{:S(2)}, u32[]{:S(2)}) collective-permute-start(bf16[32,768]{1,0:T(8,128)(2,1)} %param.4), channel_id=1, source_target_pairs={{0,12},{4,8},{8,4},{12,0},{1,13},{5,9},{9,5},{13,1},{2,14},{6,10},... | collective-permute-start | bytes 147464 | tf_op jit(solution)/shard_map/ppermute | solution.py:29
  6.2 5.7 %collective-permute-start.1 = (bf16[32,768]{1,0:T(8,128)(2,1)}, bf16[32,768]{1,0:T(8,128)(2,1)S(1)}, u32[]{:S(2)}, u32[]{:S(2)}) collective-permute-start(bf16[32,768]{1,0:T(8,128)(2,1)} %param.4), channel_id=1, source_target_pairs={{0,8},{4,12},{8,0},{12,4},{1,9},{5,13},{9,1},{13,5},{2,10},{6,14},... | collective-permute-start | bytes 147464 | tf_op jit(solution)/shard_map/ppermute | solution.py:29
  12.0 6.0 %collective-permute-start.3 = (bf16[144,768]{1,0:T(8,128)(2,1)S(1)}, bf16[144,768]{1,0:T(8,128)(2,1)S(1)}, u32[]{:S(2)}, u32[]{:S(2)}) collective-permute-start(bf16[144,768]{1,0:T(8,128)(2,1)S(1)} %get-tuple-element.20), channel_id=1, source_target_pairs={{0,2},{2,0},{1,3},{3,1},{4,6},{6,4},{5,7},{7,5},{8,10},{10,8},{9,1... | collective-permute-start | bytes 663560 | tf_op jit(solution)/shard_map/ppermute | solution.py:29
  18.4 1.9 %collective-permute-start.4 = (bf16[2,144,768]{2,1,0:T(8,128)(2,1)S(1)}, bf16[2,144,768]{2,1,0:T(8,128)(2,1)S(1)}, u32[]{:S(2)}, u32[]{:S(2)}) collective-permute-start(bf16[2,144,768]{2,1,0:T(8,128)(2,1)S(1)} %get-tuple-element.17), channel_id=1, source_target_pairs={{0,1},{1,0},{2,3},{3,2},{4,5},{5,4},{6,7},{7,6},{8,9},{9,8},{10,11... | collective-permute-start | bytes 1327112 | tf_op jit(solution)/shard_map/ppermute | solution.py:29
  22.1 4.8 %collective-permute-start.6 = (f32[3,2,2,4,32]{4,3,2,1,0:T(4,128)S(1)}, f32[3,2,2,4,32]{4,3,2,1,0:T(4,128)S(1)}, u32[]{:S(2)}, u32[]{:S(2)}) collective-permute-start(f32[3,2,2,4,32]{4,3,2,1,0:T(4,128)S(1)} %get-tuple-element.24), channel_id=1, source_target_pairs={{0,8},{4,12},{8,0},{12,4},{1,9},{5,13},{9,1},{13,5},{2,10},{6,14},... | collective-permute-start | bytes 18440 | tf_op jit(solution)/shard_map/ppermute | solution.py:29
  22.8 4.4 %collective-permute-start.5 = (f32[3,2,2,4,32]{4,3,2,1,0:T(4,128)S(1)}, f32[3,2,2,4,32]{4,3,2,1,0:T(4,128)S(1)}, u32[]{:S(2)}, u32[]{:S(2)}) collective-permute-start(f32[3,2,2,4,32]{4,3,2,1,0:T(4,128)S(1)} %get-tuple-element.24), channel_id=1, source_target_pairs={{0,4},{4,0},{8,12},{12,8},{1,5},{5,1},{9,13},{13,9},{2,6},{6,2},{1... | collective-permute-start | bytes 18440 | tf_op jit(solution)/shard_map/ppermute | solution.py:29
  25.4 5.6 %collective-permute-start.7 = (f32[3,2,2,4,32]{4,3,2,1,0:T(4,128)S(1)}, f32[3,2,2,4,32]{4,3,2,1,0:T(4,128)S(1)}, u32[]{:S(2)}, u32[]{:S(2)}) collective-permute-start(f32[3,2,2,4,32]{4,3,2,1,0:T(4,128)S(1)} %get-tuple-element.24), channel_id=1, source_target_pairs={{0,12},{4,8},{8,4},{12,0},{1,13},{5,9},{9,5},{13,1},{2,14},{6,10},... | collective-permute-start | bytes 18440 | tf_op jit(solution)/shard_map/ppermute | solution.py:29
  31.3 1.3 %collective-permute-start.8 = (f32[3,2,2,4,32]{4,3,2,1,0:T(4,128)S(1)}, f32[3,2,2,4,32]{4,3,2,1,0:T(4,128)S(1)}, u32[]{:S(2)}, u32[]{:S(2)}) collective-permute-start(f32[3,2,2,4,32]{4,3,2,1,0:T(4,128)S(1)} %get-tuple-element.22), channel_id=1, source_target_pairs={{0,1},{1,0},{2,3},{3,2},{4,5},{5,4},{6,7},{7,6},{8,9},{9,8},{10,11... | collective-permute-start | bytes 18440 | tf_op jit(solution)/shard_map/ppermute | solution.py:29
  35.7 1.4 %copy-start = (f32[512,768]{1,0:T(8,128)}, f32[512,768]{1,0:T(8,128)S(1)}, u32[]{:S(2)}) copy-start(f32[512,768]{1,0:T(8,128)S(1)} %get-tuple-element.10) | copy-start | bytes 4718596

commit v18 on v14

--- a/solution.py
+++ b/solution.py
@@ -109,12 +109,13 @@
     weight_float = stats[2].reshape(-1)
     log_sum = (stats[0] + jnp.log(stats[1])).reshape(-1)
 
-    if sum(rows.size for rows in halves) * 2 <= (4 << 20):
-        own_scores = jnp.stack([blocks_of_half[0] for blocks_of_half in score_blocks]).reshape(n_groups, -1, own_count)
-        grouped_rows = jnp.stack(halves).reshape(n_groups, -1, width)
+    if n_rows * width * 2 <= (4 << 20):
+        grouped_rows = normalize(payload[:, :, :cent_rows].reshape(-1, width)).astype(jnp.bfloat16)
+        grouped_rows = grouped_rows.reshape(n_groups, -1, width)
+        own_scores = jnp.concatenate([blocks_of_half[0] for blocks_of_half in score_blocks], axis=0)
         grouped_resp = (
-            weight_float.reshape(n_groups, -1, 1) * jnp.exp(own_scores - log_sum.reshape(n_groups, -1, 1))
-        ).astype(jnp.bfloat16)
+            weight_float[:, None] * jnp.exp(own_scores - log_sum[:, None])
+        ).astype(jnp.bfloat16).reshape(n_groups, -1, own_count)
         partial_value = lax.dot_general(
             grouped_resp, grouped_rows, (((1,), (1,)), ((0,), (0,))), preferred_element_type=jnp.float32
         ).astype(jnp.bfloat16)

time: 36.3 us -> 34.5 us (0.950)
  other arithmetic: 10.6 us -> 9.19 us
    another operation x2 -> x0, other arithmetic: 2.02 us -> none  [the longest x1 1.95 us: shards(): grouped_rows = jnp.stack(halves).reshape(n_groups, -1, width)]
    convert_element_type x0 -> x1, other arithmetic: none -> 1.04 us  [shards(): normalize(payload[:, :, :cent_rows].reshape(-1, width)).astype(jnp.bfloat16)]
    convert_element_type x3 -> x2, other arithmetic: 1.1 us -> 0.22 us  [shards(): normalize(payload[half, :, :cent_rows].reshape(-1, width))]
    reduce_sum x4 -> x5, other arithmetic: 2.49 us -> 2.72 us  [normalize(): jnp.sum(floats * floats, axis=-1, keepdims=True) + 1e-06]
  transfers between devices with their start and end apart: 9 -> 9, of which waited for: 6 -> 6; matrix products, arithmetic and copies ran while one was open for 20% -> 18% of each run, Pallas kernels for 0% -> 0%
where the time goes in v18:
time: 34.5 us; the launch traced here: 34.3 us
  starting transfers between devices  12.4 us (36%)
  other arithmetic  9.19 us (27%)
  waiting for transfers between devices  7.54 us (22%)
  matrix products  2.91 us (8%)
  between operations  1.61 us (5%)
  local copies, waits for them, and re-layouts  0.72 us (2%)
    ppermute x9, starting transfers between devices, gather_stage(): lax.ppermute(value, name, [(j, (j + q) % size) for j in range(size)])  12.4 us
    ppermute x9, waiting for transfers between devices, gather_stage(): lax.ppermute(value, name, [(j, (j + q) % size) for j in range(size)])  7.54 us
    reduce_sum x5, other arithmetic, normalize(): jnp.sum(floats * floats, axis=-1, keepdims=True) + 1e-06  2.72 us
    dot_general x4, matrix products, shards(): lax.dot_general(rows, cents, (((1,), (1,)), ((), ())), preferred_element_...  1.94 us
    convert_element_type x1, other arithmetic, shards(): score_cents = [lax.optimization_barrier(normalize(lax.dynamic_slice_in_di...  1.69 us
    convert_element_type x1, other arithmetic, shards(): renormed = normalize(moved).astype(jnp.bfloat16)  1.25 us
    convert_element_type x1, other arithmetic, shards(): normalize(payload[:, :, :cent_rows].reshape(-1, width)).astype(jnp.bfloat16)  1.04 us
    dot_general x1, matrix products, shards(): lax.dot_general(grouped_resp, grouped_rows, (((1,), (1,)), ((0,), (0,))),...  0.98 us
  transfers between devices with their start and end apart: 9, of which 6 were waited for; matrix products, arithmetic and copies ran while one was open for 18% of the time, Pallas kernels for 0%

profile of v18, /device:TPU:0, one launch (start us, length us, event | category | flops | bytes accessed | tf_op | source)
XLA Modules:
  0.0 34.3 jit_solution(6269755864950799869)
XLA Ops:
  0.6 3.1 %collective-permute-start = (bf16[32,768]{1,0:T(8,128)(2,1)}, bf16[32,768]{1,0:T(8,128)(2,1)S(1)}, u32[]{:S(2)}, u32[]{:S(2)}) collective-permute-start(bf16[32,768]{1,0:T(8,128)(2,1)} %param.4), channel_id=1, source_target_pairs={{0,4},{4,8},{8,12},{12,0},{1,5},{5,9},{9,13},{13,1},{2,6},{6,10},{... | collective-permute-start | bytes 147464 | tf_op jit(solution)/shard_map/ppermute | solution.py:23
  3.7 2.1 %collective-permute-start.2 = (bf16[32,768]{1,0:T(8,128)(2,1)}, bf16[32,768]{1,0:T(8,128)(2,1)S(1)}, u32[]{:S(2)}, u32[]{:S(2)}) collective-permute-start(bf16[32,768]{1,0:T(8,128)(2,1)} %param.4), channel_id=1, source_target_pairs={{0,12},{4,0},{8,4},{12,8},{1,13},{5,1},{9,5},{13,9},{2,14},{6,2},{... | collective-permute-start | bytes 147464 | tf_op jit(solution)/shard_map/ppermute | solution.py:23
  5.8 0.9 %collective-permute-start.1 = (bf16[32,768]{1,0:T(8,128)(2,1)}, bf16[32,768]{1,0:T(8,128)(2,1)S(1)}, u32[]{:S(2)}, u32[]{:S(2)}) collective-permute-start(bf16[32,768]{1,0:T(8,128)(2,1)} %param.4), channel_id=1, source_target_pairs={{0,8},{4,12},{8,0},{12,4},{1,9},{5,13},{9,1},{13,5},{2,10},{6,14},... | collective-permute-start | bytes 147464 | tf_op jit(solution)/shard_map/ppermute | solution.py:23
  6.8 1.7 %fusion.2 = (f32[512]{0:T(512)S(1)}, f32[512]{0:T(512)S(1)}) fusion(bf16[2048,768]{1,0:T(8,128)(2,1)} %param.6, s32[]{:T(128)S(6)} %select_n.20, s32[]{:T(128)S(6)} %select_n.18), kind=kLoop, calls=%fused_computation.7 | loop fusion | flops 2358272 | bytes 1576968 | tf_op jit(solution)/shard_map/reduce_sum | solution.py:12
  9.2 0.0 collective-permute-done
  9.2 0.0 collective-permute-done.2
  9.2 1.9 %collective-permute-done.1 = bf16[32,768]{1,0:T(8,128)(2,1)S(1)} collective-permute-done((bf16[32,768]{1,0:T(8,128)(2,1)}, bf16[32,768]{1,0:T(8,128)(2,1)S(1)}, u32[]{:S(2)}, u32[]{:S(2)}) %collective-permute-start.1) | collective-permute-done | bytes 49184 | tf_op jit(solution)/shard_map/ppermute | solution.py:23
  11.2 1.6 %collective-permute-start.3 = (bf16[144,768]{1,0:T(8,128)(2,1)S(1)}, bf16[144,768]{1,0:T(8,128)(2,1)S(1)}, u32[]{:S(2)}, u32[]{:S(2)}) collective-permute-start(bf16[144,768]{1,0:T(8,128)(2,1)S(1)} %get-tuple-element.14), channel_id=1, source_target_pairs={{0,2},{2,0},{1,3},{3,1},{4,6},{6,4},{5,7},{7,5},{8,10},{10,8},{9,1... | collective-permute-start | bytes 663560 | tf_op jit(solution)/shard_map/ppermute | solution.py:23
  12.8 1.7 %fusion.3 = (bf16[512,768]{1,0:T(8,128)(2,1)S(1)}, bf16[512,768]{1,0:T(8,128)(2,1)S(1)}) fusion(f32[512]{0:T(512)S(1)} %get-tuple-element.31, bf16[2048,768]{1,0:T(8,128)(2,1)} %param.6, s32[]{:T(128)S(6)} %select_n.20, f32[512]{0:T(512)S(1)} %get-tuple-element.32, s32[]{:T(128)S(6)} %select_n.18), kind=kLoop, calls=%fused_computation.8 | loop fusion | flops 2359296 | bytes 3149832 | tf_op jit(solution)/shard_map/convert_element_type | solution.py:76
  14.5 2.9 %collective-permute-done.3 = bf16[144,768]{1,0:T(8,128)(2,1)S(1)} collective-permute-done((bf16[144,768]{1,0:T(8,128)(2,1)S(1)}, bf16[144,768]{1,0:T(8,128)(2,1)S(1)}, u32[]{:S(2)}, u32[]{:S(2)}) %collective-permute-start.3) | collective-permute-done | bytes 221216 | tf_op jit(solution)/shard_map/ppermute | solution.py:23
  17.4 0.1 fusion.31
  17.5 0.2 multiply_reduce_fusion.3
  17.6 0.1 slice_convert_fusion.1
  17.7 0.1 collective-permute-start.4
  17.8 0.1 fusion.7
  17.9 0.5 %fusion.37 = (f32[256]{0:T(256)S(1)}, f32[256,512]{1,0:T(8,128)S(1)}) fusion(f32[]{:T(128)} %bitcast.105, bf16[256,768]{1,0:T(8,128)(2,1)S(1)} %fusion.7, bf16[512,768]{1,0:T(8,128)(2,1)S(1)} %get-tuple-element.9), kind=kOutput, calls=%fused_computation.99 | convolution fusion | flops 201588480 | bytes 1704964 | tf_op jit(solution)/shard_map/dot_general | solution.py:87
  18.4 0.5 %fusion.36 = (f32[256]{0:T(256)S(1)}, f32[256,512]{1,0:T(8,128)S(1)}) fusion(f32[]{:T(128)} %bitcast.101, bf16[256,768]{1,0:T(8,128)(2,1)S(1)} %fusion.7, bf16[512,768]{1,0:T(8,128)(2,1)S(1)} %get-tuple-element.10), kind=kOutput, calls=%fused_computation.98 | convolution fusion | flops 201588480 | bytes 1704964 | tf_op jit(solution)/shard_map/dot_general | solution.py:87
  18.9 0.3 exponential_reduce_fusion.2
  19.2 0.4 %collective-permute-done.4 = bf16[2,144,768]{2,1,0:T(8,128)(2,1)S(1)} collective-permute-done((bf16[2,144,768]{2,1,0:T(8,128)(2,1)S(1)}, bf16[2,144,768]{2,1,0:T(8,128)(2,1)S(1)}, u32[]{:S(2)}, u32[]{:S(2)}) %collective-permute-start.4) | collective-permute-done | bytes 442400 | tf_op jit(solution)/shard_map/ppermute | solution.py:23
  19.5 0.2 multiply_reduce_fusion.2
  19.7 0.2 multiply_reduce_fusion.1
  19.9 0.1 slice_convert_fusion
  20.0 0.1 fusion.5
  20.2 0.1 fusion.6
  20.3 0.5 %fusion.35 = (f32[256]{0:T(256)S(1)}, f32[256,512]{1,0:T(8,128)S(1)}) fusion(f32[]{:T(128)} %bitcast.103, bf16[256,768]{1,0:T(8,128)(2,1)S(1)} %fusion.6, bf16[512,768]{1,0:T(8,128)(2,1)S(1)} %get-tuple-element.9), kind=kOutput, calls=%fused_computation.97 | convolution fusion | flops 201588480 | bytes 1704964 | tf_op jit(solution)/shard_map/dot_general | solution.py:87
  20.7 0.5 %fusion.34 = (f32[256]{0:T(256)S(1)}, f32[256,512]{1,0:T(8,128)S(1)}) fusion(f32[]{:T(128)} %bitcast.104, bf16[256,768]{1,0:T(8,128)(2,1)S(1)} %fusion.6, bf16[512,768]{1,0:T(8,128)(2,1)S(1)} %get-tuple-element.10), kind=kOutput, calls=%fused_computation.96 | convolution fusion | flops 201588480 | bytes 1704964 | tf_op jit(solution)/shard_map/dot_general | solution.py:87
  21.3 0.3 exponential_reduce_fusion
  21.6 0.1 stack_reshape.7
  21.7 0.1 stack_reshape.6
  21.8 0.7 %collective-permute-start.6 = (f32[3,2,2,4,32]{4,3,2,1,0:T(4,128)S(1)}, f32[3,2,2,4,32]{4,3,2,1,0:T(4,128)S(1)}, u32[]{:S(2)}, u32[]{:S(2)}) collective-permute-start(f32[3,2,2,4,32]{4,3,2,1,0:T(4,128)S(1)} %get-tuple-element.20), channel_id=1, source_target_pairs={{0,8},{4,12},{8,0},{12,4},{1,9},{5,13},{9,1},{13,5},{2,10},{6,14},... | collective-permute-start | bytes 18440 | tf_op jit(solution)/shard_map/ppermute | solution.py:23
  22.5 2.7 %collective-permute-start.5 = (f32[3,2,2,4,32]{4,3,2,1,0:T(4,128)S(1)}, f32[3,2,2,4,32]{4,3,2,1,0:T(4,128)S(1)}, u32[]{:S(2)}, u32[]{:S(2)}) collective-permute-start(f32[3,2,2,4,32]{4,3,2,1,0:T(4,128)S(1)} %get-tuple-element.20), channel_id=1, source_target_pairs={{0,4},{4,8},{8,12},{12,0},{1,5},{5,9},{9,13},{13,1},{2,6},{6,10},{... | collective-permute-start | bytes 18440 | tf_op jit(solution)/shard_map/ppermute | solution.py:23
  25.2 1.1 %collective-permute-start.7 = (f32[3,2,2,4,32]{4,3,2,1,0:T(4,128)S(1)}, f32[3,2,2,4,32]{4,3,2,1,0:T(4,128)S(1)}, u32[]{:S(2)}, u32[]{:S(2)}) collective-permute-start(f32[3,2,2,4,32]{4,3,2,1,0:T(4,128)S(1)} %get-tuple-element.20), channel_id=1, source_target_pairs={{0,12},{4,0},{8,4},{12,8},{1,13},{5,1},{9,5},{13,9},{2,14},{6,2},{... | collective-permute-start | bytes 18440 | tf_op jit(solution)/shard_map/ppermute | solution.py:23
  26.3 1.0 %fusion.4 = bf16[4,128,768]{2,1,0:T(8,128)(2,1)} fusion(f32[2,2,128,768]{3,2,1,0:T(8,128)S(1)} %fusion.5, f32[4,128]{1,0:T(4,128)S(1)} %bitcast.126), kind=kLoop, calls=%fused_computation.10 | loop fusion | flops 786432 | bytes 2361344 | tf_op jit(solution)/shard_map/convert_element_type | solution.py:113
  27.4 0.7 %collective-permute-done.5 = f32[3,2,2,4,32]{4,3,2,1,0:T(4,128)S(1)} collective-permute-done((f32[3,2,2,4,32]{4,3,2,1,0:T(4,128)S(1)}, f32[3,2,2,4,32]{4,3,2,1,0:T(4,128)S(1)}, u32[]{:S(2)}, u32[]{:S(2)}) %collective-permute-start.5) | collective-permute-done | bytes 6176 | tf_op jit(solution)/shard_map/ppermute | solution.py:23
  28.2 0.9 %collective-permute-done.7 = f32[3,2,2,4,32]{4,3,2,1,0:T(4,128)S(1)} collective-permute-done((f32[3,2,2,4,32]{4,3,2,1,0:T(4,128)S(1)}, f32[3,2,2,4,32]{4,3,2,1,0:T(4,128)S(1)}, u32[]{:S(2)}, u32[]{:S(2)}) %collective-permute-start.7) | collective-permute-done | bytes 6176 | tf_op jit(solution)/shard_map/ppermute | solution.py:23
  29.2 0.1 collective-permute-start.8
  29.3 0.1 pad_maximum_fusion
  29.4 0.3 copy.12
  29.7 0.0 copy-start.1
  29.7 0.8 %collective-permute-done.8 = f32[3,2,2,4,32]{4,3,2,1,0:T(4,128)S(1)} collective-permute-done((f32[3,2,2,4,32]{4,3,2,1,0:T(4,128)S(1)}, f32[3,2,2,4,32]{4,3,2,1,0:T(4,128)S(1)}, u32[]{:S(2)}, u32[]{:S(2)}) %collective-permute-start.8) | collective-permute-done | bytes 6176 | tf_op jit(solution)/shard_map/ppermute | solution.py:23
  30.6 0.1 mul.142
  30.6 0.1 add.120
  30.7 0.5 %fusion.27 = f32[32]{0:T(128)} fusion(f32[2,2,4,32]{3,2,1,0:T(4,128)S(1)} %bitcast.122, s32[32]{0:T(128)S(1)} %copy-done.3, f32[]{:T(128)} %bitcast.102), kind=kLoop, calls=%fused_computation.88 | loop fusion | flops 96 | bytes 388 | tf_op jit(solution)/shard_map/div | solution.py:147
  31.3 0.4 %fusion.10 = bf16[4,512]{1,0:T(4,128)(2,1)S(1)} fusion(f32[4,128,512]{1,2,0:T(8,128)S(1)} %copy.12, f32[4,128]{1,0:T(4,128)S(1)} %add.120, f32[4,128]{1,0:T(4,128)S(1)} %mul.142), kind=kLoop, calls=%fused_computation.41 | loop fusion | flops 1046528 | bytes 1056768 | tf_op jit(solution)/shard_map/reduce_sum | solution.py:123
  31.6 1.0 %convert_reduce_fusion = f32[512,768]{1,0:T(8,128)S(1)} fusion(bf16[4,128,768]{2,1,0:T(8,128)(2,1)S(1)} %copy-done.1, f32[4,128,512]{1,2,0:T(8,128)S(1)} %copy.12, f32[4,128]{1,0:T(4,128)S(1)} %add.120, f32[4,128]{1,0:T(4,128)S(1)} %mul.142), kind=kOutput, calls=%fused_computation | convolution fusion | flops 407764992 | bytes 3411968 | tf_op jit(solution)/shard_map/dot_general | solution.py:119
  32.6 0.0 copy-start
  32.7 0.4 %multiply_reduce_fusion = f32[512]{0:T(512)S(1)} fusion(f32[512,768]{1,0:T(8,128)S(1)} %convert_reduce_fusion, f32[512]{0:T(512)S(1)} %broadcast_add_fusion, bf16[512,768]{1,0:T(8,128)(2,1)S(1)} %get-tuple-element.10), kind=kLoop, calls=%fused_computation.12 | loop fusion | flops 1965568 | bytes 2363392 | tf_op jit(solution)/shard_map/reduce_sum | solution.py:12
  33.1 1.2 %multiply_convert_fusion = bf16[512,768]{1,0:T(8,128)(2,1)} fusion(f32[512]{0:T(512)S(1)} %add_rsqrt_fusion, f32[512,768]{1,0:T(8,128)S(1)} %convert_reduce_fusion, f32[512]{0:T(512)S(1)} %broadcast_add_fusion, bf16[512,768]{1,0:T(8,128)(2,1)S(1)} %get-tuple-element.10), kind=kLoop, calls=%fused_computation.11 | loop fusion | flops 1966080 | bytes 3149824 | tf_op jit(solution)/shard_map/convert_element_type | solution.py:144
  (43 shorter events, 0.5 us)
Async XLA Ops:
  0.6 10.5 %copy-start.2 = (bf16[32,768]{1,0:T(8,128)(2,1)S(1)}, bf16[32,768]{1,0:T(8,128)(2,1)}, u32[]{:S(2)}) copy-start(bf16[32,768]{1,0:T(8,128)(2,1)} %param.4) | copy-start | bytes 147460
  0.6 7.9 %copy-start.3 = (s32[32]{0:T(128)S(1)}, s32[32]{0:T(128)}, u32[]{:S(2)}) copy-start(s32[32]{0:T(128)} %param.5) | copy-start | bytes 388
  0.6 8.6 %collective-permute-start = (bf16[32,768]{1,0:T(8,128)(2,1)}, bf16[32,768]{1,0:T(8,128)(2,1)S(1)}, u32[]{:S(2)}, u32[]{:S(2)}) collective-permute-start(bf16[32,768]{1,0:T(8,128)(2,1)} %param.4), channel_id=1, source_target_pairs={{0,4},{4,8},{8,12},{12,0},{1,5},{5,9},{9,13},{13,1},{2,6},{6,10},{... | collective-permute-start | bytes 147464 | tf_op jit(solution)/shard_map/ppermute | solution.py:23
  3.7 5.5 %collective-permute-start.2 = (bf16[32,768]{1,0:T(8,128)(2,1)}, bf16[32,768]{1,0:T(8,128)(2,1)S(1)}, u32[]{:S(2)}, u32[]{:S(2)}) collective-permute-start(bf16[32,768]{1,0:T(8,128)(2,1)} %param.4), channel_id=1, source_target_pairs={{0,12},{4,0},{8,4},{12,8},{1,13},{5,1},{9,5},{13,9},{2,14},{6,2},{... | collective-permute-start | bytes 147464 | tf_op jit(solution)/shard_map/ppermute | solution.py:23
  5.8 5.3 %collective-permute-start.1 = (bf16[32,768]{1,0:T(8,128)(2,1)}, bf16[32,768]{1,0:T(8,128)(2,1)S(1)}, u32[]{:S(2)}, u32[]{:S(2)}) collective-permute-start(bf16[32,768]{1,0:T(8,128)(2,1)} %param.4), channel_id=1, source_target_pairs={{0,8},{4,12},{8,0},{12,4},{1,9},{5,13},{9,1},{13,5},{2,10},{6,14},... | collective-permute-start | bytes 147464 | tf_op jit(solution)/shard_map/ppermute | solution.py:23
  11.2 6.2 %collective-permute-start.3 = (bf16[144,768]{1,0:T(8,128)(2,1)S(1)}, bf16[144,768]{1,0:T(8,128)(2,1)S(1)}, u32[]{:S(2)}, u32[]{:S(2)}) collective-permute-start(bf16[144,768]{1,0:T(8,128)(2,1)S(1)} %get-tuple-element.14), channel_id=1, source_target_pairs={{0,2},{2,0},{1,3},{3,1},{4,6},{6,4},{5,7},{7,5},{8,10},{10,8},{9,1... | collective-permute-start | bytes 663560 | tf_op jit(solution)/shard_map/ppermute | solution.py:23
  17.7 1.9 %collective-permute-start.4 = (bf16[2,144,768]{2,1,0:T(8,128)(2,1)S(1)}, bf16[2,144,768]{2,1,0:T(8,128)(2,1)S(1)}, u32[]{:S(2)}, u32[]{:S(2)}) collective-permute-start(bf16[2,144,768]{2,1,0:T(8,128)(2,1)S(1)} %get-tuple-element.12), channel_id=1, source_target_pairs={{0,1},{1,0},{2,3},{3,2},{4,5},{5,4},{6,7},{7,6},{8,9},{9,8},{10,11... | collective-permute-start | bytes 1327112 | tf_op jit(solution)/shard_map/ppermute | solution.py:23
  21.8 5.6 %collective-permute-start.6 = (f32[3,2,2,4,32]{4,3,2,1,0:T(4,128)S(1)}, f32[3,2,2,4,32]{4,3,2,1,0:T(4,128)S(1)}, u32[]{:S(2)}, u32[]{:S(2)}) collective-permute-start(f32[3,2,2,4,32]{4,3,2,1,0:T(4,128)S(1)} %get-tuple-element.20), channel_id=1, source_target_pairs={{0,8},{4,12},{8,0},{12,4},{1,9},{5,13},{9,1},{13,5},{2,10},{6,14},... | collective-permute-start | bytes 18440 | tf_op jit(solution)/shard_map/ppermute | solution.py:23
  22.5 5.6 %collective-permute-start.5 = (f32[3,2,2,4,32]{4,3,2,1,0:T(4,128)S(1)}, f32[3,2,2,4,32]{4,3,2,1,0:T(4,128)S(1)}, u32[]{:S(2)}, u32[]{:S(2)}) collective-permute-start(f32[3,2,2,4,32]{4,3,2,1,0:T(4,128)S(1)} %get-tuple-element.20), channel_id=1, source_target_pairs={{0,4},{4,8},{8,12},{12,0},{1,5},{5,9},{9,13},{13,1},{2,6},{6,10},{... | collective-permute-start | bytes 18440 | tf_op jit(solution)/shard_map/ppermute | solution.py:23
  25.2 3.8 %collective-permute-start.7 = (f32[3,2,2,4,32]{4,3,2,1,0:T(4,128)S(1)}, f32[3,2,2,4,32]{4,3,2,1,0:T(4,128)S(1)}, u32[]{:S(2)}, u32[]{:S(2)}) collective-permute-start(f32[3,2,2,4,32]{4,3,2,1,0:T(4,128)S(1)} %get-tuple-element.20), channel_id=1, source_target_pairs={{0,12},{4,0},{8,4},{12,8},{1,13},{5,1},{9,5},{13,9},{2,14},{6,2},{... | collective-permute-start | bytes 18440 | tf_op jit(solution)/shard_map/ppermute | solution.py:23
  29.2 1.3 %collective-permute-start.8 = (f32[3,2,2,4,32]{4,3,2,1,0:T(4,128)S(1)}, f32[3,2,2,4,32]{4,3,2,1,0:T(4,128)S(1)}, u32[]{:S(2)}, u32[]{:S(2)}) collective-permute-start(f32[3,2,2,4,32]{4,3,2,1,0:T(4,128)S(1)} %get-tuple-element.16), channel_id=1, source_target_pairs={{0,1},{1,0},{2,3},{3,2},{4,5},{5,4},{6,7},{7,6},{8,9},{9,8},{10,11... | collective-permute-start | bytes 18440 | tf_op jit(solution)/shard_map/ppermute | solution.py:23
  29.7 1.9 %copy-start.1 = (bf16[4,128,768]{2,1,0:T(8,128)(2,1)S(1)}, bf16[4,128,768]{2,1,0:T(8,128)(2,1)}, u32[]{:S(2)}) copy-start(bf16[4,128,768]{2,1,0:T(8,128)(2,1)} %fusion.4) | copy-start | bytes 2359300
  32.6 1.7 %copy-start = (f32[512,768]{1,0:T(8,128)}, f32[512,768]{1,0:T(8,128)S(1)}, u32[]{:S(2)}) copy-start(f32[512,768]{1,0:T(8,128)S(1)} %convert_reduce_fusion) | copy-start | bytes 4718596

commit v19 on v18

--- a/solution.py
+++ b/solution.py
@@ -57,11 +57,13 @@
     cent_rows = blocks.shape[0]
     weight_block = jnp.pad(weights.astype(jnp.bfloat16)[None, :], ((0, 15), (0, width - row_dev)))
     payload = jnp.concatenate([blocks, weight_block], axis=0)
-    for name in STAGES[1:]:
+    for name in STAGES[1:-1]:
         payload = gather_stage(payload, name)
-    halves = [
-        normalize(payload[half, :, :cent_rows].reshape(-1, width)).astype(jnp.bfloat16) for half in range(sizes["sub"])
-    ]
+    payload = jnp.concatenate(
+        [normalize(payload[..., :cent_rows, :]).astype(jnp.bfloat16), payload[..., cent_rows:, :]], axis=-2
+    )
+    payload = gather_stage(payload, STAGES[-1])
+    halves = [payload[half, :, :cent_rows].reshape(-1, width) for half in range(sizes["sub"])]
     cent_weights = payload[:, :, cent_rows, :row_dev].astype(jnp.float32)
 
     offset = lax.axis_index(("dp", "sub")) * own_count
@@ -110,8 +112,7 @@
     log_sum = (stats[0] + jnp.log(stats[1])).reshape(-1)
 
     if n_rows * width * 2 <= (4 << 20):
-        grouped_rows = normalize(payload[:, :, :cent_rows].reshape(-1, width)).astype(jnp.bfloat16)
-        grouped_rows = grouped_rows.reshape(n_groups, -1, width)
+        grouped_rows = payload[:, :, :cent_rows].reshape(n_groups, -1, width)
         own_scores = jnp.concatenate([blocks_of_half[0] for blocks_of_half in score_blocks], axis=0)
         grouped_resp = (
             weight_float[:, None] * jnp.exp(own_scores - log_sum[:, None])

time: 34.5 us -> 35.5 us (1.029)
  waiting for transfers between devices: 7.54 us -> 7.94 us
    another operation x3, other arithmetic: 0.12 us -> 1.99 us  [gather_stage(): return jnp.stack(parts)]
    convert_element_type x6 -> x1, other arithmetic: 1.48 us -> 0.14 us  [shards(): normalize(payload[..., :cent_rows, :]).astype(jnp.bfloat16)]
    ppermute x9, waiting for transfers between devices: 7.54 us -> 7.94 us  [gather_stage(): lax.ppermute(value, name, [(j, (j + q) % size) for j in range(size)])]
    reduce_sum x5 -> x3, other arithmetic: 2.72 us -> 2.33 us  [normalize(): jnp.sum(floats * floats, axis=-1, keepdims=True) + 1e-06]
  transfers between devices with their start and end apart: 9 -> 9, of which waited for: 6 -> 6; matrix products, arithmetic and copies ran while one was open for 18% -> 20% of each run, Pallas kernels for 0% -> 0%
where the time goes in v19:
time: 35.5 us; the launch traced here: 35.3 us
  starting transfers between devices  12.4 us (35%)
  other arithmetic  9.39 us (26%)
  waiting for transfers between devices  7.94 us (22%)
  matrix products  2.91 us (8%)
  between operations  1.61 us (5%)
  local copies, waits for them, and re-layouts  1.01 us (3%)
    ppermute x9, starting transfers between devices, gather_stage(): lax.ppermute(value, name, [(j, (j + q) % size) for j in range(size)])  12.4 us
    ppermute x9, waiting for transfers between devices, gather_stage(): lax.ppermute(value, name, [(j, (j + q) % size) for j in range(size)])  7.94 us
    reduce_sum x3, other arithmetic, normalize(): jnp.sum(floats * floats, axis=-1, keepdims=True) + 1e-06  2.33 us
    another operation x3, other arithmetic, gather_stage(): return jnp.stack(parts)  1.99 us
    dot_general x4, matrix products, shards(): lax.dot_general(rows, cents, (((1,), (1,)), ((), ())), preferred_element_...  1.93 us
    convert_element_type x1, other arithmetic, shards(): score_cents = [lax.optimization_barrier(normalize(lax.dynamic_slice_in_di...  1.69 us
    convert_element_type x1, other arithmetic, shards(): renormed = normalize(moved).astype(jnp.bfloat16)  1.25 us
    dot_general x1, matrix products, shards(): lax.dot_general(grouped_resp, grouped_rows, (((1,), (1,)), ((0,), (0,))),...  0.98 us
  transfers between devices with their start and end apart: 9, of which 6 were waited for; matrix products, arithmetic and copies ran while one was open for 20% of the time, Pallas kernels for 0%

profile of v19, /device:TPU:0, one launch (start us, length us, event | category | flops | bytes accessed | tf_op | source)
XLA Modules:
  0.0 35.3 jit_solution(476882987295801063)
XLA Ops:
  0.6 0.0 copy-start.3
  0.6 0.0 copy-start.4
  0.6 3.1 %collective-permute-start = (bf16[32,768]{1,0:T(8,128)(2,1)}, bf16[32,768]{1,0:T(8,128)(2,1)S(1)}, u32[]{:S(2)}, u32[]{:S(2)}) collective-permute-start(bf16[32,768]{1,0:T(8,128)(2,1)} %param.4), channel_id=1, source_target_pairs={{0,4},{4,8},{8,12},{12,0},{1,5},{5,9},{9,13},{13,1},{2,6},{6,10},{... | collective-permute-start | bytes 147464 | tf_op jit(solution)/shard_map/ppermute | solution.py:23
  3.7 2.1 %collective-permute-start.2 = (bf16[32,768]{1,0:T(8,128)(2,1)}, bf16[32,768]{1,0:T(8,128)(2,1)S(1)}, u32[]{:S(2)}, u32[]{:S(2)}) collective-permute-start(bf16[32,768]{1,0:T(8,128)(2,1)} %param.4), channel_id=1, source_target_pairs={{0,12},{4,0},{8,4},{12,8},{1,13},{5,1},{9,5},{13,9},{2,14},{6,2},{... | collective-permute-start | bytes 147464 | tf_op jit(solution)/shard_map/ppermute | solution.py:23
  5.8 0.9 %collective-permute-start.1 = (bf16[32,768]{1,0:T(8,128)(2,1)}, bf16[32,768]{1,0:T(8,128)(2,1)S(1)}, u32[]{:S(2)}, u32[]{:S(2)}) collective-permute-start(bf16[32,768]{1,0:T(8,128)(2,1)} %param.4), channel_id=1, source_target_pairs={{0,8},{4,12},{8,0},{12,4},{1,9},{5,13},{9,1},{13,5},{2,10},{6,14},... | collective-permute-start | bytes 147464 | tf_op jit(solution)/shard_map/ppermute | solution.py:23
  6.8 1.7 %fusion.2 = (f32[512]{0:T(512)S(1)}, f32[512]{0:T(512)S(1)}) fusion(bf16[2048,768]{1,0:T(8,128)(2,1)} %param.6, s32[]{:T(128)S(6)} %select_n.20, s32[]{:T(128)S(6)} %select_n.18), kind=kLoop, calls=%fused_computation.7 | loop fusion | flops 2358272 | bytes 1576968 | tf_op jit(solution)/shard_map/reduce_sum | solution.py:12
  8.5 0.0 copy-done.4
  9.2 0.0 collective-permute-done
  9.2 0.0 collective-permute-done.2
  9.2 1.9 %collective-permute-done.1 = bf16[32,768]{1,0:T(8,128)(2,1)S(1)} collective-permute-done((bf16[32,768]{1,0:T(8,128)(2,1)}, bf16[32,768]{1,0:T(8,128)(2,1)S(1)}, u32[]{:S(2)}, u32[]{:S(2)}) %collective-permute-start.1) | collective-permute-done | bytes 49184 | tf_op jit(solution)/shard_map/ppermute | solution.py:23
  11.1 0.0 copy-done.3
  11.2 1.6 %collective-permute-start.3 = (bf16[144,768]{1,0:T(8,128)(2,1)S(1)}, bf16[144,768]{1,0:T(8,128)(2,1)S(1)}, u32[]{:S(2)}, u32[]{:S(2)}) collective-permute-start(bf16[144,768]{1,0:T(8,128)(2,1)S(1)} %get-tuple-element.11), channel_id=1, source_target_pairs={{0,2},{2,0},{1,3},{3,1},{4,6},{6,4},{5,7},{7,5},{8,10},{10,8},{9,1... | collective-permute-start | bytes 663560 | tf_op jit(solution)/shard_map/ppermute | solution.py:23
  12.8 1.7 %fusion.3 = (bf16[512,768]{1,0:T(8,128)(2,1)S(1)}, bf16[512,768]{1,0:T(8,128)(2,1)S(1)}) fusion(f32[512]{0:T(512)S(1)} %get-tuple-element.29, bf16[2048,768]{1,0:T(8,128)(2,1)} %param.6, s32[]{:T(128)S(6)} %select_n.20, f32[512]{0:T(512)S(1)} %get-tuple-element.30, s32[]{:T(128)S(6)} %select_n.18), kind=kLoop, calls=%fused_computation.8 | loop fusion | flops 2359296 | bytes 3149832 | tf_op jit(solution)/shard_map/convert_element_type | solution.py:78
  14.5 2.9 %collective-permute-done.3 = bf16[144,768]{1,0:T(8,128)(2,1)S(1)} collective-permute-done((bf16[144,768]{1,0:T(8,128)(2,1)S(1)}, bf16[144,768]{1,0:T(8,128)(2,1)S(1)}, u32[]{:S(2)}, u32[]{:S(2)}) %collective-permute-start.3) | collective-permute-done | bytes 221216 | tf_op jit(solution)/shard_map/ppermute | solution.py:23
  17.4 0.2 fusion.6
  17.6 0.1 fusion.7
  17.8 0.1 collective-permute-start.4
  17.9 0.5 %fusion.39 = (f32[256]{0:T(256)S(1)}, f32[256,512]{1,0:T(8,128)S(1)}) fusion(f32[]{:T(128)} %bitcast.91, bf16[256,768]{1,0:T(8,128)(2,1)S(1)} %bitcast.100, bf16[512,768]{1,0:T(8,128)(2,1)S(1)} %get-tuple-element.9), kind=kOutput, calls=%fused_computation.95 | convolution fusion | flops 201588480 | bytes 1704964 | tf_op jit(solution)/shard_map/dot_general | solution.py:89
  18.4 0.5 %fusion.38 = (f32[256]{0:T(256)S(1)}, f32[256,512]{1,0:T(8,128)S(1)}) fusion(f32[]{:T(128)} %bitcast.87, bf16[256,768]{1,0:T(8,128)(2,1)S(1)} %bitcast.101, bf16[512,768]{1,0:T(8,128)(2,1)S(1)} %get-tuple-element.10), kind=kOutput, calls=%fused_computation.94 | convolution fusion | flops 201588480 | bytes 1704964 | tf_op jit(solution)/shard_map/dot_general | solution.py:89
  18.9 0.3 exponential_reduce_fusion.2
  19.2 0.5 %collective-permute-done.4 = bf16[2,144,768]{2,1,0:T(8,128)(2,1)S(1)} collective-permute-done((bf16[2,144,768]{2,1,0:T(8,128)(2,1)S(1)}, bf16[2,144,768]{2,1,0:T(8,128)(2,1)S(1)}, u32[]{:S(2)}, u32[]{:S(2)}) %collective-permute-start.4) | collective-permute-done | bytes 442400 | tf_op jit(solution)/shard_map/ppermute | solution.py:23
  19.7 0.5 %fusion.37 = (f32[256]{0:T(256)S(1)}, f32[256,512]{1,0:T(8,128)S(1)}) fusion(f32[]{:T(128)} %bitcast.89, bf16[256,768]{1,0:T(8,128)(2,1)S(1)} %bitcast.102, bf16[512,768]{1,0:T(8,128)(2,1)S(1)} %get-tuple-element.9), kind=kOutput, calls=%fused_computation.93 | convolution fusion | flops 201588480 | bytes 1704964 | tf_op jit(solution)/shard_map/dot_general | solution.py:89
  20.2 0.2 copy-done.1
  20.4 0.5 %fusion.36 = (f32[256]{0:T(256)S(1)}, f32[256,512]{1,0:T(8,128)S(1)}) fusion(f32[]{:T(128)} %bitcast.90, bf16[256,768]{1,0:T(8,128)(2,1)S(1)} %bitcast.103, bf16[512,768]{1,0:T(8,128)(2,1)S(1)} %get-tuple-element.10), kind=kOutput, calls=%fused_computation.92 | convolution fusion | flops 201588480 | bytes 1704964 | tf_op jit(solution)/shard_map/dot_general | solution.py:89
  20.9 0.3 exponential_reduce_fusion
  21.3 0.1 stack_reshape.7
  21.4 0.1 stack_reshape.6
  21.5 0.7 %collective-permute-start.6 = (f32[3,2,2,4,32]{4,3,2,1,0:T(4,128)S(1)}, f32[3,2,2,4,32]{4,3,2,1,0:T(4,128)S(1)}, u32[]{:S(2)}, u32[]{:S(2)}) collective-permute-start(f32[3,2,2,4,32]{4,3,2,1,0:T(4,128)S(1)} %get-tuple-element.18), channel_id=1, source_target_pairs={{0,8},{4,12},{8,0},{12,4},{1,9},{5,13},{9,1},{13,5},{2,10},{6,14},... | collective-permute-start | bytes 18440 | tf_op jit(solution)/shard_map/ppermute | solution.py:23
  22.2 0.1 pad_maximum_fusion
  22.2 2.8 %collective-permute-start.5 = (f32[3,2,2,4,32]{4,3,2,1,0:T(4,128)S(1)}, f32[3,2,2,4,32]{4,3,2,1,0:T(4,128)S(1)}, u32[]{:S(2)}, u32[]{:S(2)}) collective-permute-start(f32[3,2,2,4,32]{4,3,2,1,0:T(4,128)S(1)} %get-tuple-element.18), channel_id=1, source_target_pairs={{0,4},{4,8},{8,12},{12,0},{1,5},{5,9},{9,13},{13,1},{2,6},{6,10},{... | collective-permute-start | bytes 18440 | tf_op jit(solution)/shard_map/ppermute | solution.py:23
  25.0 1.1 %collective-permute-start.7 = (f32[3,2,2,4,32]{4,3,2,1,0:T(4,128)S(1)}, f32[3,2,2,4,32]{4,3,2,1,0:T(4,128)S(1)}, u32[]{:S(2)}, u32[]{:S(2)}) collective-permute-start(f32[3,2,2,4,32]{4,3,2,1,0:T(4,128)S(1)} %get-tuple-element.18), channel_id=1, source_target_pairs={{0,12},{4,0},{8,4},{12,8},{1,13},{5,1},{9,5},{13,9},{2,14},{6,2},{... | collective-permute-start | bytes 18440 | tf_op jit(solution)/shard_map/ppermute | solution.py:23
  26.1 0.3 collective-permute-done.6
  26.4 1.5 %collective-permute-done.5 = f32[3,2,2,4,32]{4,3,2,1,0:T(4,128)S(1)} collective-permute-done((f32[3,2,2,4,32]{4,3,2,1,0:T(4,128)S(1)}, f32[3,2,2,4,32]{4,3,2,1,0:T(4,128)S(1)}, u32[]{:S(2)}, u32[]{:S(2)}) %collective-permute-start.5) | collective-permute-done | bytes 6176 | tf_op jit(solution)/shard_map/ppermute | solution.py:23
  28.0 0.9 %collective-permute-done.7 = f32[3,2,2,4,32]{4,3,2,1,0:T(4,128)S(1)} collective-permute-done((f32[3,2,2,4,32]{4,3,2,1,0:T(4,128)S(1)}, f32[3,2,2,4,32]{4,3,2,1,0:T(4,128)S(1)}, u32[]{:S(2)}, u32[]{:S(2)}) %collective-permute-start.7) | collective-permute-done | bytes 6176 | tf_op jit(solution)/shard_map/ppermute | solution.py:23
  29.0 0.1 collective-permute-start.8
  29.1 1.9 %pad_maximum_fusion.1 = bf16[2,2,128,768]{3,2,1,0:T(8,128)(2,1)} fusion(bf16[1,2,144,768]{3,2,1,0:T(8,128)(2,1)} %bitcast.95, bf16[1,2,144,768]{3,2,1,0:T(8,128)(2,1)S(1)} %fusion.49), kind=kLoop, calls=%fused_computation.25 | loop fusion | flops 1572864 | bytes 1671168 | tf_op jit(solution)/shard_map/stack | solution.py:25
  31.0 0.3 copy.12
  31.4 0.0 copy-start.2
  31.4 0.0 collective-permute-done.8
  31.5 0.1 mul.113
  31.6 0.1 add.104
  31.7 0.5 %fusion.30 = f32[32]{0:T(128)} fusion(f32[2,2,4,32]{3,2,1,0:T(4,128)S(1)} %bitcast.114, s32[32]{0:T(128)S(1)} %copy-done.4, f32[]{:T(128)} %bitcast.88), kind=kLoop, calls=%fused_computation.85 | loop fusion | flops 96 | bytes 388 | tf_op jit(solution)/shard_map/div | solution.py:148
  32.2 0.4 %fusion.13 = bf16[4,512]{1,0:T(4,128)(2,1)S(1)} fusion(f32[4,128,512]{1,2,0:T(8,128)S(1)} %copy.12, f32[4,128]{1,0:T(4,128)S(1)} %add.104, f32[4,128]{1,0:T(4,128)S(1)} %mul.113), kind=kLoop, calls=%fused_computation.40 | loop fusion | flops 1046528 | bytes 1056768 | tf_op jit(solution)/shard_map/reduce_sum | solution.py:124
  32.5 0.0 copy-done.2
  32.6 1.0 %convert_reduce_fusion = f32[512,768]{1,0:T(8,128)S(1)} fusion(bf16[4,128,768]{2,1,0:T(8,128)(2,1)S(1)} %bitcast.104, f32[4,128,512]{1,2,0:T(8,128)S(1)} %copy.12, f32[4,128]{1,0:T(4,128)S(1)} %add.104, f32[4,128]{1,0:T(4,128)S(1)} %mul.113), kind=kOutput, calls=%fused_computation | convolution fusion | flops 407764992 | bytes 3411968 | tf_op jit(solution)/shard_map/dot_general | solution.py:120
  33.5 0.0 copy-start
  33.6 0.4 %multiply_reduce_fusion = f32[512]{0:T(512)S(1)} fusion(f32[512,768]{1,0:T(8,128)S(1)} %convert_reduce_fusion, f32[512]{0:T(512)S(1)} %broadcast_add_fusion, bf16[512,768]{1,0:T(8,128)(2,1)S(1)} %get-tuple-element.10), kind=kLoop, calls=%fused_computation.10 | loop fusion | flops 1965568 | bytes 2363392 | tf_op jit(solution)/shard_map/reduce_sum | solution.py:12
  34.0 1.2 %multiply_convert_fusion = bf16[512,768]{1,0:T(8,128)(2,1)} fusion(f32[512]{0:T(512)S(1)} %add_rsqrt_fusion, f32[512,768]{1,0:T(8,128)S(1)} %convert_reduce_fusion, f32[512]{0:T(512)S(1)} %broadcast_add_fusion, bf16[512,768]{1,0:T(8,128)(2,1)S(1)} %get-tuple-element.10), kind=kLoop, calls=%fused_computation.9 | loop fusion | flops 1966080 | bytes 3149824 | tf_op jit(solution)/shard_map/convert_element_type | solution.py:145
  (40 shorter events, 0.6 us)
Async XLA Ops:
  0.6 10.5 %copy-start.3 = (bf16[32,768]{1,0:T(8,128)(2,1)S(1)}, bf16[32,768]{1,0:T(8,128)(2,1)}, u32[]{:S(2)}) copy-start(bf16[32,768]{1,0:T(8,128)(2,1)} %param.4) | copy-start | bytes 147460
  0.6 7.9 %copy-start.4 = (s32[32]{0:T(128)S(1)}, s32[32]{0:T(128)}, u32[]{:S(2)}) copy-start(s32[32]{0:T(128)} %param.5) | copy-start | bytes 388
  0.6 8.6 %collective-permute-start = (bf16[32,768]{1,0:T(8,128)(2,1)}, bf16[32,768]{1,0:T(8,128)(2,1)S(1)}, u32[]{:S(2)}, u32[]{:S(2)}) collective-permute-start(bf16[32,768]{1,0:T(8,128)(2,1)} %param.4), channel_id=1, source_target_pairs={{0,4},{4,8},{8,12},{12,0},{1,5},{5,9},{9,13},{13,1},{2,6},{6,10},{... | collective-permute-start | bytes 147464 | tf_op jit(solution)/shard_map/ppermute | solution.py:23
  3.7 5.5 %collective-permute-start.2 = (bf16[32,768]{1,0:T(8,128)(2,1)}, bf16[32,768]{1,0:T(8,128)(2,1)S(1)}, u32[]{:S(2)}, u32[]{:S(2)}) collective-permute-start(bf16[32,768]{1,0:T(8,128)(2,1)} %param.4), channel_id=1, source_target_pairs={{0,12},{4,0},{8,4},{12,8},{1,13},{5,1},{9,5},{13,9},{2,14},{6,2},{... | collective-permute-start | bytes 147464 | tf_op jit(solution)/shard_map/ppermute | solution.py:23
  5.8 5.3 %collective-permute-start.1 = (bf16[32,768]{1,0:T(8,128)(2,1)}, bf16[32,768]{1,0:T(8,128)(2,1)S(1)}, u32[]{:S(2)}, u32[]{:S(2)}) collective-permute-start(bf16[32,768]{1,0:T(8,128)(2,1)} %param.4), channel_id=1, source_target_pairs={{0,8},{4,12},{8,0},{12,4},{1,9},{5,13},{9,1},{13,5},{2,10},{6,14},... | collective-permute-start | bytes 147464 | tf_op jit(solution)/shard_map/ppermute | solution.py:23
  11.2 6.2 %collective-permute-start.3 = (bf16[144,768]{1,0:T(8,128)(2,1)S(1)}, bf16[144,768]{1,0:T(8,128)(2,1)S(1)}, u32[]{:S(2)}, u32[]{:S(2)}) collective-permute-start(bf16[144,768]{1,0:T(8,128)(2,1)S(1)} %get-tuple-element.11), channel_id=1, source_target_pairs={{0,2},{2,0},{1,3},{3,1},{4,6},{6,4},{5,7},{7,5},{8,10},{10,8},{9,1... | collective-permute-start | bytes 663560 | tf_op jit(solution)/shard_map/ppermute | solution.py:23
  17.8 1.9 %collective-permute-start.4 = (bf16[2,144,768]{2,1,0:T(8,128)(2,1)S(1)}, bf16[2,144,768]{2,1,0:T(8,128)(2,1)S(1)}, u32[]{:S(2)}, u32[]{:S(2)}) collective-permute-start(bf16[2,144,768]{2,1,0:T(8,128)(2,1)S(1)} %fusion.9), channel_id=1, source_target_pairs={{0,1},{1,0},{2,3},{3,2},{4,5},{5,4},{6,7},{7,6},{8,9},{9,8},{10,11... | collective-permute-start | bytes 1327112 | tf_op jit(solution)/shard_map/ppermute | solution.py:23
  19.7 0.8 %copy-start.1 = (bf16[2,144,768]{2,1,0:T(8,128)(2,1)}, bf16[2,144,768]{2,1,0:T(8,128)(2,1)S(1)}, u32[]{:S(2)}) copy-start(bf16[2,144,768]{2,1,0:T(8,128)(2,1)S(1)} %collective-permute-done.4) | copy-start | bytes 1327108
  21.5 4.9 %collective-permute-start.6 = (f32[3,2,2,4,32]{4,3,2,1,0:T(4,128)S(1)}, f32[3,2,2,4,32]{4,3,2,1,0:T(4,128)S(1)}, u32[]{:S(2)}, u32[]{:S(2)}) collective-permute-start(f32[3,2,2,4,32]{4,3,2,1,0:T(4,128)S(1)} %get-tuple-element.18), channel_id=1, source_target_pairs={{0,8},{4,12},{8,0},{12,4},{1,9},{5,13},{9,1},{13,5},{2,10},{6,14},... | collective-permute-start | bytes 18440 | tf_op jit(solution)/shard_map/ppermute | solution.py:23
  22.2 5.7 %collective-permute-start.5 = (f32[3,2,2,4,32]{4,3,2,1,0:T(4,128)S(1)}, f32[3,2,2,4,32]{4,3,2,1,0:T(4,128)S(1)}, u32[]{:S(2)}, u32[]{:S(2)}) collective-permute-start(f32[3,2,2,4,32]{4,3,2,1,0:T(4,128)S(1)} %get-tuple-element.18), channel_id=1, source_target_pairs={{0,4},{4,8},{8,12},{12,0},{1,5},{5,9},{9,13},{13,1},{2,6},{6,10},{... | collective-permute-start | bytes 18440 | tf_op jit(solution)/shard_map/ppermute | solution.py:23
  25.0 3.8 %collective-permute-start.7 = (f32[3,2,2,4,32]{4,3,2,1,0:T(4,128)S(1)}, f32[3,2,2,4,32]{4,3,2,1,0:T(4,128)S(1)}, u32[]{:S(2)}, u32[]{:S(2)}) collective-permute-start(f32[3,2,2,4,32]{4,3,2,1,0:T(4,128)S(1)} %get-tuple-element.18), channel_id=1, source_target_pairs={{0,12},{4,0},{8,4},{12,8},{1,13},{5,1},{9,5},{13,9},{2,14},{6,2},{... | collective-permute-start | bytes 18440 | tf_op jit(solution)/shard_map/ppermute | solution.py:23
  29.0 2.4 %collective-permute-start.8 = (f32[3,2,2,4,32]{4,3,2,1,0:T(4,128)S(1)}, f32[3,2,2,4,32]{4,3,2,1,0:T(4,128)S(1)}, u32[]{:S(2)}, u32[]{:S(2)}) collective-permute-start(f32[3,2,2,4,32]{4,3,2,1,0:T(4,128)S(1)} %get-tuple-element.14), channel_id=1, source_target_pairs={{0,1},{1,0},{2,3},{3,2},{4,5},{5,4},{6,7},{7,6},{8,9},{9,8},{10,11... | collective-permute-start | bytes 18440 | tf_op jit(solution)/shard_map/ppermute | solution.py:23
  31.4 1.2 %copy-start.2 = (bf16[2,2,128,768]{3,2,1,0:T(8,128)(2,1)S(1)}, bf16[2,2,128,768]{3,2,1,0:T(8,128)(2,1)}, u32[]{:S(2)}) copy-start(bf16[2,2,128,768]{3,2,1,0:T(8,128)(2,1)} %pad_maximum_fusion.1) | copy-start | bytes 2359300
  33.5 1.7 %copy-start = (f32[512,768]{1,0:T(8,128)}, f32[512,768]{1,0:T(8,128)S(1)}, u32[]{:S(2)}) copy-start(f32[512,768]{1,0:T(8,128)S(1)} %convert_reduce_fusion) | copy-start | bytes 4718596

commit v20 on v19

--- a/solution.py
+++ b/solution.py
@@ -112,17 +112,20 @@
     log_sum = (stats[0] + jnp.log(stats[1])).reshape(-1)
 
     if n_rows * width * 2 <= (4 << 20):
-        grouped_rows = payload[:, :, :cent_rows].reshape(n_groups, -1, width)
+        group_shape = (sizes["sub"], sizes["dp"], cent_rows)
         own_scores = jnp.concatenate([blocks_of_half[0] for blocks_of_half in score_blocks], axis=0)
         grouped_resp = (
             weight_float[:, None] * jnp.exp(own_scores - log_sum[:, None])
-        ).astype(jnp.bfloat16).reshape(n_groups, -1, own_count)
+        ).astype(jnp.bfloat16).reshape(group_shape + (own_count,))
         partial_value = lax.dot_general(
-            grouped_resp, grouped_rows, (((1,), (1,)), ((0,), (0,))), preferred_element_type=jnp.float32
+            grouped_resp,
+            payload[:, :, :cent_rows],
+            (((2,), (2,)), ((0, 1), (0, 1))),
+            preferred_element_type=jnp.float32,
         ).astype(jnp.bfloat16)
-        centroid_sums = jnp.sum(partial_value.astype(jnp.float32), axis=0)
-        weight_mass = jnp.sum(grouped_resp.astype(jnp.float32), axis=1).astype(jnp.bfloat16)
-        own_mass = jnp.sum(weight_mass.astype(jnp.float32), axis=0)
+        centroid_sums = jnp.sum(partial_value.astype(jnp.float32), axis=(0, 1))
+        weight_mass = jnp.sum(grouped_resp.astype(jnp.float32), axis=2).astype(jnp.bfloat16)
+        own_mass = jnp.sum(weight_mass.astype(jnp.float32), axis=(0, 1))
     else:
         half_log_sum = log_sum.reshape(sizes["sub"], -1)
         half_weight = weight_float.reshape(sizes["sub"], -1)

time: 35.5 us -> 35.4 us (level)
  other arithmetic: 9.39 us -> 7.52 us
  matrix products: 2.91 us -> 4.03 us
  waiting for transfers between devices: 7.94 us -> 8.71 us
    another operation x3 -> x2, other arithmetic: 1.99 us -> 0.06 us  [gather_stage(): return jnp.stack(parts)]
    dot_general x1, matrix products: 0.98 us -> 2.1 us  [shards(): lax.dot_general(grouped_resp, payload[:, :, :cent_rows], (((2,), (2,)), (...]
    ppermute x9, waiting for transfers between devices: 7.94 us -> 8.71 us  [gather_stage(): lax.ppermute(value, name, [(j, (j + q) % size) for j in range(size)])]
  transfers between devices with their start and end apart: 9 -> 9, of which waited for: 6 -> 7; matrix products, arithmetic and copies ran while one was open for 20% -> 15% of each run, Pallas kernels for 0% -> 0%
where the time goes in v20:
time: 35.4 us; the launch traced here: 35.2 us
  starting transfers between devices  12.4 us (35%)
  waiting for transfers between devices  8.71 us (25%)
  other arithmetic  7.52 us (21%)
  matrix products  4.03 us (11%)
  between operations  1.58 us (4%)
  local copies, waits for them, and re-layouts  1 us (3%)
    ppermute x9, starting transfers between devices, gather_stage(): lax.ppermute(value, name, [(j, (j + q) % size) for j in range(size)])  12.4 us
    ppermute x9, waiting for transfers between devices, gather_stage(): lax.ppermute(value, name, [(j, (j + q) % size) for j in range(size)])  8.71 us
    reduce_sum x3, other arithmetic, normalize(): jnp.sum(floats * floats, axis=-1, keepdims=True) + 1e-06  2.33 us
    dot_general x1, matrix products, shards(): lax.dot_general(grouped_resp, payload[:, :, :cent_rows], (((2,), (2,)), (...  2.1 us
    dot_general x4, matrix products, shards(): lax.dot_general(rows, cents, (((1,), (1,)), ((), ())), preferred_element_...  1.93 us
    convert_element_type x1, other arithmetic, shards(): score_cents = [lax.optimization_barrier(normalize(lax.dynamic_slice_in_di...  1.69 us
    convert_element_type x1, other arithmetic, shards(): renormed = normalize(moved).astype(jnp.bfloat16)  1.25 us
  transfers between devices with their start and end apart: 9, of which 7 were waited for; matrix products, arithmetic and copies ran while one was open for 15% of the time, Pallas kernels for 0%

profile of v20, /device:TPU:0, one launch (start us, length us, event | category | flops | bytes accessed | tf_op | source)
XLA Modules:
  0.0 35.2 jit_solution(12733096469709343258)
XLA Ops:
  0.6 0.0 copy-start.2
  0.6 0.0 copy-start.3
  0.6 3.1 %collective-permute-start = (bf16[32,768]{1,0:T(8,128)(2,1)}, bf16[32,768]{1,0:T(8,128)(2,1)S(1)}, u32[]{:S(2)}, u32[]{:S(2)}) collective-permute-start(bf16[32,768]{1,0:T(8,128)(2,1)} %param.4), channel_id=1, source_target_pairs={{0,4},{4,8},{8,12},{12,0},{1,5},{5,9},{9,13},{13,1},{2,6},{6,10},{... | collective-permute-start | bytes 147464 | tf_op jit(solution)/shard_map/ppermute | solution.py:23
  3.7 2.1 %collective-permute-start.2 = (bf16[32,768]{1,0:T(8,128)(2,1)}, bf16[32,768]{1,0:T(8,128)(2,1)S(1)}, u32[]{:S(2)}, u32[]{:S(2)}) collective-permute-start(bf16[32,768]{1,0:T(8,128)(2,1)} %param.4), channel_id=1, source_target_pairs={{0,12},{4,0},{8,4},{12,8},{1,13},{5,1},{9,5},{13,9},{2,14},{6,2},{... | collective-permute-start | bytes 147464 | tf_op jit(solution)/shard_map/ppermute | solution.py:23
  5.8 0.9 %collective-permute-start.1 = (bf16[32,768]{1,0:T(8,128)(2,1)}, bf16[32,768]{1,0:T(8,128)(2,1)S(1)}, u32[]{:S(2)}, u32[]{:S(2)}) collective-permute-start(bf16[32,768]{1,0:T(8,128)(2,1)} %param.4), channel_id=1, source_target_pairs={{0,8},{4,12},{8,0},{12,4},{1,9},{5,13},{9,1},{13,5},{2,10},{6,14},... | collective-permute-start | bytes 147464 | tf_op jit(solution)/shard_map/ppermute | solution.py:23
  6.8 1.7 %fusion.2 = (f32[512]{0:T(512)S(1)}, f32[512]{0:T(512)S(1)}) fusion(bf16[2048,768]{1,0:T(8,128)(2,1)} %param.6, s32[]{:T(128)S(6)} %select_n.20, s32[]{:T(128)S(6)} %select_n.18), kind=kLoop, calls=%fused_computation.7 | loop fusion | flops 2358272 | bytes 1576968 | tf_op jit(solution)/shard_map/reduce_sum | solution.py:12
  8.5 0.0 copy-done.3
  9.2 0.0 collective-permute-done
  9.2 0.0 collective-permute-done.2
  9.2 1.9 %collective-permute-done.1 = bf16[32,768]{1,0:T(8,128)(2,1)S(1)} collective-permute-done((bf16[32,768]{1,0:T(8,128)(2,1)}, bf16[32,768]{1,0:T(8,128)(2,1)S(1)}, u32[]{:S(2)}, u32[]{:S(2)}) %collective-permute-start.1) | collective-permute-done | bytes 49184 | tf_op jit(solution)/shard_map/ppermute | solution.py:23
  11.1 0.0 copy-done.2
  11.2 1.6 %collective-permute-start.3 = (bf16[144,768]{1,0:T(8,128)(2,1)S(1)}, bf16[144,768]{1,0:T(8,128)(2,1)S(1)}, u32[]{:S(2)}, u32[]{:S(2)}) collective-permute-start(bf16[144,768]{1,0:T(8,128)(2,1)S(1)} %get-tuple-element.11), channel_id=1, source_target_pairs={{0,2},{2,0},{1,3},{3,1},{4,6},{6,4},{5,7},{7,5},{8,10},{10,8},{9,1... | collective-permute-start | bytes 663560 | tf_op jit(solution)/shard_map/ppermute | solution.py:23
  12.8 1.7 %fusion.3 = (bf16[512,768]{1,0:T(8,128)(2,1)S(1)}, bf16[512,768]{1,0:T(8,128)(2,1)S(1)}) fusion(f32[512]{0:T(512)S(1)} %get-tuple-element.29, bf16[2048,768]{1,0:T(8,128)(2,1)} %param.6, s32[]{:T(128)S(6)} %select_n.20, f32[512]{0:T(512)S(1)} %get-tuple-element.30, s32[]{:T(128)S(6)} %select_n.18), kind=kLoop, calls=%fused_computation.8 | loop fusion | flops 2359296 | bytes 3149832 | tf_op jit(solution)/shard_map/convert_element_type | solution.py:78
  14.5 2.9 %collective-permute-done.3 = bf16[144,768]{1,0:T(8,128)(2,1)S(1)} collective-permute-done((bf16[144,768]{1,0:T(8,128)(2,1)S(1)}, bf16[144,768]{1,0:T(8,128)(2,1)S(1)}, u32[]{:S(2)}, u32[]{:S(2)}) %collective-permute-start.3) | collective-permute-done | bytes 221216 | tf_op jit(solution)/shard_map/ppermute | solution.py:23
  17.4 0.2 fusion.6
  17.6 0.1 fusion.7
  17.8 0.1 collective-permute-start.4
  17.9 0.5 %fusion.41 = (f32[256]{0:T(256)S(1)}, f32[256,512]{1,0:T(8,128)S(1)}) fusion(f32[]{:T(128)} %bitcast.89, bf16[256,768]{1,0:T(8,128)(2,1)S(1)} %bitcast.95, bf16[512,768]{1,0:T(8,128)(2,1)S(1)} %get-tuple-element.9), kind=kOutput, calls=%fused_computation.97 | convolution fusion | flops 201588480 | bytes 1704964 | tf_op jit(solution)/shard_map/dot_general | solution.py:89
  18.4 0.5 %fusion.40 = (f32[256]{0:T(256)S(1)}, f32[256,512]{1,0:T(8,128)S(1)}) fusion(f32[]{:T(128)} %bitcast.85, bf16[256,768]{1,0:T(8,128)(2,1)S(1)} %bitcast.96, bf16[512,768]{1,0:T(8,128)(2,1)S(1)} %get-tuple-element.10), kind=kOutput, calls=%fused_computation.96 | convolution fusion | flops 201588480 | bytes 1704964 | tf_op jit(solution)/shard_map/dot_general | solution.py:89
  18.9 0.3 exponential_reduce_fusion.2
  19.2 0.5 %collective-permute-done.4 = bf16[2,144,768]{2,1,0:T(8,128)(2,1)S(1)} collective-permute-done((bf16[2,144,768]{2,1,0:T(8,128)(2,1)S(1)}, bf16[2,144,768]{2,1,0:T(8,128)(2,1)S(1)}, u32[]{:S(2)}, u32[]{:S(2)}) %collective-permute-start.4) | collective-permute-done | bytes 442400 | tf_op jit(solution)/shard_map/ppermute | solution.py:23
  19.7 0.0 copy-start.1
  19.7 0.5 %fusion.39 = (f32[256]{0:T(256)S(1)}, f32[256,512]{1,0:T(8,128)S(1)}) fusion(f32[]{:T(128)} %bitcast.87, bf16[256,768]{1,0:T(8,128)(2,1)S(1)} %bitcast.97, bf16[512,768]{1,0:T(8,128)(2,1)S(1)} %get-tuple-element.9), kind=kOutput, calls=%fused_computation.95 | convolution fusion | flops 201588480 | bytes 1704964 | tf_op jit(solution)/shard_map/dot_general | solution.py:89
  20.2 0.2 copy-done.1
  20.4 0.5 %fusion.38 = (f32[256]{0:T(256)S(1)}, f32[256,512]{1,0:T(8,128)S(1)}) fusion(f32[]{:T(128)} %bitcast.88, bf16[256,768]{1,0:T(8,128)(2,1)S(1)} %bitcast.98, bf16[512,768]{1,0:T(8,128)(2,1)S(1)} %get-tuple-element.10), kind=kOutput, calls=%fused_computation.94 | convolution fusion | flops 201588480 | bytes 1704964 | tf_op jit(solution)/shard_map/dot_general | solution.py:89
  20.9 0.3 exponential_reduce_fusion
  21.3 0.1 stack_reshape.7
  21.4 0.1 stack_reshape.6
  21.5 0.7 %collective-permute-start.6 = (f32[3,2,2,4,32]{4,3,2,1,0:T(4,128)S(1)}, f32[3,2,2,4,32]{4,3,2,1,0:T(4,128)S(1)}, u32[]{:S(2)}, u32[]{:S(2)}) collective-permute-start(f32[3,2,2,4,32]{4,3,2,1,0:T(4,128)S(1)} %get-tuple-element.18), channel_id=1, source_target_pairs={{0,8},{4,12},{8,0},{12,4},{1,9},{5,13},{9,1},{13,5},{2,10},{6,14},... | collective-permute-start | bytes 18440 | tf_op jit(solution)/shard_map/ppermute | solution.py:23
  22.2 2.7 %collective-permute-start.5 = (f32[3,2,2,4,32]{4,3,2,1,0:T(4,128)S(1)}, f32[3,2,2,4,32]{4,3,2,1,0:T(4,128)S(1)}, u32[]{:S(2)}, u32[]{:S(2)}) collective-permute-start(f32[3,2,2,4,32]{4,3,2,1,0:T(4,128)S(1)} %get-tuple-element.18), channel_id=1, source_target_pairs={{0,4},{4,8},{8,12},{12,0},{1,5},{5,9},{9,13},{13,1},{2,6},{6,10},{... | collective-permute-start | bytes 18440 | tf_op jit(solution)/shard_map/ppermute | solution.py:23
  24.9 1.1 %collective-permute-start.7 = (f32[3,2,2,4,32]{4,3,2,1,0:T(4,128)S(1)}, f32[3,2,2,4,32]{4,3,2,1,0:T(4,128)S(1)}, u32[]{:S(2)}, u32[]{:S(2)}) collective-permute-start(f32[3,2,2,4,32]{4,3,2,1,0:T(4,128)S(1)} %get-tuple-element.18), channel_id=1, source_target_pairs={{0,12},{4,0},{8,4},{12,8},{1,13},{5,1},{9,5},{13,9},{2,14},{6,2},{... | collective-permute-start | bytes 18440 | tf_op jit(solution)/shard_map/ppermute | solution.py:23
  26.0 0.4 %collective-permute-done.6 = f32[3,2,2,4,32]{4,3,2,1,0:T(4,128)S(1)} collective-permute-done((f32[3,2,2,4,32]{4,3,2,1,0:T(4,128)S(1)}, f32[3,2,2,4,32]{4,3,2,1,0:T(4,128)S(1)}, u32[]{:S(2)}, u32[]{:S(2)}) %collective-permute-start.6) | collective-permute-done | bytes 6176 | tf_op jit(solution)/shard_map/ppermute | solution.py:23
  26.4 1.4 %collective-permute-done.5 = f32[3,2,2,4,32]{4,3,2,1,0:T(4,128)S(1)} collective-permute-done((f32[3,2,2,4,32]{4,3,2,1,0:T(4,128)S(1)}, f32[3,2,2,4,32]{4,3,2,1,0:T(4,128)S(1)}, u32[]{:S(2)}, u32[]{:S(2)}) %collective-permute-start.5) | collective-permute-done | bytes 6176 | tf_op jit(solution)/shard_map/ppermute | solution.py:23
  27.8 0.9 %collective-permute-done.7 = f32[3,2,2,4,32]{4,3,2,1,0:T(4,128)S(1)} collective-permute-done((f32[3,2,2,4,32]{4,3,2,1,0:T(4,128)S(1)}, f32[3,2,2,4,32]{4,3,2,1,0:T(4,128)S(1)}, u32[]{:S(2)}, u32[]{:S(2)}) %collective-permute-start.7) | collective-permute-done | bytes 6176 | tf_op jit(solution)/shard_map/ppermute | solution.py:23
  28.9 0.1 collective-permute-start.8
  29.0 0.1 pad_maximum_fusion
  29.0 0.3 copy.12
  29.4 0.8 %collective-permute-done.8 = f32[3,2,2,4,32]{4,3,2,1,0:T(4,128)S(1)} collective-permute-done((f32[3,2,2,4,32]{4,3,2,1,0:T(4,128)S(1)}, f32[3,2,2,4,32]{4,3,2,1,0:T(4,128)S(1)}, u32[]{:S(2)}, u32[]{:S(2)}) %collective-permute-start.8) | collective-permute-done | bytes 6176 | tf_op jit(solution)/shard_map/ppermute | solution.py:23
  30.2 0.1 mul.113
  30.3 0.1 add.104
  30.4 0.4 %fusion.14 = bf16[2,2,512]{2,1,0:T(2,128)(2,1)S(1)} fusion(f32[2,2,128,512]{2,3,1,0:T(8,128)S(1)} %copy.12, f32[2,2,128]{2,1,0:T(2,128)S(1)} %add.104, f32[2,2,128]{2,1,0:T(2,128)S(1)} %mul.113), kind=kLoop, calls=%fused_computation.41 | loop fusion | flops 1046528 | bytes 1056768 | tf_op jit(solution)/shard_map/reduce_sum | solution.py:127
  30.8 2.1 %convert_reduce_fusion = f32[512,768]{1,0:T(8,128)S(1)} fusion(bf16[1,2,144,768]{3,2,1,0:T(8,128)(2,1)} %bitcast.101, bf16[1,2,144,768]{3,2,1,0:T(8,128)(2,1)S(1)} %fusion.50, f32[2,2,128,512]{2,3,1,0:T(8,128)S(1)} %copy.12, f32[2,2,128]{2,1,0:T(2,128)S(1)} %add.104, f32[2,2,128]{2,1,0:T(2,128)S(1)} %mul.113), kind=kOutput, calls=%fused_computation | convolution fusion | flops 409337856 | bytes 3510272 | tf_op jit(solution)/shard_map/dot_general | solution.py:120
  32.9 0.0 copy-start
  32.9 0.6 %fusion.31 = f32[32]{0:T(128)} fusion(f32[2,2,4,32]{3,2,1,0:T(4,128)S(1)} %bitcast.111, s32[32]{0:T(128)S(1)} %copy-done.3, f32[]{:T(128)} %bitcast.86), kind=kLoop, calls=%fused_computation.86 | loop fusion | flops 96 | bytes 388 | tf_op jit(solution)/shard_map/div | solution.py:151
  33.5 0.4 %multiply_reduce_fusion = f32[512]{0:T(512)S(1)} fusion(f32[512,768]{1,0:T(8,128)S(1)} %convert_reduce_fusion, f32[512]{0:T(512)S(1)} %broadcast_add_fusion, bf16[512,768]{1,0:T(8,128)(2,1)S(1)} %get-tuple-element.10), kind=kLoop, calls=%fused_computation.10 | loop fusion | flops 1965568 | bytes 2363392 | tf_op jit(solution)/shard_map/reduce_sum | solution.py:12
  33.9 1.2 %multiply_convert_fusion = bf16[512,768]{1,0:T(8,128)(2,1)} fusion(f32[512]{0:T(512)S(1)} %add_rsqrt_fusion, f32[512,768]{1,0:T(8,128)S(1)} %convert_reduce_fusion, f32[512]{0:T(512)S(1)} %broadcast_add_fusion, bf16[512,768]{1,0:T(8,128)(2,1)S(1)} %get-tuple-element.10), kind=kLoop, calls=%fused_computation.9 | loop fusion | flops 1966080 | bytes 3149824 | tf_op jit(solution)/shard_map/convert_element_type | solution.py:148
  35.2 0.0 copy-done
  (38 shorter events, 0.6 us)
Async XLA Ops:
  0.6 10.5 %copy-start.2 = (bf16[32,768]{1,0:T(8,128)(2,1)S(1)}, bf16[32,768]{1,0:T(8,128)(2,1)}, u32[]{:S(2)}) copy-start(bf16[32,768]{1,0:T(8,128)(2,1)} %param.4) | copy-start | bytes 147460
  0.6 7.9 %copy-start.3 = (s32[32]{0:T(128)S(1)}, s32[32]{0:T(128)}, u32[]{:S(2)}) copy-start(s32[32]{0:T(128)} %param.5) | copy-start | bytes 388
  0.6 8.6 %collective-permute-start = (bf16[32,768]{1,0:T(8,128)(2,1)}, bf16[32,768]{1,0:T(8,128)(2,1)S(1)}, u32[]{:S(2)}, u32[]{:S(2)}) collective-permute-start(bf16[32,768]{1,0:T(8,128)(2,1)} %param.4), channel_id=1, source_target_pairs={{0,4},{4,8},{8,12},{12,0},{1,5},{5,9},{9,13},{13,1},{2,6},{6,10},{... | collective-permute-start | bytes 147464 | tf_op jit(solution)/shard_map/ppermute | solution.py:23
  3.7 5.5 %collective-permute-start.2 = (bf16[32,768]{1,0:T(8,128)(2,1)}, bf16[32,768]{1,0:T(8,128)(2,1)S(1)}, u32[]{:S(2)}, u32[]{:S(2)}) collective-permute-start(bf16[32,768]{1,0:T(8,128)(2,1)} %param.4), channel_id=1, source_target_pairs={{0,12},{4,0},{8,4},{12,8},{1,13},{5,1},{9,5},{13,9},{2,14},{6,2},{... | collective-permute-start | bytes 147464 | tf_op jit(solution)/shard_map/ppermute | solution.py:23
  5.8 5.3 %collective-permute-start.1 = (bf16[32,768]{1,0:T(8,128)(2,1)}, bf16[32,768]{1,0:T(8,128)(2,1)S(1)}, u32[]{:S(2)}, u32[]{:S(2)}) collective-permute-start(bf16[32,768]{1,0:T(8,128)(2,1)} %param.4), channel_id=1, source_target_pairs={{0,8},{4,12},{8,0},{12,4},{1,9},{5,13},{9,1},{13,5},{2,10},{6,14},... | collective-permute-start | bytes 147464 | tf_op jit(solution)/shard_map/ppermute | solution.py:23
  11.2 6.2 %collective-permute-start.3 = (bf16[144,768]{1,0:T(8,128)(2,1)S(1)}, bf16[144,768]{1,0:T(8,128)(2,1)S(1)}, u32[]{:S(2)}, u32[]{:S(2)}) collective-permute-start(bf16[144,768]{1,0:T(8,128)(2,1)S(1)} %get-tuple-element.11), channel_id=1, source_target_pairs={{0,2},{2,0},{1,3},{3,1},{4,6},{6,4},{5,7},{7,5},{8,10},{10,8},{9,1... | collective-permute-start | bytes 663560 | tf_op jit(solution)/shard_map/ppermute | solution.py:23
  17.8 1.9 %collective-permute-start.4 = (bf16[2,144,768]{2,1,0:T(8,128)(2,1)S(1)}, bf16[2,144,768]{2,1,0:T(8,128)(2,1)S(1)}, u32[]{:S(2)}, u32[]{:S(2)}) collective-permute-start(bf16[2,144,768]{2,1,0:T(8,128)(2,1)S(1)} %fusion.10), channel_id=1, source_target_pairs={{0,1},{1,0},{2,3},{3,2},{4,5},{5,4},{6,7},{7,6},{8,9},{9,8},{10,11... | collective-permute-start | bytes 1327112 | tf_op jit(solution)/shard_map/ppermute | solution.py:23
  19.7 0.8 %copy-start.1 = (bf16[2,144,768]{2,1,0:T(8,128)(2,1)}, bf16[2,144,768]{2,1,0:T(8,128)(2,1)S(1)}, u32[]{:S(2)}) copy-start(bf16[2,144,768]{2,1,0:T(8,128)(2,1)S(1)} %collective-permute-done.4) | copy-start | bytes 1327108
  21.5 4.9 %collective-permute-start.6 = (f32[3,2,2,4,32]{4,3,2,1,0:T(4,128)S(1)}, f32[3,2,2,4,32]{4,3,2,1,0:T(4,128)S(1)}, u32[]{:S(2)}, u32[]{:S(2)}) collective-permute-start(f32[3,2,2,4,32]{4,3,2,1,0:T(4,128)S(1)} %get-tuple-element.18), channel_id=1, source_target_pairs={{0,8},{4,12},{8,0},{12,4},{1,9},{5,13},{9,1},{13,5},{2,10},{6,14},... | collective-permute-start | bytes 18440 | tf_op jit(solution)/shard_map/ppermute | solution.py:23
  22.2 5.6 %collective-permute-start.5 = (f32[3,2,2,4,32]{4,3,2,1,0:T(4,128)S(1)}, f32[3,2,2,4,32]{4,3,2,1,0:T(4,128)S(1)}, u32[]{:S(2)}, u32[]{:S(2)}) collective-permute-start(f32[3,2,2,4,32]{4,3,2,1,0:T(4,128)S(1)} %get-tuple-element.18), channel_id=1, source_target_pairs={{0,4},{4,8},{8,12},{12,0},{1,5},{5,9},{9,13},{13,1},{2,6},{6,10},{... | collective-permute-start | bytes 18440 | tf_op jit(solution)/shard_map/ppermute | solution.py:23
  24.9 3.8 %collective-permute-start.7 = (f32[3,2,2,4,32]{4,3,2,1,0:T(4,128)S(1)}, f32[3,2,2,4,32]{4,3,2,1,0:T(4,128)S(1)}, u32[]{:S(2)}, u32[]{:S(2)}) collective-permute-start(f32[3,2,2,4,32]{4,3,2,1,0:T(4,128)S(1)} %get-tuple-element.18), channel_id=1, source_target_pairs={{0,12},{4,0},{8,4},{12,8},{1,13},{5,1},{9,5},{13,9},{2,14},{6,2},{... | collective-permute-start | bytes 18440 | tf_op jit(solution)/shard_map/ppermute | solution.py:23
  28.9 1.3 %collective-permute-start.8 = (f32[3,2,2,4,32]{4,3,2,1,0:T(4,128)S(1)}, f32[3,2,2,4,32]{4,3,2,1,0:T(4,128)S(1)}, u32[]{:S(2)}, u32[]{:S(2)}) collective-permute-start(f32[3,2,2,4,32]{4,3,2,1,0:T(4,128)S(1)} %get-tuple-element.14), channel_id=1, source_target_pairs={{0,1},{1,0},{2,3},{3,2},{4,5},{5,4},{6,7},{7,6},{8,9},{9,8},{10,11... | collective-permute-start | bytes 18440 | tf_op jit(solution)/shard_map/ppermute | solution.py:23
  32.9 2.3 %copy-start = (f32[512,768]{1,0:T(8,128)}, f32[512,768]{1,0:T(8,128)S(1)}, u32[]{:S(2)}) copy-start(f32[512,768]{1,0:T(8,128)S(1)} %convert_reduce_fusion) | copy-start | bytes 4718596

commit v21 on v18

--- a/solution.py
+++ b/solution.py
@@ -143,8 +143,8 @@
     moved = own_cents.astype(jnp.float32) + centroid_sums / (own_mass + 1.0)[:, None]
     renormed = normalize(moved).astype(jnp.bfloat16)
 
-    own_log_sum = log_sum.reshape(block_shape)[own_block("sub"), own_block("dp"), own_cent]
-    objective = weights.astype(jnp.float32) * own_log_sum / sharpness
+    own_rows = (own_block("sub"), own_block("dp"), own_cent)
+    objective = (weight_float.reshape(block_shape)[own_rows] * log_sum.reshape(block_shape)[own_rows]) / sharpness
     return (centroid_sums, renormed, objective)
 
 

time: 34.5 us -> 34.5 us (level)
  no operation moved by 1% of the time
where the time goes in v21:
time: 34.5 us; the launch traced here: 34.3 us
  starting transfers between devices  12.4 us (36%)
  other arithmetic  9.18 us (27%)
  waiting for transfers between devices  7.54 us (22%)
  matrix products  2.92 us (8%)
  between operations  1.62 us (5%)
  local copies, waits for them, and re-layouts  0.71 us (2%)
    ppermute x9, starting transfers between devices, gather_stage(): lax.ppermute(value, name, [(j, (j + q) % size) for j in range(size)])  12.4 us
    ppermute x9, waiting for transfers between devices, gather_stage(): lax.ppermute(value, name, [(j, (j + q) % size) for j in range(size)])  7.54 us
    reduce_sum x5, other arithmetic, normalize(): jnp.sum(floats * floats, axis=-1, keepdims=True) + 1e-06  2.72 us
    dot_general x4, matrix products, shards(): lax.dot_general(rows, cents, (((1,), (1,)), ((), ())), preferred_element_...  1.94 us
    convert_element_type x1, other arithmetic, shards(): score_cents = [lax.optimization_barrier(normalize(lax.dynamic_slice_in_di...  1.69 us
    convert_element_type x1, other arithmetic, shards(): renormed = normalize(moved).astype(jnp.bfloat16)  1.25 us
    convert_element_type x1, other arithmetic, shards(): normalize(payload[:, :, :cent_rows].reshape(-1, width)).astype(jnp.bfloat16)  1.04 us
    dot_general x1, matrix products, shards(): lax.dot_general(grouped_resp, grouped_rows, (((1,), (1,)), ((0,), (0,))),...  0.98 us
  transfers between devices with their start and end apart: 9, of which 6 were waited for; matrix products, arithmetic and copies ran while one was open for 18% of the time, Pallas kernels for 0%

profile of v21, /device:TPU:0, one launch (start us, length us, event | category | flops | bytes accessed | tf_op | source)
XLA Modules:
  0.0 34.3 jit_solution(4381924078531542847)
XLA Ops:
  0.6 3.1 %collective-permute-start = (bf16[32,768]{1,0:T(8,128)(2,1)}, bf16[32,768]{1,0:T(8,128)(2,1)S(1)}, u32[]{:S(2)}, u32[]{:S(2)}) collective-permute-start(bf16[32,768]{1,0:T(8,128)(2,1)} %param.4), channel_id=1, source_target_pairs={{0,4},{4,8},{8,12},{12,0},{1,5},{5,9},{9,13},{13,1},{2,6},{6,10},{... | collective-permute-start | bytes 147464 | tf_op jit(solution)/shard_map/ppermute | solution.py:23
  3.7 2.1 %collective-permute-start.2 = (bf16[32,768]{1,0:T(8,128)(2,1)}, bf16[32,768]{1,0:T(8,128)(2,1)S(1)}, u32[]{:S(2)}, u32[]{:S(2)}) collective-permute-start(bf16[32,768]{1,0:T(8,128)(2,1)} %param.4), channel_id=1, source_target_pairs={{0,12},{4,0},{8,4},{12,8},{1,13},{5,1},{9,5},{13,9},{2,14},{6,2},{... | collective-permute-start | bytes 147464 | tf_op jit(solution)/shard_map/ppermute | solution.py:23
  5.8 0.9 %collective-permute-start.1 = (bf16[32,768]{1,0:T(8,128)(2,1)}, bf16[32,768]{1,0:T(8,128)(2,1)S(1)}, u32[]{:S(2)}, u32[]{:S(2)}) collective-permute-start(bf16[32,768]{1,0:T(8,128)(2,1)} %param.4), channel_id=1, source_target_pairs={{0,8},{4,12},{8,0},{12,4},{1,9},{5,13},{9,1},{13,5},{2,10},{6,14},... | collective-permute-start | bytes 147464 | tf_op jit(solution)/shard_map/ppermute | solution.py:23
  6.8 1.7 %fusion.2 = (f32[512]{0:T(512)S(1)}, f32[512]{0:T(512)S(1)}) fusion(bf16[2048,768]{1,0:T(8,128)(2,1)} %param.6, s32[]{:T(128)S(6)} %select_n.20, s32[]{:T(128)S(6)} %select_n.18), kind=kLoop, calls=%fused_computation.7 | loop fusion | flops 2358272 | bytes 1576968 | tf_op jit(solution)/shard_map/reduce_sum | solution.py:12
  9.2 0.0 collective-permute-done
  9.2 0.0 collective-permute-done.2
  9.2 1.9 %collective-permute-done.1 = bf16[32,768]{1,0:T(8,128)(2,1)S(1)} collective-permute-done((bf16[32,768]{1,0:T(8,128)(2,1)}, bf16[32,768]{1,0:T(8,128)(2,1)S(1)}, u32[]{:S(2)}, u32[]{:S(2)}) %collective-permute-start.1) | collective-permute-done | bytes 49184 | tf_op jit(solution)/shard_map/ppermute | solution.py:23
  11.2 1.6 %collective-permute-start.3 = (bf16[144,768]{1,0:T(8,128)(2,1)S(1)}, bf16[144,768]{1,0:T(8,128)(2,1)S(1)}, u32[]{:S(2)}, u32[]{:S(2)}) collective-permute-start(bf16[144,768]{1,0:T(8,128)(2,1)S(1)} %get-tuple-element.14), channel_id=1, source_target_pairs={{0,2},{2,0},{1,3},{3,1},{4,6},{6,4},{5,7},{7,5},{8,10},{10,8},{9,1... | collective-permute-start | bytes 663560 | tf_op jit(solution)/shard_map/ppermute | solution.py:23
  12.8 1.7 %fusion.3 = (bf16[512,768]{1,0:T(8,128)(2,1)S(1)}, bf16[512,768]{1,0:T(8,128)(2,1)S(1)}) fusion(f32[512]{0:T(512)S(1)} %get-tuple-element.31, bf16[2048,768]{1,0:T(8,128)(2,1)} %param.6, s32[]{:T(128)S(6)} %select_n.20, f32[512]{0:T(512)S(1)} %get-tuple-element.32, s32[]{:T(128)S(6)} %select_n.18), kind=kLoop, calls=%fused_computation.8 | loop fusion | flops 2359296 | bytes 3149832 | tf_op jit(solution)/shard_map/convert_element_type | solution.py:76
  14.5 2.9 %collective-permute-done.3 = bf16[144,768]{1,0:T(8,128)(2,1)S(1)} collective-permute-done((bf16[144,768]{1,0:T(8,128)(2,1)S(1)}, bf16[144,768]{1,0:T(8,128)(2,1)S(1)}, u32[]{:S(2)}, u32[]{:S(2)}) %collective-permute-start.3) | collective-permute-done | bytes 221216 | tf_op jit(solution)/shard_map/ppermute | solution.py:23
  17.4 0.1 fusion.31
  17.5 0.2 multiply_reduce_fusion.3
  17.6 0.1 slice_convert_fusion.1
  17.7 0.1 collective-permute-start.4
  17.8 0.1 fusion.7
  17.9 0.5 %fusion.37 = (f32[256]{0:T(256)S(1)}, f32[256,512]{1,0:T(8,128)S(1)}) fusion(f32[]{:T(128)} %bitcast.101, bf16[256,768]{1,0:T(8,128)(2,1)S(1)} %fusion.7, bf16[512,768]{1,0:T(8,128)(2,1)S(1)} %get-tuple-element.9), kind=kOutput, calls=%fused_computation.99 | convolution fusion | flops 201588480 | bytes 1704964 | tf_op jit(solution)/shard_map/dot_general | solution.py:87
  18.4 0.5 %fusion.36 = (f32[256]{0:T(256)S(1)}, f32[256,512]{1,0:T(8,128)S(1)}) fusion(f32[]{:T(128)} %bitcast.97, bf16[256,768]{1,0:T(8,128)(2,1)S(1)} %fusion.7, bf16[512,768]{1,0:T(8,128)(2,1)S(1)} %get-tuple-element.10), kind=kOutput, calls=%fused_computation.98 | convolution fusion | flops 201588480 | bytes 1704964 | tf_op jit(solution)/shard_map/dot_general | solution.py:87
  18.9 0.3 exponential_reduce_fusion.2
  19.2 0.4 %collective-permute-done.4 = bf16[2,144,768]{2,1,0:T(8,128)(2,1)S(1)} collective-permute-done((bf16[2,144,768]{2,1,0:T(8,128)(2,1)S(1)}, bf16[2,144,768]{2,1,0:T(8,128)(2,1)S(1)}, u32[]{:S(2)}, u32[]{:S(2)}) %collective-permute-start.4) | collective-permute-done | bytes 442400 | tf_op jit(solution)/shard_map/ppermute | solution.py:23
  19.5 0.2 multiply_reduce_fusion.2
  19.7 0.2 multiply_reduce_fusion.1
  19.9 0.1 slice_convert_fusion
  20.0 0.1 fusion.5
  20.2 0.1 fusion.6
  20.3 0.5 %fusion.35 = (f32[256]{0:T(256)S(1)}, f32[256,512]{1,0:T(8,128)S(1)}) fusion(f32[]{:T(128)} %bitcast.99, bf16[256,768]{1,0:T(8,128)(2,1)S(1)} %fusion.6, bf16[512,768]{1,0:T(8,128)(2,1)S(1)} %get-tuple-element.9), kind=kOutput, calls=%fused_computation.97 | convolution fusion | flops 201588480 | bytes 1704964 | tf_op jit(solution)/shard_map/dot_general | solution.py:87
  20.7 0.5 %fusion.34 = (f32[256]{0:T(256)S(1)}, f32[256,512]{1,0:T(8,128)S(1)}) fusion(f32[]{:T(128)} %bitcast.100, bf16[256,768]{1,0:T(8,128)(2,1)S(1)} %fusion.6, bf16[512,768]{1,0:T(8,128)(2,1)S(1)} %get-tuple-element.10), kind=kOutput, calls=%fused_computation.96 | convolution fusion | flops 201588480 | bytes 1704964 | tf_op jit(solution)/shard_map/dot_general | solution.py:87
  21.3 0.3 exponential_reduce_fusion
  21.6 0.1 stack_reshape.7
  21.7 0.1 stack_reshape.6
  21.8 0.7 %collective-permute-start.6 = (f32[3,2,2,4,32]{4,3,2,1,0:T(4,128)S(1)}, f32[3,2,2,4,32]{4,3,2,1,0:T(4,128)S(1)}, u32[]{:S(2)}, u32[]{:S(2)}) collective-permute-start(f32[3,2,2,4,32]{4,3,2,1,0:T(4,128)S(1)} %get-tuple-element.20), channel_id=1, source_target_pairs={{0,8},{4,12},{8,0},{12,4},{1,9},{5,13},{9,1},{13,5},{2,10},{6,14},... | collective-permute-start | bytes 18440 | tf_op jit(solution)/shard_map/ppermute | solution.py:23
  22.5 2.7 %collective-permute-start.5 = (f32[3,2,2,4,32]{4,3,2,1,0:T(4,128)S(1)}, f32[3,2,2,4,32]{4,3,2,1,0:T(4,128)S(1)}, u32[]{:S(2)}, u32[]{:S(2)}) collective-permute-start(f32[3,2,2,4,32]{4,3,2,1,0:T(4,128)S(1)} %get-tuple-element.20), channel_id=1, source_target_pairs={{0,4},{4,8},{8,12},{12,0},{1,5},{5,9},{9,13},{13,1},{2,6},{6,10},{... | collective-permute-start | bytes 18440 | tf_op jit(solution)/shard_map/ppermute | solution.py:23
  25.2 1.1 %collective-permute-start.7 = (f32[3,2,2,4,32]{4,3,2,1,0:T(4,128)S(1)}, f32[3,2,2,4,32]{4,3,2,1,0:T(4,128)S(1)}, u32[]{:S(2)}, u32[]{:S(2)}) collective-permute-start(f32[3,2,2,4,32]{4,3,2,1,0:T(4,128)S(1)} %get-tuple-element.20), channel_id=1, source_target_pairs={{0,12},{4,0},{8,4},{12,8},{1,13},{5,1},{9,5},{13,9},{2,14},{6,2},{... | collective-permute-start | bytes 18440 | tf_op jit(solution)/shard_map/ppermute | solution.py:23
  26.3 1.0 %fusion.4 = bf16[4,128,768]{2,1,0:T(8,128)(2,1)} fusion(f32[2,2,128,768]{3,2,1,0:T(8,128)S(1)} %fusion.5, f32[4,128]{1,0:T(4,128)S(1)} %bitcast.122), kind=kLoop, calls=%fused_computation.10 | loop fusion | flops 786432 | bytes 2361344 | tf_op jit(solution)/shard_map/convert_element_type | solution.py:113
  27.4 0.7 %collective-permute-done.5 = f32[3,2,2,4,32]{4,3,2,1,0:T(4,128)S(1)} collective-permute-done((f32[3,2,2,4,32]{4,3,2,1,0:T(4,128)S(1)}, f32[3,2,2,4,32]{4,3,2,1,0:T(4,128)S(1)}, u32[]{:S(2)}, u32[]{:S(2)}) %collective-permute-start.5) | collective-permute-done | bytes 6176 | tf_op jit(solution)/shard_map/ppermute | solution.py:23
  28.2 0.9 %collective-permute-done.7 = f32[3,2,2,4,32]{4,3,2,1,0:T(4,128)S(1)} collective-permute-done((f32[3,2,2,4,32]{4,3,2,1,0:T(4,128)S(1)}, f32[3,2,2,4,32]{4,3,2,1,0:T(4,128)S(1)}, u32[]{:S(2)}, u32[]{:S(2)}) %collective-permute-start.7) | collective-permute-done | bytes 6176 | tf_op jit(solution)/shard_map/ppermute | solution.py:23
  29.2 0.1 collective-permute-start.8
  29.3 0.1 pad_maximum_fusion
  29.4 0.3 copy.12
  29.7 0.0 copy-start.1
  29.7 0.8 %collective-permute-done.8 = f32[3,2,2,4,32]{4,3,2,1,0:T(4,128)S(1)} collective-permute-done((f32[3,2,2,4,32]{4,3,2,1,0:T(4,128)S(1)}, f32[3,2,2,4,32]{4,3,2,1,0:T(4,128)S(1)}, u32[]{:S(2)}, u32[]{:S(2)}) %collective-permute-start.8) | collective-permute-done | bytes 6176 | tf_op jit(solution)/shard_map/ppermute | solution.py:23
  30.5 0.1 mul.143
  30.6 0.1 add.120
  30.7 0.5 %fusion.27 = f32[32]{0:T(128)} fusion(f32[2,2,4,32]{3,2,1,0:T(4,128)S(1)} %bitcast.118, f32[2,2,4,32]{3,2,1,0:T(4,128)S(1)} %fusion.16, f32[]{:T(128)} %bitcast.98), kind=kLoop, calls=%fused_computation.89 | loop fusion | flops 64 | bytes 388 | tf_op jit(solution)/shard_map/div | solution.py:147
  31.3 0.4 %fusion.10 = bf16[4,512]{1,0:T(4,128)(2,1)S(1)} fusion(f32[4,128,512]{1,2,0:T(8,128)S(1)} %copy.12, f32[4,128]{1,0:T(4,128)S(1)} %add.120, f32[4,128]{1,0:T(4,128)S(1)} %mul.143), kind=kLoop, calls=%fused_computation.41 | loop fusion | flops 1046528 | bytes 1056768 | tf_op jit(solution)/shard_map/reduce_sum | solution.py:123
  31.6 1.0 %convert_reduce_fusion = f32[512,768]{1,0:T(8,128)S(1)} fusion(bf16[4,128,768]{2,1,0:T(8,128)(2,1)S(1)} %copy-done.1, f32[4,128,512]{1,2,0:T(8,128)S(1)} %copy.12, f32[4,128]{1,0:T(4,128)S(1)} %add.120, f32[4,128]{1,0:T(4,128)S(1)} %mul.143), kind=kOutput, calls=%fused_computation | convolution fusion | flops 407764992 | bytes 3411968 | tf_op jit(solution)/shard_map/dot_general | solution.py:119
  32.6 0.0 copy-start
  32.7 0.4 %multiply_reduce_fusion = f32[512]{0:T(512)S(1)} fusion(f32[512,768]{1,0:T(8,128)S(1)} %convert_reduce_fusion, f32[512]{0:T(512)S(1)} %broadcast_add_fusion, bf16[512,768]{1,0:T(8,128)(2,1)S(1)} %get-tuple-element.10), kind=kLoop, calls=%fused_computation.12 | loop fusion | flops 1965568 | bytes 2363392 | tf_op jit(solution)/shard_map/reduce_sum | solution.py:12
  33.1 1.2 %multiply_convert_fusion = bf16[512,768]{1,0:T(8,128)(2,1)} fusion(f32[512]{0:T(512)S(1)} %add_rsqrt_fusion, f32[512,768]{1,0:T(8,128)S(1)} %convert_reduce_fusion, f32[512]{0:T(512)S(1)} %broadcast_add_fusion, bf16[512,768]{1,0:T(8,128)(2,1)S(1)} %get-tuple-element.10), kind=kLoop, calls=%fused_computation.11 | loop fusion | flops 1966080 | bytes 3149824 | tf_op jit(solution)/shard_map/convert_element_type | solution.py:144
  (43 shorter events, 0.5 us)
Async XLA Ops:
  0.6 10.5 %copy-start.2 = (bf16[32,768]{1,0:T(8,128)(2,1)S(1)}, bf16[32,768]{1,0:T(8,128)(2,1)}, u32[]{:S(2)}) copy-start(bf16[32,768]{1,0:T(8,128)(2,1)} %param.4) | copy-start | bytes 147460
  0.6 7.9 %copy-start.3 = (s32[32]{0:T(128)S(1)}, s32[32]{0:T(128)}, u32[]{:S(2)}) copy-start(s32[32]{0:T(128)} %param.5) | copy-start | bytes 388
  0.6 8.6 %collective-permute-start = (bf16[32,768]{1,0:T(8,128)(2,1)}, bf16[32,768]{1,0:T(8,128)(2,1)S(1)}, u32[]{:S(2)}, u32[]{:S(2)}) collective-permute-start(bf16[32,768]{1,0:T(8,128)(2,1)} %param.4), channel_id=1, source_target_pairs={{0,4},{4,8},{8,12},{12,0},{1,5},{5,9},{9,13},{13,1},{2,6},{6,10},{... | collective-permute-start | bytes 147464 | tf_op jit(solution)/shard_map/ppermute | solution.py:23
  3.7 5.5 %collective-permute-start.2 = (bf16[32,768]{1,0:T(8,128)(2,1)}, bf16[32,768]{1,0:T(8,128)(2,1)S(1)}, u32[]{:S(2)}, u32[]{:S(2)}) collective-permute-start(bf16[32,768]{1,0:T(8,128)(2,1)} %param.4), channel_id=1, source_target_pairs={{0,12},{4,0},{8,4},{12,8},{1,13},{5,1},{9,5},{13,9},{2,14},{6,2},{... | collective-permute-start | bytes 147464 | tf_op jit(solution)/shard_map/ppermute | solution.py:23
  5.8 5.3 %collective-permute-start.1 = (bf16[32,768]{1,0:T(8,128)(2,1)}, bf16[32,768]{1,0:T(8,128)(2,1)S(1)}, u32[]{:S(2)}, u32[]{:S(2)}) collective-permute-start(bf16[32,768]{1,0:T(8,128)(2,1)} %param.4), channel_id=1, source_target_pairs={{0,8},{4,12},{8,0},{12,4},{1,9},{5,13},{9,1},{13,5},{2,10},{6,14},... | collective-permute-start | bytes 147464 | tf_op jit(solution)/shard_map/ppermute | solution.py:23
  11.2 6.2 %collective-permute-start.3 = (bf16[144,768]{1,0:T(8,128)(2,1)S(1)}, bf16[144,768]{1,0:T(8,128)(2,1)S(1)}, u32[]{:S(2)}, u32[]{:S(2)}) collective-permute-start(bf16[144,768]{1,0:T(8,128)(2,1)S(1)} %get-tuple-element.14), channel_id=1, source_target_pairs={{0,2},{2,0},{1,3},{3,1},{4,6},{6,4},{5,7},{7,5},{8,10},{10,8},{9,1... | collective-permute-start | bytes 663560 | tf_op jit(solution)/shard_map/ppermute | solution.py:23
  17.7 1.9 %collective-permute-start.4 = (bf16[2,144,768]{2,1,0:T(8,128)(2,1)S(1)}, bf16[2,144,768]{2,1,0:T(8,128)(2,1)S(1)}, u32[]{:S(2)}, u32[]{:S(2)}) collective-permute-start(bf16[2,144,768]{2,1,0:T(8,128)(2,1)S(1)} %get-tuple-element.12), channel_id=1, source_target_pairs={{0,1},{1,0},{2,3},{3,2},{4,5},{5,4},{6,7},{7,6},{8,9},{9,8},{10,11... | collective-permute-start | bytes 1327112 | tf_op jit(solution)/shard_map/ppermute | solution.py:23
  21.8 5.6 %collective-permute-start.6 = (f32[3,2,2,4,32]{4,3,2,1,0:T(4,128)S(1)}, f32[3,2,2,4,32]{4,3,2,1,0:T(4,128)S(1)}, u32[]{:S(2)}, u32[]{:S(2)}) collective-permute-start(f32[3,2,2,4,32]{4,3,2,1,0:T(4,128)S(1)} %get-tuple-element.20), channel_id=1, source_target_pairs={{0,8},{4,12},{8,0},{12,4},{1,9},{5,13},{9,1},{13,5},{2,10},{6,14},... | collective-permute-start | bytes 18440 | tf_op jit(solution)/shard_map/ppermute | solution.py:23
  22.5 5.6 %collective-permute-start.5 = (f32[3,2,2,4,32]{4,3,2,1,0:T(4,128)S(1)}, f32[3,2,2,4,32]{4,3,2,1,0:T(4,128)S(1)}, u32[]{:S(2)}, u32[]{:S(2)}) collective-permute-start(f32[3,2,2,4,32]{4,3,2,1,0:T(4,128)S(1)} %get-tuple-element.20), channel_id=1, source_target_pairs={{0,4},{4,8},{8,12},{12,0},{1,5},{5,9},{9,13},{13,1},{2,6},{6,10},{... | collective-permute-start | bytes 18440 | tf_op jit(solution)/shard_map/ppermute | solution.py:23
  25.2 3.8 %collective-permute-start.7 = (f32[3,2,2,4,32]{4,3,2,1,0:T(4,128)S(1)}, f32[3,2,2,4,32]{4,3,2,1,0:T(4,128)S(1)}, u32[]{:S(2)}, u32[]{:S(2)}) collective-permute-start(f32[3,2,2,4,32]{4,3,2,1,0:T(4,128)S(1)} %get-tuple-element.20), channel_id=1, source_target_pairs={{0,12},{4,0},{8,4},{12,8},{1,13},{5,1},{9,5},{13,9},{2,14},{6,2},{... | collective-permute-start | bytes 18440 | tf_op jit(solution)/shard_map/ppermute | solution.py:23
  29.2 1.3 %collective-permute-start.8 = (f32[3,2,2,4,32]{4,3,2,1,0:T(4,128)S(1)}, f32[3,2,2,4,32]{4,3,2,1,0:T(4,128)S(1)}, u32[]{:S(2)}, u32[]{:S(2)}) collective-permute-start(f32[3,2,2,4,32]{4,3,2,1,0:T(4,128)S(1)} %get-tuple-element.16), channel_id=1, source_target_pairs={{0,1},{1,0},{2,3},{3,2},{4,5},{5,4},{6,7},{7,6},{8,9},{9,8},{10,11... | collective-permute-start | bytes 18440 | tf_op jit(solution)/shard_map/ppermute | solution.py:23
  29.7 1.9 %copy-start.1 = (bf16[4,128,768]{2,1,0:T(8,128)(2,1)S(1)}, bf16[4,128,768]{2,1,0:T(8,128)(2,1)}, u32[]{:S(2)}) copy-start(bf16[4,128,768]{2,1,0:T(8,128)(2,1)} %fusion.4) | copy-start | bytes 2359300
  32.6 1.7 %copy-start = (f32[512,768]{1,0:T(8,128)}, f32[512,768]{1,0:T(8,128)S(1)}, u32[]{:S(2)}) copy-start(f32[512,768]{1,0:T(8,128)S(1)} %convert_reduce_fusion) | copy-start | bytes 4718596

commit v22 on v18

--- a/solution.py
+++ b/solution.py
@@ -110,8 +110,7 @@
     log_sum = (stats[0] + jnp.log(stats[1])).reshape(-1)
 
     if n_rows * width * 2 <= (4 << 20):
-        grouped_rows = normalize(payload[:, :, :cent_rows].reshape(-1, width)).astype(jnp.bfloat16)
-        grouped_rows = grouped_rows.reshape(n_groups, -1, width)
+        grouped_rows = jnp.concatenate(halves, axis=0).reshape(n_groups, -1, width)
         own_scores = jnp.concatenate([blocks_of_half[0] for blocks_of_half in score_blocks], axis=0)
         grouped_resp = (
             weight_float[:, None] * jnp.exp(own_scores - log_sum[:, None])

time: 34.5 us -> 36.6 us (1.061)
  waiting for transfers between devices: 7.54 us -> 9.17 us
  other arithmetic: 9.19 us -> 9.62 us
    ppermute x9, waiting for transfers between devices: 7.54 us -> 9.17 us  [gather_stage(): lax.ppermute(value, name, [(j, (j + q) % size) for j in range(size)])]
    convert_element_type x1 -> x0, other arithmetic: 1.04 us -> none  [shards(): normalize(payload[:, :, :cent_rows].reshape(-1, width)).astype(jnp.bfloat16)]
    concatenate x1, other arithmetic: 0.07 us -> 1.04 us  [shards(): jnp.concatenate([blocks_of_half[0] for blocks_of_half in score_blocks], a...]
    concatenate x0 -> x1, other arithmetic: none -> 0.93 us  [shards(): grouped_rows = jnp.concatenate(halves, axis=0).reshape(n_groups, -1, width)]
    reduce_sum x5 -> x4, other arithmetic: 2.72 us -> 2.49 us  [normalize(): jnp.sum(floats * floats, axis=-1, keepdims=True) + 1e-06]
  transfers between devices with their start and end apart: 9 -> 9, of which waited for: 6 -> 5; matrix products, arithmetic and copies ran while one was open for 18% -> 16% of each run, Pallas kernels for 0% -> 0%
where the time goes in v22:
time: 36.6 us; the launch traced here: 36.4 us
  starting transfers between devices  12.4 us (34%)
  other arithmetic  9.62 us (26%)
  waiting for transfers between devices  9.17 us (25%)
  matrix products  2.92 us (8%)
  between operations  1.62 us (4%)
  local copies, waits for them, and re-layouts  0.72 us (2%)
    ppermute x9, starting transfers between devices, gather_stage(): lax.ppermute(value, name, [(j, (j + q) % size) for j in range(size)])  12.4 us
    ppermute x9, waiting for transfers between devices, gather_stage(): lax.ppermute(value, name, [(j, (j + q) % size) for j in range(size)])  9.17 us
    reduce_sum x4, other arithmetic, normalize(): jnp.sum(floats * floats, axis=-1, keepdims=True) + 1e-06  2.49 us
    dot_general x4, matrix products, shards(): lax.dot_general(rows, cents, (((1,), (1,)), ((), ())), preferred_element_...  1.95 us
    convert_element_type x1, other arithmetic, shards(): score_cents = [lax.optimization_barrier(normalize(lax.dynamic_slice_in_di...  1.69 us
    convert_element_type x1, other arithmetic, shards(): renormed = normalize(moved).astype(jnp.bfloat16)  1.25 us
    concatenate x1, other arithmetic, shards(): jnp.concatenate([blocks_of_half[0] for blocks_of_half in score_blocks], a...  1.04 us
    dot_general x1, matrix products, shards(): lax.dot_general(grouped_resp, grouped_rows, (((1,), (1,)), ((0,), (0,))),...  0.97 us
  transfers between devices with their start and end apart: 9, of which 5 were waited for; matrix products, arithmetic and copies ran while one was open for 16% of the time, Pallas kernels for 0%

profile of v22, /device:TPU:0, one launch (start us, length us, event | category | flops | bytes accessed | tf_op | source)
XLA Modules:
  0.0 36.4 jit_solution(16583280797180318494)
XLA Ops:
  0.6 0.0 copy-start.3
  0.6 3.1 %collective-permute-start = (bf16[32,768]{1,0:T(8,128)(2,1)}, bf16[32,768]{1,0:T(8,128)(2,1)S(1)}, u32[]{:S(2)}, u32[]{:S(2)}) collective-permute-start(bf16[32,768]{1,0:T(8,128)(2,1)} %param.4), channel_id=1, source_target_pairs={{0,4},{4,8},{8,12},{12,0},{1,5},{5,9},{9,13},{13,1},{2,6},{6,10},{... | collective-permute-start | bytes 147464 | tf_op jit(solution)/shard_map/ppermute | solution.py:23
  3.7 2.1 %collective-permute-start.2 = (bf16[32,768]{1,0:T(8,128)(2,1)}, bf16[32,768]{1,0:T(8,128)(2,1)S(1)}, u32[]{:S(2)}, u32[]{:S(2)}) collective-permute-start(bf16[32,768]{1,0:T(8,128)(2,1)} %param.4), channel_id=1, source_target_pairs={{0,12},{4,0},{8,4},{12,8},{1,13},{5,1},{9,5},{13,9},{2,14},{6,2},{... | collective-permute-start | bytes 147464 | tf_op jit(solution)/shard_map/ppermute | solution.py:23
  5.8 0.9 %collective-permute-start.1 = (bf16[32,768]{1,0:T(8,128)(2,1)}, bf16[32,768]{1,0:T(8,128)(2,1)S(1)}, u32[]{:S(2)}, u32[]{:S(2)}) collective-permute-start(bf16[32,768]{1,0:T(8,128)(2,1)} %param.4), channel_id=1, source_target_pairs={{0,8},{4,12},{8,0},{12,4},{1,9},{5,13},{9,1},{13,5},{2,10},{6,14},... | collective-permute-start | bytes 147464 | tf_op jit(solution)/shard_map/ppermute | solution.py:23
  6.8 1.7 %fusion.2 = (f32[512]{0:T(512)S(1)}, f32[512]{0:T(512)S(1)}) fusion(bf16[2048,768]{1,0:T(8,128)(2,1)} %param.6, s32[]{:T(128)S(6)} %select_n.20, s32[]{:T(128)S(6)} %select_n.18), kind=kLoop, calls=%fused_computation.7 | loop fusion | flops 2358272 | bytes 1576968 | tf_op jit(solution)/shard_map/reduce_sum | solution.py:12
  9.2 0.0 collective-permute-done
  9.2 0.0 collective-permute-done.2
  9.2 1.9 %collective-permute-done.1 = bf16[32,768]{1,0:T(8,128)(2,1)S(1)} collective-permute-done((bf16[32,768]{1,0:T(8,128)(2,1)}, bf16[32,768]{1,0:T(8,128)(2,1)S(1)}, u32[]{:S(2)}, u32[]{:S(2)}) %collective-permute-start.1) | collective-permute-done | bytes 49184 | tf_op jit(solution)/shard_map/ppermute | solution.py:23
  11.2 1.6 %collective-permute-start.3 = (bf16[144,768]{1,0:T(8,128)(2,1)S(1)}, bf16[144,768]{1,0:T(8,128)(2,1)S(1)}, u32[]{:S(2)}, u32[]{:S(2)}) collective-permute-start(bf16[144,768]{1,0:T(8,128)(2,1)S(1)} %get-tuple-element.14), channel_id=1, source_target_pairs={{0,2},{2,0},{1,3},{3,1},{4,6},{6,4},{5,7},{7,5},{8,10},{10,8},{9,1... | collective-permute-start | bytes 663560 | tf_op jit(solution)/shard_map/ppermute | solution.py:23
  12.8 1.7 %fusion.3 = (bf16[512,768]{1,0:T(8,128)(2,1)S(1)}, bf16[512,768]{1,0:T(8,128)(2,1)S(1)}) fusion(f32[512]{0:T(512)S(1)} %get-tuple-element.33, bf16[2048,768]{1,0:T(8,128)(2,1)} %param.6, s32[]{:T(128)S(6)} %select_n.20, f32[512]{0:T(512)S(1)} %get-tuple-element.34, s32[]{:T(128)S(6)} %select_n.18), kind=kLoop, calls=%fused_computation.8 | loop fusion | flops 2359296 | bytes 3149832 | tf_op jit(solution)/shard_map/convert_element_type | solution.py:76
  14.5 2.9 %collective-permute-done.3 = bf16[144,768]{1,0:T(8,128)(2,1)S(1)} collective-permute-done((bf16[144,768]{1,0:T(8,128)(2,1)S(1)}, bf16[144,768]{1,0:T(8,128)(2,1)S(1)}, u32[]{:S(2)}, u32[]{:S(2)}) %collective-permute-start.3) | collective-permute-done | bytes 221216 | tf_op jit(solution)/shard_map/ppermute | solution.py:23
  17.4 0.1 fusion.29
  17.5 0.2 multiply_reduce_fusion.2
  17.6 0.1 collective-permute-start.4
  17.7 0.1 slice_convert_fusion.1
  17.8 1.7 %collective-permute-done.4 = bf16[2,144,768]{2,1,0:T(8,128)(2,1)S(1)} collective-permute-done((bf16[2,144,768]{2,1,0:T(8,128)(2,1)S(1)}, bf16[2,144,768]{2,1,0:T(8,128)(2,1)S(1)}, u32[]{:S(2)}, u32[]{:S(2)}) %collective-permute-start.4) | collective-permute-done | bytes 442400 | tf_op jit(solution)/shard_map/ppermute | solution.py:23
  19.5 0.2 multiply_reduce_fusion.1
  19.6 0.1 slice_convert_fusion
  19.7 0.1 fusion.4
  19.9 0.5 %fusion.33 = (f32[256]{0:T(256)S(1)}, f32[256,512]{1,0:T(8,128)S(1)}) fusion(f32[]{:T(128)} %bitcast.99, bf16[256,768]{1,0:T(8,128)(2,1)S(1)} %get-tuple-element.31, bf16[512,768]{1,0:T(8,128)(2,1)S(1)} %get-tuple-element.9), kind=kOutput, calls=%fused_computation.92 | convolution fusion | flops 201588480 | bytes 1704964 | tf_op jit(solution)/shard_map/dot_general | solution.py:87
  20.4 0.5 %fusion.35 = (f32[256]{0:T(256)S(1)}, f32[256,512]{1,0:T(8,128)S(1)}) fusion(f32[]{:T(128)} %bitcast.101, bf16[256,768]{1,0:T(8,128)(2,1)S(1)} %get-tuple-element.32, bf16[512,768]{1,0:T(8,128)(2,1)S(1)} %get-tuple-element.9), kind=kOutput, calls=%fused_computation.94 | convolution fusion | flops 201588480 | bytes 1704964 | tf_op jit(solution)/shard_map/dot_general | solution.py:87
  20.8 0.5 %fusion.34 = (f32[256]{0:T(256)S(1)}, f32[256,512]{1,0:T(8,128)S(1)}) fusion(f32[]{:T(128)} %bitcast.97, bf16[256,768]{1,0:T(8,128)(2,1)S(1)} %get-tuple-element.32, bf16[512,768]{1,0:T(8,128)(2,1)S(1)} %get-tuple-element.10), kind=kOutput, calls=%fused_computation.93 | convolution fusion | flops 201588480 | bytes 1704964 | tf_op jit(solution)/shard_map/dot_general | solution.py:87
  21.3 0.5 %fusion.32 = (f32[256]{0:T(256)S(1)}, f32[256,512]{1,0:T(8,128)S(1)}) fusion(f32[]{:T(128)} %bitcast.100, bf16[256,768]{1,0:T(8,128)(2,1)S(1)} %get-tuple-element.31, bf16[512,768]{1,0:T(8,128)(2,1)S(1)} %get-tuple-element.10), kind=kOutput, calls=%fused_computation.91 | convolution fusion | flops 201588480 | bytes 1704964 | tf_op jit(solution)/shard_map/dot_general | solution.py:87
  21.9 0.3 exponential_reduce_fusion.2
  22.2 0.3 exponential_reduce_fusion
  22.5 0.1 stack_reshape.7
  22.6 0.1 stack_reshape.6
  22.7 0.7 %collective-permute-start.6 = (f32[3,2,2,4,32]{4,3,2,1,0:T(4,128)S(1)}, f32[3,2,2,4,32]{4,3,2,1,0:T(4,128)S(1)}, u32[]{:S(2)}, u32[]{:S(2)}) collective-permute-start(f32[3,2,2,4,32]{4,3,2,1,0:T(4,128)S(1)} %get-tuple-element.20), channel_id=1, source_target_pairs={{0,8},{4,12},{8,0},{12,4},{1,9},{5,13},{9,1},{13,5},{2,10},{6,14},... | collective-permute-start | bytes 18440 | tf_op jit(solution)/shard_map/ppermute | solution.py:23
  23.4 1.0 %pad_maximum_fusion = f32[512,512]{1,0:T(8,128)} fusion(f32[256,512]{1,0:T(8,128)S(1)} %get-tuple-element.24, f32[256,512]{1,0:T(8,128)S(1)} %get-tuple-element.28), kind=kLoop, calls=%fused_computation.16 | loop fusion | flops 262144 | bytes 2097152 | tf_op jit(solution)/shard_map/concatenate | solution.py:114
  24.4 2.7 %collective-permute-start.5 = (f32[3,2,2,4,32]{4,3,2,1,0:T(4,128)S(1)}, f32[3,2,2,4,32]{4,3,2,1,0:T(4,128)S(1)}, u32[]{:S(2)}, u32[]{:S(2)}) collective-permute-start(f32[3,2,2,4,32]{4,3,2,1,0:T(4,128)S(1)} %get-tuple-element.20), channel_id=1, source_target_pairs={{0,4},{4,8},{8,12},{12,0},{1,5},{5,9},{9,13},{13,1},{2,6},{6,10},{... | collective-permute-start | bytes 18440 | tf_op jit(solution)/shard_map/ppermute | solution.py:23
  27.1 1.1 %collective-permute-start.7 = (f32[3,2,2,4,32]{4,3,2,1,0:T(4,128)S(1)}, f32[3,2,2,4,32]{4,3,2,1,0:T(4,128)S(1)}, u32[]{:S(2)}, u32[]{:S(2)}) collective-permute-start(f32[3,2,2,4,32]{4,3,2,1,0:T(4,128)S(1)} %get-tuple-element.20), channel_id=1, source_target_pairs={{0,12},{4,0},{8,4},{12,8},{1,13},{5,1},{9,5},{13,9},{2,14},{6,2},{... | collective-permute-start | bytes 18440 | tf_op jit(solution)/shard_map/ppermute | solution.py:23
  28.3 0.0 collective-permute-done.6
  28.3 1.8 %collective-permute-done.5 = f32[3,2,2,4,32]{4,3,2,1,0:T(4,128)S(1)} collective-permute-done((f32[3,2,2,4,32]{4,3,2,1,0:T(4,128)S(1)}, f32[3,2,2,4,32]{4,3,2,1,0:T(4,128)S(1)}, u32[]{:S(2)}, u32[]{:S(2)}) %collective-permute-start.5) | collective-permute-done | bytes 6176 | tf_op jit(solution)/shard_map/ppermute | solution.py:23
  30.1 0.9 %collective-permute-done.7 = f32[3,2,2,4,32]{4,3,2,1,0:T(4,128)S(1)} collective-permute-done((f32[3,2,2,4,32]{4,3,2,1,0:T(4,128)S(1)}, f32[3,2,2,4,32]{4,3,2,1,0:T(4,128)S(1)}, u32[]{:S(2)}, u32[]{:S(2)}) %collective-permute-start.7) | collective-permute-done | bytes 6176 | tf_op jit(solution)/shard_map/ppermute | solution.py:23
  31.2 0.1 collective-permute-start.8
  31.2 0.9 %pad_maximum_fusion.1 = bf16[512,768]{1,0:T(8,128)(2,1)} fusion(bf16[256,768]{1,0:T(8,128)(2,1)S(1)} %get-tuple-element.31, bf16[256,768]{1,0:T(8,128)(2,1)S(1)} %get-tuple-element.32), kind=kLoop, calls=%fused_computation.18 | loop fusion | flops 1572864 | bytes 1572864 | tf_op jit(solution)/shard_map/concatenate | solution.py:113
  32.2 0.3 copy.12
  32.5 0.0 copy-start.2
  32.5 0.0 collective-permute-done.8
  32.6 0.1 mul.129
  32.7 0.1 add.111
  32.8 0.5 %fusion.25 = f32[32]{0:T(128)} fusion(f32[2,2,4,32]{3,2,1,0:T(4,128)S(1)} %bitcast.117, s32[32]{0:T(128)S(1)} %copy-done.4, f32[]{:T(128)} %bitcast.98), kind=kLoop, calls=%fused_computation.83 | loop fusion | flops 96 | bytes 388 | tf_op jit(solution)/shard_map/div | solution.py:146
  33.3 0.4 fusion.8
  33.7 1.0 %convert_reduce_fusion = f32[512,768]{1,0:T(8,128)S(1)} fusion(bf16[4,128,768]{2,1,0:T(8,128)(2,1)S(1)} %bitcast.106, f32[4,128,512]{1,2,0:T(8,128)S(1)} %copy.12, f32[4,128]{1,0:T(4,128)S(1)} %add.111, f32[4,128]{1,0:T(4,128)S(1)} %mul.129), kind=kOutput, calls=%fused_computation | convolution fusion | flops 407764992 | bytes 3411968 | tf_op jit(solution)/shard_map/dot_general | solution.py:118
  34.7 0.0 copy-start
  34.7 0.4 %multiply_reduce_fusion = f32[512]{0:T(512)S(1)} fusion(f32[512,768]{1,0:T(8,128)S(1)} %convert_reduce_fusion, f32[512]{0:T(512)S(1)} %broadcast_add_fusion, bf16[512,768]{1,0:T(8,128)(2,1)S(1)} %get-tuple-element.10), kind=kLoop, calls=%fused_computation.10 | loop fusion | flops 1965568 | bytes 2363392 | tf_op jit(solution)/shard_map/reduce_sum | solution.py:12
  35.2 1.2 %multiply_convert_fusion = bf16[512,768]{1,0:T(8,128)(2,1)} fusion(f32[512]{0:T(512)S(1)} %add_rsqrt_fusion, f32[512,768]{1,0:T(8,128)S(1)} %convert_reduce_fusion, f32[512]{0:T(512)S(1)} %broadcast_add_fusion, bf16[512,768]{1,0:T(8,128)(2,1)S(1)} %get-tuple-element.10), kind=kLoop, calls=%fused_computation.9 | loop fusion | flops 1966080 | bytes 3149824 | tf_op jit(solution)/shard_map/convert_element_type | solution.py:143
  36.4 0.0 copy-done
  (41 shorter events, 0.5 us)
Async XLA Ops:
  0.6 10.5 %copy-start.3 = (bf16[32,768]{1,0:T(8,128)(2,1)S(1)}, bf16[32,768]{1,0:T(8,128)(2,1)}, u32[]{:S(2)}) copy-start(bf16[32,768]{1,0:T(8,128)(2,1)} %param.4) | copy-start | bytes 147460
  0.6 7.9 %copy-start.4 = (s32[32]{0:T(128)S(1)}, s32[32]{0:T(128)}, u32[]{:S(2)}) copy-start(s32[32]{0:T(128)} %param.5) | copy-start | bytes 388
  0.6 8.6 %collective-permute-start = (bf16[32,768]{1,0:T(8,128)(2,1)}, bf16[32,768]{1,0:T(8,128)(2,1)S(1)}, u32[]{:S(2)}, u32[]{:S(2)}) collective-permute-start(bf16[32,768]{1,0:T(8,128)(2,1)} %param.4), channel_id=1, source_target_pairs={{0,4},{4,8},{8,12},{12,0},{1,5},{5,9},{9,13},{13,1},{2,6},{6,10},{... | collective-permute-start | bytes 147464 | tf_op jit(solution)/shard_map/ppermute | solution.py:23
  3.7 5.5 %collective-permute-start.2 = (bf16[32,768]{1,0:T(8,128)(2,1)}, bf16[32,768]{1,0:T(8,128)(2,1)S(1)}, u32[]{:S(2)}, u32[]{:S(2)}) collective-permute-start(bf16[32,768]{1,0:T(8,128)(2,1)} %param.4), channel_id=1, source_target_pairs={{0,12},{4,0},{8,4},{12,8},{1,13},{5,1},{9,5},{13,9},{2,14},{6,2},{... | collective-permute-start | bytes 147464 | tf_op jit(solution)/shard_map/ppermute | solution.py:23
  5.8 5.3 %collective-permute-start.1 = (bf16[32,768]{1,0:T(8,128)(2,1)}, bf16[32,768]{1,0:T(8,128)(2,1)S(1)}, u32[]{:S(2)}, u32[]{:S(2)}) collective-permute-start(bf16[32,768]{1,0:T(8,128)(2,1)} %param.4), channel_id=1, source_target_pairs={{0,8},{4,12},{8,0},{12,4},{1,9},{5,13},{9,1},{13,5},{2,10},{6,14},... | collective-permute-start | bytes 147464 | tf_op jit(solution)/shard_map/ppermute | solution.py:23
  11.2 6.2 %collective-permute-start.3 = (bf16[144,768]{1,0:T(8,128)(2,1)S(1)}, bf16[144,768]{1,0:T(8,128)(2,1)S(1)}, u32[]{:S(2)}, u32[]{:S(2)}) collective-permute-start(bf16[144,768]{1,0:T(8,128)(2,1)S(1)} %get-tuple-element.14), channel_id=1, source_target_pairs={{0,2},{2,0},{1,3},{3,1},{4,6},{6,4},{5,7},{7,5},{8,10},{10,8},{9,1... | collective-permute-start | bytes 663560 | tf_op jit(solution)/shard_map/ppermute | solution.py:23
  17.6 1.9 %collective-permute-start.4 = (bf16[2,144,768]{2,1,0:T(8,128)(2,1)S(1)}, bf16[2,144,768]{2,1,0:T(8,128)(2,1)S(1)}, u32[]{:S(2)}, u32[]{:S(2)}) collective-permute-start(bf16[2,144,768]{2,1,0:T(8,128)(2,1)S(1)} %get-tuple-element.12), channel_id=1, source_target_pairs={{0,1},{1,0},{2,3},{3,2},{4,5},{5,4},{6,7},{7,6},{8,9},{9,8},{10,11... | collective-permute-start | bytes 1327112 | tf_op jit(solution)/shard_map/ppermute | solution.py:23
  22.7 5.6 %collective-permute-start.6 = (f32[3,2,2,4,32]{4,3,2,1,0:T(4,128)S(1)}, f32[3,2,2,4,32]{4,3,2,1,0:T(4,128)S(1)}, u32[]{:S(2)}, u32[]{:S(2)}) collective-permute-start(f32[3,2,2,4,32]{4,3,2,1,0:T(4,128)S(1)} %get-tuple-element.20), channel_id=1, source_target_pairs={{0,8},{4,12},{8,0},{12,4},{1,9},{5,13},{9,1},{13,5},{2,10},{6,14},... | collective-permute-start | bytes 18440 | tf_op jit(solution)/shard_map/ppermute | solution.py:23
  24.4 7.7 %copy-start.1 = (f32[512,512]{1,0:T(8,128)S(1)}, f32[512,512]{1,0:T(8,128)}, u32[]{:S(2)}) copy-start(f32[512,512]{1,0:T(8,128)} %pad_maximum_fusion) | copy-start | bytes 3145732
  24.4 5.6 %collective-permute-start.5 = (f32[3,2,2,4,32]{4,3,2,1,0:T(4,128)S(1)}, f32[3,2,2,4,32]{4,3,2,1,0:T(4,128)S(1)}, u32[]{:S(2)}, u32[]{:S(2)}) collective-permute-start(f32[3,2,2,4,32]{4,3,2,1,0:T(4,128)S(1)} %get-tuple-element.20), channel_id=1, source_target_pairs={{0,4},{4,8},{8,12},{12,0},{1,5},{5,9},{9,13},{13,1},{2,6},{6,10},{... | collective-permute-start | bytes 18440 | tf_op jit(solution)/shard_map/ppermute | solution.py:23
  27.1 3.8 %collective-permute-start.7 = (f32[3,2,2,4,32]{4,3,2,1,0:T(4,128)S(1)}, f32[3,2,2,4,32]{4,3,2,1,0:T(4,128)S(1)}, u32[]{:S(2)}, u32[]{:S(2)}) collective-permute-start(f32[3,2,2,4,32]{4,3,2,1,0:T(4,128)S(1)} %get-tuple-element.20), channel_id=1, source_target_pairs={{0,12},{4,0},{8,4},{12,8},{1,13},{5,1},{9,5},{13,9},{2,14},{6,2},{... | collective-permute-start | bytes 18440 | tf_op jit(solution)/shard_map/ppermute | solution.py:23
  31.2 1.4 %collective-permute-start.8 = (f32[3,2,2,4,32]{4,3,2,1,0:T(4,128)S(1)}, f32[3,2,2,4,32]{4,3,2,1,0:T(4,128)S(1)}, u32[]{:S(2)}, u32[]{:S(2)}) collective-permute-start(f32[3,2,2,4,32]{4,3,2,1,0:T(4,128)S(1)} %get-tuple-element.16), channel_id=1, source_target_pairs={{0,1},{1,0},{2,3},{3,2},{4,5},{5,4},{6,7},{7,6},{8,9},{9,8},{10,11... | collective-permute-start | bytes 18440 | tf_op jit(solution)/shard_map/ppermute | solution.py:23
  32.5 1.2 %copy-start.2 = (bf16[512,768]{1,0:T(8,128)(2,1)S(1)}, bf16[512,768]{1,0:T(8,128)(2,1)}, u32[]{:S(2)}) copy-start(bf16[512,768]{1,0:T(8,128)(2,1)} %pad_maximum_fusion.1) | copy-start | bytes 2359300
  34.7 1.7 %copy-start = (f32[512,768]{1,0:T(8,128)}, f32[512,768]{1,0:T(8,128)S(1)}, u32[]{:S(2)}) copy-start(f32[512,768]{1,0:T(8,128)S(1)} %convert_reduce_fusion) | copy-start | bytes 4718596
